TPU v7x, 32 devices: a whole 2x2x4 slice. The times are simulated.
32 devices in a mesh: slab: 2 (over x), run: 2 (over core), tx: 8 (over z, y).
Axes of the slice: x: 2, y: 2, z: 4, core: 2. Of those that a mesh axis runs over, the one named last changes fastest.
Arguments:
- snapshots: bfloat16 [1024, 128, 512], P(('slab', 'tx'), None, 'run'), parts along dimension 0, may hold values from -60 to 60, as said below
- coefficient: float32 [1024, 128], P(('slab', 'tx')), parts along dimension 0, may hold values from 0.02 to 0.2
- start_first: int32 [512, 128], replicated, may hold values from -4 to 4
- start_merge: int32 [256, 128], replicated, may hold values from -4 to 4
Outputs:
- modes: float32 [1024, 128, 128], P(('slab', 'tx'), None, 'run'), parts along dimension 0
There are 2 independent parts, one for each index of `slab`. A program takes and returns all parts, laid end to end along the dimension named above; an argument that names none is the same for every part. Nothing has to cross between parts.
Inputs may be any that keep to these rules, and one draw needn't show every extreme that they name: `snapshots`: snapshot values are real-valued and bounded.
All inputs are finite; a program needn't handle non-finite values.
Results may differ from a plain program's by a relative error of at most 0.0003.
Values may be sent and summed in bfloat16 or wider, within the bound.
No kernel may reach another device: no remote copies, remote signals or barrier semaphores. Data moves between devices by JAX's collectives and lax.ppermute only.
A program may use at most 128 MiB of HBM per device.

v0:
```python
import jax
import jax.numpy as jnp
from jax import lax
from jax.sharding import PartitionSpec as P
import functools
from jax.experimental import pallas as pl
from jax.experimental.pallas import tpu as pltpu

ITERS = 2


highest = lax.Precision.HIGHEST
high = lax.Precision.HIGH


def halos(block, axis, width):
    count = lax.axis_size(axis)
    forward = [(i, i + 1) for i in range(count - 1)]
    backward = [(target, source) for source, target in forward]
    low = lax.ppermute(lax.slice_in_dim(block, block.shape[0] - width, None, axis=0), axis, forward)
    high = lax.ppermute(lax.slice_in_dim(block, 0, width, axis=0), axis, backward)
    return low, high


def partner(block, axis, stride):
    count = lax.axis_size(axis)
    route = []
    for low in range(count):
        high = low | 1 << stride
        if high != low and high < count:
            route += [(low, high), (high, low)]
    return lax.ppermute(block, axis, route)


def tree_sum(value, axis):
    count = lax.axis_size(axis)
    if count & (count - 1):
        return lax.psum(value, axis)
    step = 1
    while step < count:
        route = [(i, i ^ step) for i in range(count)]
        value = value + lax.ppermute(value, axis, route)
        step *= 2
    return value


def fourth_order(values, axis_dim):
    length_kept = values.shape[axis_dim] - 4

    def shifted(offset):
        return lax.slice_in_dim(values, offset, offset + length_kept, axis=axis_dim)

    return (8.0 * (shifted(3) - shifted(1)) - (shifted(4) - shifted(0))) / 12.0


def flux_kernel(count, low_ref, high_ref, prev_ref, main_ref, next_ref, coef_ref, out_ref):
    i = pl.program_id(0)
    above = jnp.where(i == 0, low_ref[...], prev_ref[-2:])
    below = jnp.where(i == count - 1, high_ref[...], next_ref[:2])
    rows = jnp.concatenate([above, main_ref[...], below], axis=0).astype(jnp.float32)
    squared = 0.5 * jnp.square(rows)
    along_rows = fourth_order(squared, 0)
    mid = squared[2:-2]
    cols = mid.shape[1]
    ids = lax.broadcasted_iota(jnp.int32, mid.shape, 1)

    def shift(offset):
        moved = pltpu.roll(mid, (-offset) % cols, 1)
        inside = (ids + offset >= 0) & (ids + offset < cols)
        return jnp.where(inside, moved, 0.0)

    along_cols = (8.0 * (shift(1) - shift(-1)) - (shift(2) - shift(-2))) / 12.0
    central = rows[2:-2]
    out_ref[...] = central - coef_ref[...][:, :, None] * (along_rows + along_cols)


def fluxes(low, block, high, coefficient):
    nx, ny, ns = block.shape
    bx = 8 if nx % 8 == 0 else nx
    count = nx // bx

    def spec(index):
        return pl.BlockSpec((bx, ny, ns), index)

    return pl.pallas_call(
        functools.partial(flux_kernel, count),
        grid=(count,),
        in_specs=[
            pl.BlockSpec(low.shape, lambda i: (0, 0, 0)),
            pl.BlockSpec(high.shape, lambda i: (0, 0, 0)),
            spec(lambda i: (jnp.maximum(i - 1, 0), 0, 0)),
            spec(lambda i: (i, 0, 0)),
            spec(lambda i: (jnp.minimum(i + 1, count - 1), 0, 0)),
            pl.BlockSpec((bx, ny), lambda i: (i, 0)),
        ],
        out_specs=spec(lambda i: (i, 0, 0)),
        out_shape=jax.ShapeDtypeStruct((nx, ny, ns), jnp.float32),
    )(low, high, block, block, block, coefficient)


def gram_schmidt_kernel(rows_ref, out_ref, work):
    count, width = rows_ref.shape
    blocks = count // 8
    group = 4 if blocks % 4 == 0 else 1
    work[...] = rows_ref[...]
    for first in range(0, blocks, group):

        def sweep(block, carry, first=first):
            base = pl.multiple_of(block * 8, 8)
            for lane_row in range(8):
                j = base + lane_row
                vector = work[pl.ds(j, 1), :]
                inverse = 1.0 / jnp.sum(vector * vector, axis=1, keepdims=True)
                for i in range(first, blocks):
                    rows = work[i * 8:(i + 1) * 8, :]
                    weight = jnp.sum(rows * vector, axis=1, keepdims=True) * inverse
                    ids = lax.broadcasted_iota(jnp.int32, weight.shape, 0) + i * 8
                    weight = jnp.where(ids > j, weight, 0.0)
                    work[i * 8:(i + 1) * 8, :] = rows - weight * vector
            return carry

        lax.fori_loop(first, first + group, sweep, 0)
    for i in range(blocks):
        rows = work[i * 8:(i + 1) * 8, :]
        norm = jnp.sqrt(jnp.sum(rows * rows, axis=1, keepdims=True))
        out_ref[i * 8:(i + 1) * 8, :] = rows / norm


def orthonormal(matrix):
    rows = matrix.T
    done = pl.pallas_call(
        gram_schmidt_kernel,
        out_shape=jax.ShapeDtypeStruct(rows.shape, jnp.float32),
        scratch_shapes=[pltpu.VMEM(rows.shape, jnp.float32)],
    )(rows)
    return done.T


def iterate(gram_matrix, basis_set):
    def sweep(sweep_index, basis_set):
        return orthonormal(jnp.dot(gram_matrix, basis_set, precision=highest))

    return lax.fori_loop(0, ITERS, sweep, basis_set)


def cross_gram(left_rows, right_rows):
    return lax.dot_general(left_rows, right_rows, (((0,), (0,)), ((), ())), precision=high)


def self_gram(rows):
    upper = lax.reduce_precision(rows, exponent_bits=8, mantissa_bits=7)
    lower = lax.reduce_precision(rows - upper, exponent_bits=8, mantissa_bits=7)
    missing = jnp.sum(lower * lower, axis=0)
    return cross_gram(rows, rows) + jnp.diag(missing)


def on_device(snapshots, coefficient, start_first, start_merge):
    halo_low, halo_high = halos(snapshots, "tx", 2)
    rows_here = snapshots.shape[0] * snapshots.shape[1]
    order_size = snapshots.shape[2]
    modes_count = start_first.shape[1]
    share_count = modes_count // lax.axis_size("run")
    cells_total = rows_here * lax.axis_size("tx")
    member = lax.axis_index("run")
    is_first = member == 0
    own_start = lax.dynamic_slice_in_dim(start_first, member * order_size, order_size, 0)
    own_start = own_start.astype(jnp.float32)
    merge_start = start_merge.astype(jnp.float32)
    if lax.axis_size("tx") % 2:
        first_basis = orthonormal(own_start)
        merge_basis = orthonormal(merge_start)
    else:
        is_even = lax.axis_index("tx") % 2 == 0
        mine = orthonormal(jnp.where(is_even, own_start, merge_start))
        theirs = partner(mine, "tx", 0)
        first_basis = jnp.where(is_even, mine, theirs)
        merge_basis = jnp.where(is_even, theirs, mine)
    own_flux = fluxes(halo_low, snapshots, halo_high, coefficient).reshape(rows_here, order_size)
    own_gram = tree_sum(self_gram(own_flux), "tx") / cells_total
    own_basis = iterate(own_gram, first_basis)
    own_modes = jnp.dot(own_flux, own_basis, precision=high)
    other_modes = partner(own_modes, "run", 0)
    own_block = self_gram(own_modes)
    half_rows = rows_here // 2
    half_start = member * half_rows
    mixed_half = cross_gram(
        lax.dynamic_slice_in_dim(own_modes, half_start, half_rows, 0),
        lax.dynamic_slice_in_dim(other_modes, half_start, half_rows, 0),
    )
    mixed_half = jnp.where(is_first, mixed_half, mixed_half.T)
    summed = tree_sum(jnp.stack([own_block, mixed_half]), "tx")
    swapped = partner(summed, "run", 0)
    own_block = summed[0] / cells_total
    other_block = swapped[0] / cells_total
    mixed_block = (summed[1] + swapped[1]) / cells_total
    first_block = jnp.where(is_first, own_block, other_block)
    last_block = jnp.where(is_first, other_block, own_block)
    merge_gram = jnp.concatenate(
        [
            jnp.concatenate([first_block, mixed_block], axis=1),
            jnp.concatenate([mixed_block.T, last_block], axis=1),
        ],
        axis=0,
    )
    rotation = iterate(merge_gram, merge_basis)
    rotation_share = lax.dynamic_slice_in_dim(rotation, member * share_count, share_count, 1)
    top_rows = rotation_share[:modes_count]
    bottom_rows = rotation_share[modes_count:]
    own_rotation = jnp.where(is_first, top_rows, bottom_rows)
    other_rotation = jnp.where(is_first, bottom_rows, top_rows)
    result = jnp.dot(own_modes, own_rotation, precision=high) + jnp.dot(
        other_modes, other_rotation, precision=high
    )
    return result.reshape(snapshots.shape[0], snapshots.shape[1], share_count)


def solution(mesh):
    in_specs = (P(("slab", "tx"), None, "run"), P(("slab", "tx"), None), P(), P())
    out_specs = P(("slab", "tx"), None, "run")
    return jax.shard_map(
        on_device, mesh=mesh, in_specs=in_specs, out_specs=out_specs, check_vma=False
    )
```

profile of v0, /device:TPU:0, one launch (start us, length us, event | category | flops | bytes accessed | tf_op | source)
XLA Modules:
  0.0 189.5 jit_solution(3075044252267349272)
XLA Ops:
  0.0 1.0 fusion.29
  1.0 4.9 %collective-permute-start = (bf16[2,128,256]{2,1,0:T(8,128)(2,1)S(1)}, bf16[2,128,256]{2,1,0:T(8,128)(2,1)S(1)}, u32[]{:S(2)}, u32[]{:S(2)}) collective-permute-start(bf16[2,128,256]{2,1,0:T(8,128)(2,1)S(1)} %get-tuple-element.54), channel_id=1, source_target_pairs={{0,1},{1,2},{2,3},{3,4},{4,5},{5,6},{6,7},{8,9},{9,10},{10,11},{11... | collective-permute-start | bytes 393224 | tf_op jit(solution)/shard_map/ppermute | solution.py:20
  5.9 1.3 collective-permute-start.1
  7.2 1.4 collective-permute-done.low_ref
  8.7 4.1 %collective-permute-done.1.high_ref = bf16[2,128,256]{2,1,0:T(8,128)(2,1)S(1)} collective-permute-done((bf16[2,128,256]{2,1,0:T(8,128)(2,1)S(1)}, bf16[2,128,256]{2,1,0:T(8,128)(2,1)S(1)}, u32[]{:S(2)}, u32[]{:S(2)}) %collective-permute-start.1) | collective-permute-done | bytes 131104 | tf_op jit(solution)/shard_map/ppermute | solution.py:21
  12.8 0.7 copy-done.4
  13.4 13.7 %shard_map.46 = f32[64,128,256]{2,1,0:T(8,128)} custom-call(bf16[2,128,256]{2,1,0:T(8,128)(2,1)} %copy-done.3, bf16[2,128,256]{2,1,0:T(8,128)(2,1)} %copy-done.4, bf16[64,128,256]{2,1,0:T(8,128)(2,1)} %next_ref.1, bf16[64,128,256]{2,1,0:T(8,128)(2,1)} %next_ref.1, bf16[64,128,256]{2,1,0:T(8,128)(2,1)} %next_ref.1, f32[64,128]{1,0:T(8,128)} %coef_ref.1), custom_call_target="tpu_custom_call" | custom-call | tf_op jit(solution)/shard_map/pallas_call | solution.py:85
  27.1 5.0 %fusion.2 = f32[256]{0:T(256)S(1)} fusion(f32[64,128,256]{2,1,0:T(8,128)} %shard_map.46), kind=kLoop, calls=%fused_computation.4 | loop fusion | flops 10485504 | bytes 8389632 | tf_op jit(solution)/shard_map/reduce_sum | solution.py:153
  32.1 0.8 copy-done.1
  32.9 6.9 %fusion.10 = f32[256,256]{1,0:T(8,128)S(1)} fusion(f32[64,128,256]{2,1,0:T(8,128)S(1)} %copy-done.1, f32[256]{0:T(256)S(1)} %fusion.2), kind=kOutput, calls=%fused_computation.15 | convolution fusion | flops 3221422080 | bytes 8651776 | tf_op jit(solution)/shard_map/dot_general | solution.py:147
  39.8 2.5 %collective-permute-start.3 = (f32[256,256]{1,0:T(8,128)S(1)}, f32[256,256]{1,0:T(8,128)S(1)}, u32[]{:S(2)}, u32[]{:S(2)}) collective-permute-start(f32[256,256]{1,0:T(8,128)S(1)} %fusion.10), channel_id=1, source_target_pairs={{0,1},{1,0},{2,3},{3,2},{4,5},{5,4},{6,7},{7,6},{8,9},{9,8},{10,11... | collective-permute-start | bytes 786440 | tf_op jit(solution)/shard_map/ppermute | solution.py:42
  42.3 0.1 copy.16
  42.4 0.1 copy.6
  42.6 4.6 %collective-permute-done.3 = f32[256,256]{1,0:T(8,128)S(1)} collective-permute-done((f32[256,256]{1,0:T(8,128)S(1)}, f32[256,256]{1,0:T(8,128)S(1)}, u32[]{:S(2)}, u32[]{:S(2)}) %collective-permute-start.3) | collective-permute-done | bytes 262176 | tf_op jit(solution)/shard_map/ppermute | solution.py:42
  47.2 2.3 %collective-permute-start.4 = (f32[256,256]{1,0:T(8,128)S(1)}, f32[256,256]{1,0:T(8,128)S(1)}, u32[]{:S(2)}, u32[]{:S(2)}) collective-permute-start(f32[256,256]{1,0:T(8,128)S(1)} %add.54), channel_id=1, source_target_pairs={{0,2},{1,3},{2,0},{3,1},{4,6},{5,7},{6,4},{7,5},{8,10},{9,11},{10,... | collective-permute-start | bytes 786440 | tf_op jit(solution)/shard_map/ppermute | solution.py:42
  49.5 0.7 select_bitcast_fusion.rows_ref
  50.2 14.7 %shard_map.47 = f32[128,256]{1,0:T(8,128)} custom-call(f32[128,256]{1,0:T(8,128)} %select_bitcast_fusion.rows_ref), custom_call_target="tpu_custom_call" | custom-call | tf_op jit(solution)/shard_map/pallas_call | solution.py:131
  64.9 1.1 collective-permute-start.2
  66.0 1.9 collective-permute-start.5
  67.9 2.2 %collective-permute-done.2 = f32[256,128]{0,1:T(8,128)S(1)} collective-permute-done((f32[256,128]{0,1:T(8,128)}, f32[256,128]{0,1:T(8,128)S(1)}, u32[]{:S(2)}, u32[]{:S(2)}) %collective-permute-start.2) | collective-permute-done | bytes 131104 | tf_op jit(solution)/shard_map/ppermute | solution.py:32
  70.1 0.9 broadcast_select_fusion
  71.0 6.7 %collective-permute-done.5 = f32[256,256]{1,0:T(8,128)S(1)} collective-permute-done((f32[256,256]{1,0:T(8,128)S(1)}, f32[256,256]{1,0:T(8,128)S(1)}, u32[]{:S(2)}, u32[]{:S(2)}) %collective-permute-start.5) | collective-permute-done | bytes 262176 | tf_op jit(solution)/shard_map/ppermute | solution.py:42
  77.7 30.4 %while.20 = (s32[]{:T(128)}, f32[256,128]{0,1:T(8,128)S(1)}, f32[256,256]{1,0:T(8,128)S(1)}, s32[]{:T(128)}) while((s32[]{:T(128)}, f32[256,128]{0,1:T(8,128)S(1)}, f32[256,256]{1,0:T(8,128)S(1)}, s32[]{:T(128)}) %tuple.37), condition=%wide.region_2.3_spmd, body=%wide.region_1.2_spmd.sunk | while | flops 100663296 | bytes 524341 | solution.py:143
  77.9 1.1 fusion.53.rows_ref
  79.0 14.0 %eval_jaxpr.2 = f32[128,256]{1,0:T(8,128)S(1)} custom-call(f32[128,256]{1,0:T(8,128)} %fusion.53.rows_ref), custom_call_target="tpu_custom_call" | custom-call | tf_op jit(solution)/shard_map/while/body/eval_jaxpr/pallas_call | solution.py:131
  93.0 1.1 fusion.53.rows_ref
  94.1 14.0 %eval_jaxpr.2 = f32[128,256]{1,0:T(8,128)S(1)} custom-call(f32[128,256]{1,0:T(8,128)} %fusion.53.rows_ref), custom_call_target="tpu_custom_call" | custom-call | tf_op jit(solution)/shard_map/while/body/eval_jaxpr/pallas_call | solution.py:131
  108.2 8.8 %fusion.5 = (f32[128]{0:T(128)S(1)}, f32[8192,128]{1,0:T(8,128)}) fusion(f32[8192,256]{1,0:T(8,128)} %bitcast.58, f32[256,128]{0,1:T(8,128)S(1)} %get-tuple-element.39), kind=kOutput, calls=%fused_computation.8 | convolution fusion | flops 1615855488 | bytes 12714496 | tf_op jit(solution)/shard_map/dot_general | solution.py:181
  116.9 6.9 %fusion.11 = f32[1,128,128]{1,2,0:T(8,128)S(1)} fusion(f32[8192,128]{1,0:T(8,128)} %get-tuple-element.63, f32[128]{0:T(128)S(1)} %get-tuple-element.62), kind=kOutput, calls=%fused_computation.17 | convolution fusion | flops 805355520 | bytes 4260352 | tf_op jit(solution)/shard_map/dot_general | solution.py:147
  123.9 0.6 collective-permute-done.6
  124.4 4.0 %fusion.6 = f32[128,128]{1,0:T(8,128)S(1)} fusion(f32[8192,128]{1,0:T(8,128)} %collective-permute-done.6, s32[]{:T(128)S(6)} %select_n.90, f32[8192,128]{1,0:T(8,128)} %get-tuple-element.63), kind=kOutput, calls=%fused_computation.10 | convolution fusion | flops 402653184 | bytes 4260864 | tf_op jit(solution)/shard_map/dot_general | solution.py:147
  128.5 0.1 copy.8
  128.6 1.7 collective-permute-start.7
  130.3 3.9 %collective-permute-done.7 = f32[2,128,128]{1,2,0:T(8,128)S(1)} collective-permute-done((f32[2,128,128]{1,2,0:T(8,128)S(1)}, f32[2,128,128]{1,2,0:T(8,128)S(1)}, u32[]{:S(2)}, u32[]{:S(2)}) %collective-permute-start.7) | collective-permute-done | bytes 131104 | tf_op jit(solution)/shard_map/ppermute | solution.py:42
  134.3 5.0 %collective-permute-done.8 = f32[2,128,128]{1,2,0:T(8,128)S(1)} collective-permute-done((f32[2,128,128]{1,2,0:T(8,128)S(1)}, f32[2,128,128]{1,2,0:T(8,128)S(1)}, u32[]{:S(2)}, u32[]{:S(2)}) %collective-permute-start.8) | collective-permute-done | bytes 131104 | tf_op jit(solution)/shard_map/ppermute | solution.py:42
  139.3 1.3 collective-permute-start.9
  140.6 6.1 %collective-permute-done.9 = f32[2,128,128]{1,2,0:T(8,128)S(1)} collective-permute-done((f32[2,128,128]{1,2,0:T(8,128)S(1)}, f32[2,128,128]{1,2,0:T(8,128)S(1)}, u32[]{:S(2)}, u32[]{:S(2)}) %collective-permute-start.9) | collective-permute-done | bytes 131104 | tf_op jit(solution)/shard_map/ppermute | solution.py:42
  146.6 0.1 copy.9
  146.8 1.3 collective-permute-done.10
  148.3 0.1 copy.13
  148.4 30.5 %while.21 = (s32[]{:T(128)}, f32[256,128]{0,1:T(8,128)S(1)}, f32[256,256]{1,0:T(8,128)S(1)}, s32[]{:T(128)}) while((s32[]{:T(128)}, f32[256,128]{0,1:T(8,128)S(1)}, f32[256,256]{1,0:T(8,128)S(1)}, s32[]{:T(128)}) %tuple.40), condition=%wide.region_5.6_spmd, body=%wide.region_4.5_spmd.sunk | while | flops 100663296 | bytes 524341 | solution.py:143
  148.7 1.1 fusion.56.rows_ref
  149.7 14.0 %eval_jaxpr.3 = f32[128,256]{1,0:T(8,128)S(1)} custom-call(f32[128,256]{1,0:T(8,128)} %fusion.56.rows_ref), custom_call_target="tpu_custom_call" | custom-call | tf_op jit(solution)/shard_map/while/body/eval_jaxpr/pallas_call | solution.py:131
  163.8 1.1 fusion.56.rows_ref
  164.8 14.0 %eval_jaxpr.3 = f32[128,256]{1,0:T(8,128)S(1)} custom-call(f32[128,256]{1,0:T(8,128)} %fusion.56.rows_ref), custom_call_target="tpu_custom_call" | custom-call | tf_op jit(solution)/shard_map/while/body/eval_jaxpr/pallas_call | solution.py:131
  178.9 4.5 %fusion.15 = f32[8192,64]{0,1:T(8,128)S(1)} fusion(f32[8192,128]{1,0:T(8,128)} %get-tuple-element.63, f32[256,128]{0,1:T(8,128)S(1)} %get-tuple-element.40, s32[]{:T(128)S(6)} %select_n.96, s32[]{:T(128)S(6)} %add.65, pred[]{:T(512)S(6)} %eq.18), kind=kOutput, calls=%fused_computation.35 | convolution fusion | flops 402661376 | bytes 6357001 | tf_op jit(solution)/shard_map/dot_general | solution.py:211
  183.4 4.5 %fusion.9 = f32[8,64,8,128]{3,2,1,0:T(8,128)S(1)} fusion(f32[8192,64]{0,1:T(8,128)S(1)} %fusion.15, f32[8192,128]{1,0:T(8,128)} %collective-permute-done.6, f32[256,128]{0,1:T(8,128)S(1)} %get-tuple-element.40, s32[]{:T(128)S(6)} %select_n.96, s32[]{:T(128)S(6)} %add.65, pred[]{:T(512)S(6)} %eq.18), kind=kOutput, calls=%fused_computation.13 | convolution fusion | flops 403185664 | bytes 8454153 | tf_op jit(solution)/shard_map/dot_general | solution.py:211
  187.9 1.6 copy.19
  (25 shorter events, 0.5 us)
Async XLA Ops:
  0.0 42.3 %copy-start = (s32[512,128]{1,0:T(8,128)S(1)}, s32[512,128]{1,0:T(8,128)}, u32[]{:S(2)}) copy-start(s32[512,128]{1,0:T(8,128)} %param.10) | copy-start | bytes 786436
  1.0 7.6 %collective-permute-start = (bf16[2,128,256]{2,1,0:T(8,128)(2,1)S(1)}, bf16[2,128,256]{2,1,0:T(8,128)(2,1)S(1)}, u32[]{:S(2)}, u32[]{:S(2)}) collective-permute-start(bf16[2,128,256]{2,1,0:T(8,128)(2,1)S(1)} %get-tuple-element.54), channel_id=1, source_target_pairs={{0,1},{1,2},{2,3},{3,4},{4,5},{5,6},{6,7},{8,9},{9,10},{10,11},{11... | collective-permute-start | bytes 393224 | tf_op jit(solution)/shard_map/ppermute | solution.py:20
  5.9 6.9 %collective-permute-start.1 = (bf16[2,128,256]{2,1,0:T(8,128)(2,1)S(1)}, bf16[2,128,256]{2,1,0:T(8,128)(2,1)S(1)}, u32[]{:S(2)}, u32[]{:S(2)}) collective-permute-start(bf16[2,128,256]{2,1,0:T(8,128)(2,1)S(1)} %get-tuple-element.53), channel_id=1, source_target_pairs={{1,0},{2,1},{3,2},{4,3},{5,4},{6,5},{7,6},{9,8},{10,9},{11,10},{12... | collective-permute-start | bytes 393224 | tf_op jit(solution)/shard_map/ppermute | solution.py:21
  8.7 4.1 %copy-start.3 = (bf16[2,128,256]{2,1,0:T(8,128)(2,1)}, bf16[2,128,256]{2,1,0:T(8,128)(2,1)S(1)}, u32[]{:S(2)}) copy-start(bf16[2,128,256]{2,1,0:T(8,128)(2,1)S(1)} %collective-permute-done.low_ref) | copy-start | bytes 393220
  12.8 0.7 copy-start.4
  27.1 5.8 %copy-start.1 = (f32[64,128,256]{2,1,0:T(8,128)S(1)}, f32[64,128,256]{2,1,0:T(8,128)}, u32[]{:S(2)}) copy-start(f32[64,128,256]{2,1,0:T(8,128)} %shard_map.46) | copy-start | bytes 25165828
  32.9 9.5 %copy-start.2 = (s32[256,128]{1,0:T(8,128)S(1)}, s32[256,128]{1,0:T(8,128)}, u32[]{:S(2)}) copy-start(s32[256,128]{1,0:T(8,128)} %param.11) | copy-start | bytes 393220
  39.8 7.4 %collective-permute-start.3 = (f32[256,256]{1,0:T(8,128)S(1)}, f32[256,256]{1,0:T(8,128)S(1)}, u32[]{:S(2)}, u32[]{:S(2)}) collective-permute-start(f32[256,256]{1,0:T(8,128)S(1)} %fusion.10), channel_id=1, source_target_pairs={{0,1},{1,0},{2,3},{3,2},{4,5},{5,4},{6,7},{7,6},{8,9},{9,8},{10,11... | collective-permute-start | bytes 786440 | tf_op jit(solution)/shard_map/ppermute | solution.py:42
  47.2 18.8 %collective-permute-start.4 = (f32[256,256]{1,0:T(8,128)S(1)}, f32[256,256]{1,0:T(8,128)S(1)}, u32[]{:S(2)}, u32[]{:S(2)}) collective-permute-start(f32[256,256]{1,0:T(8,128)S(1)} %add.54), channel_id=1, source_target_pairs={{0,2},{1,3},{2,0},{3,1},{4,6},{5,7},{6,4},{7,5},{8,10},{9,11},{10,... | collective-permute-start | bytes 786440 | tf_op jit(solution)/shard_map/ppermute | solution.py:42
  64.9 5.2 %collective-permute-start.2 = (f32[256,128]{0,1:T(8,128)}, f32[256,128]{0,1:T(8,128)S(1)}, u32[]{:S(2)}, u32[]{:S(2)}) collective-permute-start(f32[256,128]{0,1:T(8,128)} %bitcast.61), channel_id=1, source_target_pairs={{0,1},{1,0},{2,3},{3,2},{4,5},{5,4},{6,7},{7,6},{8,9},{9,8},{10,11... | collective-permute-start | bytes 393224 | tf_op jit(solution)/shard_map/ppermute | solution.py:32
  66.0 11.7 %collective-permute-start.5 = (f32[256,256]{1,0:T(8,128)S(1)}, f32[256,256]{1,0:T(8,128)S(1)}, u32[]{:S(2)}, u32[]{:S(2)}) collective-permute-start(f32[256,256]{1,0:T(8,128)S(1)} %add.55), channel_id=1, source_target_pairs={{0,4},{1,5},{2,6},{3,7},{4,0},{5,1},{6,2},{7,3},{8,12},{9,13},{10,... | collective-permute-start | bytes 786440 | tf_op jit(solution)/shard_map/ppermute | solution.py:42
  116.9 7.5 %collective-permute-start.6 = (f32[8192,128]{1,0:T(8,128)}, f32[8192,128]{1,0:T(8,128)}, u32[]{:S(2)}, u32[]{:S(2)}) collective-permute-start(f32[8192,128]{1,0:T(8,128)} %get-tuple-element.63), channel_id=1, source_target_pairs={{0,8},{8,0},{1,9},{9,1},{2,10},{10,2},{3,11},{11,3},{4,12},{12,4},... | collective-permute-start | bytes 12582920 | tf_op jit(solution)/shard_map/ppermute | solution.py:32
  128.6 5.6 %collective-permute-start.7 = (f32[2,128,128]{1,2,0:T(8,128)S(1)}, f32[2,128,128]{1,2,0:T(8,128)S(1)}, u32[]{:S(2)}, u32[]{:S(2)}) collective-permute-start(f32[2,128,128]{1,2,0:T(8,128)S(1)} %pad_maximum_fusion), channel_id=1, source_target_pairs={{0,1},{1,0},{2,3},{3,2},{4,5},{5,4},{6,7},{7,6},{8,9},{9,8},{10,11... | collective-permute-start | bytes 393224 | tf_op jit(solution)/shard_map/ppermute | solution.py:42
  134.2 5.0 %collective-permute-start.8 = (f32[2,128,128]{1,2,0:T(8,128)S(1)}, f32[2,128,128]{1,2,0:T(8,128)S(1)}, u32[]{:S(2)}, u32[]{:S(2)}) collective-permute-start(f32[2,128,128]{1,2,0:T(8,128)S(1)} %fusion.28), channel_id=1, source_target_pairs={{0,2},{1,3},{2,0},{3,1},{4,6},{5,7},{6,4},{7,5},{8,10},{9,11},{10,... | collective-permute-start | bytes 393224 | tf_op jit(solution)/shard_map/ppermute | solution.py:42
  139.3 7.3 %collective-permute-start.9 = (f32[2,128,128]{1,2,0:T(8,128)S(1)}, f32[2,128,128]{1,2,0:T(8,128)S(1)}, u32[]{:S(2)}, u32[]{:S(2)}) collective-permute-start(f32[2,128,128]{1,2,0:T(8,128)S(1)} %fusion.44), channel_id=1, source_target_pairs={{0,4},{1,5},{2,6},{3,7},{4,0},{5,1},{6,2},{7,3},{8,12},{9,13},{10,... | collective-permute-start | bytes 393224 | tf_op jit(solution)/shard_map/ppermute | solution.py:42
  146.7 1.4 collective-permute-start.10
where the time goes:
time: 190 us
  Pallas kernels  84.6 us (45%)
  matrix products  39.9 us (21%)
  waiting for transfers between devices  36 us (19%)
  starting transfers between devices  17 us (9%)
  other arithmetic  6.81 us (4%)
  local copies, waits for them, and re-layouts  4.64 us (2%)
    pallas_call x5, Pallas kernels, orthonormal(): pl.pallas_call(gram_schmidt_kernel, out_shape=jax.ShapeDtypeStruct(rows.s...  70.9 us
    ppermute x6, waiting for transfers between devices, tree_sum(): value = value + lax.ppermute(value, axis, route)  26.3 us
    dot_general x3, matrix products, cross_gram(): lax.dot_general(left_rows, right_rows, (((0,), (0,)), ((), ())), precisio...  17.8 us
    pallas_call x1, Pallas kernels, fluxes(): pl.pallas_call(functools.partial(flux_kernel, count), grid=(count,), in_s...  13.7 us
    ppermute x6, starting transfers between devices, tree_sum(): value = value + lax.ppermute(value, axis, route)  9.64 us
    dot_general x1, matrix products, on_device(): own_modes = jnp.dot(own_flux, own_basis, precision=high)  8.79 us
    reduce_sum x1, other arithmetic, self_gram(): missing = jnp.sum(lower * lower, axis=0)  4.98 us
    ppermute x1, starting transfers between devices, halos(): lax.ppermute(lax.slice_in_dim(block, block.shape[0] - width, None, axis=0...  4.88 us
  transfers between devices with their start and end apart: 11, of which 10 were waited for; matrix products, arithmetic and copies ran while one was open for 5% of the time, Pallas kernels for 8%

commit v1 on v0

--- a/solution.py
+++ b/solution.py
@@ -176,23 +176,29 @@
         first_basis = jnp.where(is_even, mine, theirs)
         merge_basis = jnp.where(is_even, theirs, mine)
     own_flux = fluxes(halo_low, snapshots, halo_high, coefficient).reshape(rows_here, order_size)
-    own_gram = tree_sum(self_gram(own_flux), "tx") / cells_total
+    half_rows = rows_here // 2
+    half_start = member * half_rows
+    sent_rows = lax.dynamic_slice_in_dim(own_flux, (1 - member) * half_rows, half_rows, 0)
+    other_rows = partner(sent_rows, "run", 0)
+    mixed_half = cross_gram(
+        lax.dynamic_slice_in_dim(own_flux, half_start, half_rows, 0), other_rows
+    )
+    mixed_half = jnp.where(is_first, mixed_half, mixed_half.T)
+    summed = tree_sum(jnp.stack([self_gram(own_flux), mixed_half]), "tx")
+    own_gram = summed[0] / cells_total
+    mixed_gram = summed[1] + partner(summed[1], "run", 0)
     own_basis = iterate(own_gram, first_basis)
     own_modes = jnp.dot(own_flux, own_basis, precision=high)
     other_modes = partner(own_modes, "run", 0)
-    own_block = self_gram(own_modes)
-    half_rows = rows_here // 2
-    half_start = member * half_rows
-    mixed_half = cross_gram(
-        lax.dynamic_slice_in_dim(own_modes, half_start, half_rows, 0),
-        lax.dynamic_slice_in_dim(other_modes, half_start, half_rows, 0),
-    )
-    mixed_half = jnp.where(is_first, mixed_half, mixed_half.T)
-    summed = tree_sum(jnp.stack([own_block, mixed_half]), "tx")
-    swapped = partner(summed, "run", 0)
-    own_block = summed[0] / cells_total
-    other_block = swapped[0] / cells_total
-    mixed_block = (summed[1] + swapped[1]) / cells_total
+    own_block = jnp.dot(own_basis.T, jnp.dot(own_gram, own_basis, precision=highest), precision=highest)
+    other_block, other_basis = partner((own_block, own_basis), "run", 0)
+    first_basis_set = jnp.where(is_first, own_basis, other_basis)
+    last_basis_set = jnp.where(is_first, other_basis, own_basis)
+    mixed_block = jnp.dot(
+        first_basis_set.T,
+        jnp.dot(mixed_gram / cells_total, last_basis_set, precision=highest),
+        precision=highest,
+    )
     first_block = jnp.where(is_first, own_block, other_block)
     last_block = jnp.where(is_first, other_block, own_block)
     merge_gram = jnp.concatenate(

time: 190 us -> 194 us (1.021)
  waiting for transfers between devices: 36 us -> 40.7 us
  local copies, waits for them, and re-layouts: 4.64 us -> 9.06 us
  matrix products: 39.9 us -> 36.3 us
    ppermute x3 -> x6, waiting for transfers between devices: 4.13 us -> 9.45 us  [partner(): return lax.ppermute(block, axis, route)]
    dot_general x3 -> x2, matrix products: 17.8 us -> 12.8 us  [cross_gram(): lax.dot_general(left_rows, right_rows, (((0,), (0,)), ((), ())), precisio...]
    dynamic_slice x0 -> x1, local copies, waits for them, and re-layouts: none -> 4.43 us  [on_device(): lax.dynamic_slice_in_dim(own_flux, (1 - member) * half_rows, half_rows, 0)]
    ppermute x6 -> x3, starting transfers between devices: 9.64 us -> 6.63 us  [tree_sum(): value = value + lax.ppermute(value, axis, route)]
    ppermute x6 -> x3, waiting for transfers between devices: 26.3 us -> 25.7 us  [tree_sum(): value = value + lax.ppermute(value, axis, route)]
  transfers between devices with their start and end apart: 11 -> 11, of which waited for: 10 -> 8; matrix products, arithmetic and copies ran while one was open for 5% -> 11% of each run, Pallas kernels for 8% -> 22%
where the time goes in v1:
time: 194 us
  Pallas kernels  84.6 us (44%)
  waiting for transfers between devices  40.7 us (21%)
  matrix products  36.3 us (19%)
  starting transfers between devices  15.6 us (8%)
  local copies, waits for them, and re-layouts  9.06 us (5%)
  other arithmetic  6.95 us (4%)
    pallas_call x5, Pallas kernels, orthonormal(): pl.pallas_call(gram_schmidt_kernel, out_shape=jax.ShapeDtypeStruct(rows.s...  70.9 us
    ppermute x3, waiting for transfers between devices, tree_sum(): value = value + lax.ppermute(value, axis, route)  25.7 us
    pallas_call x1, Pallas kernels, fluxes(): pl.pallas_call(functools.partial(flux_kernel, count), grid=(count,), in_s...  13.7 us
    dot_general x2, matrix products, cross_gram(): lax.dot_general(left_rows, right_rows, (((0,), (0,)), ((), ())), precisio...  12.8 us
    ppermute x6, waiting for transfers between devices, partner(): return lax.ppermute(block, axis, route)  9.45 us
    dot_general x1, matrix products, on_device(): own_modes = jnp.dot(own_flux, own_basis, precision=high)  8.79 us
    ppermute x3, starting transfers between devices, tree_sum(): value = value + lax.ppermute(value, axis, route)  6.63 us
    reduce_sum x1, other arithmetic, self_gram(): missing = jnp.sum(lower * lower, axis=0)  4.98 us
  transfers between devices with their start and end apart: 11, of which 8 were waited for; matrix products, arithmetic and copies ran while one was open for 11% of the time, Pallas kernels for 22%

profile of v1, /device:TPU:0, one launch (start us, length us, event | category | flops | bytes accessed | tf_op | source)
XLA Modules:
  0.0 193.8 jit_solution(8880075019877580925)
XLA Ops:
  0.0 1.0 fusion.35
  1.0 4.9 %collective-permute-start = (bf16[2,128,256]{2,1,0:T(8,128)(2,1)S(1)}, bf16[2,128,256]{2,1,0:T(8,128)(2,1)S(1)}, u32[]{:S(2)}, u32[]{:S(2)}) collective-permute-start(bf16[2,128,256]{2,1,0:T(8,128)(2,1)S(1)} %get-tuple-element.57), channel_id=1, source_target_pairs={{0,1},{1,2},{2,3},{3,4},{4,5},{5,6},{6,7},{8,9},{9,10},{10,11},{11... | collective-permute-start | bytes 393224 | tf_op jit(solution)/shard_map/ppermute | solution.py:20
  5.9 1.3 collective-permute-start.1
  7.2 1.4 collective-permute-done.low_ref
  8.7 4.1 %collective-permute-done.1.high_ref = bf16[2,128,256]{2,1,0:T(8,128)(2,1)S(1)} collective-permute-done((bf16[2,128,256]{2,1,0:T(8,128)(2,1)S(1)}, bf16[2,128,256]{2,1,0:T(8,128)(2,1)S(1)}, u32[]{:S(2)}, u32[]{:S(2)}) %collective-permute-start.1) | collective-permute-done | bytes 131104 | tf_op jit(solution)/shard_map/ppermute | solution.py:21
  12.8 0.6 copy-done.4
  13.4 13.7 %shard_map.46 = f32[64,128,256]{2,1,0:T(8,128)} custom-call(bf16[2,128,256]{2,1,0:T(8,128)(2,1)} %copy-done.3, bf16[2,128,256]{2,1,0:T(8,128)(2,1)} %copy-done.4, bf16[64,128,256]{2,1,0:T(8,128)(2,1)} %next_ref.1, bf16[64,128,256]{2,1,0:T(8,128)(2,1)} %next_ref.1, bf16[64,128,256]{2,1,0:T(8,128)(2,1)} %next_ref.1, f32[64,128]{1,0:T(8,128)} %coef_ref.1), custom_call_target="tpu_custom_call" | custom-call | tf_op jit(solution)/shard_map/pallas_call | solution.py:85
  27.1 4.4 %constant_dynamic-slice_fusion = f32[4096,256]{1,0:T(8,128)} fusion(f32[8192,256]{1,0:T(8,128)} %bitcast.63, s32[]{:T(128)S(6)} %select_n.90), kind=kLoop, calls=%fused_computation.45 | loop fusion | bytes 8388612 | tf_op jit(solution)/shard_map/dynamic_slice | solution.py:181
  31.6 5.0 %fusion.2 = f32[256]{0:T(256)S(1)} fusion(f32[64,128,256]{2,1,0:T(8,128)} %shard_map.46), kind=kLoop, calls=%fused_computation.4 | loop fusion | flops 10485504 | bytes 8389632 | tf_op jit(solution)/shard_map/reduce_sum | solution.py:153
  36.6 0.8 copy-done.1
  37.4 6.9 %fusion.7 = f32[1,256,256]{2,1,0:T(8,128)S(1)} fusion(f32[64,128,256]{2,1,0:T(8,128)S(1)} %copy-done.1, f32[256]{0:T(256)S(1)} %fusion.2), kind=kOutput, calls=%fused_computation.11 | convolution fusion | flops 3221422080 | bytes 8651776 | tf_op jit(solution)/shard_map/dot_general | solution.py:147
  44.3 5.9 %fusion.3 = f32[256,256]{1,0:T(8,128)S(1)} fusion(f32[4096,256]{1,0:T(8,128)} %collective-permute-done.3, f32[8192,256]{1,0:T(8,128)S(1)} %bitcast.65, s32[]{:T(128)S(6)} %select_n.89), kind=kOutput, calls=%fused_computation.5 | convolution fusion | flops 1610612736 | bytes 8650756 | tf_op jit(solution)/shard_map/dot_general | solution.py:147
  50.2 0.1 copy.8
  50.6 2.5 %collective-permute-start.4 = (f32[2,256,256]{2,1,0:T(8,128)S(1)}, f32[2,256,256]{2,1,0:T(8,128)S(1)}, u32[]{:S(2)}, u32[]{:S(2)}) collective-permute-start(f32[2,256,256]{2,1,0:T(8,128)S(1)} %pad_maximum_fusion), channel_id=1, source_target_pairs={{0,1},{1,0},{2,3},{3,2},{4,5},{5,4},{6,7},{7,6},{8,9},{9,8},{10,11... | collective-permute-start | bytes 1572872 | tf_op jit(solution)/shard_map/ppermute | solution.py:42
  53.1 12.6 %collective-permute-done.4 = f32[2,256,256]{2,1,0:T(8,128)S(1)} collective-permute-done((f32[2,256,256]{2,1,0:T(8,128)S(1)}, f32[2,256,256]{2,1,0:T(8,128)S(1)}, u32[]{:S(2)}, u32[]{:S(2)}) %collective-permute-start.4) | collective-permute-done | bytes 524320 | tf_op jit(solution)/shard_map/ppermute | solution.py:42
  65.7 1.6 collective-permute-start.5
  67.6 12.0 %collective-permute-done.5 = f32[2,256,256]{2,1,0:T(8,128)S(1)} collective-permute-done((f32[2,256,256]{2,1,0:T(8,128)S(1)}, f32[2,256,256]{2,1,0:T(8,128)S(1)}, u32[]{:S(2)}, u32[]{:S(2)}) %collective-permute-start.5) | collective-permute-done | bytes 524320 | tf_op jit(solution)/shard_map/ppermute | solution.py:42
  79.6 0.1 fusion.55
  79.7 2.5 %collective-permute-start.6 = (f32[2,256,256]{2,1,0:T(8,128)S(1)}, f32[2,256,256]{2,1,0:T(8,128)S(1)}, u32[]{:S(2)}, u32[]{:S(2)}) collective-permute-start(f32[2,256,256]{2,1,0:T(8,128)S(1)} %fusion.55), channel_id=1, source_target_pairs={{0,4},{1,5},{2,6},{3,7},{4,0},{5,1},{6,2},{7,3},{8,12},{9,13},{10,... | collective-permute-start | bytes 1572872 | tf_op jit(solution)/shard_map/ppermute | solution.py:42
  82.2 0.7 select_bitcast_fusion.rows_ref
  82.8 14.7 %shard_map.47 = f32[128,256]{1,0:T(8,128)} custom-call(f32[128,256]{1,0:T(8,128)} %select_bitcast_fusion.rows_ref), custom_call_target="tpu_custom_call" | custom-call | tf_op jit(solution)/shard_map/pallas_call | solution.py:131
  97.5 1.7 collective-permute-start.2
  99.2 3.5 %collective-permute-done.2 = f32[256,128]{0,1:T(8,128)S(1)} collective-permute-done((f32[256,128]{0,1:T(8,128)}, f32[256,128]{0,1:T(8,128)S(1)}, u32[]{:S(2)}, u32[]{:S(2)}) %collective-permute-start.2) | collective-permute-done | bytes 131104 | tf_op jit(solution)/shard_map/ppermute | solution.py:32
  102.7 0.9 broadcast_select_fusion
  103.6 1.1 collective-permute-done.6
  104.9 30.2 %while.20 = (s32[]{:T(128)}, f32[256,128]{0,1:T(8,128)S(1)}, f32[256,256]{1,0:T(8,128)S(1)}, s32[]{:T(128)}) while((s32[]{:T(128)}, f32[256,128]{0,1:T(8,128)S(1)}, f32[256,256]{1,0:T(8,128)S(1)}, s32[]{:T(128)}) %tuple.36), condition=%wide.region_2.3_spmd, body=%wide.region_1.2_spmd.sunk | while | flops 100663296 | bytes 524341 | solution.py:143
  104.9 1.1 fusion.64.rows_ref
  105.9 14.0 %eval_jaxpr.2 = f32[128,256]{1,0:T(8,128)S(1)} custom-call(f32[128,256]{1,0:T(8,128)} %fusion.64.rows_ref), custom_call_target="tpu_custom_call" | custom-call | tf_op jit(solution)/shard_map/while/body/eval_jaxpr/pallas_call | solution.py:131
  120.0 1.1 fusion.64.rows_ref
  121.1 14.0 %eval_jaxpr.2 = f32[128,256]{1,0:T(8,128)S(1)} custom-call(f32[128,256]{1,0:T(8,128)} %fusion.64.rows_ref), custom_call_target="tpu_custom_call" | custom-call | tf_op jit(solution)/shard_map/while/body/eval_jaxpr/pallas_call | solution.py:131
  135.1 8.8 %fusion.38 = f32[8192,128]{1,0:T(8,128)} fusion(f32[8192,256]{1,0:T(8,128)} %bitcast.64, f32[256,128]{0,1:T(8,128)S(1)} %get-tuple-element.39), kind=kOutput, calls=%fused_computation.54 | convolution fusion | flops 1610612736 | bytes 12713984 | tf_op jit(solution)/shard_map/dot_general | solution.py:191
  143.9 0.4 fusion.32
  144.3 0.4 fusion.39
  144.7 0.6 collective-permute-start.7
  145.3 0.4 collective-permute-start.8
  145.8 5.4 %collective-permute-done.7 = f32[128,128]{0,1:T(8,128)S(1)} collective-permute-done((f32[128,128]{0,1:T(8,128)S(1)}, f32[128,128]{0,1:T(8,128)S(1)}, u32[]{:S(2)}, u32[]{:S(2)}) %collective-permute-start.7) | collective-permute-done | bytes 65568 | tf_op jit(solution)/shard_map/ppermute | solution.py:32
  151.2 0.5 collective-permute-done.8
  151.7 0.4 fusion.10
  152.1 0.3 fusion.15
  152.5 0.1 copy.10
  152.7 30.5 %while.21 = (s32[]{:T(128)}, f32[256,128]{0,1:T(8,128)S(1)}, f32[256,256]{1,0:T(8,128)S(1)}, s32[]{:T(128)}) while((s32[]{:T(128)}, f32[256,128]{0,1:T(8,128)S(1)}, f32[256,256]{1,0:T(8,128)S(1)}, s32[]{:T(128)}) %tuple.39), condition=%wide.region_4.5_spmd, body=%wide.region_3.4_spmd.sunk | while | flops 100663296 | bytes 524341 | solution.py:143
  152.7 1.1 fusion.67.rows_ref
  153.7 14.0 %eval_jaxpr.3 = f32[128,256]{1,0:T(8,128)S(1)} custom-call(f32[128,256]{1,0:T(8,128)} %fusion.67.rows_ref), custom_call_target="tpu_custom_call" | custom-call | tf_op jit(solution)/shard_map/while/body/eval_jaxpr/pallas_call | solution.py:131
  167.8 1.1 fusion.67.rows_ref
  168.8 14.0 %eval_jaxpr.3 = f32[128,256]{1,0:T(8,128)S(1)} custom-call(f32[128,256]{1,0:T(8,128)} %fusion.67.rows_ref), custom_call_target="tpu_custom_call" | custom-call | tf_op jit(solution)/shard_map/while/body/eval_jaxpr/pallas_call | solution.py:131
  183.1 4.5 %fusion.20 = f32[8192,64]{0,1:T(8,128)S(1)} fusion(f32[8192,128]{1,0:T(8,128)} %fusion.38, f32[256,128]{0,1:T(8,128)S(1)} %get-tuple-element.40, s32[]{:T(128)S(6)} %select_n.100, s32[]{:T(128)S(6)} %add.51, pred[]{:T(512)S(6)} %eq.14), kind=kOutput, calls=%fused_computation.33 | convolution fusion | flops 402661376 | bytes 6357001 | tf_op jit(solution)/shard_map/dot_general | solution.py:217
  187.6 4.5 %fusion.5 = f32[8,64,8,128]{3,2,1,0:T(8,128)S(1)} fusion(f32[8192,64]{0,1:T(8,128)S(1)} %fusion.20, f32[8192,128]{1,0:T(8,128)} %collective-permute-done.10, f32[256,128]{0,1:T(8,128)S(1)} %get-tuple-element.40, s32[]{:T(128)S(6)} %select_n.100, s32[]{:T(128)S(6)} %add.51, pred[]{:T(512)S(6)} %eq.14), kind=kOutput, calls=%fused_computation.8 | convolution fusion | flops 403185664 | bytes 8454153 | tf_op jit(solution)/shard_map/dot_general | solution.py:217
  192.2 1.6 copy.16
  (25 shorter events, 0.7 us)
Async XLA Ops:
  0.0 67.4 %copy-start = (s32[512,128]{1,0:T(8,128)S(1)}, s32[512,128]{1,0:T(8,128)}, u32[]{:S(2)}) copy-start(s32[512,128]{1,0:T(8,128)} %param.10) | copy-start | bytes 786436
  1.0 7.6 %collective-permute-start = (bf16[2,128,256]{2,1,0:T(8,128)(2,1)S(1)}, bf16[2,128,256]{2,1,0:T(8,128)(2,1)S(1)}, u32[]{:S(2)}, u32[]{:S(2)}) collective-permute-start(bf16[2,128,256]{2,1,0:T(8,128)(2,1)S(1)} %get-tuple-element.57), channel_id=1, source_target_pairs={{0,1},{1,2},{2,3},{3,4},{4,5},{5,6},{6,7},{8,9},{9,10},{10,11},{11... | collective-permute-start | bytes 393224 | tf_op jit(solution)/shard_map/ppermute | solution.py:20
  5.9 6.9 %collective-permute-start.1 = (bf16[2,128,256]{2,1,0:T(8,128)(2,1)S(1)}, bf16[2,128,256]{2,1,0:T(8,128)(2,1)S(1)}, u32[]{:S(2)}, u32[]{:S(2)}) collective-permute-start(bf16[2,128,256]{2,1,0:T(8,128)(2,1)S(1)} %get-tuple-element.56), channel_id=1, source_target_pairs={{1,0},{2,1},{3,2},{4,3},{5,4},{6,5},{7,6},{9,8},{10,9},{11,10},{12... | collective-permute-start | bytes 393224 | tf_op jit(solution)/shard_map/ppermute | solution.py:21
  8.7 4.1 %copy-start.3 = (bf16[2,128,256]{2,1,0:T(8,128)(2,1)}, bf16[2,128,256]{2,1,0:T(8,128)(2,1)S(1)}, u32[]{:S(2)}) copy-start(bf16[2,128,256]{2,1,0:T(8,128)(2,1)S(1)} %collective-permute-done.low_ref) | copy-start | bytes 393220
  12.8 0.6 copy-start.4
  31.6 12.7 %collective-permute-start.3 = (f32[4096,256]{1,0:T(8,128)}, f32[4096,256]{1,0:T(8,128)}, u32[]{:S(2)}, u32[]{:S(2)}) collective-permute-start(f32[4096,256]{1,0:T(8,128)} %constant_dynamic-slice_fusion), channel_id=1, source_target_pairs={{0,8},{8,0},{1,9},{9,1},{2,10},{10,2},{3,11},{11,3},{4,12},{12,4},... | collective-permute-start | bytes 12582920 | tf_op jit(solution)/shard_map/ppermute | solution.py:32
  31.6 5.8 %copy-start.1 = (f32[64,128,256]{2,1,0:T(8,128)S(1)}, f32[64,128,256]{2,1,0:T(8,128)}, u32[]{:S(2)}) copy-start(f32[64,128,256]{2,1,0:T(8,128)} %shard_map.46) | copy-start | bytes 25165828
  50.2 17.3 %copy-start.2 = (s32[256,128]{1,0:T(8,128)S(1)}, s32[256,128]{1,0:T(8,128)}, u32[]{:S(2)}) copy-start(s32[256,128]{1,0:T(8,128)} %param.11) | copy-start | bytes 393220
  50.6 15.1 %collective-permute-start.4 = (f32[2,256,256]{2,1,0:T(8,128)S(1)}, f32[2,256,256]{2,1,0:T(8,128)S(1)}, u32[]{:S(2)}, u32[]{:S(2)}) collective-permute-start(f32[2,256,256]{2,1,0:T(8,128)S(1)} %pad_maximum_fusion), channel_id=1, source_target_pairs={{0,1},{1,0},{2,3},{3,2},{4,5},{5,4},{6,7},{7,6},{8,9},{9,8},{10,11... | collective-permute-start | bytes 1572872 | tf_op jit(solution)/shard_map/ppermute | solution.py:42
  65.7 13.8 %collective-permute-start.5 = (f32[2,256,256]{2,1,0:T(8,128)S(1)}, f32[2,256,256]{2,1,0:T(8,128)S(1)}, u32[]{:S(2)}, u32[]{:S(2)}) collective-permute-start(f32[2,256,256]{2,1,0:T(8,128)S(1)} %fusion.34), channel_id=1, source_target_pairs={{0,2},{1,3},{2,0},{3,1},{4,6},{5,7},{6,4},{7,5},{8,10},{9,11},{10,... | collective-permute-start | bytes 1572872 | tf_op jit(solution)/shard_map/ppermute | solution.py:42
  79.7 25.1 %collective-permute-start.6 = (f32[2,256,256]{2,1,0:T(8,128)S(1)}, f32[2,256,256]{2,1,0:T(8,128)S(1)}, u32[]{:S(2)}, u32[]{:S(2)}) collective-permute-start(f32[2,256,256]{2,1,0:T(8,128)S(1)} %fusion.55), channel_id=1, source_target_pairs={{0,4},{1,5},{2,6},{3,7},{4,0},{5,1},{6,2},{7,3},{8,12},{9,13},{10,... | collective-permute-start | bytes 1572872 | tf_op jit(solution)/shard_map/ppermute | solution.py:42
  97.5 5.2 %collective-permute-start.2 = (f32[256,128]{0,1:T(8,128)}, f32[256,128]{0,1:T(8,128)S(1)}, u32[]{:S(2)}, u32[]{:S(2)}) collective-permute-start(f32[256,128]{0,1:T(8,128)} %bitcast.69), channel_id=1, source_target_pairs={{0,1},{1,0},{2,3},{3,2},{4,5},{5,4},{6,7},{7,6},{8,9},{9,8},{10,11... | collective-permute-start | bytes 393224 | tf_op jit(solution)/shard_map/ppermute | solution.py:32
  143.9 43.7 %collective-permute-start.10 = (f32[8192,128]{1,0:T(8,128)}, f32[8192,128]{1,0:T(8,128)}, u32[]{:S(2)}, u32[]{:S(2)}) collective-permute-start(f32[8192,128]{1,0:T(8,128)} %fusion.38), channel_id=1, source_target_pairs={{0,8},{8,0},{1,9},{9,1},{2,10},{10,2},{3,11},{11,3},{4,12},{12,4},... | collective-permute-start | bytes 12582920 | tf_op jit(solution)/shard_map/ppermute | solution.py:32
  144.7 6.5 %collective-permute-start.7 = (f32[128,128]{0,1:T(8,128)S(1)}, f32[128,128]{0,1:T(8,128)S(1)}, u32[]{:S(2)}, u32[]{:S(2)}) collective-permute-start(f32[128,128]{0,1:T(8,128)S(1)} %fusion.39), channel_id=1, source_target_pairs={{0,8},{8,0},{1,9},{9,1},{2,10},{10,2},{3,11},{11,3},{4,12},{12,4},... | collective-permute-start | bytes 196616 | tf_op jit(solution)/shard_map/ppermute | solution.py:32
  145.3 6.5 %collective-permute-start.9 = (f32[256,256]{1,0:T(8,128)S(1)}, f32[256,256]{1,0:T(8,128)S(1)}, u32[]{:S(2)}, u32[]{:S(2)}) collective-permute-start(f32[256,256]{1,0:T(8,128)S(1)} %get-tuple-element.58), channel_id=1, source_target_pairs={{0,8},{8,0},{1,9},{9,1},{2,10},{10,2},{3,11},{11,3},{4,12},{12,4},... | collective-permute-start | bytes 786440 | tf_op jit(solution)/shard_map/ppermute | solution.py:32
  145.3 6.4 %collective-permute-start.8 = (f32[256,128]{0,1:T(8,128)S(1)}, f32[256,128]{0,1:T(8,128)S(1)}, u32[]{:S(2)}, u32[]{:S(2)}) collective-permute-start(f32[256,128]{0,1:T(8,128)S(1)} %get-tuple-element.39), channel_id=1, source_target_pairs={{0,8},{8,0},{1,9},{9,1},{2,10},{10,2},{3,11},{11,3},{4,12},{12,4},... | collective-permute-start | bytes 393224 | tf_op jit(solution)/shard_map/ppermute | solution.py:32

commit v2 on v1

--- a/solution.py
+++ b/solution.py
@@ -42,6 +42,17 @@
         value = value + lax.ppermute(value, axis, route)
         step *= 2
     return value
+
+
+def butterfly_steps(axis):
+    count = lax.axis_size(axis)
+    assert count & (count - 1) == 0
+    routes = []
+    step = 1
+    while step < count:
+        routes.append([(i, i ^ step) for i in range(count)])
+        step *= 2
+    return routes
 
 
 def fourth_order(values, axis_dim):
@@ -137,10 +148,9 @@
 
 
 def iterate(gram_matrix, basis_set):
-    def sweep(sweep_index, basis_set):
-        return orthonormal(jnp.dot(gram_matrix, basis_set, precision=highest))
-
-    return lax.fori_loop(0, ITERS, sweep, basis_set)
+    for sweep_index in range(ITERS):
+        basis_set = orthonormal(jnp.dot(gram_matrix, basis_set, precision=highest))
+    return basis_set
 
 
 def cross_gram(left_rows, right_rows):
@@ -184,11 +194,23 @@
         lax.dynamic_slice_in_dim(own_flux, half_start, half_rows, 0), other_rows
     )
     mixed_half = jnp.where(is_first, mixed_half, mixed_half.T)
-    summed = tree_sum(jnp.stack([self_gram(own_flux), mixed_half]), "tx")
-    own_gram = summed[0] / cells_total
-    mixed_gram = summed[1] + partner(summed[1], "run", 0)
-    own_basis = iterate(own_gram, first_basis)
+    own_gram = tree_sum(self_gram(own_flux), "tx") / cells_total
+    own_gram, mixed_sum = lax.optimization_barrier((own_gram, mixed_half))
+    hops = butterfly_steps("tx")
+    own_basis = first_basis
+    for sweep_index in range(ITERS):
+        product = jnp.dot(own_gram, own_basis, precision=highest)
+        if hops:
+            received = lax.ppermute(mixed_sum, "tx", hops.pop(0))
+            own_basis = orthonormal(product)
+            own_basis, received = lax.optimization_barrier((own_basis, received))
+            mixed_sum = mixed_sum + received
+        else:
+            own_basis = orthonormal(product)
+    for route in hops:
+        mixed_sum = mixed_sum + lax.ppermute(mixed_sum, "tx", route)
     own_modes = jnp.dot(own_flux, own_basis, precision=high)
+    mixed_gram = mixed_sum + partner(mixed_sum, "run", 0)
     other_modes = partner(own_modes, "run", 0)
     own_block = jnp.dot(own_basis.T, jnp.dot(own_gram, own_basis, precision=highest), precision=highest)
     other_block, other_basis = partner((own_block, own_basis), "run", 0)

time: 194 us -> 189 us (0.974)
  waiting for transfers between devices: 40.7 us -> 31.2 us
  other arithmetic: 6.95 us -> 2.38 us
  Pallas kernels: 84.6 us -> 87.4 us
  matrix products: 36.3 us -> 38.9 us
  starting transfers between devices: 15.6 us -> 17.8 us
    ppermute x3, waiting for transfers between devices: 25.7 us -> 10.7 us  [tree_sum(): value = value + lax.ppermute(value, axis, route)]
    ppermute x0 -> x3, waiting for transfers between devices: none -> 13.7 us  [the longest x1 13.7 us: on_device(): mixed_sum = mixed_sum + lax.ppermute(mixed_sum, 'tx', route)]
    ppermute x6, waiting for transfers between devices: 9.45 us -> 1.21 us  [partner(): return lax.ppermute(block, axis, route)]
    reduce_sum x1, other arithmetic: 4.98 us -> 1.45 us  [self_gram(): missing = jnp.sum(lower * lower, axis=0)]
    pallas_call x5, Pallas kernels: 70.9 us -> 73.6 us  [orthonormal(): pl.pallas_call(gram_schmidt_kernel, out_shape=jax.ShapeDtypeStruct(rows.s...]
    ppermute x0 -> x3, starting transfers between devices: none -> 2.18 us  [the longest x2 1.67 us: on_device(): received = lax.ppermute(mixed_sum, 'tx', hops.pop(0))]
  transfers between devices with their start and end apart: 11 -> 14, of which waited for: 8 -> 6; matrix products, arithmetic and copies ran while one was open for 11% -> 15% of each run, Pallas kernels for 22% -> 39%
where the time goes in v2:
time: 189 us
  Pallas kernels  87.4 us (46%)
  matrix products  38.9 us (21%)
  waiting for transfers between devices  31.2 us (17%)
  starting transfers between devices  17.8 us (9%)
  local copies, waits for them, and re-layouts  10.7 us (6%)
  other arithmetic  2.38 us (1%)
    pallas_call x5, Pallas kernels, orthonormal(): pl.pallas_call(gram_schmidt_kernel, out_shape=jax.ShapeDtypeStruct(rows.s...  73.6 us
    dot_general x2, matrix products, cross_gram(): lax.dot_general(left_rows, right_rows, (((0,), (0,)), ((), ())), precisio...  13.8 us
    ppermute x1, waiting for transfers between devices, on_device(): mixed_sum = mixed_sum + lax.ppermute(mixed_sum, 'tx', route)  13.7 us
    pallas_call x1, Pallas kernels, fluxes(): pl.pallas_call(functools.partial(flux_kernel, count), grid=(count,), in_s...  13.7 us
    ppermute x3, waiting for transfers between devices, tree_sum(): value = value + lax.ppermute(value, axis, route)  10.7 us
    dot_general x1, matrix products, on_device(): own_modes = jnp.dot(own_flux, own_basis, precision=high)  8.82 us
    ppermute x3, starting transfers between devices, tree_sum(): value = value + lax.ppermute(value, axis, route)  6.63 us
    ppermute x1, starting transfers between devices, halos(): lax.ppermute(lax.slice_in_dim(block, block.shape[0] - width, None, axis=0...  4.88 us
  transfers between devices with their start and end apart: 14, of which 6 were waited for; matrix products, arithmetic and copies ran while one was open for 15% of the time, Pallas kernels for 39%

profile of v2, /device:TPU:0, one launch (start us, length us, event | category | flops | bytes accessed | tf_op | source)
XLA Modules:
  0.0 188.5 jit_solution(4727840702316372849)
XLA Ops:
  0.0 1.0 fusion.38
  1.0 4.9 %collective-permute-start = (bf16[2,128,256]{2,1,0:T(8,128)(2,1)S(1)}, bf16[2,128,256]{2,1,0:T(8,128)(2,1)S(1)}, u32[]{:S(2)}, u32[]{:S(2)}) collective-permute-start(bf16[2,128,256]{2,1,0:T(8,128)(2,1)S(1)} %get-tuple-element.18), channel_id=1, source_target_pairs={{0,1},{1,2},{2,3},{3,4},{4,5},{5,6},{6,7},{8,9},{9,10},{10,11},{11... | collective-permute-start | bytes 393224 | tf_op jit(solution)/shard_map/ppermute | solution.py:20
  5.9 1.3 collective-permute-start.1
  7.2 1.4 collective-permute-done.low_ref
  8.7 4.1 %collective-permute-done.1.high_ref = bf16[2,128,256]{2,1,0:T(8,128)(2,1)S(1)} collective-permute-done((bf16[2,128,256]{2,1,0:T(8,128)(2,1)S(1)}, bf16[2,128,256]{2,1,0:T(8,128)(2,1)S(1)}, u32[]{:S(2)}, u32[]{:S(2)}) %collective-permute-start.1) | collective-permute-done | bytes 131104 | tf_op jit(solution)/shard_map/ppermute | solution.py:21
  12.8 0.7 copy-done.6
  13.4 13.7 %shard_map.46 = f32[64,128,256]{2,1,0:T(8,128)} custom-call(bf16[2,128,256]{2,1,0:T(8,128)(2,1)} %copy-done.5, bf16[2,128,256]{2,1,0:T(8,128)(2,1)} %copy-done.6, bf16[64,128,256]{2,1,0:T(8,128)(2,1)} %next_ref.1, bf16[64,128,256]{2,1,0:T(8,128)(2,1)} %next_ref.1, bf16[64,128,256]{2,1,0:T(8,128)(2,1)} %next_ref.1, f32[64,128]{1,0:T(8,128)} %coef_ref.1), custom_call_target="tpu_custom_call" | custom-call | tf_op jit(solution)/shard_map/pallas_call | solution.py:96
  27.2 4.8 %constant_dynamic-slice_fusion = f32[4096,256]{1,0:T(8,128)} fusion(f32[8192,256]{1,0:T(8,128)} %bitcast.44, s32[]{:T(128)S(6)} %select_n.90), kind=kLoop, calls=%fused_computation.44 | loop fusion | bytes 8388612 | tf_op jit(solution)/shard_map/dynamic_slice | solution.py:191
  31.9 1.4 copy-done.1
  33.3 1.5 fusion.2
  34.8 6.9 %fusion.6 = f32[256,256]{1,0:T(8,128)S(1)} fusion(f32[64,128,256]{2,1,0:T(8,128)S(1)} %copy-done.1, f32[256]{0:T(256)S(1)} %fusion.2), kind=kOutput, calls=%fused_computation.10 | convolution fusion | flops 3221422080 | bytes 8651776 | tf_op jit(solution)/shard_map/dot_general | solution.py:157
  41.7 2.5 %collective-permute-start.3 = (f32[256,256]{1,0:T(8,128)S(1)}, f32[256,256]{1,0:T(8,128)S(1)}, u32[]{:S(2)}, u32[]{:S(2)}) collective-permute-start(f32[256,256]{1,0:T(8,128)S(1)} %fusion.6), channel_id=1, source_target_pairs={{0,1},{1,0},{2,3},{3,2},{4,5},{5,4},{6,7},{7,6},{8,9},{9,8},{10,11... | collective-permute-start | bytes 786440 | tf_op jit(solution)/shard_map/ppermute | solution.py:42
  44.2 5.6 %collective-permute-done.3 = f32[256,256]{1,0:T(8,128)S(1)} collective-permute-done((f32[256,256]{1,0:T(8,128)S(1)}, f32[256,256]{1,0:T(8,128)S(1)}, u32[]{:S(2)}, u32[]{:S(2)}) %collective-permute-start.3) | collective-permute-done | bytes 262176 | tf_op jit(solution)/shard_map/ppermute | solution.py:42
  49.8 1.6 collective-permute-start.4
  51.4 5.1 %collective-permute-done.4 = f32[256,256]{1,0:T(8,128)S(1)} collective-permute-done((f32[256,256]{1,0:T(8,128)S(1)}, f32[256,256]{1,0:T(8,128)S(1)}, u32[]{:S(2)}, u32[]{:S(2)}) %collective-permute-start.4) | collective-permute-done | bytes 262176 | tf_op jit(solution)/shard_map/ppermute | solution.py:42
  56.6 2.5 %collective-permute-start.5 = (f32[256,256]{1,0:T(8,128)S(1)}, f32[256,256]{1,0:T(8,128)S(1)}, u32[]{:S(2)}, u32[]{:S(2)}) collective-permute-start(f32[256,256]{1,0:T(8,128)S(1)} %add.47), channel_id=1, source_target_pairs={{0,4},{1,5},{2,6},{3,7},{4,0},{5,1},{6,2},{7,3},{8,12},{9,13},{10,... | collective-permute-start | bytes 786440 | tf_op jit(solution)/shard_map/ppermute | solution.py:42
  59.1 0.1 copy.12
  59.2 0.1 copy.6
  59.3 0.7 select_bitcast_fusion.rows_ref
  60.0 14.8 %shard_map.47 = f32[128,256]{1,0:T(8,128)} custom-call(f32[128,256]{1,0:T(8,128)} %select_bitcast_fusion.rows_ref), custom_call_target="tpu_custom_call" | custom-call | tf_op jit(solution)/shard_map/pallas_call | solution.py:142
  74.9 1.9 %collective-permute-start.2 = (f32[256,128]{0,1:T(8,128)}, f32[256,128]{0,1:T(8,128)S(1)}, u32[]{:S(2)}, u32[]{:S(2)}) collective-permute-start(f32[256,128]{0,1:T(8,128)} %bitcast.53), channel_id=1, source_target_pairs={{0,1},{1,0},{2,3},{3,2},{4,5},{5,4},{6,7},{7,6},{8,9},{9,8},{10,11... | collective-permute-start | bytes 393224 | tf_op jit(solution)/shard_map/ppermute | solution.py:32
  76.9 6.9 %fusion.3 = f32[256,256]{1,0:T(8,128)S(1)} fusion(f32[4096,256]{1,0:T(8,128)} %collective-permute-done.6, f32[8192,256]{1,0:T(8,128)} %bitcast.45, s32[]{:T(128)S(6)} %select_n.89), kind=kOutput, calls=%fused_computation.5 | convolution fusion | flops 1610612736 | bytes 8650756 | tf_op jit(solution)/shard_map/dot_general | solution.py:157
  83.8 0.1 copy.8
  84.0 0.1 collective-permute-start.7
  84.1 1.1 fusion.17.rows_ref
  85.2 14.7 %shard_map.48 = f32[128,256]{1,0:T(8,128)} custom-call(f32[128,256]{1,0:T(8,128)} %fusion.17.rows_ref), custom_call_target="tpu_custom_call" | custom-call | tf_op jit(solution)/shard_map/pallas_call | solution.py:142
  99.9 1.5 collective-permute-start.8
  101.5 2.0 %fusion.39.rows_ref = f32[128,256]{1,0:T(8,128)} fusion(f32[256,128]{0,1:T(8,128)} %bitcast.56, f32[256,256]{1,0:T(8,128)S(1)} %add_multiply_fusion), kind=kOutput, calls=%fused_computation.53 | convolution fusion | flops 100663296 | bytes 524288 | tf_op jit(solution)/shard_map/dot_general | solution.py:202
  103.4 14.7 %shard_map.49 = f32[128,256]{1,0:T(8,128)} custom-call(f32[128,256]{1,0:T(8,128)} %fusion.39.rows_ref), custom_call_target="tpu_custom_call" | custom-call | tf_op jit(solution)/shard_map/pallas_call | solution.py:142
  118.1 8.8 %fusion.40 = f32[8192,128]{1,0:T(8,128)} fusion(f32[8192,256]{1,0:T(8,128)} %bitcast.46, f32[256,128]{0,1:T(8,128)} %bitcast.47), kind=kOutput, calls=%fused_computation.54 | convolution fusion | flops 1610612736 | bytes 12713984 | tf_op jit(solution)/shard_map/dot_general | solution.py:212
  127.0 0.5 collective-permute-start.11
  127.5 0.4 fusion.41
  127.9 0.4 fusion.42
  128.3 0.3 collective-permute-start.9
  128.6 13.7 %collective-permute-done.11 = f32[256,256]{1,0:T(8,128)S(1)} collective-permute-done((f32[256,256]{1,0:T(8,128)S(1)}, f32[256,256]{1,0:T(8,128)S(1)}, u32[]{:S(2)}, u32[]{:S(2)}) %collective-permute-start.11) | collective-permute-done | bytes 262176 | tf_op jit(solution)/shard_map/ppermute | solution.py:211
  142.3 0.1 collective-permute-start.12
  142.4 0.4 collective-permute-start.10
  142.9 1.2 collective-permute-done.10
  144.1 0.4 fusion.7
  144.5 0.3 fusion.13
  144.9 0.9 fusion.11.rows_ref
  145.8 14.7 %shard_map.50 = f32[128,256]{1,0:T(8,128)} custom-call(f32[128,256]{1,0:T(8,128)} %fusion.11.rows_ref), custom_call_target="tpu_custom_call" | custom-call | tf_op jit(solution)/shard_map/pallas_call | solution.py:142
  160.5 1.8 fusion.10.rows_ref
  162.3 14.7 %shard_map.51 = f32[128,256]{1,0:T(8,128)} custom-call(f32[128,256]{1,0:T(8,128)} %fusion.10.rows_ref), custom_call_target="tpu_custom_call" | custom-call | tf_op jit(solution)/shard_map/pallas_call | solution.py:142
  177.0 0.8 dynamic-slice_bitcast_fusion
  177.9 4.5 %fusion.24 = f32[8192,64]{0,1:T(8,128)S(1)} fusion(f32[8192,128]{1,0:T(8,128)} %fusion.40, f32[256,64]{0,1:T(8,128)S(1)} %dynamic-slice_bitcast_fusion, pred[]{:T(512)S(6)} %eq.14), kind=kOutput, calls=%fused_computation.34 | convolution fusion | flops 402661376 | bytes 6356993 | tf_op jit(solution)/shard_map/dot_general | solution.py:239
  182.4 4.5 %fusion.5 = f32[8,64,8,128]{3,2,1,0:T(8,128)S(1)} fusion(f32[8192,64]{0,1:T(8,128)S(1)} %fusion.24, f32[8192,128]{1,0:T(8,128)} %collective-permute-done.13, f32[256,64]{0,1:T(8,128)S(1)} %dynamic-slice_bitcast_fusion, pred[]{:T(512)S(6)} %eq.14), kind=kOutput, calls=%fused_computation.8 | convolution fusion | flops 403185664 | bytes 8454145 | tf_op jit(solution)/shard_map/dot_general | solution.py:239
  186.9 1.6 copy.15
  (32 shorter events, 0.4 us)
Async XLA Ops:
  0.0 59.1 %copy-start = (s32[512,128]{1,0:T(8,128)S(1)}, s32[512,128]{1,0:T(8,128)}, u32[]{:S(2)}) copy-start(s32[512,128]{1,0:T(8,128)} %param.6) | copy-start | bytes 786436
  1.0 7.6 %collective-permute-start = (bf16[2,128,256]{2,1,0:T(8,128)(2,1)S(1)}, bf16[2,128,256]{2,1,0:T(8,128)(2,1)S(1)}, u32[]{:S(2)}, u32[]{:S(2)}) collective-permute-start(bf16[2,128,256]{2,1,0:T(8,128)(2,1)S(1)} %get-tuple-element.18), channel_id=1, source_target_pairs={{0,1},{1,2},{2,3},{3,4},{4,5},{5,6},{6,7},{8,9},{9,10},{10,11},{11... | collective-permute-start | bytes 393224 | tf_op jit(solution)/shard_map/ppermute | solution.py:20
  5.9 6.9 %collective-permute-start.1 = (bf16[2,128,256]{2,1,0:T(8,128)(2,1)S(1)}, bf16[2,128,256]{2,1,0:T(8,128)(2,1)S(1)}, u32[]{:S(2)}, u32[]{:S(2)}) collective-permute-start(bf16[2,128,256]{2,1,0:T(8,128)(2,1)S(1)} %get-tuple-element.17), channel_id=1, source_target_pairs={{1,0},{2,1},{3,2},{4,3},{5,4},{6,5},{7,6},{9,8},{10,9},{11,10},{12... | collective-permute-start | bytes 393224 | tf_op jit(solution)/shard_map/ppermute | solution.py:21
  8.7 4.1 %copy-start.5 = (bf16[2,128,256]{2,1,0:T(8,128)(2,1)}, bf16[2,128,256]{2,1,0:T(8,128)(2,1)S(1)}, u32[]{:S(2)}) copy-start(bf16[2,128,256]{2,1,0:T(8,128)(2,1)S(1)} %collective-permute-done.low_ref) | copy-start | bytes 393220
  12.8 0.7 copy-start.6
  27.2 6.2 %copy-start.1 = (f32[64,128,256]{2,1,0:T(8,128)S(1)}, f32[64,128,256]{2,1,0:T(8,128)}, u32[]{:S(2)}) copy-start(f32[64,128,256]{2,1,0:T(8,128)} %shard_map.46) | copy-start | bytes 25165828
  31.9 45.0 %collective-permute-start.6 = (f32[4096,256]{1,0:T(8,128)}, f32[4096,256]{1,0:T(8,128)}, u32[]{:S(2)}, u32[]{:S(2)}) collective-permute-start(f32[4096,256]{1,0:T(8,128)} %constant_dynamic-slice_fusion), channel_id=1, source_target_pairs={{0,8},{8,0},{1,9},{9,1},{2,10},{10,2},{3,11},{11,3},{4,12},{12,4},... | collective-permute-start | bytes 12582920 | tf_op jit(solution)/shard_map/ppermute | solution.py:32
  34.8 24.5 %copy-start.4 = (s32[256,128]{1,0:T(8,128)S(1)}, s32[256,128]{1,0:T(8,128)}, u32[]{:S(2)}) copy-start(s32[256,128]{1,0:T(8,128)} %param.7) | copy-start | bytes 393220
  41.7 8.1 %collective-permute-start.3 = (f32[256,256]{1,0:T(8,128)S(1)}, f32[256,256]{1,0:T(8,128)S(1)}, u32[]{:S(2)}, u32[]{:S(2)}) collective-permute-start(f32[256,256]{1,0:T(8,128)S(1)} %fusion.6), channel_id=1, source_target_pairs={{0,1},{1,0},{2,3},{3,2},{4,5},{5,4},{6,7},{7,6},{8,9},{9,8},{10,11... | collective-permute-start | bytes 786440 | tf_op jit(solution)/shard_map/ppermute | solution.py:42
  49.8 6.8 %collective-permute-start.4 = (f32[256,256]{1,0:T(8,128)S(1)}, f32[256,256]{1,0:T(8,128)S(1)}, u32[]{:S(2)}, u32[]{:S(2)}) collective-permute-start(f32[256,256]{1,0:T(8,128)S(1)} %add.46), channel_id=1, source_target_pairs={{0,2},{1,3},{2,0},{3,1},{4,6},{5,7},{6,4},{7,5},{8,10},{9,11},{10,... | collective-permute-start | bytes 786440 | tf_op jit(solution)/shard_map/ppermute | solution.py:42
  56.6 20.2 %collective-permute-start.5 = (f32[256,256]{1,0:T(8,128)S(1)}, f32[256,256]{1,0:T(8,128)S(1)}, u32[]{:S(2)}, u32[]{:S(2)}) collective-permute-start(f32[256,256]{1,0:T(8,128)S(1)} %add.47), channel_id=1, source_target_pairs={{0,4},{1,5},{2,6},{3,7},{4,0},{5,1},{6,2},{7,3},{8,12},{9,13},{10,... | collective-permute-start | bytes 786440 | tf_op jit(solution)/shard_map/ppermute | solution.py:42
  74.9 9.3 %collective-permute-start.2 = (f32[256,128]{0,1:T(8,128)}, f32[256,128]{0,1:T(8,128)S(1)}, u32[]{:S(2)}, u32[]{:S(2)}) collective-permute-start(f32[256,128]{0,1:T(8,128)} %bitcast.53), channel_id=1, source_target_pairs={{0,1},{1,0},{2,3},{3,2},{4,5},{5,4},{6,7},{7,6},{8,9},{9,8},{10,11... | collective-permute-start | bytes 393224 | tf_op jit(solution)/shard_map/ppermute | solution.py:32
  76.8 7.3 %copy-start.3 = (f32[128,256]{1,0:T(8,128)S(1)}, f32[128,256]{1,0:T(8,128)}, u32[]{:S(2)}) copy-start(f32[128,256]{1,0:T(8,128)} %shard_map.47) | copy-start | bytes 393220
  84.0 15.9 %collective-permute-start.7 = (f32[256,256]{1,0:T(8,128)S(1)}, f32[256,256]{1,0:T(8,128)S(1)}, u32[]{:S(2)}, u32[]{:S(2)}) collective-permute-start(f32[256,256]{1,0:T(8,128)S(1)} %bitcast_select_fusion), channel_id=1, source_target_pairs={{0,1},{1,0},{2,3},{3,2},{4,5},{5,4},{6,7},{7,6},{8,9},{9,8},{10,11... | collective-permute-start | bytes 786440 | tf_op jit(solution)/shard_map/ppermute | solution.py:204
  99.9 18.2 %collective-permute-start.8 = (f32[256,256]{1,0:T(8,128)S(1)}, f32[256,256]{1,0:T(8,128)S(1)}, u32[]{:S(2)}, u32[]{:S(2)}) collective-permute-start(f32[256,256]{1,0:T(8,128)S(1)} %add.51), channel_id=1, source_target_pairs={{0,2},{1,3},{2,0},{3,1},{4,6},{5,7},{6,4},{7,5},{8,10},{9,11},{10,... | collective-permute-start | bytes 786440 | tf_op jit(solution)/shard_map/ppermute | solution.py:204
  118.1 9.4 %copy-start.2 = (f32[128,256]{1,0:T(8,128)S(1)}, f32[128,256]{1,0:T(8,128)}, u32[]{:S(2)}) copy-start(f32[128,256]{1,0:T(8,128)} %shard_map.49) | copy-start | bytes 393220
  126.9 55.5 %collective-permute-start.13 = (f32[8192,128]{1,0:T(8,128)}, f32[8192,128]{1,0:T(8,128)}, u32[]{:S(2)}, u32[]{:S(2)}) collective-permute-start(f32[8192,128]{1,0:T(8,128)} %fusion.40), channel_id=1, source_target_pairs={{0,8},{8,0},{1,9},{9,1},{2,10},{10,2},{3,11},{11,3},{4,12},{12,4},... | collective-permute-start | bytes 12582920 | tf_op jit(solution)/shard_map/ppermute | solution.py:32
  127.0 15.3 %collective-permute-start.11 = (f32[256,256]{1,0:T(8,128)S(1)}, f32[256,256]{1,0:T(8,128)S(1)}, u32[]{:S(2)}, u32[]{:S(2)}) collective-permute-start(f32[256,256]{1,0:T(8,128)S(1)} %add.52), channel_id=1, source_target_pairs={{0,4},{1,5},{2,6},{3,7},{4,0},{5,1},{6,2},{7,3},{8,12},{9,13},{10,... | collective-permute-start | bytes 786440 | tf_op jit(solution)/shard_map/ppermute | solution.py:211
  128.3 14.6 %collective-permute-start.9 = (f32[128,128]{0,1:T(8,128)S(1)}, f32[128,128]{0,1:T(8,128)S(1)}, u32[]{:S(2)}, u32[]{:S(2)}) collective-permute-start(f32[128,128]{0,1:T(8,128)S(1)} %fusion.42), channel_id=1, source_target_pairs={{0,8},{8,0},{1,9},{9,1},{2,10},{10,2},{3,11},{11,3},{4,12},{12,4},... | collective-permute-start | bytes 196616 | tf_op jit(solution)/shard_map/ppermute | solution.py:32
  142.3 1.8 collective-permute-start.12
  142.4 1.7 collective-permute-start.10

commit v3 on v2

--- a/solution.py
+++ b/solution.py
@@ -207,13 +207,22 @@
             mixed_sum = mixed_sum + received
         else:
             own_basis = orthonormal(product)
+    if hops:
+        received = lax.ppermute(mixed_sum, "tx", hops.pop(0))
+        own_modes = jnp.dot(own_flux, own_basis, precision=high)
+        own_modes, received = lax.optimization_barrier((own_modes, received))
+        mixed_sum = mixed_sum + received
+    else:
+        own_modes = jnp.dot(own_flux, own_basis, precision=high)
     for route in hops:
         mixed_sum = mixed_sum + lax.ppermute(mixed_sum, "tx", route)
-    own_modes = jnp.dot(own_flux, own_basis, precision=high)
     mixed_gram = mixed_sum + partner(mixed_sum, "run", 0)
-    other_modes = partner(own_modes, "run", 0)
     own_block = jnp.dot(own_basis.T, jnp.dot(own_gram, own_basis, precision=highest), precision=highest)
     other_block, other_basis = partner((own_block, own_basis), "run", 0)
+    own_modes, mixed_gram, other_block, other_basis = lax.optimization_barrier(
+        (own_modes, mixed_gram, other_block, other_basis)
+    )
+    other_modes = partner(own_modes, "run", 0)
     first_basis_set = jnp.where(is_first, own_basis, other_basis)
     last_basis_set = jnp.where(is_first, other_basis, own_basis)
     mixed_block = jnp.dot(

time: 189 us -> 177 us (0.937)
  waiting for transfers between devices: 31.2 us -> 18.5 us
    ppermute x1 -> x0, waiting for transfers between devices: 13.7 us -> none  [on_device(): mixed_sum = mixed_sum + lax.ppermute(mixed_sum, 'tx', route)]
  transfers between devices with their start and end apart: 14 -> 14, of which waited for: 6 -> 7; matrix products, arithmetic and copies ran while one was open for 15% -> 19% of each run, Pallas kernels for 39% -> 42%
where the time goes in v3:
time: 177 us; the launch traced here: 176 us
  Pallas kernels  87.4 us (49%)
  matrix products  38.9 us (22%)
  waiting for transfers between devices  18.5 us (10%)
  starting transfers between devices  17.9 us (10%)
  local copies, waits for them, and re-layouts  10.7 us (6%)
  other arithmetic  2.41 us (1%)
    pallas_call x5, Pallas kernels, orthonormal(): pl.pallas_call(gram_schmidt_kernel, out_shape=jax.ShapeDtypeStruct(rows.s...  73.6 us
    dot_general x2, matrix products, cross_gram(): lax.dot_general(left_rows, right_rows, (((0,), (0,)), ((), ())), precisio...  13.8 us
    pallas_call x1, Pallas kernels, fluxes(): pl.pallas_call(functools.partial(flux_kernel, count), grid=(count,), in_s...  13.7 us
    ppermute x3, waiting for transfers between devices, tree_sum(): value = value + lax.ppermute(value, axis, route)  10.7 us
    dot_general x1, matrix products, on_device(): own_modes = jnp.dot(own_flux, own_basis, precision=high)  8.79 us
    ppermute x3, starting transfers between devices, tree_sum(): value = value + lax.ppermute(value, axis, route)  6.63 us
    ppermute x1, starting transfers between devices, halos(): lax.ppermute(lax.slice_in_dim(block, block.shape[0] - width, None, axis=0...  4.88 us
    dynamic_slice x1, local copies, waits for them, and re-layouts, on_device(): lax.dynamic_slice_in_dim(own_flux, (1 - member) * half_rows, half_rows, 0)  4.76 us
  transfers between devices with their start and end apart: 14, of which 7 were waited for; matrix products, arithmetic and copies ran while one was open for 19% of the time, Pallas kernels for 42%

profile of v3, /device:TPU:0, one launch (start us, length us, event | category | flops | bytes accessed | tf_op | source)
XLA Modules:
  0.0 176.0 jit_solution(11810069570861125888)
XLA Ops:
  0.0 1.0 fusion.37
  1.0 4.9 %collective-permute-start = (bf16[2,128,256]{2,1,0:T(8,128)(2,1)S(1)}, bf16[2,128,256]{2,1,0:T(8,128)(2,1)S(1)}, u32[]{:S(2)}, u32[]{:S(2)}) collective-permute-start(bf16[2,128,256]{2,1,0:T(8,128)(2,1)S(1)} %get-tuple-element.30), channel_id=1, source_target_pairs={{0,1},{1,2},{2,3},{3,4},{4,5},{5,6},{6,7},{8,9},{9,10},{10,11},{11... | collective-permute-start | bytes 393224 | tf_op jit(solution)/shard_map/ppermute | solution.py:20
  5.9 1.3 collective-permute-start.1
  7.2 1.4 collective-permute-done.low_ref
  8.7 4.1 %collective-permute-done.1.high_ref = bf16[2,128,256]{2,1,0:T(8,128)(2,1)S(1)} collective-permute-done((bf16[2,128,256]{2,1,0:T(8,128)(2,1)S(1)}, bf16[2,128,256]{2,1,0:T(8,128)(2,1)S(1)}, u32[]{:S(2)}, u32[]{:S(2)}) %collective-permute-start.1) | collective-permute-done | bytes 131104 | tf_op jit(solution)/shard_map/ppermute | solution.py:21
  12.8 0.7 copy-done.6
  13.4 13.7 %shard_map.46 = f32[64,128,256]{2,1,0:T(8,128)} custom-call(bf16[2,128,256]{2,1,0:T(8,128)(2,1)} %copy-done.5, bf16[2,128,256]{2,1,0:T(8,128)(2,1)} %copy-done.6, bf16[64,128,256]{2,1,0:T(8,128)(2,1)} %next_ref.1, bf16[64,128,256]{2,1,0:T(8,128)(2,1)} %next_ref.1, bf16[64,128,256]{2,1,0:T(8,128)(2,1)} %next_ref.1, f32[64,128]{1,0:T(8,128)} %coef_ref.1), custom_call_target="tpu_custom_call" | custom-call | tf_op jit(solution)/shard_map/pallas_call | solution.py:96
  27.2 4.8 %constant_dynamic-slice_fusion = f32[4096,256]{1,0:T(8,128)} fusion(f32[8192,256]{1,0:T(8,128)} %bitcast.44, s32[]{:T(128)S(6)} %select_n.90), kind=kLoop, calls=%fused_computation.43 | loop fusion | bytes 8388612 | tf_op jit(solution)/shard_map/dynamic_slice | solution.py:191
  31.9 1.4 copy-done.1
  33.3 1.5 fusion.2
  34.8 6.9 %fusion.6 = f32[256,256]{1,0:T(8,128)S(1)} fusion(f32[64,128,256]{2,1,0:T(8,128)S(1)} %copy-done.1, f32[256]{0:T(256)S(1)} %fusion.2), kind=kOutput, calls=%fused_computation.10 | convolution fusion | flops 3221422080 | bytes 8651776 | tf_op jit(solution)/shard_map/dot_general | solution.py:157
  41.7 2.5 %collective-permute-start.3 = (f32[256,256]{1,0:T(8,128)S(1)}, f32[256,256]{1,0:T(8,128)S(1)}, u32[]{:S(2)}, u32[]{:S(2)}) collective-permute-start(f32[256,256]{1,0:T(8,128)S(1)} %fusion.6), channel_id=1, source_target_pairs={{0,1},{1,0},{2,3},{3,2},{4,5},{5,4},{6,7},{7,6},{8,9},{9,8},{10,11... | collective-permute-start | bytes 786440 | tf_op jit(solution)/shard_map/ppermute | solution.py:42
  44.2 5.6 %collective-permute-done.3 = f32[256,256]{1,0:T(8,128)S(1)} collective-permute-done((f32[256,256]{1,0:T(8,128)S(1)}, f32[256,256]{1,0:T(8,128)S(1)}, u32[]{:S(2)}, u32[]{:S(2)}) %collective-permute-start.3) | collective-permute-done | bytes 262176 | tf_op jit(solution)/shard_map/ppermute | solution.py:42
  49.8 1.6 collective-permute-start.4
  51.4 5.1 %collective-permute-done.4 = f32[256,256]{1,0:T(8,128)S(1)} collective-permute-done((f32[256,256]{1,0:T(8,128)S(1)}, f32[256,256]{1,0:T(8,128)S(1)}, u32[]{:S(2)}, u32[]{:S(2)}) %collective-permute-start.4) | collective-permute-done | bytes 262176 | tf_op jit(solution)/shard_map/ppermute | solution.py:42
  56.6 2.5 %collective-permute-start.5 = (f32[256,256]{1,0:T(8,128)S(1)}, f32[256,256]{1,0:T(8,128)S(1)}, u32[]{:S(2)}, u32[]{:S(2)}) collective-permute-start(f32[256,256]{1,0:T(8,128)S(1)} %add.47), channel_id=1, source_target_pairs={{0,4},{1,5},{2,6},{3,7},{4,0},{5,1},{6,2},{7,3},{8,12},{9,13},{10,... | collective-permute-start | bytes 786440 | tf_op jit(solution)/shard_map/ppermute | solution.py:42
  59.1 0.1 copy.12
  59.2 0.1 copy.6
  59.3 0.7 select_bitcast_fusion.rows_ref
  60.0 14.8 %shard_map.47 = f32[128,256]{1,0:T(8,128)} custom-call(f32[128,256]{1,0:T(8,128)} %select_bitcast_fusion.rows_ref), custom_call_target="tpu_custom_call" | custom-call | tf_op jit(solution)/shard_map/pallas_call | solution.py:142
  74.9 1.9 %collective-permute-start.2 = (f32[256,128]{0,1:T(8,128)}, f32[256,128]{0,1:T(8,128)S(1)}, u32[]{:S(2)}, u32[]{:S(2)}) collective-permute-start(f32[256,128]{0,1:T(8,128)} %bitcast.53), channel_id=1, source_target_pairs={{0,1},{1,0},{2,3},{3,2},{4,5},{5,4},{6,7},{7,6},{8,9},{9,8},{10,11... | collective-permute-start | bytes 393224 | tf_op jit(solution)/shard_map/ppermute | solution.py:32
  76.9 6.9 %fusion.3 = f32[256,256]{1,0:T(8,128)S(1)} fusion(f32[4096,256]{1,0:T(8,128)} %collective-permute-done.6, f32[8192,256]{1,0:T(8,128)} %bitcast.45, s32[]{:T(128)S(6)} %select_n.89), kind=kOutput, calls=%fused_computation.5 | convolution fusion | flops 1610612736 | bytes 8650756 | tf_op jit(solution)/shard_map/dot_general | solution.py:157
  83.8 0.1 copy.8
  84.0 0.1 collective-permute-start.7
  84.1 1.1 fusion.16.rows_ref
  85.2 14.7 %shard_map.48 = f32[128,256]{1,0:T(8,128)} custom-call(f32[128,256]{1,0:T(8,128)} %fusion.16.rows_ref), custom_call_target="tpu_custom_call" | custom-call | tf_op jit(solution)/shard_map/pallas_call | solution.py:142
  99.9 1.5 collective-permute-start.8
  101.5 2.0 %fusion.38.rows_ref = f32[128,256]{1,0:T(8,128)} fusion(f32[256,128]{0,1:T(8,128)} %bitcast.56, f32[256,256]{1,0:T(8,128)S(1)} %add_multiply_fusion), kind=kOutput, calls=%fused_computation.52 | convolution fusion | flops 100663296 | bytes 524288 | tf_op jit(solution)/shard_map/dot_general | solution.py:202
  103.4 14.7 %shard_map.49 = f32[128,256]{1,0:T(8,128)} custom-call(f32[128,256]{1,0:T(8,128)} %fusion.38.rows_ref), custom_call_target="tpu_custom_call" | custom-call | tf_op jit(solution)/shard_map/pallas_call | solution.py:142
  118.2 0.5 collective-permute-start.9
  118.7 8.8 %fusion.39 = f32[8192,128]{1,0:T(8,128)} fusion(f32[8192,256]{1,0:T(8,128)} %bitcast.46, f32[256,128]{0,1:T(8,128)} %bitcast.47), kind=kOutput, calls=%fused_computation.53 | convolution fusion | flops 1610612736 | bytes 12713984 | tf_op jit(solution)/shard_map/dot_general | solution.py:212
  127.5 0.4 fusion.40
  127.8 1.3 collective-permute-done.9
  129.3 0.4 fusion.41
  129.7 0.6 collective-permute-start.11
  130.2 0.6 collective-permute-done.10
  130.9 0.3 collective-permute-done.11
  131.2 0.4 collective-permute-start.13
  131.5 0.4 fusion.7
  131.9 0.3 fusion.12
  132.3 0.9 fusion.10.rows_ref
  133.2 14.7 %shard_map.50 = f32[128,256]{1,0:T(8,128)} custom-call(f32[128,256]{1,0:T(8,128)} %fusion.10.rows_ref), custom_call_target="tpu_custom_call" | custom-call | tf_op jit(solution)/shard_map/pallas_call | solution.py:142
  147.9 1.8 %fusion.9.rows_ref = f32[128,256]{1,0:T(8,128)} fusion(f32[128,256]{1,0:T(8,128)} %shard_map.50, f32[128,128]{0,1:T(8,128)S(1)} %get-tuple-element.32, f32[128,128]{0,1:T(8,128)S(1)} %bitcast.55, f32[128,128]{0,1:T(8,128)S(1)} %copy.9, f32[128,128]{0,1:T(8,128)S(1)} %get-tuple-element.31), kind=kOutput, calls=%fused_computation.17 | convolution fusion | flops 100859904 | bytes 524288 | tf_op jit(solution)/shard_map/dot_general | solution.py:152
  149.8 14.7 %shard_map.51 = f32[128,256]{1,0:T(8,128)} custom-call(f32[128,256]{1,0:T(8,128)} %fusion.9.rows_ref), custom_call_target="tpu_custom_call" | custom-call | tf_op jit(solution)/shard_map/pallas_call | solution.py:142
  164.5 0.8 dynamic-slice_bitcast_fusion
  165.3 4.5 %fusion.22 = f32[8192,64]{0,1:T(8,128)S(1)} fusion(f32[8192,128]{1,0:T(8,128)} %collective-permute-done.13, f32[256,64]{0,1:T(8,128)S(1)} %dynamic-slice_bitcast_fusion, pred[]{:T(512)S(6)} %eq.14), kind=kOutput, calls=%fused_computation.32 | convolution fusion | flops 402661376 | bytes 6356993 | tf_op jit(solution)/shard_map/dot_general | solution.py:248
  169.8 4.5 %fusion.5 = f32[8,64,8,128]{3,2,1,0:T(8,128)S(1)} fusion(f32[8192,64]{0,1:T(8,128)S(1)} %fusion.22, f32[8192,128]{1,0:T(8,128)} %fusion.39, f32[256,64]{0,1:T(8,128)S(1)} %dynamic-slice_bitcast_fusion, pred[]{:T(512)S(6)} %eq.14), kind=kOutput, calls=%fused_computation.8 | convolution fusion | flops 403185664 | bytes 8454145 | tf_op jit(solution)/shard_map/dot_general | solution.py:248
  174.4 1.6 copy.15
  (33 shorter events, 0.5 us)
Async XLA Ops:
  0.0 59.1 %copy-start = (s32[512,128]{1,0:T(8,128)S(1)}, s32[512,128]{1,0:T(8,128)}, u32[]{:S(2)}) copy-start(s32[512,128]{1,0:T(8,128)} %param.6) | copy-start | bytes 786436
  1.0 7.6 %collective-permute-start = (bf16[2,128,256]{2,1,0:T(8,128)(2,1)S(1)}, bf16[2,128,256]{2,1,0:T(8,128)(2,1)S(1)}, u32[]{:S(2)}, u32[]{:S(2)}) collective-permute-start(bf16[2,128,256]{2,1,0:T(8,128)(2,1)S(1)} %get-tuple-element.30), channel_id=1, source_target_pairs={{0,1},{1,2},{2,3},{3,4},{4,5},{5,6},{6,7},{8,9},{9,10},{10,11},{11... | collective-permute-start | bytes 393224 | tf_op jit(solution)/shard_map/ppermute | solution.py:20
  5.9 6.9 %collective-permute-start.1 = (bf16[2,128,256]{2,1,0:T(8,128)(2,1)S(1)}, bf16[2,128,256]{2,1,0:T(8,128)(2,1)S(1)}, u32[]{:S(2)}, u32[]{:S(2)}) collective-permute-start(bf16[2,128,256]{2,1,0:T(8,128)(2,1)S(1)} %get-tuple-element.29), channel_id=1, source_target_pairs={{1,0},{2,1},{3,2},{4,3},{5,4},{6,5},{7,6},{9,8},{10,9},{11,10},{12... | collective-permute-start | bytes 393224 | tf_op jit(solution)/shard_map/ppermute | solution.py:21
  8.7 4.1 %copy-start.5 = (bf16[2,128,256]{2,1,0:T(8,128)(2,1)}, bf16[2,128,256]{2,1,0:T(8,128)(2,1)S(1)}, u32[]{:S(2)}) copy-start(bf16[2,128,256]{2,1,0:T(8,128)(2,1)S(1)} %collective-permute-done.low_ref) | copy-start | bytes 393220
  12.8 0.7 copy-start.6
  27.2 6.2 %copy-start.1 = (f32[64,128,256]{2,1,0:T(8,128)S(1)}, f32[64,128,256]{2,1,0:T(8,128)}, u32[]{:S(2)}) copy-start(f32[64,128,256]{2,1,0:T(8,128)} %shard_map.46) | copy-start | bytes 25165828
  31.9 45.0 %collective-permute-start.6 = (f32[4096,256]{1,0:T(8,128)}, f32[4096,256]{1,0:T(8,128)}, u32[]{:S(2)}, u32[]{:S(2)}) collective-permute-start(f32[4096,256]{1,0:T(8,128)} %constant_dynamic-slice_fusion), channel_id=1, source_target_pairs={{0,8},{8,0},{1,9},{9,1},{2,10},{10,2},{3,11},{11,3},{4,12},{12,4},... | collective-permute-start | bytes 12582920 | tf_op jit(solution)/shard_map/ppermute | solution.py:32
  34.8 24.5 %copy-start.4 = (s32[256,128]{1,0:T(8,128)S(1)}, s32[256,128]{1,0:T(8,128)}, u32[]{:S(2)}) copy-start(s32[256,128]{1,0:T(8,128)} %param.7) | copy-start | bytes 393220
  41.7 8.1 %collective-permute-start.3 = (f32[256,256]{1,0:T(8,128)S(1)}, f32[256,256]{1,0:T(8,128)S(1)}, u32[]{:S(2)}, u32[]{:S(2)}) collective-permute-start(f32[256,256]{1,0:T(8,128)S(1)} %fusion.6), channel_id=1, source_target_pairs={{0,1},{1,0},{2,3},{3,2},{4,5},{5,4},{6,7},{7,6},{8,9},{9,8},{10,11... | collective-permute-start | bytes 786440 | tf_op jit(solution)/shard_map/ppermute | solution.py:42
  49.8 6.8 %collective-permute-start.4 = (f32[256,256]{1,0:T(8,128)S(1)}, f32[256,256]{1,0:T(8,128)S(1)}, u32[]{:S(2)}, u32[]{:S(2)}) collective-permute-start(f32[256,256]{1,0:T(8,128)S(1)} %add.46), channel_id=1, source_target_pairs={{0,2},{1,3},{2,0},{3,1},{4,6},{5,7},{6,4},{7,5},{8,10},{9,11},{10,... | collective-permute-start | bytes 786440 | tf_op jit(solution)/shard_map/ppermute | solution.py:42
  56.6 20.2 %collective-permute-start.5 = (f32[256,256]{1,0:T(8,128)S(1)}, f32[256,256]{1,0:T(8,128)S(1)}, u32[]{:S(2)}, u32[]{:S(2)}) collective-permute-start(f32[256,256]{1,0:T(8,128)S(1)} %add.47), channel_id=1, source_target_pairs={{0,4},{1,5},{2,6},{3,7},{4,0},{5,1},{6,2},{7,3},{8,12},{9,13},{10,... | collective-permute-start | bytes 786440 | tf_op jit(solution)/shard_map/ppermute | solution.py:42
  74.9 9.3 %collective-permute-start.2 = (f32[256,128]{0,1:T(8,128)}, f32[256,128]{0,1:T(8,128)S(1)}, u32[]{:S(2)}, u32[]{:S(2)}) collective-permute-start(f32[256,128]{0,1:T(8,128)} %bitcast.53), channel_id=1, source_target_pairs={{0,1},{1,0},{2,3},{3,2},{4,5},{5,4},{6,7},{7,6},{8,9},{9,8},{10,11... | collective-permute-start | bytes 393224 | tf_op jit(solution)/shard_map/ppermute | solution.py:32
  76.8 7.3 %copy-start.3 = (f32[128,256]{1,0:T(8,128)S(1)}, f32[128,256]{1,0:T(8,128)}, u32[]{:S(2)}) copy-start(f32[128,256]{1,0:T(8,128)} %shard_map.47) | copy-start | bytes 393220
  84.0 15.9 %collective-permute-start.7 = (f32[256,256]{1,0:T(8,128)S(1)}, f32[256,256]{1,0:T(8,128)S(1)}, u32[]{:S(2)}, u32[]{:S(2)}) collective-permute-start(f32[256,256]{1,0:T(8,128)S(1)} %bitcast_select_fusion), channel_id=1, source_target_pairs={{0,1},{1,0},{2,3},{3,2},{4,5},{5,4},{6,7},{7,6},{8,9},{9,8},{10,11... | collective-permute-start | bytes 786440 | tf_op jit(solution)/shard_map/ppermute | solution.py:204
  99.9 18.2 %collective-permute-start.8 = (f32[256,256]{1,0:T(8,128)S(1)}, f32[256,256]{1,0:T(8,128)S(1)}, u32[]{:S(2)}, u32[]{:S(2)}) collective-permute-start(f32[256,256]{1,0:T(8,128)S(1)} %add.51), channel_id=1, source_target_pairs={{0,2},{1,3},{2,0},{3,1},{4,6},{5,7},{6,4},{7,5},{8,10},{9,11},{10,... | collective-permute-start | bytes 786440 | tf_op jit(solution)/shard_map/ppermute | solution.py:204
  118.1 9.3 %copy-start.2 = (f32[128,256]{1,0:T(8,128)S(1)}, f32[128,256]{1,0:T(8,128)}, u32[]{:S(2)}) copy-start(f32[128,256]{1,0:T(8,128)} %shard_map.49) | copy-start | bytes 393220
  118.2 11.0 %collective-permute-start.9 = (f32[256,256]{1,0:T(8,128)S(1)}, f32[256,256]{1,0:T(8,128)S(1)}, u32[]{:S(2)}, u32[]{:S(2)}) collective-permute-start(f32[256,256]{1,0:T(8,128)S(1)} %add.52), channel_id=1, source_target_pairs={{0,4},{1,5},{2,6},{3,7},{4,0},{5,1},{6,2},{7,3},{8,12},{9,13},{10,... | collective-permute-start | bytes 786440 | tf_op jit(solution)/shard_map/ppermute | solution.py:211
  127.5 3.7 %collective-permute-start.12 = (f32[256,128]{0,1:T(8,128)S(1)}, f32[256,128]{0,1:T(8,128)S(1)}, u32[]{:S(2)}, u32[]{:S(2)}) collective-permute-start(f32[256,128]{0,1:T(8,128)S(1)} %bitcast.48), channel_id=1, source_target_pairs={{0,8},{8,0},{1,9},{9,1},{2,10},{10,2},{3,11},{11,3},{4,12},{12,4},... | collective-permute-start | bytes 393224 | tf_op jit(solution)/shard_map/ppermute | solution.py:32
  129.2 1.6 collective-permute-start.10
  129.7 1.5 collective-permute-start.11
  131.2 34.2 %collective-permute-start.13 = (f32[8192,128]{1,0:T(8,128)}, f32[8192,128]{1,0:T(8,128)}, u32[]{:S(2)}, u32[]{:S(2)}) collective-permute-start(f32[8192,128]{1,0:T(8,128)} %fusion.39), channel_id=1, source_target_pairs={{0,8},{8,0},{1,9},{9,1},{2,10},{10,2},{3,11},{11,3},{4,12},{12,4},... | collective-permute-start | bytes 12582920 | tf_op jit(solution)/shard_map/ppermute | solution.py:32

commit v4 on v3

--- a/solution.py
+++ b/solution.py
@@ -188,10 +188,10 @@
     own_flux = fluxes(halo_low, snapshots, halo_high, coefficient).reshape(rows_here, order_size)
     half_rows = rows_here // 2
     half_start = member * half_rows
-    sent_rows = lax.dynamic_slice_in_dim(own_flux, (1 - member) * half_rows, half_rows, 0)
-    other_rows = partner(sent_rows, "run", 0)
+    other_flux = partner(own_flux, "run", 0)
     mixed_half = cross_gram(
-        lax.dynamic_slice_in_dim(own_flux, half_start, half_rows, 0), other_rows
+        lax.dynamic_slice_in_dim(own_flux, half_start, half_rows, 0),
+        lax.dynamic_slice_in_dim(other_flux, half_start, half_rows, 0),
     )
     mixed_half = jnp.where(is_first, mixed_half, mixed_half.T)
     own_gram = tree_sum(self_gram(own_flux), "tx") / cells_total

time: 177 us -> 178 us (level)
  local copies, waits for them, and re-layouts: 10.7 us -> 5.34 us
  other arithmetic: 2.41 us -> 5.94 us
  waiting for transfers between devices: 18.5 us -> 21 us
    dynamic_slice x1 -> x0, local copies, waits for them, and re-layouts: 4.76 us -> none  [on_device(): lax.dynamic_slice_in_dim(own_flux, (1 - member) * half_rows, half_rows, 0)]
    reduce_sum x1, other arithmetic: 1.45 us -> 4.98 us  [self_gram(): missing = jnp.sum(lower * lower, axis=0)]
  transfers between devices with their start and end apart: 14 -> 14, of which waited for: 7 -> 7; matrix products, arithmetic and copies ran while one was open for 19% -> 21% of each run, Pallas kernels for 42% -> 42%
where the time goes in v4:
time: 178 us; the launch traced here: 177 us
  Pallas kernels  87.4 us (49%)
  matrix products  38.9 us (22%)
  waiting for transfers between devices  21 us (12%)
  starting transfers between devices  18.3 us (10%)
  other arithmetic  5.94 us (3%)
  local copies, waits for them, and re-layouts  5.34 us (3%)
    pallas_call x5, Pallas kernels, orthonormal(): pl.pallas_call(gram_schmidt_kernel, out_shape=jax.ShapeDtypeStruct(rows.s...  73.6 us
    dot_general x2, matrix products, cross_gram(): lax.dot_general(left_rows, right_rows, (((0,), (0,)), ((), ())), precisio...  13.8 us
    pallas_call x1, Pallas kernels, fluxes(): pl.pallas_call(functools.partial(flux_kernel, count), grid=(count,), in_s...  13.7 us
    ppermute x3, waiting for transfers between devices, tree_sum(): value = value + lax.ppermute(value, axis, route)  12.2 us
    dot_general x1, matrix products, on_device(): own_modes = jnp.dot(own_flux, own_basis, precision=high)  8.79 us
    ppermute x3, starting transfers between devices, tree_sum(): value = value + lax.ppermute(value, axis, route)  6.99 us
    reduce_sum x1, other arithmetic, self_gram(): missing = jnp.sum(lower * lower, axis=0)  4.98 us
    ppermute x1, starting transfers between devices, halos(): lax.ppermute(lax.slice_in_dim(block, block.shape[0] - width, None, axis=0...  4.88 us
  transfers between devices with their start and end apart: 14, of which 7 were waited for; matrix products, arithmetic and copies ran while one was open for 21% of the time, Pallas kernels for 42%

profile of v4, /device:TPU:0, one launch (start us, length us, event | category | flops | bytes accessed | tf_op | source)
XLA Modules:
  0.0 177.0 jit_solution(15798912399026995584)
XLA Ops:
  0.0 1.0 fusion.38
  1.0 4.9 %collective-permute-start = (bf16[2,128,256]{2,1,0:T(8,128)(2,1)S(1)}, bf16[2,128,256]{2,1,0:T(8,128)(2,1)S(1)}, u32[]{:S(2)}, u32[]{:S(2)}) collective-permute-start(bf16[2,128,256]{2,1,0:T(8,128)(2,1)S(1)} %get-tuple-element.30), channel_id=1, source_target_pairs={{0,1},{1,2},{2,3},{3,4},{4,5},{5,6},{6,7},{8,9},{9,10},{10,11},{11... | collective-permute-start | bytes 393224 | tf_op jit(solution)/shard_map/ppermute | solution.py:20
  5.9 1.3 collective-permute-start.1
  7.2 1.4 collective-permute-done.low_ref
  8.7 4.1 %collective-permute-done.1.high_ref = bf16[2,128,256]{2,1,0:T(8,128)(2,1)S(1)} collective-permute-done((bf16[2,128,256]{2,1,0:T(8,128)(2,1)S(1)}, bf16[2,128,256]{2,1,0:T(8,128)(2,1)S(1)}, u32[]{:S(2)}, u32[]{:S(2)}) %collective-permute-start.1) | collective-permute-done | bytes 131104 | tf_op jit(solution)/shard_map/ppermute | solution.py:21
  12.8 0.7 copy-done.6
  13.4 13.7 %shard_map.46 = f32[64,128,256]{2,1,0:T(8,128)} custom-call(bf16[2,128,256]{2,1,0:T(8,128)(2,1)} %copy-done.5, bf16[2,128,256]{2,1,0:T(8,128)(2,1)} %copy-done.6, bf16[64,128,256]{2,1,0:T(8,128)(2,1)} %next_ref.1, bf16[64,128,256]{2,1,0:T(8,128)(2,1)} %next_ref.1, bf16[64,128,256]{2,1,0:T(8,128)(2,1)} %next_ref.1, f32[64,128]{1,0:T(8,128)} %coef_ref.1), custom_call_target="tpu_custom_call" | custom-call | tf_op jit(solution)/shard_map/pallas_call | solution.py:96
  27.2 5.0 %fusion.2 = f32[256]{0:T(256)S(1)} fusion(f32[64,128,256]{2,1,0:T(8,128)} %shard_map.46), kind=kLoop, calls=%fused_computation.4 | loop fusion | flops 10485504 | bytes 8389632 | tf_op jit(solution)/shard_map/reduce_sum | solution.py:163
  32.1 0.8 copy-done.1
  32.9 6.9 %fusion.7 = f32[256,256]{1,0:T(8,128)S(1)} fusion(f32[64,128,256]{2,1,0:T(8,128)S(1)} %copy-done.1, f32[256]{0:T(256)S(1)} %fusion.2), kind=kOutput, calls=%fused_computation.11 | convolution fusion | flops 3221422080 | bytes 8651776 | tf_op jit(solution)/shard_map/dot_general | solution.py:157
  39.9 2.5 %collective-permute-start.3 = (f32[256,256]{1,0:T(8,128)S(1)}, f32[256,256]{1,0:T(8,128)S(1)}, u32[]{:S(2)}, u32[]{:S(2)}) collective-permute-start(f32[256,256]{1,0:T(8,128)S(1)} %fusion.7), channel_id=1, source_target_pairs={{0,1},{1,0},{2,3},{3,2},{4,5},{5,4},{6,7},{7,6},{8,9},{9,8},{10,11... | collective-permute-start | bytes 786440 | tf_op jit(solution)/shard_map/ppermute | solution.py:42
  42.3 6.3 %collective-permute-done.3 = f32[256,256]{1,0:T(8,128)S(1)} collective-permute-done((f32[256,256]{1,0:T(8,128)S(1)}, f32[256,256]{1,0:T(8,128)S(1)}, u32[]{:S(2)}, u32[]{:S(2)}) %collective-permute-start.3) | collective-permute-done | bytes 262176 | tf_op jit(solution)/shard_map/ppermute | solution.py:42
  48.7 1.8 collective-permute-start.4
  50.5 5.8 %collective-permute-done.4 = f32[256,256]{1,0:T(8,128)S(1)} collective-permute-done((f32[256,256]{1,0:T(8,128)S(1)}, f32[256,256]{1,0:T(8,128)S(1)}, u32[]{:S(2)}, u32[]{:S(2)}) %collective-permute-start.4) | collective-permute-done | bytes 262176 | tf_op jit(solution)/shard_map/ppermute | solution.py:42
  56.3 2.7 %collective-permute-start.5 = (f32[256,256]{1,0:T(8,128)S(1)}, f32[256,256]{1,0:T(8,128)S(1)}, u32[]{:S(2)}, u32[]{:S(2)}) collective-permute-start(f32[256,256]{1,0:T(8,128)S(1)} %add.45), channel_id=1, source_target_pairs={{0,4},{1,5},{2,6},{3,7},{4,0},{5,1},{6,2},{7,3},{8,12},{9,13},{10,... | collective-permute-start | bytes 786440 | tf_op jit(solution)/shard_map/ppermute | solution.py:42
  59.1 0.1 copy.12
  59.2 0.1 copy.6
  59.3 0.7 select_bitcast_fusion.rows_ref
  60.0 14.8 %shard_map.47 = f32[128,256]{1,0:T(8,128)} custom-call(f32[128,256]{1,0:T(8,128)} %select_bitcast_fusion.rows_ref), custom_call_target="tpu_custom_call" | custom-call | tf_op jit(solution)/shard_map/pallas_call | solution.py:142
  74.8 1.3 collective-permute-start.2
  76.2 6.9 %fusion.3 = f32[256,256]{1,0:T(8,128)S(1)} fusion(f32[8192,256]{1,0:T(8,128)} %collective-permute-done.6, s32[]{:T(128)S(6)} %select_n.87, f32[8192,256]{1,0:T(8,128)} %bitcast.44), kind=kOutput, calls=%fused_computation.5 | convolution fusion | flops 1610612736 | bytes 8651776 | tf_op jit(solution)/shard_map/dot_general | solution.py:157
  83.2 0.1 copy.8
  83.3 0.8 collective-permute-start.7
  84.1 1.1 fusion.17.rows_ref
  85.2 14.7 %shard_map.48 = f32[128,256]{1,0:T(8,128)} custom-call(f32[128,256]{1,0:T(8,128)} %fusion.17.rows_ref), custom_call_target="tpu_custom_call" | custom-call | tf_op jit(solution)/shard_map/pallas_call | solution.py:142
  99.9 1.6 collective-permute-start.8
  101.6 2.0 %fusion.39.rows_ref = f32[128,256]{1,0:T(8,128)} fusion(f32[256,128]{0,1:T(8,128)} %bitcast.55, f32[256,256]{1,0:T(8,128)S(1)} %add_multiply_fusion), kind=kOutput, calls=%fused_computation.52 | convolution fusion | flops 100663296 | bytes 524288 | tf_op jit(solution)/shard_map/dot_general | solution.py:202
  103.5 14.7 %shard_map.49 = f32[128,256]{1,0:T(8,128)} custom-call(f32[128,256]{1,0:T(8,128)} %fusion.39.rows_ref), custom_call_target="tpu_custom_call" | custom-call | tf_op jit(solution)/shard_map/pallas_call | solution.py:142
  118.3 0.4 collective-permute-start.9
  118.7 8.8 %fusion.40 = f32[8192,128]{1,0:T(8,128)} fusion(f32[8192,256]{1,0:T(8,128)} %bitcast.45, f32[256,128]{0,1:T(8,128)} %bitcast.46), kind=kOutput, calls=%fused_computation.53 | convolution fusion | flops 1610612736 | bytes 12713984 | tf_op jit(solution)/shard_map/dot_general | solution.py:212
  127.5 0.4 fusion.41
  127.8 2.3 %collective-permute-done.9 = f32[256,256]{1,0:T(8,128)S(1)} collective-permute-done((f32[256,256]{1,0:T(8,128)S(1)}, f32[256,256]{1,0:T(8,128)S(1)}, u32[]{:S(2)}, u32[]{:S(2)}) %collective-permute-start.9) | collective-permute-done | bytes 262176 | tf_op jit(solution)/shard_map/ppermute | solution.py:211
  130.3 0.4 fusion.42
  130.7 0.6 collective-permute-start.11
  131.3 0.6 collective-permute-done.10
  131.9 0.3 collective-permute-done.11
  132.2 0.4 collective-permute-start.13
  132.5 0.4 fusion.8
  132.9 0.3 fusion.13
  133.2 0.1 copy.9
  133.3 0.9 fusion.11.rows_ref
  134.2 14.7 %shard_map.50 = f32[128,256]{1,0:T(8,128)} custom-call(f32[128,256]{1,0:T(8,128)} %fusion.11.rows_ref), custom_call_target="tpu_custom_call" | custom-call | tf_op jit(solution)/shard_map/pallas_call | solution.py:142
  148.9 1.8 %fusion.10.rows_ref = f32[128,256]{1,0:T(8,128)} fusion(f32[128,256]{1,0:T(8,128)} %shard_map.50, f32[128,128]{0,1:T(8,128)S(1)} %get-tuple-element.32, f32[128,128]{0,1:T(8,128)S(1)} %bitcast.54, f32[128,128]{0,1:T(8,128)S(1)} %copy.9, f32[128,128]{0,1:T(8,128)S(1)} %get-tuple-element.31), kind=kOutput, calls=%fused_computation.18 | convolution fusion | flops 100859904 | bytes 524288 | tf_op jit(solution)/shard_map/dot_general | solution.py:152
  150.8 14.7 %shard_map.51 = f32[128,256]{1,0:T(8,128)} custom-call(f32[128,256]{1,0:T(8,128)} %fusion.10.rows_ref), custom_call_target="tpu_custom_call" | custom-call | tf_op jit(solution)/shard_map/pallas_call | solution.py:142
  165.5 0.8 dynamic-slice_bitcast_fusion
  166.3 4.5 %fusion.23 = f32[8192,64]{0,1:T(8,128)S(1)} fusion(f32[8192,128]{1,0:T(8,128)} %collective-permute-done.13, f32[256,64]{0,1:T(8,128)S(1)} %dynamic-slice_bitcast_fusion, pred[]{:T(512)S(6)} %eq.14), kind=kOutput, calls=%fused_computation.33 | convolution fusion | flops 402661376 | bytes 6356993 | tf_op jit(solution)/shard_map/dot_general | solution.py:248
  170.8 4.5 %fusion.6 = f32[8,64,8,128]{3,2,1,0:T(8,128)S(1)} fusion(f32[8192,64]{0,1:T(8,128)S(1)} %fusion.23, f32[8192,128]{1,0:T(8,128)} %fusion.40, f32[256,64]{0,1:T(8,128)S(1)} %dynamic-slice_bitcast_fusion, pred[]{:T(512)S(6)} %eq.14), kind=kOutput, calls=%fused_computation.9 | convolution fusion | flops 403185664 | bytes 8454145 | tf_op jit(solution)/shard_map/dot_general | solution.py:248
  175.4 1.6 copy.15
  (32 shorter events, 0.4 us)
Async XLA Ops:
  0.0 59.1 %copy-start = (s32[512,128]{1,0:T(8,128)S(1)}, s32[512,128]{1,0:T(8,128)}, u32[]{:S(2)}) copy-start(s32[512,128]{1,0:T(8,128)} %param.6) | copy-start | bytes 786436
  1.0 7.6 %collective-permute-start = (bf16[2,128,256]{2,1,0:T(8,128)(2,1)S(1)}, bf16[2,128,256]{2,1,0:T(8,128)(2,1)S(1)}, u32[]{:S(2)}, u32[]{:S(2)}) collective-permute-start(bf16[2,128,256]{2,1,0:T(8,128)(2,1)S(1)} %get-tuple-element.30), channel_id=1, source_target_pairs={{0,1},{1,2},{2,3},{3,4},{4,5},{5,6},{6,7},{8,9},{9,10},{10,11},{11... | collective-permute-start | bytes 393224 | tf_op jit(solution)/shard_map/ppermute | solution.py:20
  5.9 6.9 %collective-permute-start.1 = (bf16[2,128,256]{2,1,0:T(8,128)(2,1)S(1)}, bf16[2,128,256]{2,1,0:T(8,128)(2,1)S(1)}, u32[]{:S(2)}, u32[]{:S(2)}) collective-permute-start(bf16[2,128,256]{2,1,0:T(8,128)(2,1)S(1)} %get-tuple-element.29), channel_id=1, source_target_pairs={{1,0},{2,1},{3,2},{4,3},{5,4},{6,5},{7,6},{9,8},{10,9},{11,10},{12... | collective-permute-start | bytes 393224 | tf_op jit(solution)/shard_map/ppermute | solution.py:21
  8.7 4.1 %copy-start.5 = (bf16[2,128,256]{2,1,0:T(8,128)(2,1)}, bf16[2,128,256]{2,1,0:T(8,128)(2,1)S(1)}, u32[]{:S(2)}) copy-start(bf16[2,128,256]{2,1,0:T(8,128)(2,1)S(1)} %collective-permute-done.low_ref) | copy-start | bytes 393220
  12.8 0.7 copy-start.6
  27.2 5.8 %copy-start.1 = (f32[64,128,256]{2,1,0:T(8,128)S(1)}, f32[64,128,256]{2,1,0:T(8,128)}, u32[]{:S(2)}) copy-start(f32[64,128,256]{2,1,0:T(8,128)} %shard_map.46) | copy-start | bytes 25165828
  27.2 49.1 %collective-permute-start.6 = (f32[8192,256]{1,0:T(8,128)}, f32[8192,256]{1,0:T(8,128)}, u32[]{:S(2)}, u32[]{:S(2)}) collective-permute-start(f32[8192,256]{1,0:T(8,128)} %bitcast.43), channel_id=1, source_target_pairs={{0,8},{8,0},{1,9},{9,1},{2,10},{10,2},{3,11},{11,3},{4,12},{12,4},... | collective-permute-start | bytes 25165832 | tf_op jit(solution)/shard_map/ppermute | solution.py:32
  32.9 26.3 %copy-start.4 = (s32[256,128]{1,0:T(8,128)S(1)}, s32[256,128]{1,0:T(8,128)}, u32[]{:S(2)}) copy-start(s32[256,128]{1,0:T(8,128)} %param.7) | copy-start | bytes 393220
  39.9 8.8 %collective-permute-start.3 = (f32[256,256]{1,0:T(8,128)S(1)}, f32[256,256]{1,0:T(8,128)S(1)}, u32[]{:S(2)}, u32[]{:S(2)}) collective-permute-start(f32[256,256]{1,0:T(8,128)S(1)} %fusion.7), channel_id=1, source_target_pairs={{0,1},{1,0},{2,3},{3,2},{4,5},{5,4},{6,7},{7,6},{8,9},{9,8},{10,11... | collective-permute-start | bytes 786440 | tf_op jit(solution)/shard_map/ppermute | solution.py:42
  48.7 7.6 %collective-permute-start.4 = (f32[256,256]{1,0:T(8,128)S(1)}, f32[256,256]{1,0:T(8,128)S(1)}, u32[]{:S(2)}, u32[]{:S(2)}) collective-permute-start(f32[256,256]{1,0:T(8,128)S(1)} %add.44), channel_id=1, source_target_pairs={{0,2},{1,3},{2,0},{3,1},{4,6},{5,7},{6,4},{7,5},{8,10},{9,11},{10,... | collective-permute-start | bytes 786440 | tf_op jit(solution)/shard_map/ppermute | solution.py:42
  56.3 19.8 %collective-permute-start.5 = (f32[256,256]{1,0:T(8,128)S(1)}, f32[256,256]{1,0:T(8,128)S(1)}, u32[]{:S(2)}, u32[]{:S(2)}) collective-permute-start(f32[256,256]{1,0:T(8,128)S(1)} %add.45), channel_id=1, source_target_pairs={{0,4},{1,5},{2,6},{3,7},{4,0},{5,1},{6,2},{7,3},{8,12},{9,13},{10,... | collective-permute-start | bytes 786440 | tf_op jit(solution)/shard_map/ppermute | solution.py:42
  74.8 9.3 %collective-permute-start.2 = (f32[256,128]{0,1:T(8,128)}, f32[256,128]{0,1:T(8,128)S(1)}, u32[]{:S(2)}, u32[]{:S(2)}) collective-permute-start(f32[256,128]{0,1:T(8,128)} %bitcast.52), channel_id=1, source_target_pairs={{0,1},{1,0},{2,3},{3,2},{4,5},{5,4},{6,7},{7,6},{8,9},{9,8},{10,11... | collective-permute-start | bytes 393224 | tf_op jit(solution)/shard_map/ppermute | solution.py:32
  76.2 7.9 %copy-start.3 = (f32[128,256]{1,0:T(8,128)S(1)}, f32[128,256]{1,0:T(8,128)}, u32[]{:S(2)}) copy-start(f32[128,256]{1,0:T(8,128)} %shard_map.47) | copy-start | bytes 393220
  83.3 16.5 %collective-permute-start.7 = (f32[256,256]{1,0:T(8,128)S(1)}, f32[256,256]{1,0:T(8,128)S(1)}, u32[]{:S(2)}, u32[]{:S(2)}) collective-permute-start(f32[256,256]{1,0:T(8,128)S(1)} %bitcast_select_fusion), channel_id=1, source_target_pairs={{0,1},{1,0},{2,3},{3,2},{4,5},{5,4},{6,7},{7,6},{8,9},{9,8},{10,11... | collective-permute-start | bytes 786440 | tf_op jit(solution)/shard_map/ppermute | solution.py:204
  99.9 18.3 %collective-permute-start.8 = (f32[256,256]{1,0:T(8,128)S(1)}, f32[256,256]{1,0:T(8,128)S(1)}, u32[]{:S(2)}, u32[]{:S(2)}) collective-permute-start(f32[256,256]{1,0:T(8,128)S(1)} %add.48), channel_id=1, source_target_pairs={{0,2},{1,3},{2,0},{3,1},{4,6},{5,7},{6,4},{7,5},{8,10},{9,11},{10,... | collective-permute-start | bytes 786440 | tf_op jit(solution)/shard_map/ppermute | solution.py:204
  118.2 9.2 %copy-start.2 = (f32[128,256]{1,0:T(8,128)S(1)}, f32[128,256]{1,0:T(8,128)}, u32[]{:S(2)}) copy-start(f32[128,256]{1,0:T(8,128)} %shard_map.49) | copy-start | bytes 393220
  118.3 11.9 %collective-permute-start.9 = (f32[256,256]{1,0:T(8,128)S(1)}, f32[256,256]{1,0:T(8,128)S(1)}, u32[]{:S(2)}, u32[]{:S(2)}) collective-permute-start(f32[256,256]{1,0:T(8,128)S(1)} %add.49), channel_id=1, source_target_pairs={{0,4},{1,5},{2,6},{3,7},{4,0},{5,1},{6,2},{7,3},{8,12},{9,13},{10,... | collective-permute-start | bytes 786440 | tf_op jit(solution)/shard_map/ppermute | solution.py:211
  127.4 4.7 %collective-permute-start.12 = (f32[256,128]{0,1:T(8,128)S(1)}, f32[256,128]{0,1:T(8,128)S(1)}, u32[]{:S(2)}, u32[]{:S(2)}) collective-permute-start(f32[256,128]{0,1:T(8,128)S(1)} %bitcast.47), channel_id=1, source_target_pairs={{0,8},{8,0},{1,9},{9,1},{2,10},{10,2},{3,11},{11,3},{4,12},{12,4},... | collective-permute-start | bytes 393224 | tf_op jit(solution)/shard_map/ppermute | solution.py:32
  130.2 1.6 collective-permute-start.10
  130.7 1.5 collective-permute-start.11
  132.2 34.2 %collective-permute-start.13 = (f32[8192,128]{1,0:T(8,128)}, f32[8192,128]{1,0:T(8,128)}, u32[]{:S(2)}, u32[]{:S(2)}) collective-permute-start(f32[8192,128]{1,0:T(8,128)} %fusion.40), channel_id=1, source_target_pairs={{0,8},{8,0},{1,9},{9,1},{2,10},{10,2},{3,11},{11,3},{4,12},{12,4},... | collective-permute-start | bytes 12582920 | tf_op jit(solution)/shard_map/ppermute | solution.py:32

commit v5 on v3

--- a/solution.py
+++ b/solution.py
@@ -194,7 +194,15 @@
         lax.dynamic_slice_in_dim(own_flux, half_start, half_rows, 0), other_rows
     )
     mixed_half = jnp.where(is_first, mixed_half, mixed_half.T)
-    own_gram = tree_sum(self_gram(own_flux), "tx") / cells_total
+    gram_hops = butterfly_steps("tx")
+    own_gram = self_gram(own_flux)
+    if gram_hops:
+        received = lax.ppermute(own_gram, "tx", gram_hops.pop(0))
+        received, mixed_half = lax.optimization_barrier((received, mixed_half))
+        own_gram = own_gram + received
+    for route in gram_hops:
+        own_gram = own_gram + lax.ppermute(own_gram, "tx", route)
+    own_gram = own_gram / cells_total
     own_gram, mixed_sum = lax.optimization_barrier((own_gram, mixed_half))
     hops = butterfly_steps("tx")
     own_basis = first_basis

time: 177 us -> 180 us (1.017)
  other arithmetic: 2.41 us -> 5.94 us
    ppermute x6, waiting for transfers between devices: 0.88 us -> 5.38 us  [partner(): return lax.ppermute(block, axis, route)]
    reduce_sum x1, other arithmetic: 1.45 us -> 4.98 us  [self_gram(): missing = jnp.sum(lower * lower, axis=0)]
    ppermute x3, waiting for transfers between devices: 10.7 us -> 7.32 us  [the longest x2 6.57 us: on_device(): own_gram = own_gram + lax.ppermute(own_gram, 'tx', route)]
  transfers between devices with their start and end apart: 14 -> 14, of which waited for: 7 -> 8; matrix products, arithmetic and copies ran while one was open for 19% -> 21% of each run, Pallas kernels for 42% -> 41%
where the time goes in v5:
time: 180 us; the launch traced here: 179 us
  Pallas kernels  87.4 us (49%)
  matrix products  38.7 us (22%)
  waiting for transfers between devices  18.9 us (10%)
  starting transfers between devices  17.9 us (10%)
  local copies, waits for them, and re-layouts  9.96 us (6%)
  other arithmetic  5.94 us (3%)
    pallas_call x5, Pallas kernels, orthonormal(): pl.pallas_call(gram_schmidt_kernel, out_shape=jax.ShapeDtypeStruct(rows.s...  73.7 us
    pallas_call x1, Pallas kernels, fluxes(): pl.pallas_call(functools.partial(flux_kernel, count), grid=(count,), in_s...  13.7 us
    dot_general x2, matrix products, cross_gram(): lax.dot_general(left_rows, right_rows, (((0,), (0,)), ((), ())), precisio...  12.8 us
    dot_general x1, matrix products, on_device(): own_modes = jnp.dot(own_flux, own_basis, precision=high)  8.79 us
    ppermute x2, waiting for transfers between devices, on_device(): own_gram = own_gram + lax.ppermute(own_gram, 'tx', route)  6.57 us
    ppermute x6, waiting for transfers between devices, partner(): return lax.ppermute(block, axis, route)  5.38 us
    reduce_sum x1, other arithmetic, self_gram(): missing = jnp.sum(lower * lower, axis=0)  4.98 us
    ppermute x1, starting transfers between devices, halos(): lax.ppermute(lax.slice_in_dim(block, block.shape[0] - width, None, axis=0...  4.88 us
  transfers between devices with their start and end apart: 14, of which 8 were waited for; matrix products, arithmetic and copies ran while one was open for 21% of the time, Pallas kernels for 41%

profile of v5, /device:TPU:0, one launch (start us, length us, event | category | flops | bytes accessed | tf_op | source)
XLA Modules:
  0.0 179.1 jit_solution(1331047317726010290)
XLA Ops:
  0.0 1.0 fusion.37
  1.0 4.9 %collective-permute-start = (bf16[2,128,256]{2,1,0:T(8,128)(2,1)S(1)}, bf16[2,128,256]{2,1,0:T(8,128)(2,1)S(1)}, u32[]{:S(2)}, u32[]{:S(2)}) collective-permute-start(bf16[2,128,256]{2,1,0:T(8,128)(2,1)S(1)} %get-tuple-element.34), channel_id=1, source_target_pairs={{0,1},{1,2},{2,3},{3,4},{4,5},{5,6},{6,7},{8,9},{9,10},{10,11},{11... | collective-permute-start | bytes 393224 | tf_op jit(solution)/shard_map/ppermute | solution.py:20
  5.9 1.3 collective-permute-start.1
  7.2 1.4 collective-permute-done.low_ref
  8.7 4.1 %collective-permute-done.1.high_ref = bf16[2,128,256]{2,1,0:T(8,128)(2,1)S(1)} collective-permute-done((bf16[2,128,256]{2,1,0:T(8,128)(2,1)S(1)}, bf16[2,128,256]{2,1,0:T(8,128)(2,1)S(1)}, u32[]{:S(2)}, u32[]{:S(2)}) %collective-permute-start.1) | collective-permute-done | bytes 131104 | tf_op jit(solution)/shard_map/ppermute | solution.py:21
  12.8 0.7 copy-done.6
  13.4 13.7 %shard_map.46 = f32[64,128,256]{2,1,0:T(8,128)} custom-call(bf16[2,128,256]{2,1,0:T(8,128)(2,1)} %copy-done.5, bf16[2,128,256]{2,1,0:T(8,128)(2,1)} %copy-done.6, bf16[64,128,256]{2,1,0:T(8,128)(2,1)} %next_ref.1, bf16[64,128,256]{2,1,0:T(8,128)(2,1)} %next_ref.1, bf16[64,128,256]{2,1,0:T(8,128)(2,1)} %next_ref.1, f32[64,128]{1,0:T(8,128)} %coef_ref.1), custom_call_target="tpu_custom_call" | custom-call | tf_op jit(solution)/shard_map/pallas_call | solution.py:96
  27.2 4.4 %constant_dynamic-slice_fusion = f32[4096,256]{1,0:T(8,128)} fusion(f32[8192,256]{1,0:T(8,128)} %bitcast.44, s32[]{:T(128)S(6)} %select_n.90), kind=kLoop, calls=%fused_computation.43 | loop fusion | bytes 8388612 | tf_op jit(solution)/shard_map/dynamic_slice | solution.py:191
  31.6 5.0 %fusion.2 = f32[256]{0:T(256)S(1)} fusion(f32[64,128,256]{2,1,0:T(8,128)} %shard_map.46), kind=kLoop, calls=%fused_computation.4 | loop fusion | flops 10485504 | bytes 8389632 | tf_op jit(solution)/shard_map/reduce_sum | solution.py:163
  36.6 0.8 copy-done.1
  37.4 6.9 %fusion.6 = f32[256,256]{1,0:T(8,128)S(1)} fusion(f32[64,128,256]{2,1,0:T(8,128)S(1)} %copy-done.1, f32[256]{0:T(256)S(1)} %fusion.2), kind=kOutput, calls=%fused_computation.10 | convolution fusion | flops 3221422080 | bytes 8651776 | tf_op jit(solution)/shard_map/dot_general | solution.py:157
  44.3 2.5 %collective-permute-start.3 = (f32[256,256]{1,0:T(8,128)S(1)}, f32[256,256]{1,0:T(8,128)S(1)}, u32[]{:S(2)}, u32[]{:S(2)}) collective-permute-start(f32[256,256]{1,0:T(8,128)S(1)} %fusion.6), channel_id=1, source_target_pairs={{0,1},{1,0},{2,3},{3,2},{4,5},{5,4},{6,7},{7,6},{8,9},{9,8},{10,11... | collective-permute-start | bytes 786440 | tf_op jit(solution)/shard_map/ppermute | solution.py:200
  46.8 5.9 %fusion.3 = f32[256,256]{1,0:T(8,128)S(1)} fusion(f32[4096,256]{1,0:T(8,128)} %collective-permute-done.4, f32[8192,256]{1,0:T(8,128)S(1)} %bitcast.46, s32[]{:T(128)S(6)} %select_n.89), kind=kOutput, calls=%fused_computation.5 | convolution fusion | flops 1610612736 | bytes 8650756 | tf_op jit(solution)/shard_map/dot_general | solution.py:157
  52.7 0.3 copy.8
  53.0 0.8 collective-permute-done.3
  53.8 1.6 collective-permute-start.5
  55.4 6.6 %collective-permute-done.5 = f32[256,256]{1,0:T(8,128)S(1)} collective-permute-done((f32[256,256]{1,0:T(8,128)S(1)}, f32[256,256]{1,0:T(8,128)S(1)}, u32[]{:S(2)}, u32[]{:S(2)}) %collective-permute-start.5) | collective-permute-done | bytes 262176 | tf_op jit(solution)/shard_map/ppermute | solution.py:204
  62.0 2.5 %collective-permute-start.6 = (f32[256,256]{1,0:T(8,128)S(1)}, f32[256,256]{1,0:T(8,128)S(1)}, u32[]{:S(2)}, u32[]{:S(2)}) collective-permute-start(f32[256,256]{1,0:T(8,128)S(1)} %add.49), channel_id=1, source_target_pairs={{0,4},{1,5},{2,6},{3,7},{4,0},{5,1},{6,2},{7,3},{8,12},{9,13},{10,... | collective-permute-start | bytes 786440 | tf_op jit(solution)/shard_map/ppermute | solution.py:204
  64.6 0.1 copy.12
  64.8 0.7 select_bitcast_fusion.rows_ref
  65.5 14.7 %shard_map.47 = f32[128,256]{1,0:T(8,128)} custom-call(f32[128,256]{1,0:T(8,128)} %select_bitcast_fusion.rows_ref), custom_call_target="tpu_custom_call" | custom-call | tf_op jit(solution)/shard_map/pallas_call | solution.py:142
  80.2 1.7 collective-permute-start.2
  81.9 0.4 collective-permute-start.7
  82.3 4.5 %collective-permute-done.2 = f32[256,128]{0,1:T(8,128)S(1)} collective-permute-done((f32[256,128]{0,1:T(8,128)}, f32[256,128]{0,1:T(8,128)S(1)}, u32[]{:S(2)}, u32[]{:S(2)}) %collective-permute-start.2) | collective-permute-done | bytes 131104 | tf_op jit(solution)/shard_map/ppermute | solution.py:32
  86.8 2.0 %fusion.16.rows_ref = f32[128,256]{1,0:T(8,128)} fusion(f32[256,256]{1,0:T(8,128)S(1)} %add_multiply_fusion, f32[256,128]{0,1:T(8,128)S(1)} %collective-permute-done.2, pred[]{:T(512)S(6)} %eq.12, f32[128,256]{1,0:T(8,128)} %shard_map.47), kind=kOutput, calls=%fused_computation.24 | convolution fusion | flops 100696064 | bytes 655361 | tf_op jit(solution)/shard_map/dot_general | solution.py:210
  88.8 14.7 %shard_map.48 = f32[128,256]{1,0:T(8,128)} custom-call(f32[128,256]{1,0:T(8,128)} %fusion.16.rows_ref), custom_call_target="tpu_custom_call" | custom-call | tf_op jit(solution)/shard_map/pallas_call | solution.py:142
  103.5 1.4 collective-permute-start.8
  104.9 2.0 %fusion.38.rows_ref = f32[128,256]{1,0:T(8,128)} fusion(f32[256,128]{0,1:T(8,128)} %bitcast.56, f32[256,256]{1,0:T(8,128)S(1)} %add_multiply_fusion), kind=kOutput, calls=%fused_computation.52 | convolution fusion | flops 100663296 | bytes 524288 | tf_op jit(solution)/shard_map/dot_general | solution.py:210
  106.9 14.7 %shard_map.49 = f32[128,256]{1,0:T(8,128)} custom-call(f32[128,256]{1,0:T(8,128)} %fusion.38.rows_ref), custom_call_target="tpu_custom_call" | custom-call | tf_op jit(solution)/shard_map/pallas_call | solution.py:142
  121.7 0.6 collective-permute-start.9
  122.3 8.8 %fusion.39 = f32[8192,128]{1,0:T(8,128)} fusion(f32[8192,256]{1,0:T(8,128)} %bitcast.45, f32[256,128]{0,1:T(8,128)} %bitcast.47), kind=kOutput, calls=%fused_computation.53 | convolution fusion | flops 1610612736 | bytes 12713984 | tf_op jit(solution)/shard_map/dot_general | solution.py:220
  131.1 0.4 fusion.40
  131.5 0.7 collective-permute-done.9
  132.2 0.4 fusion.41
  132.6 0.6 collective-permute-start.11
  133.2 0.6 collective-permute-done.10
  133.8 0.3 collective-permute-done.11
  134.1 0.4 collective-permute-start.13
  134.5 0.4 fusion.7
  134.8 0.3 fusion.12
  135.2 0.9 fusion.10.rows_ref
  136.2 14.7 %shard_map.50 = f32[128,256]{1,0:T(8,128)} custom-call(f32[128,256]{1,0:T(8,128)} %fusion.10.rows_ref), custom_call_target="tpu_custom_call" | custom-call | tf_op jit(solution)/shard_map/pallas_call | solution.py:142
  150.9 1.8 %fusion.9.rows_ref = f32[128,256]{1,0:T(8,128)} fusion(f32[128,256]{1,0:T(8,128)} %shard_map.50, f32[128,128]{0,1:T(8,128)S(1)} %get-tuple-element.36, f32[128,128]{0,1:T(8,128)S(1)} %bitcast.55, f32[128,128]{0,1:T(8,128)S(1)} %copy.9, f32[128,128]{0,1:T(8,128)S(1)} %get-tuple-element.35), kind=kOutput, calls=%fused_computation.17 | convolution fusion | flops 100859904 | bytes 524288 | tf_op jit(solution)/shard_map/dot_general | solution.py:152
  152.7 14.9 %shard_map.51 = f32[128,256]{1,0:T(8,128)} custom-call(f32[128,256]{1,0:T(8,128)} %fusion.9.rows_ref), custom_call_target="tpu_custom_call" | custom-call | tf_op jit(solution)/shard_map/pallas_call | solution.py:142
  167.6 0.8 dynamic-slice_bitcast_fusion
  168.5 4.5 %fusion.22 = f32[8192,64]{0,1:T(8,128)S(1)} fusion(f32[8192,128]{1,0:T(8,128)} %collective-permute-done.13, f32[256,64]{0,1:T(8,128)S(1)} %dynamic-slice_bitcast_fusion, pred[]{:T(512)S(6)} %eq.14), kind=kOutput, calls=%fused_computation.32 | convolution fusion | flops 402661376 | bytes 6356993 | tf_op jit(solution)/shard_map/dot_general | solution.py:256
  173.0 4.5 %fusion.5 = f32[8,64,8,128]{3,2,1,0:T(8,128)S(1)} fusion(f32[8192,64]{0,1:T(8,128)S(1)} %fusion.22, f32[8192,128]{1,0:T(8,128)} %fusion.39, f32[256,64]{0,1:T(8,128)S(1)} %dynamic-slice_bitcast_fusion, pred[]{:T(512)S(6)} %eq.14), kind=kOutput, calls=%fused_computation.8 | convolution fusion | flops 403185664 | bytes 8454145 | tf_op jit(solution)/shard_map/dot_general | solution.py:256
  177.5 1.6 copy.15
  (33 shorter events, 0.6 us)
Async XLA Ops:
  0.0 64.5 %copy-start = (s32[512,128]{1,0:T(8,128)S(1)}, s32[512,128]{1,0:T(8,128)}, u32[]{:S(2)}) copy-start(s32[512,128]{1,0:T(8,128)} %param.6) | copy-start | bytes 786436
  1.0 7.6 %collective-permute-start = (bf16[2,128,256]{2,1,0:T(8,128)(2,1)S(1)}, bf16[2,128,256]{2,1,0:T(8,128)(2,1)S(1)}, u32[]{:S(2)}, u32[]{:S(2)}) collective-permute-start(bf16[2,128,256]{2,1,0:T(8,128)(2,1)S(1)} %get-tuple-element.34), channel_id=1, source_target_pairs={{0,1},{1,2},{2,3},{3,4},{4,5},{5,6},{6,7},{8,9},{9,10},{10,11},{11... | collective-permute-start | bytes 393224 | tf_op jit(solution)/shard_map/ppermute | solution.py:20
  5.9 6.9 %collective-permute-start.1 = (bf16[2,128,256]{2,1,0:T(8,128)(2,1)S(1)}, bf16[2,128,256]{2,1,0:T(8,128)(2,1)S(1)}, u32[]{:S(2)}, u32[]{:S(2)}) collective-permute-start(bf16[2,128,256]{2,1,0:T(8,128)(2,1)S(1)} %get-tuple-element.33), channel_id=1, source_target_pairs={{1,0},{2,1},{3,2},{4,3},{5,4},{6,5},{7,6},{9,8},{10,9},{11,10},{12... | collective-permute-start | bytes 393224 | tf_op jit(solution)/shard_map/ppermute | solution.py:21
  8.7 4.1 %copy-start.5 = (bf16[2,128,256]{2,1,0:T(8,128)(2,1)}, bf16[2,128,256]{2,1,0:T(8,128)(2,1)S(1)}, u32[]{:S(2)}) copy-start(bf16[2,128,256]{2,1,0:T(8,128)(2,1)S(1)} %collective-permute-done.low_ref) | copy-start | bytes 393220
  12.8 0.7 copy-start.6
  31.6 15.2 %collective-permute-start.4 = (f32[4096,256]{1,0:T(8,128)}, f32[4096,256]{1,0:T(8,128)}, u32[]{:S(2)}, u32[]{:S(2)}) collective-permute-start(f32[4096,256]{1,0:T(8,128)} %constant_dynamic-slice_fusion), channel_id=1, source_target_pairs={{0,8},{8,0},{1,9},{9,1},{2,10},{10,2},{3,11},{11,3},{4,12},{12,4},... | collective-permute-start | bytes 12582920 | tf_op jit(solution)/shard_map/ppermute | solution.py:32
  31.6 5.8 %copy-start.1 = (f32[64,128,256]{2,1,0:T(8,128)S(1)}, f32[64,128,256]{2,1,0:T(8,128)}, u32[]{:S(2)}) copy-start(f32[64,128,256]{2,1,0:T(8,128)} %shard_map.46) | copy-start | bytes 25165828
  44.3 20.4 %copy-start.4 = (s32[256,128]{1,0:T(8,128)S(1)}, s32[256,128]{1,0:T(8,128)}, u32[]{:S(2)}) copy-start(s32[256,128]{1,0:T(8,128)} %param.7) | copy-start | bytes 393220
  44.3 9.5 %collective-permute-start.3 = (f32[256,256]{1,0:T(8,128)S(1)}, f32[256,256]{1,0:T(8,128)S(1)}, u32[]{:S(2)}, u32[]{:S(2)}) collective-permute-start(f32[256,256]{1,0:T(8,128)S(1)} %fusion.6), channel_id=1, source_target_pairs={{0,1},{1,0},{2,3},{3,2},{4,5},{5,4},{6,7},{7,6},{8,9},{9,8},{10,11... | collective-permute-start | bytes 786440 | tf_op jit(solution)/shard_map/ppermute | solution.py:200
  53.8 8.2 %collective-permute-start.5 = (f32[256,256]{1,0:T(8,128)S(1)}, f32[256,256]{1,0:T(8,128)S(1)}, u32[]{:S(2)}, u32[]{:S(2)}) collective-permute-start(f32[256,256]{1,0:T(8,128)S(1)} %add.48), channel_id=1, source_target_pairs={{0,2},{1,3},{2,0},{3,1},{4,6},{5,7},{6,4},{7,5},{8,10},{9,11},{10,... | collective-permute-start | bytes 786440 | tf_op jit(solution)/shard_map/ppermute | solution.py:204
  62.0 19.8 %collective-permute-start.6 = (f32[256,256]{1,0:T(8,128)S(1)}, f32[256,256]{1,0:T(8,128)S(1)}, u32[]{:S(2)}, u32[]{:S(2)}) collective-permute-start(f32[256,256]{1,0:T(8,128)S(1)} %add.49), channel_id=1, source_target_pairs={{0,4},{1,5},{2,6},{3,7},{4,0},{5,1},{6,2},{7,3},{8,12},{9,13},{10,... | collective-permute-start | bytes 786440 | tf_op jit(solution)/shard_map/ppermute | solution.py:204
  80.2 6.6 %collective-permute-start.2 = (f32[256,128]{0,1:T(8,128)}, f32[256,128]{0,1:T(8,128)S(1)}, u32[]{:S(2)}, u32[]{:S(2)}) collective-permute-start(f32[256,128]{0,1:T(8,128)} %bitcast.53), channel_id=1, source_target_pairs={{0,1},{1,0},{2,3},{3,2},{4,5},{5,4},{6,7},{7,6},{8,9},{9,8},{10,11... | collective-permute-start | bytes 393224 | tf_op jit(solution)/shard_map/ppermute | solution.py:32
  81.9 21.6 %collective-permute-start.7 = (f32[256,256]{1,0:T(8,128)S(1)}, f32[256,256]{1,0:T(8,128)S(1)}, u32[]{:S(2)}, u32[]{:S(2)}) collective-permute-start(f32[256,256]{1,0:T(8,128)S(1)} %bitcast_select_fusion), channel_id=1, source_target_pairs={{0,1},{1,0},{2,3},{3,2},{4,5},{5,4},{6,7},{7,6},{8,9},{9,8},{10,11... | collective-permute-start | bytes 786440 | tf_op jit(solution)/shard_map/ppermute | solution.py:212
  103.5 18.1 %collective-permute-start.8 = (f32[256,256]{1,0:T(8,128)S(1)}, f32[256,256]{1,0:T(8,128)S(1)}, u32[]{:S(2)}, u32[]{:S(2)}) collective-permute-start(f32[256,256]{1,0:T(8,128)S(1)} %add.51), channel_id=1, source_target_pairs={{0,2},{1,3},{2,0},{3,1},{4,6},{5,7},{6,4},{7,5},{8,10},{9,11},{10,... | collective-permute-start | bytes 786440 | tf_op jit(solution)/shard_map/ppermute | solution.py:212
  121.7 9.4 %copy-start.2 = (f32[128,256]{1,0:T(8,128)S(1)}, f32[128,256]{1,0:T(8,128)}, u32[]{:S(2)}) copy-start(f32[128,256]{1,0:T(8,128)} %shard_map.49) | copy-start | bytes 393220
  121.7 13.6 %copy-start.3 = (f32[128,256]{1,0:T(8,128)S(1)}, f32[128,256]{1,0:T(8,128)}, u32[]{:S(2)}) copy-start(f32[128,256]{1,0:T(8,128)} %shard_map.47) | copy-start | bytes 393220
  121.7 10.5 %collective-permute-start.9 = (f32[256,256]{1,0:T(8,128)S(1)}, f32[256,256]{1,0:T(8,128)S(1)}, u32[]{:S(2)}, u32[]{:S(2)}) collective-permute-start(f32[256,256]{1,0:T(8,128)S(1)} %add.52), channel_id=1, source_target_pairs={{0,4},{1,5},{2,6},{3,7},{4,0},{5,1},{6,2},{7,3},{8,12},{9,13},{10,... | collective-permute-start | bytes 786440 | tf_op jit(solution)/shard_map/ppermute | solution.py:219
  131.1 3.0 %collective-permute-start.12 = (f32[256,128]{0,1:T(8,128)S(1)}, f32[256,128]{0,1:T(8,128)S(1)}, u32[]{:S(2)}, u32[]{:S(2)}) collective-permute-start(f32[256,128]{0,1:T(8,128)S(1)} %bitcast.48), channel_id=1, source_target_pairs={{0,8},{8,0},{1,9},{9,1},{2,10},{10,2},{3,11},{11,3},{4,12},{12,4},... | collective-permute-start | bytes 393224 | tf_op jit(solution)/shard_map/ppermute | solution.py:32
  132.2 1.6 collective-permute-start.10
  132.6 1.5 collective-permute-start.11
  134.1 34.4 %collective-permute-start.13 = (f32[8192,128]{1,0:T(8,128)}, f32[8192,128]{1,0:T(8,128)}, u32[]{:S(2)}, u32[]{:S(2)}) collective-permute-start(f32[8192,128]{1,0:T(8,128)} %fusion.39), channel_id=1, source_target_pairs={{0,8},{8,0},{1,9},{9,1},{2,10},{10,2},{3,11},{11,3},{4,12},{12,4},... | collective-permute-start | bytes 12582920 | tf_op jit(solution)/shard_map/ppermute | solution.py:32

commit v6 on v3

--- a/solution.py
+++ b/solution.py
@@ -112,7 +112,7 @@
 def gram_schmidt_kernel(rows_ref, out_ref, work):
     count, width = rows_ref.shape
     blocks = count // 8
-    group = 4 if blocks % 4 == 0 else 1
+    group = 2 if blocks % 2 == 0 else 1
     work[...] = rows_ref[...]
     for first in range(0, blocks, group):
 

time: 177 us -> 176 us (level)
  no operation moved by 1% of the time
where the time goes in v6:
time: 176 us
  Pallas kernels  87.1 us (49%)
  matrix products  38.9 us (22%)
  waiting for transfers between devices  18.5 us (11%)
  starting transfers between devices  17.9 us (10%)
  local copies, waits for them, and re-layouts  10.7 us (6%)
  other arithmetic  2.41 us (1%)
    pallas_call x5, Pallas kernels, orthonormal(): pl.pallas_call(gram_schmidt_kernel, out_shape=jax.ShapeDtypeStruct(rows.s...  73.3 us
    dot_general x2, matrix products, cross_gram(): lax.dot_general(left_rows, right_rows, (((0,), (0,)), ((), ())), precisio...  13.8 us
    pallas_call x1, Pallas kernels, fluxes(): pl.pallas_call(functools.partial(flux_kernel, count), grid=(count,), in_s...  13.8 us
    ppermute x3, waiting for transfers between devices, tree_sum(): value = value + lax.ppermute(value, axis, route)  10.7 us
    dot_general x1, matrix products, on_device(): own_modes = jnp.dot(own_flux, own_basis, precision=high)  8.79 us
    ppermute x3, starting transfers between devices, tree_sum(): value = value + lax.ppermute(value, axis, route)  6.63 us
    ppermute x1, starting transfers between devices, halos(): lax.ppermute(lax.slice_in_dim(block, block.shape[0] - width, None, axis=0...  4.88 us
    dynamic_slice x1, local copies, waits for them, and re-layouts, on_device(): lax.dynamic_slice_in_dim(own_flux, (1 - member) * half_rows, half_rows, 0)  4.76 us
  transfers between devices with their start and end apart: 14, of which 7 were waited for; matrix products, arithmetic and copies ran while one was open for 19% of the time, Pallas kernels for 42%

profile of v6, /device:TPU:0, one launch (start us, length us, event | category | flops | bytes accessed | tf_op | source)
XLA Modules:
  0.0 175.7 jit_solution(16248688596058728552)
XLA Ops:
  0.0 1.0 fusion.37
  1.0 4.9 %collective-permute-start = (bf16[2,128,256]{2,1,0:T(8,128)(2,1)S(1)}, bf16[2,128,256]{2,1,0:T(8,128)(2,1)S(1)}, u32[]{:S(2)}, u32[]{:S(2)}) collective-permute-start(bf16[2,128,256]{2,1,0:T(8,128)(2,1)S(1)} %get-tuple-element.30), channel_id=1, source_target_pairs={{0,1},{1,2},{2,3},{3,4},{4,5},{5,6},{6,7},{8,9},{9,10},{10,11},{11... | collective-permute-start | bytes 393224 | tf_op jit(solution)/shard_map/ppermute | solution.py:20
  5.9 1.3 collective-permute-start.1
  7.2 1.4 collective-permute-done.low_ref
  8.7 4.1 %collective-permute-done.1.high_ref = bf16[2,128,256]{2,1,0:T(8,128)(2,1)S(1)} collective-permute-done((bf16[2,128,256]{2,1,0:T(8,128)(2,1)S(1)}, bf16[2,128,256]{2,1,0:T(8,128)(2,1)S(1)}, u32[]{:S(2)}, u32[]{:S(2)}) %collective-permute-start.1) | collective-permute-done | bytes 131104 | tf_op jit(solution)/shard_map/ppermute | solution.py:21
  12.8 0.7 copy-done.6
  13.4 13.8 %shard_map.46 = f32[64,128,256]{2,1,0:T(8,128)} custom-call(bf16[2,128,256]{2,1,0:T(8,128)(2,1)} %copy-done.5, bf16[2,128,256]{2,1,0:T(8,128)(2,1)} %copy-done.6, bf16[64,128,256]{2,1,0:T(8,128)(2,1)} %next_ref.1, bf16[64,128,256]{2,1,0:T(8,128)(2,1)} %next_ref.1, bf16[64,128,256]{2,1,0:T(8,128)(2,1)} %next_ref.1, f32[64,128]{1,0:T(8,128)} %coef_ref.1), custom_call_target="tpu_custom_call" | custom-call | tf_op jit(solution)/shard_map/pallas_call | solution.py:96
  27.2 4.8 %constant_dynamic-slice_fusion = f32[4096,256]{1,0:T(8,128)} fusion(f32[8192,256]{1,0:T(8,128)} %bitcast.44, s32[]{:T(128)S(6)} %select_n.90), kind=kLoop, calls=%fused_computation.43 | loop fusion | bytes 8388612 | tf_op jit(solution)/shard_map/dynamic_slice | solution.py:191
  32.0 1.4 copy-done.1
  33.4 1.5 fusion.2
  34.8 6.9 %fusion.6 = f32[256,256]{1,0:T(8,128)S(1)} fusion(f32[64,128,256]{2,1,0:T(8,128)S(1)} %copy-done.1, f32[256]{0:T(256)S(1)} %fusion.2), kind=kOutput, calls=%fused_computation.10 | convolution fusion | flops 3221422080 | bytes 8651776 | tf_op jit(solution)/shard_map/dot_general | solution.py:157
  41.8 2.5 %collective-permute-start.3 = (f32[256,256]{1,0:T(8,128)S(1)}, f32[256,256]{1,0:T(8,128)S(1)}, u32[]{:S(2)}, u32[]{:S(2)}) collective-permute-start(f32[256,256]{1,0:T(8,128)S(1)} %fusion.6), channel_id=1, source_target_pairs={{0,1},{1,0},{2,3},{3,2},{4,5},{5,4},{6,7},{7,6},{8,9},{9,8},{10,11... | collective-permute-start | bytes 786440 | tf_op jit(solution)/shard_map/ppermute | solution.py:42
  44.2 5.6 %collective-permute-done.3 = f32[256,256]{1,0:T(8,128)S(1)} collective-permute-done((f32[256,256]{1,0:T(8,128)S(1)}, f32[256,256]{1,0:T(8,128)S(1)}, u32[]{:S(2)}, u32[]{:S(2)}) %collective-permute-start.3) | collective-permute-done | bytes 262176 | tf_op jit(solution)/shard_map/ppermute | solution.py:42
  49.9 1.6 collective-permute-start.4
  51.5 5.1 %collective-permute-done.4 = f32[256,256]{1,0:T(8,128)S(1)} collective-permute-done((f32[256,256]{1,0:T(8,128)S(1)}, f32[256,256]{1,0:T(8,128)S(1)}, u32[]{:S(2)}, u32[]{:S(2)}) %collective-permute-start.4) | collective-permute-done | bytes 262176 | tf_op jit(solution)/shard_map/ppermute | solution.py:42
  56.6 2.5 %collective-permute-start.5 = (f32[256,256]{1,0:T(8,128)S(1)}, f32[256,256]{1,0:T(8,128)S(1)}, u32[]{:S(2)}, u32[]{:S(2)}) collective-permute-start(f32[256,256]{1,0:T(8,128)S(1)} %add.47), channel_id=1, source_target_pairs={{0,4},{1,5},{2,6},{3,7},{4,0},{5,1},{6,2},{7,3},{8,12},{9,13},{10,... | collective-permute-start | bytes 786440 | tf_op jit(solution)/shard_map/ppermute | solution.py:42
  59.2 0.1 copy.12
  59.3 0.1 copy.6
  59.4 0.7 select_bitcast_fusion.rows_ref
  60.1 14.7 %shard_map.47 = f32[128,256]{1,0:T(8,128)} custom-call(f32[128,256]{1,0:T(8,128)} %select_bitcast_fusion.rows_ref), custom_call_target="tpu_custom_call" | custom-call | tf_op jit(solution)/shard_map/pallas_call | solution.py:142
  74.8 1.9 %collective-permute-start.2 = (f32[256,128]{0,1:T(8,128)}, f32[256,128]{0,1:T(8,128)S(1)}, u32[]{:S(2)}, u32[]{:S(2)}) collective-permute-start(f32[256,128]{0,1:T(8,128)} %bitcast.53), channel_id=1, source_target_pairs={{0,1},{1,0},{2,3},{3,2},{4,5},{5,4},{6,7},{7,6},{8,9},{9,8},{10,11... | collective-permute-start | bytes 393224 | tf_op jit(solution)/shard_map/ppermute | solution.py:32
  76.8 6.9 %fusion.3 = f32[256,256]{1,0:T(8,128)S(1)} fusion(f32[4096,256]{1,0:T(8,128)} %collective-permute-done.6, f32[8192,256]{1,0:T(8,128)} %bitcast.45, s32[]{:T(128)S(6)} %select_n.89), kind=kOutput, calls=%fused_computation.5 | convolution fusion | flops 1610612736 | bytes 8650756 | tf_op jit(solution)/shard_map/dot_general | solution.py:157
  83.7 0.1 copy.8
  83.9 0.2 collective-permute-start.7
  84.0 1.1 fusion.16.rows_ref
  85.1 14.6 %shard_map.48 = f32[128,256]{1,0:T(8,128)} custom-call(f32[128,256]{1,0:T(8,128)} %fusion.16.rows_ref), custom_call_target="tpu_custom_call" | custom-call | tf_op jit(solution)/shard_map/pallas_call | solution.py:142
  99.7 1.5 collective-permute-start.8
  101.2 2.0 %fusion.38.rows_ref = f32[128,256]{1,0:T(8,128)} fusion(f32[256,128]{0,1:T(8,128)} %bitcast.56, f32[256,256]{1,0:T(8,128)S(1)} %add_multiply_fusion), kind=kOutput, calls=%fused_computation.52 | convolution fusion | flops 100663296 | bytes 524288 | tf_op jit(solution)/shard_map/dot_general | solution.py:202
  103.2 14.7 %shard_map.49 = f32[128,256]{1,0:T(8,128)} custom-call(f32[128,256]{1,0:T(8,128)} %fusion.38.rows_ref), custom_call_target="tpu_custom_call" | custom-call | tf_op jit(solution)/shard_map/pallas_call | solution.py:142
  118.0 0.5 collective-permute-start.9
  118.5 8.8 %fusion.39 = f32[8192,128]{1,0:T(8,128)} fusion(f32[8192,256]{1,0:T(8,128)} %bitcast.46, f32[256,128]{0,1:T(8,128)} %bitcast.47), kind=kOutput, calls=%fused_computation.53 | convolution fusion | flops 1610612736 | bytes 12713984 | tf_op jit(solution)/shard_map/dot_general | solution.py:212
  127.3 0.4 fusion.40
  127.6 1.3 collective-permute-done.9
  129.1 0.4 fusion.41
  129.5 0.6 collective-permute-start.11
  130.0 0.6 collective-permute-done.10
  130.7 0.3 collective-permute-done.11
  131.0 0.4 collective-permute-start.13
  131.3 0.4 fusion.7
  131.7 0.3 fusion.12
  132.1 0.9 fusion.10.rows_ref
  133.0 14.6 %shard_map.50 = f32[128,256]{1,0:T(8,128)} custom-call(f32[128,256]{1,0:T(8,128)} %fusion.10.rows_ref), custom_call_target="tpu_custom_call" | custom-call | tf_op jit(solution)/shard_map/pallas_call | solution.py:142
  147.6 1.8 %fusion.9.rows_ref = f32[128,256]{1,0:T(8,128)} fusion(f32[128,256]{1,0:T(8,128)} %shard_map.50, f32[128,128]{0,1:T(8,128)S(1)} %get-tuple-element.32, f32[128,128]{0,1:T(8,128)S(1)} %bitcast.55, f32[128,128]{0,1:T(8,128)S(1)} %copy.9, f32[128,128]{0,1:T(8,128)S(1)} %get-tuple-element.31), kind=kOutput, calls=%fused_computation.17 | convolution fusion | flops 100859904 | bytes 524288 | tf_op jit(solution)/shard_map/dot_general | solution.py:152
  149.4 14.8 %shard_map.51 = f32[128,256]{1,0:T(8,128)} custom-call(f32[128,256]{1,0:T(8,128)} %fusion.9.rows_ref), custom_call_target="tpu_custom_call" | custom-call | tf_op jit(solution)/shard_map/pallas_call | solution.py:142
  164.2 0.8 dynamic-slice_bitcast_fusion
  165.0 4.5 %fusion.22 = f32[8192,64]{0,1:T(8,128)S(1)} fusion(f32[8192,128]{1,0:T(8,128)} %collective-permute-done.13, f32[256,64]{0,1:T(8,128)S(1)} %dynamic-slice_bitcast_fusion, pred[]{:T(512)S(6)} %eq.14), kind=kOutput, calls=%fused_computation.32 | convolution fusion | flops 402661376 | bytes 6356993 | tf_op jit(solution)/shard_map/dot_general | solution.py:248
  169.5 4.5 %fusion.5 = f32[8,64,8,128]{3,2,1,0:T(8,128)S(1)} fusion(f32[8192,64]{0,1:T(8,128)S(1)} %fusion.22, f32[8192,128]{1,0:T(8,128)} %fusion.39, f32[256,64]{0,1:T(8,128)S(1)} %dynamic-slice_bitcast_fusion, pred[]{:T(512)S(6)} %eq.14), kind=kOutput, calls=%fused_computation.8 | convolution fusion | flops 403185664 | bytes 8454145 | tf_op jit(solution)/shard_map/dot_general | solution.py:248
  174.1 1.6 copy.15
  (33 shorter events, 0.5 us)
Async XLA Ops:
  0.0 59.2 %copy-start = (s32[512,128]{1,0:T(8,128)S(1)}, s32[512,128]{1,0:T(8,128)}, u32[]{:S(2)}) copy-start(s32[512,128]{1,0:T(8,128)} %param.6) | copy-start | bytes 786436
  1.0 7.6 %collective-permute-start = (bf16[2,128,256]{2,1,0:T(8,128)(2,1)S(1)}, bf16[2,128,256]{2,1,0:T(8,128)(2,1)S(1)}, u32[]{:S(2)}, u32[]{:S(2)}) collective-permute-start(bf16[2,128,256]{2,1,0:T(8,128)(2,1)S(1)} %get-tuple-element.30), channel_id=1, source_target_pairs={{0,1},{1,2},{2,3},{3,4},{4,5},{5,6},{6,7},{8,9},{9,10},{10,11},{11... | collective-permute-start | bytes 393224 | tf_op jit(solution)/shard_map/ppermute | solution.py:20
  5.9 6.9 %collective-permute-start.1 = (bf16[2,128,256]{2,1,0:T(8,128)(2,1)S(1)}, bf16[2,128,256]{2,1,0:T(8,128)(2,1)S(1)}, u32[]{:S(2)}, u32[]{:S(2)}) collective-permute-start(bf16[2,128,256]{2,1,0:T(8,128)(2,1)S(1)} %get-tuple-element.29), channel_id=1, source_target_pairs={{1,0},{2,1},{3,2},{4,3},{5,4},{6,5},{7,6},{9,8},{10,9},{11,10},{12... | collective-permute-start | bytes 393224 | tf_op jit(solution)/shard_map/ppermute | solution.py:21
  8.7 4.1 %copy-start.5 = (bf16[2,128,256]{2,1,0:T(8,128)(2,1)}, bf16[2,128,256]{2,1,0:T(8,128)(2,1)S(1)}, u32[]{:S(2)}) copy-start(bf16[2,128,256]{2,1,0:T(8,128)(2,1)S(1)} %collective-permute-done.low_ref) | copy-start | bytes 393220
  12.8 0.7 copy-start.6
  27.2 6.2 %copy-start.1 = (f32[64,128,256]{2,1,0:T(8,128)S(1)}, f32[64,128,256]{2,1,0:T(8,128)}, u32[]{:S(2)}) copy-start(f32[64,128,256]{2,1,0:T(8,128)} %shard_map.46) | copy-start | bytes 25165828
  32.0 44.8 %collective-permute-start.6 = (f32[4096,256]{1,0:T(8,128)}, f32[4096,256]{1,0:T(8,128)}, u32[]{:S(2)}, u32[]{:S(2)}) collective-permute-start(f32[4096,256]{1,0:T(8,128)} %constant_dynamic-slice_fusion), channel_id=1, source_target_pairs={{0,8},{8,0},{1,9},{9,1},{2,10},{10,2},{3,11},{11,3},{4,12},{12,4},... | collective-permute-start | bytes 12582920 | tf_op jit(solution)/shard_map/ppermute | solution.py:32
  34.8 24.5 %copy-start.4 = (s32[256,128]{1,0:T(8,128)S(1)}, s32[256,128]{1,0:T(8,128)}, u32[]{:S(2)}) copy-start(s32[256,128]{1,0:T(8,128)} %param.7) | copy-start | bytes 393220
  41.8 8.1 %collective-permute-start.3 = (f32[256,256]{1,0:T(8,128)S(1)}, f32[256,256]{1,0:T(8,128)S(1)}, u32[]{:S(2)}, u32[]{:S(2)}) collective-permute-start(f32[256,256]{1,0:T(8,128)S(1)} %fusion.6), channel_id=1, source_target_pairs={{0,1},{1,0},{2,3},{3,2},{4,5},{5,4},{6,7},{7,6},{8,9},{9,8},{10,11... | collective-permute-start | bytes 786440 | tf_op jit(solution)/shard_map/ppermute | solution.py:42
  49.9 6.8 %collective-permute-start.4 = (f32[256,256]{1,0:T(8,128)S(1)}, f32[256,256]{1,0:T(8,128)S(1)}, u32[]{:S(2)}, u32[]{:S(2)}) collective-permute-start(f32[256,256]{1,0:T(8,128)S(1)} %add.46), channel_id=1, source_target_pairs={{0,2},{1,3},{2,0},{3,1},{4,6},{5,7},{6,4},{7,5},{8,10},{9,11},{10,... | collective-permute-start | bytes 786440 | tf_op jit(solution)/shard_map/ppermute | solution.py:42
  56.6 20.1 %collective-permute-start.5 = (f32[256,256]{1,0:T(8,128)S(1)}, f32[256,256]{1,0:T(8,128)S(1)}, u32[]{:S(2)}, u32[]{:S(2)}) collective-permute-start(f32[256,256]{1,0:T(8,128)S(1)} %add.47), channel_id=1, source_target_pairs={{0,4},{1,5},{2,6},{3,7},{4,0},{5,1},{6,2},{7,3},{8,12},{9,13},{10,... | collective-permute-start | bytes 786440 | tf_op jit(solution)/shard_map/ppermute | solution.py:42
  74.8 9.3 %collective-permute-start.2 = (f32[256,128]{0,1:T(8,128)}, f32[256,128]{0,1:T(8,128)S(1)}, u32[]{:S(2)}, u32[]{:S(2)}) collective-permute-start(f32[256,128]{0,1:T(8,128)} %bitcast.53), channel_id=1, source_target_pairs={{0,1},{1,0},{2,3},{3,2},{4,5},{5,4},{6,7},{7,6},{8,9},{9,8},{10,11... | collective-permute-start | bytes 393224 | tf_op jit(solution)/shard_map/ppermute | solution.py:32
  76.7 7.3 %copy-start.3 = (f32[128,256]{1,0:T(8,128)S(1)}, f32[128,256]{1,0:T(8,128)}, u32[]{:S(2)}) copy-start(f32[128,256]{1,0:T(8,128)} %shard_map.47) | copy-start | bytes 393220
  83.9 15.8 %collective-permute-start.7 = (f32[256,256]{1,0:T(8,128)S(1)}, f32[256,256]{1,0:T(8,128)S(1)}, u32[]{:S(2)}, u32[]{:S(2)}) collective-permute-start(f32[256,256]{1,0:T(8,128)S(1)} %bitcast_select_fusion), channel_id=1, source_target_pairs={{0,1},{1,0},{2,3},{3,2},{4,5},{5,4},{6,7},{7,6},{8,9},{9,8},{10,11... | collective-permute-start | bytes 786440 | tf_op jit(solution)/shard_map/ppermute | solution.py:204
  99.7 18.2 %collective-permute-start.8 = (f32[256,256]{1,0:T(8,128)S(1)}, f32[256,256]{1,0:T(8,128)S(1)}, u32[]{:S(2)}, u32[]{:S(2)}) collective-permute-start(f32[256,256]{1,0:T(8,128)S(1)} %add.51), channel_id=1, source_target_pairs={{0,2},{1,3},{2,0},{3,1},{4,6},{5,7},{6,4},{7,5},{8,10},{9,11},{10,... | collective-permute-start | bytes 786440 | tf_op jit(solution)/shard_map/ppermute | solution.py:204
  117.9 9.3 %copy-start.2 = (f32[128,256]{1,0:T(8,128)S(1)}, f32[128,256]{1,0:T(8,128)}, u32[]{:S(2)}) copy-start(f32[128,256]{1,0:T(8,128)} %shard_map.49) | copy-start | bytes 393220
  118.0 11.0 %collective-permute-start.9 = (f32[256,256]{1,0:T(8,128)S(1)}, f32[256,256]{1,0:T(8,128)S(1)}, u32[]{:S(2)}, u32[]{:S(2)}) collective-permute-start(f32[256,256]{1,0:T(8,128)S(1)} %add.52), channel_id=1, source_target_pairs={{0,4},{1,5},{2,6},{3,7},{4,0},{5,1},{6,2},{7,3},{8,12},{9,13},{10,... | collective-permute-start | bytes 786440 | tf_op jit(solution)/shard_map/ppermute | solution.py:211
  127.3 3.7 %collective-permute-start.12 = (f32[256,128]{0,1:T(8,128)S(1)}, f32[256,128]{0,1:T(8,128)S(1)}, u32[]{:S(2)}, u32[]{:S(2)}) collective-permute-start(f32[256,128]{0,1:T(8,128)S(1)} %bitcast.48), channel_id=1, source_target_pairs={{0,8},{8,0},{1,9},{9,1},{2,10},{10,2},{3,11},{11,3},{4,12},{12,4},... | collective-permute-start | bytes 393224 | tf_op jit(solution)/shard_map/ppermute | solution.py:32
  129.0 1.6 collective-permute-start.10
  129.5 1.5 collective-permute-start.11
  131.0 34.1 %collective-permute-start.13 = (f32[8192,128]{1,0:T(8,128)}, f32[8192,128]{1,0:T(8,128)}, u32[]{:S(2)}, u32[]{:S(2)}) collective-permute-start(f32[8192,128]{1,0:T(8,128)} %fusion.39), channel_id=1, source_target_pairs={{0,8},{8,0},{1,9},{9,1},{2,10},{10,2},{3,11},{11,3},{4,12},{12,4},... | collective-permute-start | bytes 12582920 | tf_op jit(solution)/shard_map/ppermute | solution.py:32

commit v7 on v3

--- a/solution.py
+++ b/solution.py
@@ -118,16 +118,22 @@
 
         def sweep(block, carry, first=first):
             base = pl.multiple_of(block * 8, 8)
+            pivot_rows = work[pl.ds(base, 8), :]
             for lane_row in range(8):
                 j = base + lane_row
-                vector = work[pl.ds(j, 1), :]
+                vector = pivot_rows[lane_row:lane_row + 1, :]
                 inverse = 1.0 / jnp.sum(vector * vector, axis=1, keepdims=True)
+                weight = jnp.sum(pivot_rows * vector, axis=1, keepdims=True) * inverse
+                ids = lax.broadcasted_iota(jnp.int32, weight.shape, 0)
+                weight = jnp.where(ids > lane_row, weight, 0.0)
+                pivot_rows = pivot_rows - weight * vector
                 for i in range(first, blocks):
                     rows = work[i * 8:(i + 1) * 8, :]
                     weight = jnp.sum(rows * vector, axis=1, keepdims=True) * inverse
                     ids = lax.broadcasted_iota(jnp.int32, weight.shape, 0) + i * 8
                     weight = jnp.where(ids > j, weight, 0.0)
                     work[i * 8:(i + 1) * 8, :] = rows - weight * vector
+            work[pl.ds(base, 8), :] = pivot_rows
             return carry
 
         lax.fori_loop(first, first + group, sweep, 0)

time: 177 us -> 170 us (0.960)
  Pallas kernels: 87.4 us -> 80.5 us
    pallas_call x5, Pallas kernels: 73.6 us -> 66.8 us  [orthonormal(): pl.pallas_call(gram_schmidt_kernel, out_shape=jax.ShapeDtypeStruct(rows.s...]
  transfers between devices with their start and end apart: 14 -> 14, of which waited for: 7 -> 7; matrix products, arithmetic and copies ran while one was open for 19% -> 20% of each run, Pallas kernels for 42% -> 39%
where the time goes in v7:
time: 170 us; the launch traced here: 169 us
  Pallas kernels  80.5 us (47%)
  matrix products  38.9 us (23%)
  waiting for transfers between devices  18.5 us (11%)
  starting transfers between devices  17.9 us (11%)
  local copies, waits for them, and re-layouts  10.7 us (6%)
  other arithmetic  2.41 us (1%)
    pallas_call x5, Pallas kernels, orthonormal(): pl.pallas_call(gram_schmidt_kernel, out_shape=jax.ShapeDtypeStruct(rows.s...  66.8 us
    dot_general x2, matrix products, cross_gram(): lax.dot_general(left_rows, right_rows, (((0,), (0,)), ((), ())), precisio...  13.8 us
    pallas_call x1, Pallas kernels, fluxes(): pl.pallas_call(functools.partial(flux_kernel, count), grid=(count,), in_s...  13.7 us
    ppermute x3, waiting for transfers between devices, tree_sum(): value = value + lax.ppermute(value, axis, route)  10.7 us
    dot_general x1, matrix products, on_device(): own_modes = jnp.dot(own_flux, own_basis, precision=high)  8.79 us
    ppermute x3, starting transfers between devices, tree_sum(): value = value + lax.ppermute(value, axis, route)  6.63 us
    ppermute x1, starting transfers between devices, halos(): lax.ppermute(lax.slice_in_dim(block, block.shape[0] - width, None, axis=0...  4.88 us
    dynamic_slice x1, local copies, waits for them, and re-layouts, on_device(): lax.dynamic_slice_in_dim(own_flux, (1 - member) * half_rows, half_rows, 0)  4.76 us
  transfers between devices with their start and end apart: 14, of which 7 were waited for; matrix products, arithmetic and copies ran while one was open for 20% of the time, Pallas kernels for 39%

profile of v7, /device:TPU:0, one launch (start us, length us, event | category | flops | bytes accessed | tf_op | source)
XLA Modules:
  0.0 169.1 jit_solution(10945736373085121958)
XLA Ops:
  0.0 1.0 fusion.37
  1.0 4.9 %collective-permute-start = (bf16[2,128,256]{2,1,0:T(8,128)(2,1)S(1)}, bf16[2,128,256]{2,1,0:T(8,128)(2,1)S(1)}, u32[]{:S(2)}, u32[]{:S(2)}) collective-permute-start(bf16[2,128,256]{2,1,0:T(8,128)(2,1)S(1)} %get-tuple-element.30), channel_id=1, source_target_pairs={{0,1},{1,2},{2,3},{3,4},{4,5},{5,6},{6,7},{8,9},{9,10},{10,11},{11... | collective-permute-start | bytes 393224 | tf_op jit(solution)/shard_map/ppermute | solution.py:20
  5.9 1.3 collective-permute-start.1
  7.2 1.4 collective-permute-done.low_ref
  8.7 4.1 %collective-permute-done.1.high_ref = bf16[2,128,256]{2,1,0:T(8,128)(2,1)S(1)} collective-permute-done((bf16[2,128,256]{2,1,0:T(8,128)(2,1)S(1)}, bf16[2,128,256]{2,1,0:T(8,128)(2,1)S(1)}, u32[]{:S(2)}, u32[]{:S(2)}) %collective-permute-start.1) | collective-permute-done | bytes 131104 | tf_op jit(solution)/shard_map/ppermute | solution.py:21
  12.8 0.7 copy-done.6
  13.4 13.7 %shard_map.46 = f32[64,128,256]{2,1,0:T(8,128)} custom-call(bf16[2,128,256]{2,1,0:T(8,128)(2,1)} %copy-done.5, bf16[2,128,256]{2,1,0:T(8,128)(2,1)} %copy-done.6, bf16[64,128,256]{2,1,0:T(8,128)(2,1)} %next_ref.1, bf16[64,128,256]{2,1,0:T(8,128)(2,1)} %next_ref.1, bf16[64,128,256]{2,1,0:T(8,128)(2,1)} %next_ref.1, f32[64,128]{1,0:T(8,128)} %coef_ref.1), custom_call_target="tpu_custom_call" | custom-call | tf_op jit(solution)/shard_map/pallas_call | solution.py:96
  27.2 4.8 %constant_dynamic-slice_fusion = f32[4096,256]{1,0:T(8,128)} fusion(f32[8192,256]{1,0:T(8,128)} %bitcast.44, s32[]{:T(128)S(6)} %select_n.90), kind=kLoop, calls=%fused_computation.43 | loop fusion | bytes 8388612 | tf_op jit(solution)/shard_map/dynamic_slice | solution.py:197
  31.9 1.4 copy-done.1
  33.3 1.5 fusion.2
  34.8 6.9 %fusion.6 = f32[256,256]{1,0:T(8,128)S(1)} fusion(f32[64,128,256]{2,1,0:T(8,128)S(1)} %copy-done.1, f32[256]{0:T(256)S(1)} %fusion.2), kind=kOutput, calls=%fused_computation.10 | convolution fusion | flops 3221422080 | bytes 8651776 | tf_op jit(solution)/shard_map/dot_general | solution.py:163
  41.7 2.5 %collective-permute-start.3 = (f32[256,256]{1,0:T(8,128)S(1)}, f32[256,256]{1,0:T(8,128)S(1)}, u32[]{:S(2)}, u32[]{:S(2)}) collective-permute-start(f32[256,256]{1,0:T(8,128)S(1)} %fusion.6), channel_id=1, source_target_pairs={{0,1},{1,0},{2,3},{3,2},{4,5},{5,4},{6,7},{7,6},{8,9},{9,8},{10,11... | collective-permute-start | bytes 786440 | tf_op jit(solution)/shard_map/ppermute | solution.py:42
  44.2 5.6 %collective-permute-done.3 = f32[256,256]{1,0:T(8,128)S(1)} collective-permute-done((f32[256,256]{1,0:T(8,128)S(1)}, f32[256,256]{1,0:T(8,128)S(1)}, u32[]{:S(2)}, u32[]{:S(2)}) %collective-permute-start.3) | collective-permute-done | bytes 262176 | tf_op jit(solution)/shard_map/ppermute | solution.py:42
  49.8 1.6 collective-permute-start.4
  51.4 5.1 %collective-permute-done.4 = f32[256,256]{1,0:T(8,128)S(1)} collective-permute-done((f32[256,256]{1,0:T(8,128)S(1)}, f32[256,256]{1,0:T(8,128)S(1)}, u32[]{:S(2)}, u32[]{:S(2)}) %collective-permute-start.4) | collective-permute-done | bytes 262176 | tf_op jit(solution)/shard_map/ppermute | solution.py:42
  56.6 2.5 %collective-permute-start.5 = (f32[256,256]{1,0:T(8,128)S(1)}, f32[256,256]{1,0:T(8,128)S(1)}, u32[]{:S(2)}, u32[]{:S(2)}) collective-permute-start(f32[256,256]{1,0:T(8,128)S(1)} %add.47), channel_id=1, source_target_pairs={{0,4},{1,5},{2,6},{3,7},{4,0},{5,1},{6,2},{7,3},{8,12},{9,13},{10,... | collective-permute-start | bytes 786440 | tf_op jit(solution)/shard_map/ppermute | solution.py:42
  59.1 0.1 copy.12
  59.2 0.1 copy.6
  59.3 0.7 select_bitcast_fusion.rows_ref
  60.0 13.5 %shard_map.47 = f32[128,256]{1,0:T(8,128)} custom-call(f32[128,256]{1,0:T(8,128)} %select_bitcast_fusion.rows_ref), custom_call_target="tpu_custom_call" | custom-call | tf_op jit(solution)/shard_map/pallas_call | solution.py:148
  73.5 1.9 %collective-permute-start.2 = (f32[256,128]{0,1:T(8,128)}, f32[256,128]{0,1:T(8,128)S(1)}, u32[]{:S(2)}, u32[]{:S(2)}) collective-permute-start(f32[256,128]{0,1:T(8,128)} %bitcast.53), channel_id=1, source_target_pairs={{0,1},{1,0},{2,3},{3,2},{4,5},{5,4},{6,7},{7,6},{8,9},{9,8},{10,11... | collective-permute-start | bytes 393224 | tf_op jit(solution)/shard_map/ppermute | solution.py:32
  75.5 6.9 %fusion.3 = f32[256,256]{1,0:T(8,128)S(1)} fusion(f32[4096,256]{1,0:T(8,128)} %collective-permute-done.6, f32[8192,256]{1,0:T(8,128)} %bitcast.45, s32[]{:T(128)S(6)} %select_n.89), kind=kOutput, calls=%fused_computation.5 | convolution fusion | flops 1610612736 | bytes 8650756 | tf_op jit(solution)/shard_map/dot_general | solution.py:163
  82.4 0.1 copy.8
  82.6 0.1 collective-permute-start.7
  82.7 1.1 fusion.16.rows_ref
  83.8 13.3 %shard_map.48 = f32[128,256]{1,0:T(8,128)} custom-call(f32[128,256]{1,0:T(8,128)} %fusion.16.rows_ref), custom_call_target="tpu_custom_call" | custom-call | tf_op jit(solution)/shard_map/pallas_call | solution.py:148
  97.2 1.5 collective-permute-start.8
  98.7 2.0 %fusion.38.rows_ref = f32[128,256]{1,0:T(8,128)} fusion(f32[256,128]{0,1:T(8,128)} %bitcast.56, f32[256,256]{1,0:T(8,128)S(1)} %add_multiply_fusion), kind=kOutput, calls=%fused_computation.52 | convolution fusion | flops 100663296 | bytes 524288 | tf_op jit(solution)/shard_map/dot_general | solution.py:208
  100.7 13.3 %shard_map.49 = f32[128,256]{1,0:T(8,128)} custom-call(f32[128,256]{1,0:T(8,128)} %fusion.38.rows_ref), custom_call_target="tpu_custom_call" | custom-call | tf_op jit(solution)/shard_map/pallas_call | solution.py:148
  114.0 0.5 collective-permute-start.9
  114.5 8.8 %fusion.39 = f32[8192,128]{1,0:T(8,128)} fusion(f32[8192,256]{1,0:T(8,128)} %bitcast.46, f32[256,128]{0,1:T(8,128)} %bitcast.47), kind=kOutput, calls=%fused_computation.53 | convolution fusion | flops 1610612736 | bytes 12713984 | tf_op jit(solution)/shard_map/dot_general | solution.py:218
  123.3 0.4 fusion.40
  123.7 1.3 collective-permute-done.9
  125.2 0.4 fusion.41
  125.6 0.6 collective-permute-start.11
  126.1 0.6 collective-permute-done.10
  126.7 0.3 collective-permute-done.11
  127.0 0.4 collective-permute-start.13
  127.4 0.4 fusion.7
  127.8 0.3 fusion.12
  128.2 0.9 fusion.10.rows_ref
  129.1 13.3 %shard_map.50 = f32[128,256]{1,0:T(8,128)} custom-call(f32[128,256]{1,0:T(8,128)} %fusion.10.rows_ref), custom_call_target="tpu_custom_call" | custom-call | tf_op jit(solution)/shard_map/pallas_call | solution.py:148
  142.4 1.8 %fusion.9.rows_ref = f32[128,256]{1,0:T(8,128)} fusion(f32[128,256]{1,0:T(8,128)} %shard_map.50, f32[128,128]{0,1:T(8,128)S(1)} %get-tuple-element.32, f32[128,128]{0,1:T(8,128)S(1)} %bitcast.55, f32[128,128]{0,1:T(8,128)S(1)} %copy.9, f32[128,128]{0,1:T(8,128)S(1)} %get-tuple-element.31), kind=kOutput, calls=%fused_computation.17 | convolution fusion | flops 100859904 | bytes 524288 | tf_op jit(solution)/shard_map/dot_general | solution.py:158
  144.3 13.3 %shard_map.51 = f32[128,256]{1,0:T(8,128)} custom-call(f32[128,256]{1,0:T(8,128)} %fusion.9.rows_ref), custom_call_target="tpu_custom_call" | custom-call | tf_op jit(solution)/shard_map/pallas_call | solution.py:148
  157.6 0.8 dynamic-slice_bitcast_fusion
  158.4 4.5 %fusion.22 = f32[8192,64]{0,1:T(8,128)S(1)} fusion(f32[8192,128]{1,0:T(8,128)} %collective-permute-done.13, f32[256,64]{0,1:T(8,128)S(1)} %dynamic-slice_bitcast_fusion, pred[]{:T(512)S(6)} %eq.14), kind=kOutput, calls=%fused_computation.32 | convolution fusion | flops 402661376 | bytes 6356993 | tf_op jit(solution)/shard_map/dot_general | solution.py:254
  162.9 4.5 %fusion.5 = f32[8,64,8,128]{3,2,1,0:T(8,128)S(1)} fusion(f32[8192,64]{0,1:T(8,128)S(1)} %fusion.22, f32[8192,128]{1,0:T(8,128)} %fusion.39, f32[256,64]{0,1:T(8,128)S(1)} %dynamic-slice_bitcast_fusion, pred[]{:T(512)S(6)} %eq.14), kind=kOutput, calls=%fused_computation.8 | convolution fusion | flops 403185664 | bytes 8454145 | tf_op jit(solution)/shard_map/dot_general | solution.py:254
  167.5 1.6 copy.15
  (33 shorter events, 0.5 us)
Async XLA Ops:
  0.0 59.1 %copy-start = (s32[512,128]{1,0:T(8,128)S(1)}, s32[512,128]{1,0:T(8,128)}, u32[]{:S(2)}) copy-start(s32[512,128]{1,0:T(8,128)} %param.6) | copy-start | bytes 786436
  1.0 7.6 %collective-permute-start = (bf16[2,128,256]{2,1,0:T(8,128)(2,1)S(1)}, bf16[2,128,256]{2,1,0:T(8,128)(2,1)S(1)}, u32[]{:S(2)}, u32[]{:S(2)}) collective-permute-start(bf16[2,128,256]{2,1,0:T(8,128)(2,1)S(1)} %get-tuple-element.30), channel_id=1, source_target_pairs={{0,1},{1,2},{2,3},{3,4},{4,5},{5,6},{6,7},{8,9},{9,10},{10,11},{11... | collective-permute-start | bytes 393224 | tf_op jit(solution)/shard_map/ppermute | solution.py:20
  5.9 6.9 %collective-permute-start.1 = (bf16[2,128,256]{2,1,0:T(8,128)(2,1)S(1)}, bf16[2,128,256]{2,1,0:T(8,128)(2,1)S(1)}, u32[]{:S(2)}, u32[]{:S(2)}) collective-permute-start(bf16[2,128,256]{2,1,0:T(8,128)(2,1)S(1)} %get-tuple-element.29), channel_id=1, source_target_pairs={{1,0},{2,1},{3,2},{4,3},{5,4},{6,5},{7,6},{9,8},{10,9},{11,10},{12... | collective-permute-start | bytes 393224 | tf_op jit(solution)/shard_map/ppermute | solution.py:21
  8.7 4.1 %copy-start.5 = (bf16[2,128,256]{2,1,0:T(8,128)(2,1)}, bf16[2,128,256]{2,1,0:T(8,128)(2,1)S(1)}, u32[]{:S(2)}) copy-start(bf16[2,128,256]{2,1,0:T(8,128)(2,1)S(1)} %collective-permute-done.low_ref) | copy-start | bytes 393220
  12.8 0.7 copy-start.6
  27.2 6.2 %copy-start.1 = (f32[64,128,256]{2,1,0:T(8,128)S(1)}, f32[64,128,256]{2,1,0:T(8,128)}, u32[]{:S(2)}) copy-start(f32[64,128,256]{2,1,0:T(8,128)} %shard_map.46) | copy-start | bytes 25165828
  31.9 43.6 %collective-permute-start.6 = (f32[4096,256]{1,0:T(8,128)}, f32[4096,256]{1,0:T(8,128)}, u32[]{:S(2)}, u32[]{:S(2)}) collective-permute-start(f32[4096,256]{1,0:T(8,128)} %constant_dynamic-slice_fusion), channel_id=1, source_target_pairs={{0,8},{8,0},{1,9},{9,1},{2,10},{10,2},{3,11},{11,3},{4,12},{12,4},... | collective-permute-start | bytes 12582920 | tf_op jit(solution)/shard_map/ppermute | solution.py:32
  34.8 24.5 %copy-start.4 = (s32[256,128]{1,0:T(8,128)S(1)}, s32[256,128]{1,0:T(8,128)}, u32[]{:S(2)}) copy-start(s32[256,128]{1,0:T(8,128)} %param.7) | copy-start | bytes 393220
  41.7 8.1 %collective-permute-start.3 = (f32[256,256]{1,0:T(8,128)S(1)}, f32[256,256]{1,0:T(8,128)S(1)}, u32[]{:S(2)}, u32[]{:S(2)}) collective-permute-start(f32[256,256]{1,0:T(8,128)S(1)} %fusion.6), channel_id=1, source_target_pairs={{0,1},{1,0},{2,3},{3,2},{4,5},{5,4},{6,7},{7,6},{8,9},{9,8},{10,11... | collective-permute-start | bytes 786440 | tf_op jit(solution)/shard_map/ppermute | solution.py:42
  49.8 6.8 %collective-permute-start.4 = (f32[256,256]{1,0:T(8,128)S(1)}, f32[256,256]{1,0:T(8,128)S(1)}, u32[]{:S(2)}, u32[]{:S(2)}) collective-permute-start(f32[256,256]{1,0:T(8,128)S(1)} %add.46), channel_id=1, source_target_pairs={{0,2},{1,3},{2,0},{3,1},{4,6},{5,7},{6,4},{7,5},{8,10},{9,11},{10,... | collective-permute-start | bytes 786440 | tf_op jit(solution)/shard_map/ppermute | solution.py:42
  56.6 18.8 %collective-permute-start.5 = (f32[256,256]{1,0:T(8,128)S(1)}, f32[256,256]{1,0:T(8,128)S(1)}, u32[]{:S(2)}, u32[]{:S(2)}) collective-permute-start(f32[256,256]{1,0:T(8,128)S(1)} %add.47), channel_id=1, source_target_pairs={{0,4},{1,5},{2,6},{3,7},{4,0},{5,1},{6,2},{7,3},{8,12},{9,13},{10,... | collective-permute-start | bytes 786440 | tf_op jit(solution)/shard_map/ppermute | solution.py:42
  73.5 9.3 %collective-permute-start.2 = (f32[256,128]{0,1:T(8,128)}, f32[256,128]{0,1:T(8,128)S(1)}, u32[]{:S(2)}, u32[]{:S(2)}) collective-permute-start(f32[256,128]{0,1:T(8,128)} %bitcast.53), channel_id=1, source_target_pairs={{0,1},{1,0},{2,3},{3,2},{4,5},{5,4},{6,7},{7,6},{8,9},{9,8},{10,11... | collective-permute-start | bytes 393224 | tf_op jit(solution)/shard_map/ppermute | solution.py:32
  75.5 7.3 %copy-start.3 = (f32[128,256]{1,0:T(8,128)S(1)}, f32[128,256]{1,0:T(8,128)}, u32[]{:S(2)}) copy-start(f32[128,256]{1,0:T(8,128)} %shard_map.47) | copy-start | bytes 393220
  82.6 14.5 %collective-permute-start.7 = (f32[256,256]{1,0:T(8,128)S(1)}, f32[256,256]{1,0:T(8,128)S(1)}, u32[]{:S(2)}, u32[]{:S(2)}) collective-permute-start(f32[256,256]{1,0:T(8,128)S(1)} %bitcast_select_fusion), channel_id=1, source_target_pairs={{0,1},{1,0},{2,3},{3,2},{4,5},{5,4},{6,7},{7,6},{8,9},{9,8},{10,11... | collective-permute-start | bytes 786440 | tf_op jit(solution)/shard_map/ppermute | solution.py:210
  97.2 16.8 %collective-permute-start.8 = (f32[256,256]{1,0:T(8,128)S(1)}, f32[256,256]{1,0:T(8,128)S(1)}, u32[]{:S(2)}, u32[]{:S(2)}) collective-permute-start(f32[256,256]{1,0:T(8,128)S(1)} %add.51), channel_id=1, source_target_pairs={{0,2},{1,3},{2,0},{3,1},{4,6},{5,7},{6,4},{7,5},{8,10},{9,11},{10,... | collective-permute-start | bytes 786440 | tf_op jit(solution)/shard_map/ppermute | solution.py:210
  114.0 9.3 %copy-start.2 = (f32[128,256]{1,0:T(8,128)S(1)}, f32[128,256]{1,0:T(8,128)}, u32[]{:S(2)}) copy-start(f32[128,256]{1,0:T(8,128)} %shard_map.49) | copy-start | bytes 393220
  114.0 11.0 %collective-permute-start.9 = (f32[256,256]{1,0:T(8,128)S(1)}, f32[256,256]{1,0:T(8,128)S(1)}, u32[]{:S(2)}, u32[]{:S(2)}) collective-permute-start(f32[256,256]{1,0:T(8,128)S(1)} %add.52), channel_id=1, source_target_pairs={{0,4},{1,5},{2,6},{3,7},{4,0},{5,1},{6,2},{7,3},{8,12},{9,13},{10,... | collective-permute-start | bytes 786440 | tf_op jit(solution)/shard_map/ppermute | solution.py:217
  123.3 3.7 %collective-permute-start.12 = (f32[256,128]{0,1:T(8,128)S(1)}, f32[256,128]{0,1:T(8,128)S(1)}, u32[]{:S(2)}, u32[]{:S(2)}) collective-permute-start(f32[256,128]{0,1:T(8,128)S(1)} %bitcast.48), channel_id=1, source_target_pairs={{0,8},{8,0},{1,9},{9,1},{2,10},{10,2},{3,11},{11,3},{4,12},{12,4},... | collective-permute-start | bytes 393224 | tf_op jit(solution)/shard_map/ppermute | solution.py:32
  125.1 1.6 collective-permute-start.10
  125.6 1.5 collective-permute-start.11
  127.0 31.4 %collective-permute-start.13 = (f32[8192,128]{1,0:T(8,128)}, f32[8192,128]{1,0:T(8,128)}, u32[]{:S(2)}, u32[]{:S(2)}) collective-permute-start(f32[8192,128]{1,0:T(8,128)} %fusion.39), channel_id=1, source_target_pairs={{0,8},{8,0},{1,9},{9,1},{2,10},{10,2},{3,11},{11,3},{4,12},{12,4},... | collective-permute-start | bytes 12582920 | tf_op jit(solution)/shard_map/ppermute | solution.py:32

commit v8 on v7

--- a/solution.py
+++ b/solution.py
@@ -200,7 +200,18 @@
         lax.dynamic_slice_in_dim(own_flux, half_start, half_rows, 0), other_rows
     )
     mixed_half = jnp.where(is_first, mixed_half, mixed_half.T)
-    own_gram = tree_sum(self_gram(own_flux), "tx") / cells_total
+    partial_gram = self_gram(own_flux)
+    split = order_size // 2
+    packed = jnp.concatenate([partial_gram[:split], partial_gram[split:, split:]], axis=1)
+    packed = tree_sum(packed, "tx") / cells_total
+    upper = packed[:, split:order_size]
+    own_gram = jnp.concatenate(
+        [
+            jnp.concatenate([packed[:, :split], upper], axis=1),
+            jnp.concatenate([upper.T, packed[:, order_size:]], axis=1),
+        ],
+        axis=0,
+    )
     own_gram, mixed_sum = lax.optimization_barrier((own_gram, mixed_half))
     hops = butterfly_steps("tx")
     own_basis = first_basis

time: 170 us -> 167 us (0.982)
  waiting for transfers between devices: 18.5 us -> 15.4 us
    ppermute x3, waiting for transfers between devices: 10.7 us -> 8.05 us  [tree_sum(): value = value + lax.ppermute(value, axis, route)]
  transfers between devices with their start and end apart: 14 -> 14, of which waited for: 7 -> 7; matrix products, arithmetic and copies ran while one was open for 20% -> 20% of each run, Pallas kernels for 39% -> 40%
where the time goes in v8:
time: 167 us; the launch traced here: 166 us
  Pallas kernels  80.5 us (48%)
  matrix products  38.8 us (23%)
  starting transfers between devices  18.1 us (11%)
  waiting for transfers between devices  15.4 us (9%)
  local copies, waits for them, and re-layouts  10.8 us (6%)
  other arithmetic  2.41 us (1%)
    pallas_call x5, Pallas kernels, orthonormal(): pl.pallas_call(gram_schmidt_kernel, out_shape=jax.ShapeDtypeStruct(rows.s...  66.8 us
    dot_general x2, matrix products, cross_gram(): lax.dot_general(left_rows, right_rows, (((0,), (0,)), ((), ())), precisio...  13.8 us
    pallas_call x1, Pallas kernels, fluxes(): pl.pallas_call(functools.partial(flux_kernel, count), grid=(count,), in_s...  13.7 us
    dot_general x1, matrix products, on_device(): own_modes = jnp.dot(own_flux, own_basis, precision=high)  8.78 us
    ppermute x3, waiting for transfers between devices, tree_sum(): value = value + lax.ppermute(value, axis, route)  8.05 us
    ppermute x3, starting transfers between devices, tree_sum(): value = value + lax.ppermute(value, axis, route)  6.96 us
    ppermute x1, starting transfers between devices, halos(): lax.ppermute(lax.slice_in_dim(block, block.shape[0] - width, None, axis=0...  4.88 us
    dynamic_slice x1, local copies, waits for them, and re-layouts, on_device(): lax.dynamic_slice_in_dim(own_flux, (1 - member) * half_rows, half_rows, 0)  4.76 us
  transfers between devices with their start and end apart: 14, of which 7 were waited for; matrix products, arithmetic and copies ran while one was open for 20% of the time, Pallas kernels for 40%

profile of v8, /device:TPU:0, one launch (start us, length us, event | category | flops | bytes accessed | tf_op | source)
XLA Modules:
  0.0 166.3 jit_solution(10597888544374197737)
XLA Ops:
  0.0 1.0 fusion.38
  1.0 4.9 %collective-permute-start = (bf16[2,128,256]{2,1,0:T(8,128)(2,1)S(1)}, bf16[2,128,256]{2,1,0:T(8,128)(2,1)S(1)}, u32[]{:S(2)}, u32[]{:S(2)}) collective-permute-start(bf16[2,128,256]{2,1,0:T(8,128)(2,1)S(1)} %get-tuple-element.30), channel_id=1, source_target_pairs={{0,1},{1,2},{2,3},{3,4},{4,5},{5,6},{6,7},{8,9},{9,10},{10,11},{11... | collective-permute-start | bytes 393224 | tf_op jit(solution)/shard_map/ppermute | solution.py:20
  5.9 1.3 collective-permute-start.1
  7.2 1.4 collective-permute-done.low_ref
  8.7 4.1 %collective-permute-done.1.high_ref = bf16[2,128,256]{2,1,0:T(8,128)(2,1)S(1)} collective-permute-done((bf16[2,128,256]{2,1,0:T(8,128)(2,1)S(1)}, bf16[2,128,256]{2,1,0:T(8,128)(2,1)S(1)}, u32[]{:S(2)}, u32[]{:S(2)}) %collective-permute-start.1) | collective-permute-done | bytes 131104 | tf_op jit(solution)/shard_map/ppermute | solution.py:21
  12.8 0.7 copy-done.6
  13.4 13.7 %shard_map.46 = f32[64,128,256]{2,1,0:T(8,128)} custom-call(bf16[2,128,256]{2,1,0:T(8,128)(2,1)} %copy-done.5, bf16[2,128,256]{2,1,0:T(8,128)(2,1)} %copy-done.6, bf16[64,128,256]{2,1,0:T(8,128)(2,1)} %next_ref.1, bf16[64,128,256]{2,1,0:T(8,128)(2,1)} %next_ref.1, bf16[64,128,256]{2,1,0:T(8,128)(2,1)} %next_ref.1, f32[64,128]{1,0:T(8,128)} %coef_ref.1), custom_call_target="tpu_custom_call" | custom-call | tf_op jit(solution)/shard_map/pallas_call | solution.py:96
  27.2 4.8 %constant_dynamic-slice_fusion = f32[4096,256]{1,0:T(8,128)} fusion(f32[8192,256]{1,0:T(8,128)} %bitcast.45, s32[]{:T(128)S(6)} %select_n.90), kind=kLoop, calls=%fused_computation.45 | loop fusion | bytes 8388612 | tf_op jit(solution)/shard_map/dynamic_slice | solution.py:197
  31.9 1.4 copy-done.1
  33.3 1.5 fusion.2
  34.8 6.9 %fusion.6 = f32[256,256]{0,1:T(8,128)S(1)} fusion(f32[64,128,256]{2,1,0:T(8,128)S(1)} %copy-done.1, f32[256]{0:T(256)S(1)} %fusion.2), kind=kOutput, calls=%fused_computation.10 | convolution fusion | flops 3221422080 | bytes 8651776 | tf_op jit(solution)/shard_map/dot_general | solution.py:163
  41.7 2.5 %collective-permute-start.3 = (f32[128,384]{0,1:T(8,128)S(1)}, f32[128,384]{0,1:T(8,128)S(1)}, u32[]{:S(2)}, u32[]{:S(2)}) collective-permute-start(f32[128,384]{0,1:T(8,128)S(1)} %pad_maximum_fusion), channel_id=1, source_target_pairs={{0,1},{1,0},{2,3},{3,2},{4,5},{5,4},{6,7},{7,6},{8,9},{9,8},{10,11... | collective-permute-start | bytes 589832 | tf_op jit(solution)/shard_map/ppermute | solution.py:42
  44.2 4.2 %collective-permute-done.3 = f32[128,384]{0,1:T(8,128)S(1)} collective-permute-done((f32[128,384]{0,1:T(8,128)S(1)}, f32[128,384]{0,1:T(8,128)S(1)}, u32[]{:S(2)}, u32[]{:S(2)}) %collective-permute-start.3) | collective-permute-done | bytes 196640 | tf_op jit(solution)/shard_map/ppermute | solution.py:42
  48.4 1.6 collective-permute-start.4
  50.1 0.1 copy.13
  50.2 0.1 copy.6
  50.3 3.9 %collective-permute-done.4 = f32[128,384]{0,1:T(8,128)S(1)} collective-permute-done((f32[128,384]{0,1:T(8,128)S(1)}, f32[128,384]{0,1:T(8,128)S(1)}, u32[]{:S(2)}, u32[]{:S(2)}) %collective-permute-start.4) | collective-permute-done | bytes 196640 | tf_op jit(solution)/shard_map/ppermute | solution.py:42
  54.2 2.8 %collective-permute-start.5 = (f32[128,384]{0,1:T(8,128)S(1)}, f32[128,384]{0,1:T(8,128)S(1)}, u32[]{:S(2)}, u32[]{:S(2)}) collective-permute-start(f32[128,384]{0,1:T(8,128)S(1)} %add.47), channel_id=1, source_target_pairs={{0,4},{1,5},{2,6},{3,7},{4,0},{5,1},{6,2},{7,3},{8,12},{9,13},{10,... | collective-permute-start | bytes 589832 | tf_op jit(solution)/shard_map/ppermute | solution.py:42
  57.0 0.7 select_bitcast_fusion.rows_ref
  57.7 13.5 %shard_map.47 = f32[128,256]{1,0:T(8,128)} custom-call(f32[128,256]{1,0:T(8,128)} %select_bitcast_fusion.rows_ref), custom_call_target="tpu_custom_call" | custom-call | tf_op jit(solution)/shard_map/pallas_call | solution.py:148
  71.2 1.9 %collective-permute-start.2 = (f32[256,128]{0,1:T(8,128)}, f32[256,128]{0,1:T(8,128)S(1)}, u32[]{:S(2)}, u32[]{:S(2)}) collective-permute-start(f32[256,128]{0,1:T(8,128)} %bitcast.54), channel_id=1, source_target_pairs={{0,1},{1,0},{2,3},{3,2},{4,5},{5,4},{6,7},{7,6},{8,9},{9,8},{10,11... | collective-permute-start | bytes 393224 | tf_op jit(solution)/shard_map/ppermute | solution.py:32
  73.2 6.9 %fusion.3 = f32[256,256]{1,0:T(8,128)S(1)} fusion(f32[4096,256]{1,0:T(8,128)} %collective-permute-done.6, f32[8192,256]{1,0:T(8,128)} %bitcast.46, s32[]{:T(128)S(6)} %select_n.89), kind=kOutput, calls=%fused_computation.5 | convolution fusion | flops 1610612736 | bytes 8650756 | tf_op jit(solution)/shard_map/dot_general | solution.py:163
  80.2 0.1 copy.9
  80.3 0.2 collective-permute-start.7
  80.6 0.9 fusion.16.rows_ref
  81.5 13.3 %shard_map.48 = f32[128,256]{1,0:T(8,128)} custom-call(f32[128,256]{1,0:T(8,128)} %fusion.16.rows_ref), custom_call_target="tpu_custom_call" | custom-call | tf_op jit(solution)/shard_map/pallas_call | solution.py:148
  94.9 1.4 collective-permute-start.8
  96.3 1.8 %fusion.40.rows_ref = f32[128,256]{1,0:T(8,128)} fusion(f32[256,128]{0,1:T(8,128)} %bitcast.57, f32[256,256]{0,1:T(8,128)S(1)} %maximum_maximum_fusion), kind=kOutput, calls=%fused_computation.56 | convolution fusion | flops 100663296 | bytes 524288 | tf_op jit(solution)/shard_map/dot_general | solution.py:219
  98.1 13.3 %shard_map.49 = f32[128,256]{1,0:T(8,128)} custom-call(f32[128,256]{1,0:T(8,128)} %fusion.40.rows_ref), custom_call_target="tpu_custom_call" | custom-call | tf_op jit(solution)/shard_map/pallas_call | solution.py:148
  111.5 0.5 collective-permute-start.9
  112.0 8.8 %fusion.41 = f32[8192,128]{1,0:T(8,128)} fusion(f32[8192,256]{1,0:T(8,128)} %bitcast.47, f32[256,128]{0,1:T(8,128)} %bitcast.48), kind=kOutput, calls=%fused_computation.57 | convolution fusion | flops 1610612736 | bytes 12713984 | tf_op jit(solution)/shard_map/dot_general | solution.py:229
  120.7 0.6 fusion.42
  121.3 0.9 collective-permute-done.9
  122.4 0.4 fusion.43
  122.8 0.6 collective-permute-start.11
  123.4 0.6 collective-permute-done.10
  124.0 0.3 collective-permute-done.11
  124.3 0.4 collective-permute-start.13
  124.6 0.4 fusion.7
  125.0 0.3 fusion.13
  125.4 0.9 fusion.10.rows_ref
  126.3 13.3 %shard_map.50 = f32[128,256]{1,0:T(8,128)} custom-call(f32[128,256]{1,0:T(8,128)} %fusion.10.rows_ref), custom_call_target="tpu_custom_call" | custom-call | tf_op jit(solution)/shard_map/pallas_call | solution.py:148
  139.6 1.8 %fusion.9.rows_ref = f32[128,256]{1,0:T(8,128)} fusion(f32[128,256]{1,0:T(8,128)} %shard_map.50, f32[128,128]{0,1:T(8,128)S(1)} %get-tuple-element.34, f32[128,128]{0,1:T(8,128)S(1)} %bitcast.56, f32[128,128]{0,1:T(8,128)S(1)} %copy.10, f32[128,128]{0,1:T(8,128)S(1)} %get-tuple-element.33), kind=kOutput, calls=%fused_computation.19 | convolution fusion | flops 100859904 | bytes 524288 | tf_op jit(solution)/shard_map/dot_general | solution.py:158
  141.5 13.3 %shard_map.51 = f32[128,256]{1,0:T(8,128)} custom-call(f32[128,256]{1,0:T(8,128)} %fusion.9.rows_ref), custom_call_target="tpu_custom_call" | custom-call | tf_op jit(solution)/shard_map/pallas_call | solution.py:148
  154.8 0.8 dynamic-slice_bitcast_fusion
  155.7 4.5 %fusion.22 = f32[8192,64]{0,1:T(8,128)S(1)} fusion(f32[8192,128]{1,0:T(8,128)} %collective-permute-done.13, f32[256,64]{0,1:T(8,128)S(1)} %dynamic-slice_bitcast_fusion, pred[]{:T(512)S(6)} %eq.14), kind=kOutput, calls=%fused_computation.34 | convolution fusion | flops 402661376 | bytes 6356993 | tf_op jit(solution)/shard_map/dot_general | solution.py:265
  160.2 4.5 %fusion.5 = f32[8,64,8,128]{3,2,1,0:T(8,128)S(1)} fusion(f32[8192,64]{0,1:T(8,128)S(1)} %fusion.22, f32[8192,128]{1,0:T(8,128)} %fusion.41, f32[256,64]{0,1:T(8,128)S(1)} %dynamic-slice_bitcast_fusion, pred[]{:T(512)S(6)} %eq.14), kind=kOutput, calls=%fused_computation.8 | convolution fusion | flops 403185664 | bytes 8454145 | tf_op jit(solution)/shard_map/dot_general | solution.py:265
  164.7 1.6 copy.17
  (40 shorter events, 0.6 us)
Async XLA Ops:
  0.0 50.1 %copy-start = (s32[512,128]{1,0:T(8,128)S(1)}, s32[512,128]{1,0:T(8,128)}, u32[]{:S(2)}) copy-start(s32[512,128]{1,0:T(8,128)} %param.6) | copy-start | bytes 786436
  1.0 7.6 %collective-permute-start = (bf16[2,128,256]{2,1,0:T(8,128)(2,1)S(1)}, bf16[2,128,256]{2,1,0:T(8,128)(2,1)S(1)}, u32[]{:S(2)}, u32[]{:S(2)}) collective-permute-start(bf16[2,128,256]{2,1,0:T(8,128)(2,1)S(1)} %get-tuple-element.30), channel_id=1, source_target_pairs={{0,1},{1,2},{2,3},{3,4},{4,5},{5,6},{6,7},{8,9},{9,10},{10,11},{11... | collective-permute-start | bytes 393224 | tf_op jit(solution)/shard_map/ppermute | solution.py:20
  5.9 6.9 %collective-permute-start.1 = (bf16[2,128,256]{2,1,0:T(8,128)(2,1)S(1)}, bf16[2,128,256]{2,1,0:T(8,128)(2,1)S(1)}, u32[]{:S(2)}, u32[]{:S(2)}) collective-permute-start(bf16[2,128,256]{2,1,0:T(8,128)(2,1)S(1)} %get-tuple-element.29), channel_id=1, source_target_pairs={{1,0},{2,1},{3,2},{4,3},{5,4},{6,5},{7,6},{9,8},{10,9},{11,10},{12... | collective-permute-start | bytes 393224 | tf_op jit(solution)/shard_map/ppermute | solution.py:21
  8.7 4.1 %copy-start.5 = (bf16[2,128,256]{2,1,0:T(8,128)(2,1)}, bf16[2,128,256]{2,1,0:T(8,128)(2,1)S(1)}, u32[]{:S(2)}) copy-start(bf16[2,128,256]{2,1,0:T(8,128)(2,1)S(1)} %collective-permute-done.low_ref) | copy-start | bytes 393220
  12.8 0.7 copy-start.6
  27.2 6.2 %copy-start.1 = (f32[64,128,256]{2,1,0:T(8,128)S(1)}, f32[64,128,256]{2,1,0:T(8,128)}, u32[]{:S(2)}) copy-start(f32[64,128,256]{2,1,0:T(8,128)} %shard_map.46) | copy-start | bytes 25165828
  31.9 41.3 %collective-permute-start.6 = (f32[4096,256]{1,0:T(8,128)}, f32[4096,256]{1,0:T(8,128)}, u32[]{:S(2)}, u32[]{:S(2)}) collective-permute-start(f32[4096,256]{1,0:T(8,128)} %constant_dynamic-slice_fusion), channel_id=1, source_target_pairs={{0,8},{8,0},{1,9},{9,1},{2,10},{10,2},{3,11},{11,3},{4,12},{12,4},... | collective-permute-start | bytes 12582920 | tf_op jit(solution)/shard_map/ppermute | solution.py:32
  34.8 15.4 %copy-start.4 = (s32[256,128]{1,0:T(8,128)S(1)}, s32[256,128]{1,0:T(8,128)}, u32[]{:S(2)}) copy-start(s32[256,128]{1,0:T(8,128)} %param.7) | copy-start | bytes 393220
  41.7 6.7 %collective-permute-start.3 = (f32[128,384]{0,1:T(8,128)S(1)}, f32[128,384]{0,1:T(8,128)S(1)}, u32[]{:S(2)}, u32[]{:S(2)}) collective-permute-start(f32[128,384]{0,1:T(8,128)S(1)} %pad_maximum_fusion), channel_id=1, source_target_pairs={{0,1},{1,0},{2,3},{3,2},{4,5},{5,4},{6,7},{7,6},{8,9},{9,8},{10,11... | collective-permute-start | bytes 589832 | tf_op jit(solution)/shard_map/ppermute | solution.py:42
  48.4 5.7 %collective-permute-start.4 = (f32[128,384]{0,1:T(8,128)S(1)}, f32[128,384]{0,1:T(8,128)S(1)}, u32[]{:S(2)}, u32[]{:S(2)}) collective-permute-start(f32[128,384]{0,1:T(8,128)S(1)} %fusion.37), channel_id=1, source_target_pairs={{0,2},{1,3},{2,0},{3,1},{4,6},{5,7},{6,4},{7,5},{8,10},{9,11},{10,... | collective-permute-start | bytes 589832 | tf_op jit(solution)/shard_map/ppermute | solution.py:42
  54.2 18.9 %collective-permute-start.5 = (f32[128,384]{0,1:T(8,128)S(1)}, f32[128,384]{0,1:T(8,128)S(1)}, u32[]{:S(2)}, u32[]{:S(2)}) collective-permute-start(f32[128,384]{0,1:T(8,128)S(1)} %add.47), channel_id=1, source_target_pairs={{0,4},{1,5},{2,6},{3,7},{4,0},{5,1},{6,2},{7,3},{8,12},{9,13},{10,... | collective-permute-start | bytes 589832 | tf_op jit(solution)/shard_map/ppermute | solution.py:42
  71.2 9.4 %collective-permute-start.2 = (f32[256,128]{0,1:T(8,128)}, f32[256,128]{0,1:T(8,128)S(1)}, u32[]{:S(2)}, u32[]{:S(2)}) collective-permute-start(f32[256,128]{0,1:T(8,128)} %bitcast.54), channel_id=1, source_target_pairs={{0,1},{1,0},{2,3},{3,2},{4,5},{5,4},{6,7},{7,6},{8,9},{9,8},{10,11... | collective-permute-start | bytes 393224 | tf_op jit(solution)/shard_map/ppermute | solution.py:32
  73.2 7.3 %copy-start.3 = (f32[128,256]{1,0:T(8,128)S(1)}, f32[128,256]{1,0:T(8,128)}, u32[]{:S(2)}) copy-start(f32[128,256]{1,0:T(8,128)} %shard_map.47) | copy-start | bytes 393220
  80.3 14.5 %collective-permute-start.7 = (f32[256,256]{1,0:T(8,128)S(1)}, f32[256,256]{1,0:T(8,128)S(1)}, u32[]{:S(2)}, u32[]{:S(2)}) collective-permute-start(f32[256,256]{1,0:T(8,128)S(1)} %bitcast_select_fusion), channel_id=1, source_target_pairs={{0,1},{1,0},{2,3},{3,2},{4,5},{5,4},{6,7},{7,6},{8,9},{9,8},{10,11... | collective-permute-start | bytes 786440 | tf_op jit(solution)/shard_map/ppermute | solution.py:221
  94.9 16.6 %collective-permute-start.8 = (f32[256,256]{1,0:T(8,128)S(1)}, f32[256,256]{1,0:T(8,128)S(1)}, u32[]{:S(2)}, u32[]{:S(2)}) collective-permute-start(f32[256,256]{1,0:T(8,128)S(1)} %add.51), channel_id=1, source_target_pairs={{0,2},{1,3},{2,0},{3,1},{4,6},{5,7},{6,4},{7,5},{8,10},{9,11},{10,... | collective-permute-start | bytes 786440 | tf_op jit(solution)/shard_map/ppermute | solution.py:221
  111.5 9.3 %copy-start.2 = (f32[128,256]{1,0:T(8,128)S(1)}, f32[128,256]{1,0:T(8,128)}, u32[]{:S(2)}) copy-start(f32[128,256]{1,0:T(8,128)} %shard_map.49) | copy-start | bytes 393220
  111.5 10.8 %collective-permute-start.9 = (f32[256,256]{1,0:T(8,128)S(1)}, f32[256,256]{1,0:T(8,128)S(1)}, u32[]{:S(2)}, u32[]{:S(2)}) collective-permute-start(f32[256,256]{1,0:T(8,128)S(1)} %add.52), channel_id=1, source_target_pairs={{0,4},{1,5},{2,6},{3,7},{4,0},{5,1},{6,2},{7,3},{8,12},{9,13},{10,... | collective-permute-start | bytes 786440 | tf_op jit(solution)/shard_map/ppermute | solution.py:228
  120.7 3.5 %collective-permute-start.12 = (f32[256,128]{0,1:T(8,128)S(1)}, f32[256,128]{0,1:T(8,128)S(1)}, u32[]{:S(2)}, u32[]{:S(2)}) collective-permute-start(f32[256,128]{0,1:T(8,128)S(1)} %bitcast.49), channel_id=1, source_target_pairs={{0,8},{8,0},{1,9},{9,1},{2,10},{10,2},{3,11},{11,3},{4,12},{12,4},... | collective-permute-start | bytes 393224 | tf_op jit(solution)/shard_map/ppermute | solution.py:32
  122.3 1.6 collective-permute-start.10
  122.8 1.5 collective-permute-start.11
  124.3 31.4 %collective-permute-start.13 = (f32[8192,128]{1,0:T(8,128)}, f32[8192,128]{1,0:T(8,128)}, u32[]{:S(2)}, u32[]{:S(2)}) collective-permute-start(f32[8192,128]{1,0:T(8,128)} %fusion.41), channel_id=1, source_target_pairs={{0,8},{8,0},{1,9},{9,1},{2,10},{10,2},{3,11},{11,3},{4,12},{12,4},... | collective-permute-start | bytes 12582920 | tf_op jit(solution)/shard_map/ppermute | solution.py:32

commit v9 on v8

--- a/solution.py
+++ b/solution.py
@@ -64,7 +64,7 @@
     return (8.0 * (shifted(3) - shifted(1)) - (shifted(4) - shifted(0))) / 12.0
 
 
-def flux_kernel(count, low_ref, high_ref, prev_ref, main_ref, next_ref, coef_ref, out_ref):
+def flux_kernel(count, member_ref, low_ref, high_ref, prev_ref, main_ref, next_ref, coef_ref, out_ref, sent_ref):
     i = pl.program_id(0)
     above = jnp.where(i == 0, low_ref[...], prev_ref[-2:])
     below = jnp.where(i == count - 1, high_ref[...], next_ref[:2])
@@ -82,31 +82,48 @@
 
     along_cols = (8.0 * (shift(1) - shift(-1)) - (shift(2) - shift(-2))) / 12.0
     central = rows[2:-2]
-    out_ref[...] = central - coef_ref[...][:, :, None] * (along_rows + along_cols)
-
-
-def fluxes(low, block, high, coefficient):
+    result = central - coef_ref[...][:, :, None] * (along_rows + along_cols)
+    out_ref[...] = result
+    first_sent = (1 - member_ref[0]) * (count // 2)
+
+    @pl.when((i >= first_sent) & (i < first_sent + count // 2))
+    def _():
+        sent_ref[...] = result
+
+
+def fluxes(low, block, high, coefficient, member):
     nx, ny, ns = block.shape
-    bx = 8 if nx % 8 == 0 else nx
+    bx = 8 if nx % 16 == 0 else nx // 2
     count = nx // bx
+    half = count // 2
 
     def spec(index):
         return pl.BlockSpec((bx, ny, ns), index)
 
+    def sent_index(i, member_ref):
+        return (jnp.clip(i - (1 - member_ref[0]) * half, 0, half - 1), 0, 0)
+
+    grid_spec = pltpu.PrefetchScalarGridSpec(
+        num_scalar_prefetch=1,
+        grid=(count,),
+        in_specs=[
+            pl.BlockSpec(low.shape, lambda i, m: (0, 0, 0)),
+            pl.BlockSpec(high.shape, lambda i, m: (0, 0, 0)),
+            spec(lambda i, m: (jnp.maximum(i - 1, 0), 0, 0)),
+            spec(lambda i, m: (i, 0, 0)),
+            spec(lambda i, m: (jnp.minimum(i + 1, count - 1), 0, 0)),
+            pl.BlockSpec((bx, ny), lambda i, m: (i, 0)),
+        ],
+        out_specs=[spec(lambda i, m: (i, 0, 0)), spec(sent_index)],
+    )
     return pl.pallas_call(
         functools.partial(flux_kernel, count),
-        grid=(count,),
-        in_specs=[
-            pl.BlockSpec(low.shape, lambda i: (0, 0, 0)),
-            pl.BlockSpec(high.shape, lambda i: (0, 0, 0)),
-            spec(lambda i: (jnp.maximum(i - 1, 0), 0, 0)),
-            spec(lambda i: (i, 0, 0)),
-            spec(lambda i: (jnp.minimum(i + 1, count - 1), 0, 0)),
-            pl.BlockSpec((bx, ny), lambda i: (i, 0)),
-        ],
-        out_specs=spec(lambda i: (i, 0, 0)),
-        out_shape=jax.ShapeDtypeStruct((nx, ny, ns), jnp.float32),
-    )(low, high, block, block, block, coefficient)
+        grid_spec=grid_spec,
+        out_shape=[
+            jax.ShapeDtypeStruct((nx, ny, ns), jnp.float32),
+            jax.ShapeDtypeStruct((nx // 2, ny, ns), jnp.float32),
+        ],
+    )(jnp.reshape(member, (1,)).astype(jnp.int32), low, high, block, block, block, coefficient)
 
 
 def gram_schmidt_kernel(rows_ref, out_ref, work):
@@ -191,11 +208,11 @@
         theirs = partner(mine, "tx", 0)
         first_basis = jnp.where(is_even, mine, theirs)
         merge_basis = jnp.where(is_even, theirs, mine)
-    own_flux = fluxes(halo_low, snapshots, halo_high, coefficient).reshape(rows_here, order_size)
+    own_flux, sent_rows = fluxes(halo_low, snapshots, halo_high, coefficient, member)
+    own_flux = own_flux.reshape(rows_here, order_size)
     half_rows = rows_here // 2
     half_start = member * half_rows
-    sent_rows = lax.dynamic_slice_in_dim(own_flux, (1 - member) * half_rows, half_rows, 0)
-    other_rows = partner(sent_rows, "run", 0)
+    other_rows = partner(sent_rows.reshape(half_rows, order_size), "run", 0)
     mixed_half = cross_gram(
         lax.dynamic_slice_in_dim(own_flux, half_start, half_rows, 0), other_rows
     )

time: 167 us -> 170 us (1.018)
  local copies, waits for them, and re-layouts: 10.8 us -> 5.48 us
  waiting for transfers between devices: 15.4 us -> 19.4 us
  other arithmetic: 2.41 us -> 5.95 us
    dynamic_slice x1 -> x0, local copies, waits for them, and re-layouts: 4.76 us -> none  [on_device(): lax.dynamic_slice_in_dim(own_flux, (1 - member) * half_rows, half_rows, 0)]
    reduce_sum x1, other arithmetic: 1.45 us -> 4.98 us  [self_gram(): missing = jnp.sum(lower * lower, axis=0)]
    ppermute x3, waiting for transfers between devices: 8.05 us -> 10.5 us  [tree_sum(): value = value + lax.ppermute(value, axis, route)]
  transfers between devices with their start and end apart: 14 -> 14, of which waited for: 7 -> 7; matrix products, arithmetic and copies ran while one was open for 20% -> 22% of each run, Pallas kernels for 40% -> 39%
where the time goes in v9:
time: 170 us; the launch traced here: 169 us
  Pallas kernels  81.3 us (48%)
  matrix products  38.8 us (23%)
  waiting for transfers between devices  19.4 us (11%)
  starting transfers between devices  17.9 us (11%)
  other arithmetic  5.95 us (4%)
  local copies, waits for them, and re-layouts  5.48 us (3%)
    pallas_call x5, Pallas kernels, orthonormal(): pl.pallas_call(gram_schmidt_kernel, out_shape=jax.ShapeDtypeStruct(rows.s...  66.8 us
    pallas_call x1, Pallas kernels, fluxes(): pl.pallas_call(functools.partial(flux_kernel, count), grid_spec=grid_spec...  14.5 us
    dot_general x2, matrix products, cross_gram(): lax.dot_general(left_rows, right_rows, (((0,), (0,)), ((), ())), precisio...  13.8 us
    ppermute x3, waiting for transfers between devices, tree_sum(): value = value + lax.ppermute(value, axis, route)  10.5 us
    dot_general x1, matrix products, on_device(): own_modes = jnp.dot(own_flux, own_basis, precision=high)  8.79 us
    ppermute x3, starting transfers between devices, tree_sum(): value = value + lax.ppermute(value, axis, route)  6.64 us
    reduce_sum x1, other arithmetic, self_gram(): missing = jnp.sum(lower * lower, axis=0)  4.98 us
    ppermute x1, starting transfers between devices, halos(): lax.ppermute(lax.slice_in_dim(block, block.shape[0] - width, None, axis=0...  4.88 us
  transfers between devices with their start and end apart: 14, of which 7 were waited for; matrix products, arithmetic and copies ran while one was open for 22% of the time, Pallas kernels for 39%

profile of v9, /device:TPU:0, one launch (start us, length us, event | category | flops | bytes accessed | tf_op | source)
XLA Modules:
  0.0 169.2 jit_solution(6812125234144239719)
XLA Ops:
  0.0 1.0 fusion.38
  1.0 4.9 %collective-permute-start = (bf16[2,128,256]{2,1,0:T(8,128)(2,1)S(1)}, bf16[2,128,256]{2,1,0:T(8,128)(2,1)S(1)}, u32[]{:S(2)}, u32[]{:S(2)}) collective-permute-start(bf16[2,128,256]{2,1,0:T(8,128)(2,1)S(1)} %get-tuple-element.34), channel_id=1, source_target_pairs={{0,1},{1,2},{2,3},{3,4},{4,5},{5,6},{6,7},{8,9},{9,10},{10,11},{11... | collective-permute-start | bytes 393224 | tf_op jit(solution)/shard_map/ppermute | solution.py:20
  5.9 1.3 collective-permute-start.1
  7.2 1.4 collective-permute-done.low_ref
  8.7 4.1 %collective-permute-done.1.high_ref = bf16[2,128,256]{2,1,0:T(8,128)(2,1)S(1)} collective-permute-done((bf16[2,128,256]{2,1,0:T(8,128)(2,1)S(1)}, bf16[2,128,256]{2,1,0:T(8,128)(2,1)S(1)}, u32[]{:S(2)}, u32[]{:S(2)}) %collective-permute-start.1) | collective-permute-done | bytes 131104 | tf_op jit(solution)/shard_map/ppermute | solution.py:21
  12.8 0.7 copy-done.5
  13.4 14.5 %shard_map.46 = (f32[64,128,256]{2,1,0:T(8,128)}, f32[32,128,256]{2,1,0:T(8,128)}) custom-call(s32[1]{0:T(128)} %bitcast.member_ref, bf16[2,128,256]{2,1,0:T(8,128)(2,1)} %copy-done.4, bf16[2,128,256]{2,1,0:T(8,128)(2,1)} %copy-done.5, bf16[64,128,256]{2,1,0:T(8,128)(2,1)} %next_ref.1, bf16[64,128,256]{2,1,0:T(8,128)(2,1)} %next_ref.1, ...), custom_call_target="tpu_custom_call" | custom-call | tf_op jit(solution)/shard_map/pallas_call | solution.py:119
  28.0 5.0 %fusion.2 = f32[256]{0:T(256)S(1)} fusion(f32[64,128,256]{2,1,0:T(8,128)} %get-tuple-element.19), kind=kLoop, calls=%fused_computation.4 | loop fusion | flops 10485504 | bytes 8389632 | tf_op jit(solution)/shard_map/reduce_sum | solution.py:186
  33.0 0.8 copy-done.1
  33.7 6.9 %fusion.6 = f32[256,256]{0,1:T(8,128)S(1)} fusion(f32[64,128,256]{2,1,0:T(8,128)S(1)} %copy-done.1, f32[256]{0:T(256)S(1)} %fusion.2), kind=kOutput, calls=%fused_computation.10 | convolution fusion | flops 3221422080 | bytes 8651776 | tf_op jit(solution)/shard_map/dot_general | solution.py:180
  40.7 2.5 %collective-permute-start.3 = (f32[128,384]{0,1:T(8,128)S(1)}, f32[128,384]{0,1:T(8,128)S(1)}, u32[]{:S(2)}, u32[]{:S(2)}) collective-permute-start(f32[128,384]{0,1:T(8,128)S(1)} %pad_maximum_fusion), channel_id=1, source_target_pairs={{0,1},{1,0},{2,3},{3,2},{4,5},{5,4},{6,7},{7,6},{8,9},{9,8},{10,11... | collective-permute-start | bytes 589832 | tf_op jit(solution)/shard_map/ppermute | solution.py:42
  43.2 5.6 %collective-permute-done.3 = f32[128,384]{0,1:T(8,128)S(1)} collective-permute-done((f32[128,384]{0,1:T(8,128)S(1)}, f32[128,384]{0,1:T(8,128)S(1)}, u32[]{:S(2)}, u32[]{:S(2)}) %collective-permute-start.3) | collective-permute-done | bytes 196640 | tf_op jit(solution)/shard_map/ppermute | solution.py:42
  48.8 1.6 collective-permute-start.4
  50.4 0.1 copy.6
  50.6 0.1 copy.13
  50.7 4.9 %collective-permute-done.4 = f32[128,384]{0,1:T(8,128)S(1)} collective-permute-done((f32[128,384]{0,1:T(8,128)S(1)}, f32[128,384]{0,1:T(8,128)S(1)}, u32[]{:S(2)}, u32[]{:S(2)}) %collective-permute-start.4) | collective-permute-done | bytes 196640 | tf_op jit(solution)/shard_map/ppermute | solution.py:42
  55.6 2.5 %collective-permute-start.5 = (f32[128,384]{0,1:T(8,128)S(1)}, f32[128,384]{0,1:T(8,128)S(1)}, u32[]{:S(2)}, u32[]{:S(2)}) collective-permute-start(f32[128,384]{0,1:T(8,128)S(1)} %add.44), channel_id=1, source_target_pairs={{0,4},{1,5},{2,6},{3,7},{4,0},{5,1},{6,2},{7,3},{8,12},{9,13},{10,... | collective-permute-start | bytes 589832 | tf_op jit(solution)/shard_map/ppermute | solution.py:42
  58.1 0.7 select_bitcast_fusion.rows_ref
  58.8 13.5 %shard_map.47 = f32[128,256]{1,0:T(8,128)} custom-call(f32[128,256]{1,0:T(8,128)} %select_bitcast_fusion.rows_ref), custom_call_target="tpu_custom_call" | custom-call | tf_op jit(solution)/shard_map/pallas_call | solution.py:165
  72.3 1.7 collective-permute-start.2
  74.0 0.1 copy.14
  74.2 6.9 %fusion.3 = f32[256,256]{1,0:T(8,128)S(1)} fusion(f32[4096,256]{1,0:T(8,128)} %collective-permute-done.6, f32[8192,256]{1,0:T(8,128)} %bitcast.47, s32[]{:T(128)S(6)} %select_n.86), kind=kOutput, calls=%fused_computation.5 | convolution fusion | flops 1610612736 | bytes 8650756 | tf_op jit(solution)/shard_map/dot_general | solution.py:180
  81.1 0.1 copy.9
  81.3 0.4 collective-permute-start.7
  81.7 0.9 fusion.16.rows_ref
  82.6 13.3 %shard_map.48 = f32[128,256]{1,0:T(8,128)} custom-call(f32[128,256]{1,0:T(8,128)} %fusion.16.rows_ref), custom_call_target="tpu_custom_call" | custom-call | tf_op jit(solution)/shard_map/pallas_call | solution.py:165
  96.0 1.4 collective-permute-start.8
  97.4 1.8 %fusion.40.rows_ref = f32[128,256]{1,0:T(8,128)} fusion(f32[256,128]{0,1:T(8,128)} %bitcast.58, f32[256,256]{0,1:T(8,128)S(1)} %maximum_maximum_fusion), kind=kOutput, calls=%fused_computation.55 | convolution fusion | flops 100663296 | bytes 524288 | tf_op jit(solution)/shard_map/dot_general | solution.py:236
  99.3 13.3 %shard_map.49 = f32[128,256]{1,0:T(8,128)} custom-call(f32[128,256]{1,0:T(8,128)} %fusion.40.rows_ref), custom_call_target="tpu_custom_call" | custom-call | tf_op jit(solution)/shard_map/pallas_call | solution.py:165
  112.6 0.6 collective-permute-start.9
  113.2 8.8 %fusion.41 = f32[8192,128]{1,0:T(8,128)} fusion(f32[8192,256]{1,0:T(8,128)} %bitcast.48, f32[256,128]{0,1:T(8,128)} %bitcast.49), kind=kOutput, calls=%fused_computation.56 | convolution fusion | flops 1610612736 | bytes 12713984 | tf_op jit(solution)/shard_map/dot_general | solution.py:246
  122.0 0.6 fusion.42
  122.6 2.5 %collective-permute-done.9 = f32[256,256]{1,0:T(8,128)S(1)} collective-permute-done((f32[256,256]{1,0:T(8,128)S(1)}, f32[256,256]{1,0:T(8,128)S(1)}, u32[]{:S(2)}, u32[]{:S(2)}) %collective-permute-start.9) | collective-permute-done | bytes 262176 | tf_op jit(solution)/shard_map/ppermute | solution.py:245
  125.3 0.4 fusion.43
  125.6 0.6 collective-permute-start.11
  126.2 0.6 collective-permute-done.10
  126.8 0.3 collective-permute-done.11
  127.1 0.4 collective-permute-start.13
  127.5 0.4 fusion.7
  127.8 0.3 fusion.13
  128.2 0.9 fusion.10.rows_ref
  129.2 13.3 %shard_map.50 = f32[128,256]{1,0:T(8,128)} custom-call(f32[128,256]{1,0:T(8,128)} %fusion.10.rows_ref), custom_call_target="tpu_custom_call" | custom-call | tf_op jit(solution)/shard_map/pallas_call | solution.py:165
  142.5 1.8 %fusion.9.rows_ref = f32[128,256]{1,0:T(8,128)} fusion(f32[128,256]{1,0:T(8,128)} %shard_map.50, f32[128,128]{0,1:T(8,128)S(1)} %get-tuple-element.38, f32[128,128]{0,1:T(8,128)S(1)} %bitcast.57, f32[128,128]{0,1:T(8,128)S(1)} %copy.10, f32[128,128]{0,1:T(8,128)S(1)} %get-tuple-element.37), kind=kOutput, calls=%fused_computation.19 | convolution fusion | flops 100859904 | bytes 524288 | tf_op jit(solution)/shard_map/dot_general | solution.py:175
  144.4 13.3 %shard_map.51 = f32[128,256]{1,0:T(8,128)} custom-call(f32[128,256]{1,0:T(8,128)} %fusion.9.rows_ref), custom_call_target="tpu_custom_call" | custom-call | tf_op jit(solution)/shard_map/pallas_call | solution.py:165
  157.7 0.8 dynamic-slice_bitcast_fusion
  158.5 4.5 %fusion.22 = f32[8192,64]{0,1:T(8,128)S(1)} fusion(f32[8192,128]{1,0:T(8,128)} %collective-permute-done.13, f32[256,64]{0,1:T(8,128)S(1)} %dynamic-slice_bitcast_fusion, pred[]{:T(512)S(6)} %eq.14), kind=kOutput, calls=%fused_computation.34 | convolution fusion | flops 402661376 | bytes 6356993 | tf_op jit(solution)/shard_map/dot_general | solution.py:282
  163.0 4.5 %fusion.5 = f32[8,64,8,128]{3,2,1,0:T(8,128)S(1)} fusion(f32[8192,64]{0,1:T(8,128)S(1)} %fusion.22, f32[8192,128]{1,0:T(8,128)} %fusion.41, f32[256,64]{0,1:T(8,128)S(1)} %dynamic-slice_bitcast_fusion, pred[]{:T(512)S(6)} %eq.14), kind=kOutput, calls=%fused_computation.8 | convolution fusion | flops 403185664 | bytes 8454145 | tf_op jit(solution)/shard_map/dot_general | solution.py:282
  167.6 1.6 copy.17
  (39 shorter events, 0.6 us)
Async XLA Ops:
  0.0 50.5 %copy-start = (s32[512,128]{1,0:T(8,128)S(1)}, s32[512,128]{1,0:T(8,128)}, u32[]{:S(2)}) copy-start(s32[512,128]{1,0:T(8,128)} %param.6) | copy-start | bytes 786436
  1.0 7.6 %collective-permute-start = (bf16[2,128,256]{2,1,0:T(8,128)(2,1)S(1)}, bf16[2,128,256]{2,1,0:T(8,128)(2,1)S(1)}, u32[]{:S(2)}, u32[]{:S(2)}) collective-permute-start(bf16[2,128,256]{2,1,0:T(8,128)(2,1)S(1)} %get-tuple-element.34), channel_id=1, source_target_pairs={{0,1},{1,2},{2,3},{3,4},{4,5},{5,6},{6,7},{8,9},{9,10},{10,11},{11... | collective-permute-start | bytes 393224 | tf_op jit(solution)/shard_map/ppermute | solution.py:20
  5.9 6.9 %collective-permute-start.1 = (bf16[2,128,256]{2,1,0:T(8,128)(2,1)S(1)}, bf16[2,128,256]{2,1,0:T(8,128)(2,1)S(1)}, u32[]{:S(2)}, u32[]{:S(2)}) collective-permute-start(bf16[2,128,256]{2,1,0:T(8,128)(2,1)S(1)} %get-tuple-element.33), channel_id=1, source_target_pairs={{1,0},{2,1},{3,2},{4,3},{5,4},{6,5},{7,6},{9,8},{10,9},{11,10},{12... | collective-permute-start | bytes 393224 | tf_op jit(solution)/shard_map/ppermute | solution.py:21
  8.7 4.1 %copy-start.4 = (bf16[2,128,256]{2,1,0:T(8,128)(2,1)}, bf16[2,128,256]{2,1,0:T(8,128)(2,1)S(1)}, u32[]{:S(2)}) copy-start(bf16[2,128,256]{2,1,0:T(8,128)(2,1)S(1)} %collective-permute-done.low_ref) | copy-start | bytes 393220
  12.8 0.7 copy-start.5
  28.0 46.2 %collective-permute-start.6 = (f32[4096,256]{1,0:T(8,128)}, f32[4096,256]{1,0:T(8,128)}, u32[]{:S(2)}, u32[]{:S(2)}) collective-permute-start(f32[4096,256]{1,0:T(8,128)} %bitcast.60), channel_id=1, source_target_pairs={{0,8},{8,0},{1,9},{9,1},{2,10},{10,2},{3,11},{11,3},{4,12},{12,4},... | collective-permute-start | bytes 12582920 | tf_op jit(solution)/shard_map/ppermute | solution.py:32
  28.0 5.8 %copy-start.1 = (f32[64,128,256]{2,1,0:T(8,128)S(1)}, f32[64,128,256]{2,1,0:T(8,128)}, u32[]{:S(2)}) copy-start(f32[64,128,256]{2,1,0:T(8,128)} %get-tuple-element.19) | copy-start | bytes 25165828
  33.7 16.7 %copy-start.6 = (s32[256,128]{1,0:T(8,128)S(1)}, s32[256,128]{1,0:T(8,128)}, u32[]{:S(2)}) copy-start(s32[256,128]{1,0:T(8,128)} %param.7) | copy-start | bytes 393220
  40.7 8.1 %collective-permute-start.3 = (f32[128,384]{0,1:T(8,128)S(1)}, f32[128,384]{0,1:T(8,128)S(1)}, u32[]{:S(2)}, u32[]{:S(2)}) collective-permute-start(f32[128,384]{0,1:T(8,128)S(1)} %pad_maximum_fusion), channel_id=1, source_target_pairs={{0,1},{1,0},{2,3},{3,2},{4,5},{5,4},{6,7},{7,6},{8,9},{9,8},{10,11... | collective-permute-start | bytes 589832 | tf_op jit(solution)/shard_map/ppermute | solution.py:42
  48.8 6.8 %collective-permute-start.4 = (f32[128,384]{0,1:T(8,128)S(1)}, f32[128,384]{0,1:T(8,128)S(1)}, u32[]{:S(2)}, u32[]{:S(2)}) collective-permute-start(f32[128,384]{0,1:T(8,128)S(1)} %fusion.37), channel_id=1, source_target_pairs={{0,2},{1,3},{2,0},{3,1},{4,6},{5,7},{6,4},{7,5},{8,10},{9,11},{10,... | collective-permute-start | bytes 589832 | tf_op jit(solution)/shard_map/ppermute | solution.py:42
  55.6 18.3 %collective-permute-start.5 = (f32[128,384]{0,1:T(8,128)S(1)}, f32[128,384]{0,1:T(8,128)S(1)}, u32[]{:S(2)}, u32[]{:S(2)}) collective-permute-start(f32[128,384]{0,1:T(8,128)S(1)} %add.44), channel_id=1, source_target_pairs={{0,4},{1,5},{2,6},{3,7},{4,0},{5,1},{6,2},{7,3},{8,12},{9,13},{10,... | collective-permute-start | bytes 589832 | tf_op jit(solution)/shard_map/ppermute | solution.py:42
  72.3 9.4 %collective-permute-start.2 = (f32[256,128]{0,1:T(8,128)}, f32[256,128]{0,1:T(8,128)S(1)}, u32[]{:S(2)}, u32[]{:S(2)}) collective-permute-start(f32[256,128]{0,1:T(8,128)} %bitcast.55), channel_id=1, source_target_pairs={{0,1},{1,0},{2,3},{3,2},{4,5},{5,4},{6,7},{7,6},{8,9},{9,8},{10,11... | collective-permute-start | bytes 393224 | tf_op jit(solution)/shard_map/ppermute | solution.py:32
  74.1 7.5 %copy-start.3 = (f32[128,256]{1,0:T(8,128)S(1)}, f32[128,256]{1,0:T(8,128)}, u32[]{:S(2)}) copy-start(f32[128,256]{1,0:T(8,128)} %shard_map.47) | copy-start | bytes 393220
  81.3 14.7 %collective-permute-start.7 = (f32[256,256]{1,0:T(8,128)S(1)}, f32[256,256]{1,0:T(8,128)S(1)}, u32[]{:S(2)}, u32[]{:S(2)}) collective-permute-start(f32[256,256]{1,0:T(8,128)S(1)} %bitcast_select_fusion), channel_id=1, source_target_pairs={{0,1},{1,0},{2,3},{3,2},{4,5},{5,4},{6,7},{7,6},{8,9},{9,8},{10,11... | collective-permute-start | bytes 786440 | tf_op jit(solution)/shard_map/ppermute | solution.py:238
  96.0 16.6 %collective-permute-start.8 = (f32[256,256]{1,0:T(8,128)S(1)}, f32[256,256]{1,0:T(8,128)S(1)}, u32[]{:S(2)}, u32[]{:S(2)}) collective-permute-start(f32[256,256]{1,0:T(8,128)S(1)} %add.47), channel_id=1, source_target_pairs={{0,2},{1,3},{2,0},{3,1},{4,6},{5,7},{6,4},{7,5},{8,10},{9,11},{10,... | collective-permute-start | bytes 786440 | tf_op jit(solution)/shard_map/ppermute | solution.py:238
  112.6 9.4 %copy-start.2 = (f32[128,256]{1,0:T(8,128)S(1)}, f32[128,256]{1,0:T(8,128)}, u32[]{:S(2)}) copy-start(f32[128,256]{1,0:T(8,128)} %shard_map.49) | copy-start | bytes 393220
  112.6 12.5 %collective-permute-start.9 = (f32[256,256]{1,0:T(8,128)S(1)}, f32[256,256]{1,0:T(8,128)S(1)}, u32[]{:S(2)}, u32[]{:S(2)}) collective-permute-start(f32[256,256]{1,0:T(8,128)S(1)} %add.48), channel_id=1, source_target_pairs={{0,4},{1,5},{2,6},{3,7},{4,0},{5,1},{6,2},{7,3},{8,12},{9,13},{10,... | collective-permute-start | bytes 786440 | tf_op jit(solution)/shard_map/ppermute | solution.py:245
  122.0 5.1 %collective-permute-start.12 = (f32[256,128]{0,1:T(8,128)S(1)}, f32[256,128]{0,1:T(8,128)S(1)}, u32[]{:S(2)}, u32[]{:S(2)}) collective-permute-start(f32[256,128]{0,1:T(8,128)S(1)} %bitcast.50), channel_id=1, source_target_pairs={{0,8},{8,0},{1,9},{9,1},{2,10},{10,2},{3,11},{11,3},{4,12},{12,4},... | collective-permute-start | bytes 393224 | tf_op jit(solution)/shard_map/ppermute | solution.py:32
  125.2 1.6 collective-permute-start.10
  125.6 1.5 collective-permute-start.11
  127.1 31.4 %collective-permute-start.13 = (f32[8192,128]{1,0:T(8,128)}, f32[8192,128]{1,0:T(8,128)}, u32[]{:S(2)}, u32[]{:S(2)}) collective-permute-start(f32[8192,128]{1,0:T(8,128)} %fusion.41), channel_id=1, source_target_pairs={{0,8},{8,0},{1,9},{9,1},{2,10},{10,2},{3,11},{11,3},{4,12},{12,4},... | collective-permute-start | bytes 12582920 | tf_op jit(solution)/shard_map/ppermute | solution.py:32

commit v10 on v8

--- a/solution.py
+++ b/solution.py
@@ -188,6 +188,7 @@
     else:
         is_even = lax.axis_index("tx") % 2 == 0
         mine = orthonormal(jnp.where(is_even, own_start, merge_start))
+        mine, snapshots = lax.optimization_barrier((mine, snapshots))
         theirs = partner(mine, "tx", 0)
         first_basis = jnp.where(is_even, mine, theirs)
         merge_basis = jnp.where(is_even, theirs, mine)

time: 167 us -> 171 us (1.024)
  starting transfers between devices: 18.1 us -> 21.2 us
    ppermute x3, waiting for transfers between devices: 8.05 us -> 13.7 us  [tree_sum(): value = value + lax.ppermute(value, axis, route)]
    ppermute x1, waiting for transfers between devices: 4.13 us -> 0.01 us  [halos(): lax.ppermute(lax.slice_in_dim(block, 0, width, axis=0), axis, backward)]
    ppermute x3, starting transfers between devices: 2.07 us -> 4.92 us  [on_device(): received = lax.ppermute(mixed_sum, 'tx', hops.pop(0))]
    ppermute x3, starting transfers between devices: 6.96 us -> 8.72 us  [tree_sum(): value = value + lax.ppermute(value, axis, route)]
    unnamed x17 -> x15, local copies, waits for them, and re-layouts: 2.35 us -> 3.89 us
  transfers between devices with their start and end apart: 14 -> 14, of which waited for: 7 -> 6; matrix products, arithmetic and copies ran while one was open for 20% -> 20% of each run, Pallas kernels for 40% -> 39%
where the time goes in v10:
time: 171 us
  Pallas kernels  80.6 us (47%)
  matrix products  39 us (23%)
  starting transfers between devices  21.2 us (12%)
  waiting for transfers between devices  14.9 us (9%)
  local copies, waits for them, and re-layouts  12.4 us (7%)
  other arithmetic  2.41 us (1%)
    pallas_call x5, Pallas kernels, orthonormal(): pl.pallas_call(gram_schmidt_kernel, out_shape=jax.ShapeDtypeStruct(rows.s...  66.8 us
    dot_general x2, matrix products, cross_gram(): lax.dot_general(left_rows, right_rows, (((0,), (0,)), ((), ())), precisio...  14 us
    pallas_call x1, Pallas kernels, fluxes(): pl.pallas_call(functools.partial(flux_kernel, count), grid=(count,), in_s...  13.7 us
    ppermute x3, waiting for transfers between devices, tree_sum(): value = value + lax.ppermute(value, axis, route)  13.7 us
    dot_general x1, matrix products, on_device(): own_modes = jnp.dot(own_flux, own_basis, precision=high)  8.79 us
    ppermute x3, starting transfers between devices, tree_sum(): value = value + lax.ppermute(value, axis, route)  8.72 us
    ppermute x3, starting transfers between devices, on_device(): received = lax.ppermute(mixed_sum, 'tx', hops.pop(0))  4.92 us
    ppermute x1, starting transfers between devices, halos(): lax.ppermute(lax.slice_in_dim(block, block.shape[0] - width, None, axis=0...  4.88 us
  transfers between devices with their start and end apart: 14, of which 6 were waited for; matrix products, arithmetic and copies ran while one was open for 20% of the time, Pallas kernels for 39%

profile of v10, /device:TPU:0, one launch (start us, length us, event | category | flops | bytes accessed | tf_op | source)
XLA Modules:
  0.0 170.8 jit_solution(1616904132798911183)
XLA Ops:
  0.0 1.0 fusion.36
  1.0 4.9 %collective-permute-start = (bf16[2,128,256]{2,1,0:T(8,128)(2,1)S(1)}, bf16[2,128,256]{2,1,0:T(8,128)(2,1)S(1)}, u32[]{:S(2)}, u32[]{:S(2)}) collective-permute-start(bf16[2,128,256]{2,1,0:T(8,128)(2,1)S(1)} %get-tuple-element.34), channel_id=1, source_target_pairs={{0,1},{1,2},{2,3},{3,4},{4,5},{5,6},{6,7},{8,9},{9,10},{10,11},{11... | collective-permute-start | bytes 393224 | tf_op jit(solution)/shard_map/ppermute | solution.py:20
  5.9 1.3 collective-permute-start.1
  7.4 1.0 copy.6
  8.4 0.7 select_bitcast_fusion.rows_ref
  9.1 13.3 %shard_map.46 = f32[128,256]{1,0:T(8,128)} custom-call(f32[128,256]{1,0:T(8,128)} %select_bitcast_fusion.rows_ref), custom_call_target="tpu_custom_call" | custom-call | tf_op jit(solution)/shard_map/pallas_call | solution.py:148
  22.4 0.6 copy-done.4
  23.0 0.7 copy-done.5
  23.7 13.7 %shard_map.47 = f32[64,128,256]{2,1,0:T(8,128)} custom-call(bf16[2,128,256]{2,1,0:T(8,128)(2,1)} %copy-done.4, bf16[2,128,256]{2,1,0:T(8,128)(2,1)} %copy-done.5, bf16[64,128,256]{2,1,0:T(8,128)(2,1)} %next_ref, bf16[64,128,256]{2,1,0:T(8,128)(2,1)} %next_ref, bf16[64,128,256]{2,1,0:T(8,128)(2,1)} %next_ref, f32[64,128]{1,0:T(8,128)} %coef_ref.1), custom_call_target="tpu_custom_call" | custom-call | tf_op jit(solution)/shard_map/pallas_call | solution.py:96
  37.4 4.8 %constant_dynamic-slice_fusion = f32[4096,256]{1,0:T(8,128)} fusion(f32[8192,256]{1,0:T(8,128)} %bitcast.37, s32[]{:T(128)S(6)} %select_n.90), kind=kLoop, calls=%fused_computation.45 | loop fusion | bytes 8388612 | tf_op jit(solution)/shard_map/dynamic_slice | solution.py:198
  42.2 1.4 copy-done.1
  43.6 1.5 fusion.2
  45.0 6.9 %fusion.6 = f32[256,256]{0,1:T(8,128)S(1)} fusion(f32[64,128,256]{2,1,0:T(8,128)S(1)} %copy-done.1, f32[256]{0:T(256)S(1)} %fusion.2), kind=kOutput, calls=%fused_computation.10 | convolution fusion | flops 3221422080 | bytes 8651776 | tf_op jit(solution)/shard_map/dot_general | solution.py:163
  52.0 2.7 %collective-permute-start.3 = (f32[128,384]{0,1:T(8,128)S(1)}, f32[128,384]{0,1:T(8,128)S(1)}, u32[]{:S(2)}, u32[]{:S(2)}) collective-permute-start(f32[128,384]{0,1:T(8,128)S(1)} %pad_maximum_fusion), channel_id=1, source_target_pairs={{0,1},{1,0},{2,3},{3,2},{4,5},{5,4},{6,7},{7,6},{8,9},{9,8},{10,11... | collective-permute-start | bytes 589832 | tf_op jit(solution)/shard_map/ppermute | solution.py:42
  54.7 4.3 %collective-permute-done.3 = f32[128,384]{0,1:T(8,128)S(1)} collective-permute-done((f32[128,384]{0,1:T(8,128)S(1)}, f32[128,384]{0,1:T(8,128)S(1)}, u32[]{:S(2)}, u32[]{:S(2)}) %collective-permute-start.3) | collective-permute-done | bytes 196640 | tf_op jit(solution)/shard_map/ppermute | solution.py:42
  59.0 2.8 %collective-permute-start.4 = (f32[128,384]{0,1:T(8,128)S(1)}, f32[128,384]{0,1:T(8,128)S(1)}, u32[]{:S(2)}, u32[]{:S(2)}) collective-permute-start(f32[128,384]{0,1:T(8,128)S(1)} %fusion.35), channel_id=1, source_target_pairs={{0,2},{1,3},{2,0},{3,1},{4,6},{5,7},{6,4},{7,5},{8,10},{9,11},{10,... | collective-permute-start | bytes 589832 | tf_op jit(solution)/shard_map/ppermute | solution.py:42
  61.8 3.6 %collective-permute-done.4 = f32[128,384]{0,1:T(8,128)S(1)} collective-permute-done((f32[128,384]{0,1:T(8,128)S(1)}, f32[128,384]{0,1:T(8,128)S(1)}, u32[]{:S(2)}, u32[]{:S(2)}) %collective-permute-start.4) | collective-permute-done | bytes 196640 | tf_op jit(solution)/shard_map/ppermute | solution.py:42
  65.5 3.3 %collective-permute-start.5 = (f32[128,384]{0,1:T(8,128)S(1)}, f32[128,384]{0,1:T(8,128)S(1)}, u32[]{:S(2)}, u32[]{:S(2)}) collective-permute-start(f32[128,384]{0,1:T(8,128)S(1)} %add.47), channel_id=1, source_target_pairs={{0,4},{1,5},{2,6},{3,7},{4,0},{5,1},{6,2},{7,3},{8,12},{9,13},{10,... | collective-permute-start | bytes 589832 | tf_op jit(solution)/shard_map/ppermute | solution.py:42
  68.7 0.6 collective-permute-start.2
  69.4 5.7 %collective-permute-done.5 = f32[128,384]{0,1:T(8,128)S(1)} collective-permute-done((f32[128,384]{0,1:T(8,128)S(1)}, f32[128,384]{0,1:T(8,128)S(1)}, u32[]{:S(2)}, u32[]{:S(2)}) %collective-permute-start.5) | collective-permute-done | bytes 196640 | tf_op jit(solution)/shard_map/ppermute | solution.py:42
  75.2 7.1 %fusion.3 = f32[256,256]{1,0:T(8,128)S(1)} fusion(f32[4096,256]{1,0:T(8,128)} %collective-permute-done.6, f32[8192,256]{1,0:T(8,128)} %bitcast.38, s32[]{:T(128)S(6)} %select_n.89), kind=kOutput, calls=%fused_computation.5 | convolution fusion | flops 1610612736 | bytes 8650756 | tf_op jit(solution)/shard_map/dot_general | solution.py:163
  82.4 0.1 copy.9
  82.5 0.7 collective-permute-start.7
  83.3 0.9 fusion.16.rows_ref
  84.2 13.3 %shard_map.48 = f32[128,256]{1,0:T(8,128)} custom-call(f32[128,256]{1,0:T(8,128)} %fusion.16.rows_ref), custom_call_target="tpu_custom_call" | custom-call | tf_op jit(solution)/shard_map/pallas_call | solution.py:148
  97.6 0.7 collective-permute-start.8
  98.3 1.8 %fusion.38.rows_ref = f32[128,256]{1,0:T(8,128)} fusion(f32[256,128]{0,1:T(8,128)} %bitcast.51, f32[256,256]{0,1:T(8,128)S(1)} %maximum_maximum_fusion), kind=kOutput, calls=%fused_computation.54 | convolution fusion | flops 100663296 | bytes 524288 | tf_op jit(solution)/shard_map/dot_general | solution.py:220
  100.2 13.3 %shard_map.49 = f32[128,256]{1,0:T(8,128)} custom-call(f32[128,256]{1,0:T(8,128)} %fusion.38.rows_ref), custom_call_target="tpu_custom_call" | custom-call | tf_op jit(solution)/shard_map/pallas_call | solution.py:148
  113.5 3.4 %collective-permute-start.9 = (f32[256,256]{1,0:T(8,128)S(1)}, f32[256,256]{1,0:T(8,128)S(1)}, u32[]{:S(2)}, u32[]{:S(2)}) collective-permute-start(f32[256,256]{1,0:T(8,128)S(1)} %add.52), channel_id=1, source_target_pairs={{0,4},{1,5},{2,6},{3,7},{4,0},{5,1},{6,2},{7,3},{8,12},{9,13},{10,... | collective-permute-start | bytes 786440 | tf_op jit(solution)/shard_map/ppermute | solution.py:229
  117.0 8.8 %fusion.39 = f32[8192,128]{1,0:T(8,128)} fusion(f32[8192,256]{1,0:T(8,128)} %bitcast.39, f32[256,128]{0,1:T(8,128)} %bitcast.40), kind=kOutput, calls=%fused_computation.55 | convolution fusion | flops 1610612736 | bytes 12713984 | tf_op jit(solution)/shard_map/dot_general | solution.py:230
  125.8 0.6 fusion.40
  126.4 0.1 collective-permute-done.9
  126.6 0.4 collective-permute-start.10
  127.0 0.4 fusion.41
  127.4 0.2 collective-permute-start.11
  127.6 0.6 collective-permute-done.10
  128.2 0.5 collective-permute-done.11
  128.7 0.2 collective-permute-start.13
  128.9 0.4 fusion.7
  129.3 0.3 fusion.13
  129.7 0.9 fusion.10.rows_ref
  130.6 13.3 %shard_map.50 = f32[128,256]{1,0:T(8,128)} custom-call(f32[128,256]{1,0:T(8,128)} %fusion.10.rows_ref), custom_call_target="tpu_custom_call" | custom-call | tf_op jit(solution)/shard_map/pallas_call | solution.py:148
  143.9 1.8 %fusion.9.rows_ref = f32[128,256]{1,0:T(8,128)} fusion(f32[128,256]{1,0:T(8,128)} %shard_map.50, f32[128,128]{0,1:T(8,128)S(1)} %get-tuple-element.38, f32[128,128]{0,1:T(8,128)S(1)} %bitcast.50, f32[128,128]{0,1:T(8,128)S(1)} %copy.10, f32[128,128]{0,1:T(8,128)S(1)} %get-tuple-element.37), kind=kOutput, calls=%fused_computation.19 | convolution fusion | flops 100859904 | bytes 524288 | tf_op jit(solution)/shard_map/dot_general | solution.py:158
  145.8 13.6 %shard_map.51 = f32[128,256]{1,0:T(8,128)} custom-call(f32[128,256]{1,0:T(8,128)} %fusion.9.rows_ref), custom_call_target="tpu_custom_call" | custom-call | tf_op jit(solution)/shard_map/pallas_call | solution.py:148
  159.3 0.8 dynamic-slice_bitcast_fusion
  160.2 4.5 %fusion.22 = f32[8192,64]{0,1:T(8,128)S(1)} fusion(f32[8192,128]{1,0:T(8,128)} %collective-permute-done.13, f32[256,64]{0,1:T(8,128)S(1)} %dynamic-slice_bitcast_fusion, pred[]{:T(512)S(6)} %eq.14), kind=kOutput, calls=%fused_computation.34 | convolution fusion | flops 402661376 | bytes 6356993 | tf_op jit(solution)/shard_map/dot_general | solution.py:266
  164.7 4.5 %fusion.5 = f32[8,64,8,128]{3,2,1,0:T(8,128)S(1)} fusion(f32[8192,64]{0,1:T(8,128)S(1)} %fusion.22, f32[8192,128]{1,0:T(8,128)} %fusion.39, f32[256,64]{0,1:T(8,128)S(1)} %dynamic-slice_bitcast_fusion, pred[]{:T(512)S(6)} %eq.14), kind=kOutput, calls=%fused_computation.8 | convolution fusion | flops 403185664 | bytes 8454145 | tf_op jit(solution)/shard_map/dot_general | solution.py:266
  169.2 1.6 copy.17
  (38 shorter events, 0.7 us)
Async XLA Ops:
  0.0 7.2 %copy-start = (s32[512,128]{1,0:T(8,128)S(1)}, s32[512,128]{1,0:T(8,128)}, u32[]{:S(2)}) copy-start(s32[512,128]{1,0:T(8,128)} %param.6) | copy-start | bytes 786436
  1.0 21.3 %collective-permute-start = (bf16[2,128,256]{2,1,0:T(8,128)(2,1)S(1)}, bf16[2,128,256]{2,1,0:T(8,128)(2,1)S(1)}, u32[]{:S(2)}, u32[]{:S(2)}) collective-permute-start(bf16[2,128,256]{2,1,0:T(8,128)(2,1)S(1)} %get-tuple-element.34), channel_id=1, source_target_pairs={{0,1},{1,2},{2,3},{3,4},{4,5},{5,6},{6,7},{8,9},{9,10},{10,11},{11... | collective-permute-start | bytes 393224 | tf_op jit(solution)/shard_map/ppermute | solution.py:20
  5.9 16.5 %collective-permute-start.1 = (bf16[2,128,256]{2,1,0:T(8,128)(2,1)S(1)}, bf16[2,128,256]{2,1,0:T(8,128)(2,1)S(1)}, u32[]{:S(2)}, u32[]{:S(2)}) collective-permute-start(bf16[2,128,256]{2,1,0:T(8,128)(2,1)S(1)} %get-tuple-element.33), channel_id=1, source_target_pairs={{1,0},{2,1},{3,2},{4,3},{5,4},{6,5},{7,6},{9,8},{10,9},{11,10},{12... | collective-permute-start | bytes 393224 | tf_op jit(solution)/shard_map/ppermute | solution.py:21
  22.4 0.7 copy-start.4
  23.0 0.7 copy-start.5
  37.4 6.2 %copy-start.1 = (f32[64,128,256]{2,1,0:T(8,128)S(1)}, f32[64,128,256]{2,1,0:T(8,128)}, u32[]{:S(2)}) copy-start(f32[64,128,256]{2,1,0:T(8,128)} %shard_map.47) | copy-start | bytes 25165828
  42.2 33.1 %collective-permute-start.6 = (f32[4096,256]{1,0:T(8,128)}, f32[4096,256]{1,0:T(8,128)}, u32[]{:S(2)}, u32[]{:S(2)}) collective-permute-start(f32[4096,256]{1,0:T(8,128)} %constant_dynamic-slice_fusion), channel_id=1, source_target_pairs={{0,8},{8,0},{1,9},{9,1},{2,10},{10,2},{3,11},{11,3},{4,12},{12,4},... | collective-permute-start | bytes 12582920 | tf_op jit(solution)/shard_map/ppermute | solution.py:32
  45.0 23.7 %copy-start.3 = (f32[128,256]{1,0:T(8,128)S(1)}, f32[128,256]{1,0:T(8,128)}, u32[]{:S(2)}) copy-start(f32[128,256]{1,0:T(8,128)} %shard_map.46) | copy-start | bytes 393220
  52.0 7.0 %collective-permute-start.3 = (f32[128,384]{0,1:T(8,128)S(1)}, f32[128,384]{0,1:T(8,128)S(1)}, u32[]{:S(2)}, u32[]{:S(2)}) collective-permute-start(f32[128,384]{0,1:T(8,128)S(1)} %pad_maximum_fusion), channel_id=1, source_target_pairs={{0,1},{1,0},{2,3},{3,2},{4,5},{5,4},{6,7},{7,6},{8,9},{9,8},{10,11... | collective-permute-start | bytes 589832 | tf_op jit(solution)/shard_map/ppermute | solution.py:42
  59.0 6.4 %collective-permute-start.4 = (f32[128,384]{0,1:T(8,128)S(1)}, f32[128,384]{0,1:T(8,128)S(1)}, u32[]{:S(2)}, u32[]{:S(2)}) collective-permute-start(f32[128,384]{0,1:T(8,128)S(1)} %fusion.35), channel_id=1, source_target_pairs={{0,2},{1,3},{2,0},{3,1},{4,6},{5,7},{6,4},{7,5},{8,10},{9,11},{10,... | collective-permute-start | bytes 589832 | tf_op jit(solution)/shard_map/ppermute | solution.py:42
  65.5 9.6 %collective-permute-start.5 = (f32[128,384]{0,1:T(8,128)S(1)}, f32[128,384]{0,1:T(8,128)S(1)}, u32[]{:S(2)}, u32[]{:S(2)}) collective-permute-start(f32[128,384]{0,1:T(8,128)S(1)} %add.47), channel_id=1, source_target_pairs={{0,4},{1,5},{2,6},{3,7},{4,0},{5,1},{6,2},{7,3},{8,12},{9,13},{10,... | collective-permute-start | bytes 589832 | tf_op jit(solution)/shard_map/ppermute | solution.py:42
  68.7 14.6 %collective-permute-start.2 = (f32[256,128]{0,1:T(8,128)S(1)}, f32[256,128]{0,1:T(8,128)S(1)}, u32[]{:S(2)}, u32[]{:S(2)}) collective-permute-start(f32[256,128]{0,1:T(8,128)S(1)} %bitcast.46), channel_id=1, source_target_pairs={{0,1},{1,0},{2,3},{3,2},{4,5},{5,4},{6,7},{7,6},{8,9},{9,8},{10,11... | collective-permute-start | bytes 393224 | tf_op jit(solution)/shard_map/ppermute | solution.py:32
  82.5 15.0 %collective-permute-start.7 = (f32[256,256]{1,0:T(8,128)S(1)}, f32[256,256]{1,0:T(8,128)S(1)}, u32[]{:S(2)}, u32[]{:S(2)}) collective-permute-start(f32[256,256]{1,0:T(8,128)S(1)} %bitcast_select_fusion), channel_id=1, source_target_pairs={{0,1},{1,0},{2,3},{3,2},{4,5},{5,4},{6,7},{7,6},{8,9},{9,8},{10,11... | collective-permute-start | bytes 786440 | tf_op jit(solution)/shard_map/ppermute | solution.py:222
  97.6 15.9 %collective-permute-start.8 = (f32[256,256]{1,0:T(8,128)S(1)}, f32[256,256]{1,0:T(8,128)S(1)}, u32[]{:S(2)}, u32[]{:S(2)}) collective-permute-start(f32[256,256]{1,0:T(8,128)S(1)} %add.51), channel_id=1, source_target_pairs={{0,2},{1,3},{2,0},{3,1},{4,6},{5,7},{6,4},{7,5},{8,10},{9,11},{10,... | collective-permute-start | bytes 786440 | tf_op jit(solution)/shard_map/ppermute | solution.py:222
  113.5 12.2 %copy-start.2 = (f32[128,256]{1,0:T(8,128)S(1)}, f32[128,256]{1,0:T(8,128)}, u32[]{:S(2)}) copy-start(f32[128,256]{1,0:T(8,128)} %shard_map.49) | copy-start | bytes 393220
  113.5 13.0 %collective-permute-start.9 = (f32[256,256]{1,0:T(8,128)S(1)}, f32[256,256]{1,0:T(8,128)S(1)}, u32[]{:S(2)}, u32[]{:S(2)}) collective-permute-start(f32[256,256]{1,0:T(8,128)S(1)} %add.52), channel_id=1, source_target_pairs={{0,4},{1,5},{2,6},{3,7},{4,0},{5,1},{6,2},{7,3},{8,12},{9,13},{10,... | collective-permute-start | bytes 786440 | tf_op jit(solution)/shard_map/ppermute | solution.py:229
  125.8 2.9 %collective-permute-start.12 = (f32[256,128]{0,1:T(8,128)S(1)}, f32[256,128]{0,1:T(8,128)S(1)}, u32[]{:S(2)}, u32[]{:S(2)}) collective-permute-start(f32[256,128]{0,1:T(8,128)S(1)} %bitcast.41), channel_id=1, source_target_pairs={{0,8},{8,0},{1,9},{9,1},{2,10},{10,2},{3,11},{11,3},{4,12},{12,4},... | collective-permute-start | bytes 393224 | tf_op jit(solution)/shard_map/ppermute | solution.py:32
  126.6 1.6 collective-permute-start.10
  127.4 1.3 collective-permute-start.11
  128.7 31.4 %collective-permute-start.13 = (f32[8192,128]{1,0:T(8,128)}, f32[8192,128]{1,0:T(8,128)}, u32[]{:S(2)}, u32[]{:S(2)}) collective-permute-start(f32[8192,128]{1,0:T(8,128)} %fusion.39), channel_id=1, source_target_pairs={{0,8},{8,0},{1,9},{9,1},{2,10},{10,2},{3,11},{11,3},{4,12},{12,4},... | collective-permute-start | bytes 12582920 | tf_op jit(solution)/shard_map/ppermute | solution.py:32

commit v11 on v8

--- a/solution.py
+++ b/solution.py
@@ -262,10 +262,11 @@
     bottom_rows = rotation_share[modes_count:]
     own_rotation = jnp.where(is_first, top_rows, bottom_rows)
     other_rotation = jnp.where(is_first, bottom_rows, top_rows)
-    result = jnp.dot(own_modes, own_rotation, precision=high) + jnp.dot(
-        other_modes, other_rotation, precision=high
-    )
-    return result.reshape(snapshots.shape[0], snapshots.shape[1], share_count)
+    grid_shape = (snapshots.shape[0], snapshots.shape[1], modes_count)
+    result = jnp.einsum(
+        "xyk,km->xym", own_modes.reshape(grid_shape), own_rotation, precision=high
+    ) + jnp.einsum("xyk,km->xym", other_modes.reshape(grid_shape), other_rotation, precision=high)
+    return result
 
 
 def solution(mesh):

time: 167 us -> 167 us (level)
  no operation moved by 1% of the time
where the time goes in v11:
time: 167 us; the launch traced here: 166 us
  Pallas kernels  80.5 us (48%)
  matrix products  40.1 us (24%)
  starting transfers between devices  18.1 us (11%)
  waiting for transfers between devices  15.4 us (9%)
  local copies, waits for them, and re-layouts  9.24 us (6%)
  other arithmetic  2.41 us (1%)
    pallas_call x5, Pallas kernels, orthonormal(): pl.pallas_call(gram_schmidt_kernel, out_shape=jax.ShapeDtypeStruct(rows.s...  66.8 us
    dot_general x2, matrix products, cross_gram(): lax.dot_general(left_rows, right_rows, (((0,), (0,)), ((), ())), precisio...  13.8 us
    pallas_call x1, Pallas kernels, fluxes(): pl.pallas_call(functools.partial(flux_kernel, count), grid=(count,), in_s...  13.7 us
    dot_general x1, matrix products, on_device(): own_modes = jnp.dot(own_flux, own_basis, precision=high)  8.78 us
    ppermute x3, waiting for transfers between devices, tree_sum(): value = value + lax.ppermute(value, axis, route)  8.05 us
    ppermute x3, starting transfers between devices, tree_sum(): value = value + lax.ppermute(value, axis, route)  6.96 us
    dot_general x1, matrix products, on_device(): jnp.einsum('xyk,km->xym', own_modes.reshape(grid_shape), own_rotation, pr...  5.88 us
    ppermute x1, starting transfers between devices, halos(): lax.ppermute(lax.slice_in_dim(block, block.shape[0] - width, None, axis=0...  4.88 us
  transfers between devices with their start and end apart: 14, of which 7 were waited for; matrix products, arithmetic and copies ran while one was open for 20% of the time, Pallas kernels for 40%

profile of v11, /device:TPU:0, one launch (start us, length us, event | category | flops | bytes accessed | tf_op | source)
XLA Modules:
  0.0 166.0 jit_solution(15239350998748317644)
XLA Ops:
  0.0 1.0 fusion.39
  1.0 4.9 %collective-permute-start = (bf16[2,128,256]{2,1,0:T(8,128)(2,1)S(1)}, bf16[2,128,256]{2,1,0:T(8,128)(2,1)S(1)}, u32[]{:S(2)}, u32[]{:S(2)}) collective-permute-start(bf16[2,128,256]{2,1,0:T(8,128)(2,1)S(1)} %get-tuple-element.30), channel_id=1, source_target_pairs={{0,1},{1,2},{2,3},{3,4},{4,5},{5,6},{6,7},{8,9},{9,10},{10,11},{11... | collective-permute-start | bytes 393224 | tf_op jit(solution)/shard_map/ppermute | solution.py:20
  5.9 1.3 collective-permute-start.1
  7.2 1.4 collective-permute-done.low_ref
  8.7 4.1 %collective-permute-done.1.high_ref = bf16[2,128,256]{2,1,0:T(8,128)(2,1)S(1)} collective-permute-done((bf16[2,128,256]{2,1,0:T(8,128)(2,1)S(1)}, bf16[2,128,256]{2,1,0:T(8,128)(2,1)S(1)}, u32[]{:S(2)}, u32[]{:S(2)}) %collective-permute-start.1) | collective-permute-done | bytes 131104 | tf_op jit(solution)/shard_map/ppermute | solution.py:21
  12.8 0.7 copy-done.6
  13.4 13.7 %shard_map.46 = f32[64,128,256]{2,1,0:T(8,128)} custom-call(bf16[2,128,256]{2,1,0:T(8,128)(2,1)} %copy-done.5, bf16[2,128,256]{2,1,0:T(8,128)(2,1)} %copy-done.6, bf16[64,128,256]{2,1,0:T(8,128)(2,1)} %next_ref.1, bf16[64,128,256]{2,1,0:T(8,128)(2,1)} %next_ref.1, bf16[64,128,256]{2,1,0:T(8,128)(2,1)} %next_ref.1, f32[64,128]{1,0:T(8,128)} %coef_ref.1), custom_call_target="tpu_custom_call" | custom-call | tf_op jit(solution)/shard_map/pallas_call | solution.py:96
  27.2 4.8 %constant_dynamic-slice_fusion = f32[4096,256]{1,0:T(8,128)} fusion(f32[8192,256]{1,0:T(8,128)} %bitcast.48, s32[]{:T(128)S(6)} %select_n.90), kind=kLoop, calls=%fused_computation.45 | loop fusion | bytes 8388612 | tf_op jit(solution)/shard_map/dynamic_slice | solution.py:197
  31.9 1.4 copy-done.1
  33.3 1.5 fusion.2
  34.8 6.9 %fusion.5 = f32[256,256]{0,1:T(8,128)S(1)} fusion(f32[64,128,256]{2,1,0:T(8,128)S(1)} %copy-done.1, f32[256]{0:T(256)S(1)} %fusion.2), kind=kOutput, calls=%fused_computation.8 | convolution fusion | flops 3221422080 | bytes 8651776 | tf_op jit(solution)/shard_map/dot_general | solution.py:163
  41.7 2.5 %collective-permute-start.3 = (f32[128,384]{0,1:T(8,128)S(1)}, f32[128,384]{0,1:T(8,128)S(1)}, u32[]{:S(2)}, u32[]{:S(2)}) collective-permute-start(f32[128,384]{0,1:T(8,128)S(1)} %pad_maximum_fusion), channel_id=1, source_target_pairs={{0,1},{1,0},{2,3},{3,2},{4,5},{5,4},{6,7},{7,6},{8,9},{9,8},{10,11... | collective-permute-start | bytes 589832 | tf_op jit(solution)/shard_map/ppermute | solution.py:42
  44.2 4.2 %collective-permute-done.3 = f32[128,384]{0,1:T(8,128)S(1)} collective-permute-done((f32[128,384]{0,1:T(8,128)S(1)}, f32[128,384]{0,1:T(8,128)S(1)}, u32[]{:S(2)}, u32[]{:S(2)}) %collective-permute-start.3) | collective-permute-done | bytes 196640 | tf_op jit(solution)/shard_map/ppermute | solution.py:42
  48.4 1.6 collective-permute-start.4
  50.1 0.1 copy.12
  50.2 0.1 copy.6
  50.3 3.9 %collective-permute-done.4 = f32[128,384]{0,1:T(8,128)S(1)} collective-permute-done((f32[128,384]{0,1:T(8,128)S(1)}, f32[128,384]{0,1:T(8,128)S(1)}, u32[]{:S(2)}, u32[]{:S(2)}) %collective-permute-start.4) | collective-permute-done | bytes 196640 | tf_op jit(solution)/shard_map/ppermute | solution.py:42
  54.2 2.8 %collective-permute-start.5 = (f32[128,384]{0,1:T(8,128)S(1)}, f32[128,384]{0,1:T(8,128)S(1)}, u32[]{:S(2)}, u32[]{:S(2)}) collective-permute-start(f32[128,384]{0,1:T(8,128)S(1)} %add.47), channel_id=1, source_target_pairs={{0,4},{1,5},{2,6},{3,7},{4,0},{5,1},{6,2},{7,3},{8,12},{9,13},{10,... | collective-permute-start | bytes 589832 | tf_op jit(solution)/shard_map/ppermute | solution.py:42
  57.0 0.7 select_bitcast_fusion.rows_ref
  57.7 13.5 %shard_map.47 = f32[128,256]{1,0:T(8,128)} custom-call(f32[128,256]{1,0:T(8,128)} %select_bitcast_fusion.rows_ref), custom_call_target="tpu_custom_call" | custom-call | tf_op jit(solution)/shard_map/pallas_call | solution.py:148
  71.2 1.9 %collective-permute-start.2 = (f32[256,128]{0,1:T(8,128)}, f32[256,128]{0,1:T(8,128)S(1)}, u32[]{:S(2)}, u32[]{:S(2)}) collective-permute-start(f32[256,128]{0,1:T(8,128)} %bitcast.57), channel_id=1, source_target_pairs={{0,1},{1,0},{2,3},{3,2},{4,5},{5,4},{6,7},{7,6},{8,9},{9,8},{10,11... | collective-permute-start | bytes 393224 | tf_op jit(solution)/shard_map/ppermute | solution.py:32
  73.1 0.1 copy.13
  73.2 6.9 %fusion.3 = f32[256,256]{1,0:T(8,128)S(1)} fusion(f32[4096,256]{1,0:T(8,128)} %collective-permute-done.6, f32[8192,256]{1,0:T(8,128)} %bitcast.49, s32[]{:T(128)S(6)} %select_n.89), kind=kOutput, calls=%fused_computation.4 | convolution fusion | flops 1610612736 | bytes 8650756 | tf_op jit(solution)/shard_map/dot_general | solution.py:163
  80.2 0.1 copy.9
  80.3 0.2 collective-permute-start.7
  80.6 0.9 fusion.15.rows_ref
  81.5 13.3 %shard_map.48 = f32[128,256]{1,0:T(8,128)} custom-call(f32[128,256]{1,0:T(8,128)} %fusion.15.rows_ref), custom_call_target="tpu_custom_call" | custom-call | tf_op jit(solution)/shard_map/pallas_call | solution.py:148
  94.9 1.4 collective-permute-start.8
  96.3 1.8 %fusion.41.rows_ref = f32[128,256]{1,0:T(8,128)} fusion(f32[256,128]{0,1:T(8,128)} %bitcast.60, f32[256,256]{0,1:T(8,128)S(1)} %maximum_maximum_fusion), kind=kOutput, calls=%fused_computation.56 | convolution fusion | flops 100663296 | bytes 524288 | tf_op jit(solution)/shard_map/dot_general | solution.py:219
  98.1 13.3 %shard_map.49 = f32[128,256]{1,0:T(8,128)} custom-call(f32[128,256]{1,0:T(8,128)} %fusion.41.rows_ref), custom_call_target="tpu_custom_call" | custom-call | tf_op jit(solution)/shard_map/pallas_call | solution.py:148
  111.5 0.5 collective-permute-start.9
  112.0 8.8 %fusion.42 = f32[8192,128]{1,0:T(8,128)} fusion(f32[8192,256]{1,0:T(8,128)} %bitcast.50, f32[256,128]{0,1:T(8,128)} %bitcast.51), kind=kOutput, calls=%fused_computation.57 | convolution fusion | flops 1610612736 | bytes 12713984 | tf_op jit(solution)/shard_map/dot_general | solution.py:229
  120.7 0.6 fusion.43
  121.3 0.9 collective-permute-done.9
  122.4 0.4 fusion.44
  122.8 0.6 collective-permute-start.11
  123.4 0.6 collective-permute-done.10
  124.0 0.3 collective-permute-done.11
  124.3 0.4 collective-permute-start.13
  124.6 0.4 fusion.6
  125.0 0.3 fusion.12
  125.4 0.9 fusion.9.rows_ref
  126.3 13.3 %shard_map.50 = f32[128,256]{1,0:T(8,128)} custom-call(f32[128,256]{1,0:T(8,128)} %fusion.9.rows_ref), custom_call_target="tpu_custom_call" | custom-call | tf_op jit(solution)/shard_map/pallas_call | solution.py:148
  139.6 1.8 %fusion.8.rows_ref = f32[128,256]{1,0:T(8,128)} fusion(f32[128,256]{1,0:T(8,128)} %shard_map.50, f32[128,128]{0,1:T(8,128)S(1)} %get-tuple-element.34, f32[128,128]{0,1:T(8,128)S(1)} %bitcast.59, f32[128,128]{0,1:T(8,128)S(1)} %copy.10, f32[128,128]{0,1:T(8,128)S(1)} %get-tuple-element.33), kind=kOutput, calls=%fused_computation.17 | convolution fusion | flops 100859904 | bytes 524288 | tf_op jit(solution)/shard_map/dot_general | solution.py:158
  141.5 13.3 %shard_map.51 = f32[128,256]{1,0:T(8,128)} custom-call(f32[128,256]{1,0:T(8,128)} %fusion.8.rows_ref), custom_call_target="tpu_custom_call" | custom-call | tf_op jit(solution)/shard_map/pallas_call | solution.py:148
  154.8 0.8 dynamic-slice_bitcast_fusion
  155.7 4.5 %fusion.21 = f32[64,128,64]{1,2,0:T(8,128)S(1)} fusion(f32[64,128,128]{2,1,0:T(8,128)} %bitcast.12, f32[256,64]{0,1:T(8,128)S(1)} %dynamic-slice_bitcast_fusion, pred[]{:T(512)S(6)} %eq.14), kind=kOutput, calls=%fused_computation.32 | convolution fusion | flops 402661376 | bytes 6356993 | tf_op jit(solution)/shard_map/xyk,km->xym/dot_general | solution.py:268
  160.2 5.9 %convolution_add_fusion = f32[64,128,64]{1,2,0:T(8,128)} fusion(f32[64,128,64]{1,2,0:T(8,128)S(1)} %fusion.21, f32[64,128,128]{2,1,0:T(8,128)} %bitcast.8, f32[256,64]{0,1:T(8,128)S(1)} %dynamic-slice_bitcast_fusion, pred[]{:T(512)S(6)} %eq.14), kind=kOutput, calls=%fused_computation.6 | convolution fusion | flops 403185664 | bytes 8454145 | tf_op jit(solution)/shard_map/xyk,km->xym/dot_general | solution.py:266
  (39 shorter events, 0.5 us)
Async XLA Ops:
  0.0 50.1 %copy-start = (s32[512,128]{1,0:T(8,128)S(1)}, s32[512,128]{1,0:T(8,128)}, u32[]{:S(2)}) copy-start(s32[512,128]{1,0:T(8,128)} %param.6) | copy-start | bytes 786436
  1.0 7.6 %collective-permute-start = (bf16[2,128,256]{2,1,0:T(8,128)(2,1)S(1)}, bf16[2,128,256]{2,1,0:T(8,128)(2,1)S(1)}, u32[]{:S(2)}, u32[]{:S(2)}) collective-permute-start(bf16[2,128,256]{2,1,0:T(8,128)(2,1)S(1)} %get-tuple-element.30), channel_id=1, source_target_pairs={{0,1},{1,2},{2,3},{3,4},{4,5},{5,6},{6,7},{8,9},{9,10},{10,11},{11... | collective-permute-start | bytes 393224 | tf_op jit(solution)/shard_map/ppermute | solution.py:20
  5.9 6.9 %collective-permute-start.1 = (bf16[2,128,256]{2,1,0:T(8,128)(2,1)S(1)}, bf16[2,128,256]{2,1,0:T(8,128)(2,1)S(1)}, u32[]{:S(2)}, u32[]{:S(2)}) collective-permute-start(bf16[2,128,256]{2,1,0:T(8,128)(2,1)S(1)} %get-tuple-element.29), channel_id=1, source_target_pairs={{1,0},{2,1},{3,2},{4,3},{5,4},{6,5},{7,6},{9,8},{10,9},{11,10},{12... | collective-permute-start | bytes 393224 | tf_op jit(solution)/shard_map/ppermute | solution.py:21
  8.7 4.1 %copy-start.5 = (bf16[2,128,256]{2,1,0:T(8,128)(2,1)}, bf16[2,128,256]{2,1,0:T(8,128)(2,1)S(1)}, u32[]{:S(2)}) copy-start(bf16[2,128,256]{2,1,0:T(8,128)(2,1)S(1)} %collective-permute-done.low_ref) | copy-start | bytes 393220
  12.8 0.7 copy-start.6
  27.2 6.2 %copy-start.1 = (f32[64,128,256]{2,1,0:T(8,128)S(1)}, f32[64,128,256]{2,1,0:T(8,128)}, u32[]{:S(2)}) copy-start(f32[64,128,256]{2,1,0:T(8,128)} %shard_map.46) | copy-start | bytes 25165828
  31.9 41.3 %collective-permute-start.6 = (f32[4096,256]{1,0:T(8,128)}, f32[4096,256]{1,0:T(8,128)}, u32[]{:S(2)}, u32[]{:S(2)}) collective-permute-start(f32[4096,256]{1,0:T(8,128)} %constant_dynamic-slice_fusion), channel_id=1, source_target_pairs={{0,8},{8,0},{1,9},{9,1},{2,10},{10,2},{3,11},{11,3},{4,12},{12,4},... | collective-permute-start | bytes 12582920 | tf_op jit(solution)/shard_map/ppermute | solution.py:32
  34.8 15.4 %copy-start.4 = (s32[256,128]{1,0:T(8,128)S(1)}, s32[256,128]{1,0:T(8,128)}, u32[]{:S(2)}) copy-start(s32[256,128]{1,0:T(8,128)} %param.7) | copy-start | bytes 393220
  41.7 6.7 %collective-permute-start.3 = (f32[128,384]{0,1:T(8,128)S(1)}, f32[128,384]{0,1:T(8,128)S(1)}, u32[]{:S(2)}, u32[]{:S(2)}) collective-permute-start(f32[128,384]{0,1:T(8,128)S(1)} %pad_maximum_fusion), channel_id=1, source_target_pairs={{0,1},{1,0},{2,3},{3,2},{4,5},{5,4},{6,7},{7,6},{8,9},{9,8},{10,11... | collective-permute-start | bytes 589832 | tf_op jit(solution)/shard_map/ppermute | solution.py:42
  48.4 5.7 %collective-permute-start.4 = (f32[128,384]{0,1:T(8,128)S(1)}, f32[128,384]{0,1:T(8,128)S(1)}, u32[]{:S(2)}, u32[]{:S(2)}) collective-permute-start(f32[128,384]{0,1:T(8,128)S(1)} %fusion.38), channel_id=1, source_target_pairs={{0,2},{1,3},{2,0},{3,1},{4,6},{5,7},{6,4},{7,5},{8,10},{9,11},{10,... | collective-permute-start | bytes 589832 | tf_op jit(solution)/shard_map/ppermute | solution.py:42
  54.2 18.9 %collective-permute-start.5 = (f32[128,384]{0,1:T(8,128)S(1)}, f32[128,384]{0,1:T(8,128)S(1)}, u32[]{:S(2)}, u32[]{:S(2)}) collective-permute-start(f32[128,384]{0,1:T(8,128)S(1)} %add.47), channel_id=1, source_target_pairs={{0,4},{1,5},{2,6},{3,7},{4,0},{5,1},{6,2},{7,3},{8,12},{9,13},{10,... | collective-permute-start | bytes 589832 | tf_op jit(solution)/shard_map/ppermute | solution.py:42
  71.2 9.4 %collective-permute-start.2 = (f32[256,128]{0,1:T(8,128)}, f32[256,128]{0,1:T(8,128)S(1)}, u32[]{:S(2)}, u32[]{:S(2)}) collective-permute-start(f32[256,128]{0,1:T(8,128)} %bitcast.57), channel_id=1, source_target_pairs={{0,1},{1,0},{2,3},{3,2},{4,5},{5,4},{6,7},{7,6},{8,9},{9,8},{10,11... | collective-permute-start | bytes 393224 | tf_op jit(solution)/shard_map/ppermute | solution.py:32
  73.2 7.3 %copy-start.3 = (f32[128,256]{1,0:T(8,128)S(1)}, f32[128,256]{1,0:T(8,128)}, u32[]{:S(2)}) copy-start(f32[128,256]{1,0:T(8,128)} %shard_map.47) | copy-start | bytes 393220
  80.3 14.5 %collective-permute-start.7 = (f32[256,256]{1,0:T(8,128)S(1)}, f32[256,256]{1,0:T(8,128)S(1)}, u32[]{:S(2)}, u32[]{:S(2)}) collective-permute-start(f32[256,256]{1,0:T(8,128)S(1)} %bitcast_select_fusion), channel_id=1, source_target_pairs={{0,1},{1,0},{2,3},{3,2},{4,5},{5,4},{6,7},{7,6},{8,9},{9,8},{10,11... | collective-permute-start | bytes 786440 | tf_op jit(solution)/shard_map/ppermute | solution.py:221
  94.9 16.6 %collective-permute-start.8 = (f32[256,256]{1,0:T(8,128)S(1)}, f32[256,256]{1,0:T(8,128)S(1)}, u32[]{:S(2)}, u32[]{:S(2)}) collective-permute-start(f32[256,256]{1,0:T(8,128)S(1)} %add.51), channel_id=1, source_target_pairs={{0,2},{1,3},{2,0},{3,1},{4,6},{5,7},{6,4},{7,5},{8,10},{9,11},{10,... | collective-permute-start | bytes 786440 | tf_op jit(solution)/shard_map/ppermute | solution.py:221
  111.5 9.3 %copy-start.2 = (f32[128,256]{1,0:T(8,128)S(1)}, f32[128,256]{1,0:T(8,128)}, u32[]{:S(2)}) copy-start(f32[128,256]{1,0:T(8,128)} %shard_map.49) | copy-start | bytes 393220
  111.5 10.8 %collective-permute-start.9 = (f32[256,256]{1,0:T(8,128)S(1)}, f32[256,256]{1,0:T(8,128)S(1)}, u32[]{:S(2)}, u32[]{:S(2)}) collective-permute-start(f32[256,256]{1,0:T(8,128)S(1)} %add.52), channel_id=1, source_target_pairs={{0,4},{1,5},{2,6},{3,7},{4,0},{5,1},{6,2},{7,3},{8,12},{9,13},{10,... | collective-permute-start | bytes 786440 | tf_op jit(solution)/shard_map/ppermute | solution.py:228
  120.7 3.5 %collective-permute-start.12 = (f32[256,128]{0,1:T(8,128)S(1)}, f32[256,128]{0,1:T(8,128)S(1)}, u32[]{:S(2)}, u32[]{:S(2)}) collective-permute-start(f32[256,128]{0,1:T(8,128)S(1)} %bitcast.52), channel_id=1, source_target_pairs={{0,8},{8,0},{1,9},{9,1},{2,10},{10,2},{3,11},{11,3},{4,12},{12,4},... | collective-permute-start | bytes 393224 | tf_op jit(solution)/shard_map/ppermute | solution.py:32
  122.3 1.6 collective-permute-start.10
  122.8 1.5 collective-permute-start.11
  124.3 31.4 %collective-permute-start.13 = (f32[8192,128]{1,0:T(8,128)}, f32[8192,128]{1,0:T(8,128)}, u32[]{:S(2)}, u32[]{:S(2)}) collective-permute-start(f32[8192,128]{1,0:T(8,128)} %fusion.42), channel_id=1, source_target_pairs={{0,8},{8,0},{1,9},{9,1},{2,10},{10,2},{3,11},{11,3},{4,12},{12,4},... | collective-permute-start | bytes 12582920 | tf_op jit(solution)/shard_map/ppermute | solution.py:32

commit v12 on v11

--- a/solution.py
+++ b/solution.py
@@ -155,7 +155,7 @@
 
 def iterate(gram_matrix, basis_set):
     for sweep_index in range(ITERS):
-        basis_set = orthonormal(jnp.dot(gram_matrix, basis_set, precision=highest))
+        basis_set = orthonormal(jnp.dot(gram_matrix, basis_set, precision=high))
     return basis_set
 
 
@@ -216,7 +216,7 @@
     hops = butterfly_steps("tx")
     own_basis = first_basis
     for sweep_index in range(ITERS):
-        product = jnp.dot(own_gram, own_basis, precision=highest)
+        product = jnp.dot(own_gram, own_basis, precision=high)
         if hops:
             received = lax.ppermute(mixed_sum, "tx", hops.pop(0))
             own_basis = orthonormal(product)

time: 167 us -> 167 us (level)
  no operation moved by 1% of the time
where the time goes in v12:
time: 167 us; the launch traced here: 166 us
  Pallas kernels  80.7 us (48%)
  matrix products  39.9 us (24%)
  starting transfers between devices  18.1 us (11%)
  waiting for transfers between devices  15.4 us (9%)
  local copies, waits for them, and re-layouts  9.24 us (6%)
  other arithmetic  2.41 us (1%)
    pallas_call x5, Pallas kernels, orthonormal(): pl.pallas_call(gram_schmidt_kernel, out_shape=jax.ShapeDtypeStruct(rows.s...  67 us
    dot_general x2, matrix products, cross_gram(): lax.dot_general(left_rows, right_rows, (((0,), (0,)), ((), ())), precisio...  13.8 us
    pallas_call x1, Pallas kernels, fluxes(): pl.pallas_call(functools.partial(flux_kernel, count), grid=(count,), in_s...  13.7 us
    dot_general x1, matrix products, on_device(): own_modes = jnp.dot(own_flux, own_basis, precision=high)  8.78 us
    ppermute x3, waiting for transfers between devices, tree_sum(): value = value + lax.ppermute(value, axis, route)  8.05 us
    ppermute x3, starting transfers between devices, tree_sum(): value = value + lax.ppermute(value, axis, route)  6.96 us
    dot_general x1, matrix products, on_device(): jnp.einsum('xyk,km->xym', own_modes.reshape(grid_shape), own_rotation, pr...  5.87 us
    ppermute x1, starting transfers between devices, halos(): lax.ppermute(lax.slice_in_dim(block, block.shape[0] - width, None, axis=0...  4.88 us
  transfers between devices with their start and end apart: 14, of which 7 were waited for; matrix products, arithmetic and copies ran while one was open for 20% of the time, Pallas kernels for 40%

profile of v12, /device:TPU:0, one launch (start us, length us, event | category | flops | bytes accessed | tf_op | source)
XLA Modules:
  0.0 166.1 jit_solution(647720036834801848)
XLA Ops:
  0.0 1.0 fusion.39
  1.0 4.9 %collective-permute-start = (bf16[2,128,256]{2,1,0:T(8,128)(2,1)S(1)}, bf16[2,128,256]{2,1,0:T(8,128)(2,1)S(1)}, u32[]{:S(2)}, u32[]{:S(2)}) collective-permute-start(bf16[2,128,256]{2,1,0:T(8,128)(2,1)S(1)} %get-tuple-element.30), channel_id=1, source_target_pairs={{0,1},{1,2},{2,3},{3,4},{4,5},{5,6},{6,7},{8,9},{9,10},{10,11},{11... | collective-permute-start | bytes 393224 | tf_op jit(solution)/shard_map/ppermute | solution.py:20
  5.9 1.3 collective-permute-start.1
  7.2 1.4 collective-permute-done.low_ref
  8.7 4.1 %collective-permute-done.1.high_ref = bf16[2,128,256]{2,1,0:T(8,128)(2,1)S(1)} collective-permute-done((bf16[2,128,256]{2,1,0:T(8,128)(2,1)S(1)}, bf16[2,128,256]{2,1,0:T(8,128)(2,1)S(1)}, u32[]{:S(2)}, u32[]{:S(2)}) %collective-permute-start.1) | collective-permute-done | bytes 131104 | tf_op jit(solution)/shard_map/ppermute | solution.py:21
  12.8 0.7 copy-done.6
  13.4 13.7 %shard_map.46 = f32[64,128,256]{2,1,0:T(8,128)} custom-call(bf16[2,128,256]{2,1,0:T(8,128)(2,1)} %copy-done.5, bf16[2,128,256]{2,1,0:T(8,128)(2,1)} %copy-done.6, bf16[64,128,256]{2,1,0:T(8,128)(2,1)} %next_ref.1, bf16[64,128,256]{2,1,0:T(8,128)(2,1)} %next_ref.1, bf16[64,128,256]{2,1,0:T(8,128)(2,1)} %next_ref.1, f32[64,128]{1,0:T(8,128)} %coef_ref.1), custom_call_target="tpu_custom_call" | custom-call | tf_op jit(solution)/shard_map/pallas_call | solution.py:96
  27.2 4.8 %constant_dynamic-slice_fusion = f32[4096,256]{1,0:T(8,128)} fusion(f32[8192,256]{1,0:T(8,128)} %bitcast.48, s32[]{:T(128)S(6)} %select_n.90), kind=kLoop, calls=%fused_computation.45 | loop fusion | bytes 8388612 | tf_op jit(solution)/shard_map/dynamic_slice | solution.py:197
  31.9 1.4 copy-done.1
  33.3 1.5 fusion.2
  34.8 6.9 %fusion.5 = f32[256,256]{0,1:T(8,128)S(1)} fusion(f32[64,128,256]{2,1,0:T(8,128)S(1)} %copy-done.1, f32[256]{0:T(256)S(1)} %fusion.2), kind=kOutput, calls=%fused_computation.8 | convolution fusion | flops 3221422080 | bytes 8651776 | tf_op jit(solution)/shard_map/dot_general | solution.py:163
  41.7 2.5 %collective-permute-start.3 = (f32[128,384]{0,1:T(8,128)S(1)}, f32[128,384]{0,1:T(8,128)S(1)}, u32[]{:S(2)}, u32[]{:S(2)}) collective-permute-start(f32[128,384]{0,1:T(8,128)S(1)} %pad_maximum_fusion), channel_id=1, source_target_pairs={{0,1},{1,0},{2,3},{3,2},{4,5},{5,4},{6,7},{7,6},{8,9},{9,8},{10,11... | collective-permute-start | bytes 589832 | tf_op jit(solution)/shard_map/ppermute | solution.py:42
  44.2 4.2 %collective-permute-done.3 = f32[128,384]{0,1:T(8,128)S(1)} collective-permute-done((f32[128,384]{0,1:T(8,128)S(1)}, f32[128,384]{0,1:T(8,128)S(1)}, u32[]{:S(2)}, u32[]{:S(2)}) %collective-permute-start.3) | collective-permute-done | bytes 196640 | tf_op jit(solution)/shard_map/ppermute | solution.py:42
  48.4 1.6 collective-permute-start.4
  50.1 0.1 copy.12
  50.2 0.1 copy.6
  50.3 3.9 %collective-permute-done.4 = f32[128,384]{0,1:T(8,128)S(1)} collective-permute-done((f32[128,384]{0,1:T(8,128)S(1)}, f32[128,384]{0,1:T(8,128)S(1)}, u32[]{:S(2)}, u32[]{:S(2)}) %collective-permute-start.4) | collective-permute-done | bytes 196640 | tf_op jit(solution)/shard_map/ppermute | solution.py:42
  54.2 2.8 %collective-permute-start.5 = (f32[128,384]{0,1:T(8,128)S(1)}, f32[128,384]{0,1:T(8,128)S(1)}, u32[]{:S(2)}, u32[]{:S(2)}) collective-permute-start(f32[128,384]{0,1:T(8,128)S(1)} %add.47), channel_id=1, source_target_pairs={{0,4},{1,5},{2,6},{3,7},{4,0},{5,1},{6,2},{7,3},{8,12},{9,13},{10,... | collective-permute-start | bytes 589832 | tf_op jit(solution)/shard_map/ppermute | solution.py:42
  57.0 0.7 select_bitcast_fusion.rows_ref
  57.7 13.5 %shard_map.47 = f32[128,256]{1,0:T(8,128)} custom-call(f32[128,256]{1,0:T(8,128)} %select_bitcast_fusion.rows_ref), custom_call_target="tpu_custom_call" | custom-call | tf_op jit(solution)/shard_map/pallas_call | solution.py:148
  71.2 1.9 %collective-permute-start.2 = (f32[256,128]{0,1:T(8,128)}, f32[256,128]{0,1:T(8,128)S(1)}, u32[]{:S(2)}, u32[]{:S(2)}) collective-permute-start(f32[256,128]{0,1:T(8,128)} %bitcast.57), channel_id=1, source_target_pairs={{0,1},{1,0},{2,3},{3,2},{4,5},{5,4},{6,7},{7,6},{8,9},{9,8},{10,11... | collective-permute-start | bytes 393224 | tf_op jit(solution)/shard_map/ppermute | solution.py:32
  73.1 0.1 copy.13
  73.2 6.9 %fusion.3 = f32[256,256]{1,0:T(8,128)S(1)} fusion(f32[4096,256]{1,0:T(8,128)} %collective-permute-done.6, f32[8192,256]{1,0:T(8,128)} %bitcast.49, s32[]{:T(128)S(6)} %select_n.89), kind=kOutput, calls=%fused_computation.4 | convolution fusion | flops 1610612736 | bytes 8650756 | tf_op jit(solution)/shard_map/dot_general | solution.py:163
  80.2 0.1 copy.9
  80.3 0.2 collective-permute-start.7
  80.6 0.9 fusion.15.rows_ref
  81.5 13.3 %shard_map.48 = f32[128,256]{1,0:T(8,128)} custom-call(f32[128,256]{1,0:T(8,128)} %fusion.15.rows_ref), custom_call_target="tpu_custom_call" | custom-call | tf_op jit(solution)/shard_map/pallas_call | solution.py:148
  94.8 1.4 collective-permute-start.8
  96.2 1.8 %fusion.41.rows_ref = f32[128,256]{1,0:T(8,128)} fusion(f32[256,128]{0,1:T(8,128)} %bitcast.60, f32[256,256]{0,1:T(8,128)S(1)} %maximum_maximum_fusion), kind=kOutput, calls=%fused_computation.56 | convolution fusion | flops 50331648 | bytes 524288 | tf_op jit(solution)/shard_map/dot_general | solution.py:219
  98.0 13.3 %shard_map.49 = f32[128,256]{1,0:T(8,128)} custom-call(f32[128,256]{1,0:T(8,128)} %fusion.41.rows_ref), custom_call_target="tpu_custom_call" | custom-call | tf_op jit(solution)/shard_map/pallas_call | solution.py:148
  111.4 0.5 collective-permute-start.9
  111.9 8.8 %fusion.42 = f32[8192,128]{1,0:T(8,128)} fusion(f32[8192,256]{1,0:T(8,128)} %bitcast.50, f32[256,128]{0,1:T(8,128)} %bitcast.51), kind=kOutput, calls=%fused_computation.57 | convolution fusion | flops 1610612736 | bytes 12713984 | tf_op jit(solution)/shard_map/dot_general | solution.py:229
  120.7 0.6 fusion.43
  121.2 0.9 collective-permute-done.9
  122.3 0.4 fusion.44
  122.7 0.6 collective-permute-start.11
  123.3 0.6 collective-permute-done.10
  123.9 0.3 collective-permute-done.11
  124.2 0.4 collective-permute-start.13
  124.5 0.4 fusion.6
  124.9 0.3 fusion.12
  125.3 0.9 fusion.9.rows_ref
  126.2 13.5 %shard_map.50 = f32[128,256]{1,0:T(8,128)} custom-call(f32[128,256]{1,0:T(8,128)} %fusion.9.rows_ref), custom_call_target="tpu_custom_call" | custom-call | tf_op jit(solution)/shard_map/pallas_call | solution.py:148
  139.7 1.8 %fusion.8.rows_ref = f32[128,256]{1,0:T(8,128)} fusion(f32[128,256]{1,0:T(8,128)} %shard_map.50, f32[128,128]{0,1:T(8,128)S(1)} %get-tuple-element.34, f32[128,128]{0,1:T(8,128)S(1)} %bitcast.59, f32[128,128]{0,1:T(8,128)S(1)} %copy.10, f32[128,128]{0,1:T(8,128)S(1)} %get-tuple-element.33), kind=kOutput, calls=%fused_computation.17 | convolution fusion | flops 50528256 | bytes 524288 | tf_op jit(solution)/shard_map/dot_general | solution.py:158
  141.5 13.3 %shard_map.51 = f32[128,256]{1,0:T(8,128)} custom-call(f32[128,256]{1,0:T(8,128)} %fusion.8.rows_ref), custom_call_target="tpu_custom_call" | custom-call | tf_op jit(solution)/shard_map/pallas_call | solution.py:148
  154.8 0.8 dynamic-slice_bitcast_fusion
  155.7 4.5 %fusion.21 = f32[64,128,64]{1,2,0:T(8,128)S(1)} fusion(f32[64,128,128]{2,1,0:T(8,128)} %bitcast.12, f32[256,64]{0,1:T(8,128)S(1)} %dynamic-slice_bitcast_fusion, pred[]{:T(512)S(6)} %eq.14), kind=kOutput, calls=%fused_computation.32 | convolution fusion | flops 402661376 | bytes 6356993 | tf_op jit(solution)/shard_map/xyk,km->xym/dot_general | solution.py:268
  160.2 5.9 %convolution_add_fusion = f32[64,128,64]{1,2,0:T(8,128)} fusion(f32[64,128,64]{1,2,0:T(8,128)S(1)} %fusion.21, f32[64,128,128]{2,1,0:T(8,128)} %bitcast.8, f32[256,64]{0,1:T(8,128)S(1)} %dynamic-slice_bitcast_fusion, pred[]{:T(512)S(6)} %eq.14), kind=kOutput, calls=%fused_computation.6 | convolution fusion | flops 403185664 | bytes 8454145 | tf_op jit(solution)/shard_map/xyk,km->xym/dot_general | solution.py:266
  (39 shorter events, 0.5 us)
Async XLA Ops:
  0.0 50.1 %copy-start = (s32[512,128]{1,0:T(8,128)S(1)}, s32[512,128]{1,0:T(8,128)}, u32[]{:S(2)}) copy-start(s32[512,128]{1,0:T(8,128)} %param.6) | copy-start | bytes 786436
  1.0 7.6 %collective-permute-start = (bf16[2,128,256]{2,1,0:T(8,128)(2,1)S(1)}, bf16[2,128,256]{2,1,0:T(8,128)(2,1)S(1)}, u32[]{:S(2)}, u32[]{:S(2)}) collective-permute-start(bf16[2,128,256]{2,1,0:T(8,128)(2,1)S(1)} %get-tuple-element.30), channel_id=1, source_target_pairs={{0,1},{1,2},{2,3},{3,4},{4,5},{5,6},{6,7},{8,9},{9,10},{10,11},{11... | collective-permute-start | bytes 393224 | tf_op jit(solution)/shard_map/ppermute | solution.py:20
  5.9 6.9 %collective-permute-start.1 = (bf16[2,128,256]{2,1,0:T(8,128)(2,1)S(1)}, bf16[2,128,256]{2,1,0:T(8,128)(2,1)S(1)}, u32[]{:S(2)}, u32[]{:S(2)}) collective-permute-start(bf16[2,128,256]{2,1,0:T(8,128)(2,1)S(1)} %get-tuple-element.29), channel_id=1, source_target_pairs={{1,0},{2,1},{3,2},{4,3},{5,4},{6,5},{7,6},{9,8},{10,9},{11,10},{12... | collective-permute-start | bytes 393224 | tf_op jit(solution)/shard_map/ppermute | solution.py:21
  8.7 4.1 %copy-start.5 = (bf16[2,128,256]{2,1,0:T(8,128)(2,1)}, bf16[2,128,256]{2,1,0:T(8,128)(2,1)S(1)}, u32[]{:S(2)}) copy-start(bf16[2,128,256]{2,1,0:T(8,128)(2,1)S(1)} %collective-permute-done.low_ref) | copy-start | bytes 393220
  12.8 0.7 copy-start.6
  27.2 6.2 %copy-start.1 = (f32[64,128,256]{2,1,0:T(8,128)S(1)}, f32[64,128,256]{2,1,0:T(8,128)}, u32[]{:S(2)}) copy-start(f32[64,128,256]{2,1,0:T(8,128)} %shard_map.46) | copy-start | bytes 25165828
  31.9 41.3 %collective-permute-start.6 = (f32[4096,256]{1,0:T(8,128)}, f32[4096,256]{1,0:T(8,128)}, u32[]{:S(2)}, u32[]{:S(2)}) collective-permute-start(f32[4096,256]{1,0:T(8,128)} %constant_dynamic-slice_fusion), channel_id=1, source_target_pairs={{0,8},{8,0},{1,9},{9,1},{2,10},{10,2},{3,11},{11,3},{4,12},{12,4},... | collective-permute-start | bytes 12582920 | tf_op jit(solution)/shard_map/ppermute | solution.py:32
  34.8 15.4 %copy-start.4 = (s32[256,128]{1,0:T(8,128)S(1)}, s32[256,128]{1,0:T(8,128)}, u32[]{:S(2)}) copy-start(s32[256,128]{1,0:T(8,128)} %param.7) | copy-start | bytes 393220
  41.7 6.7 %collective-permute-start.3 = (f32[128,384]{0,1:T(8,128)S(1)}, f32[128,384]{0,1:T(8,128)S(1)}, u32[]{:S(2)}, u32[]{:S(2)}) collective-permute-start(f32[128,384]{0,1:T(8,128)S(1)} %pad_maximum_fusion), channel_id=1, source_target_pairs={{0,1},{1,0},{2,3},{3,2},{4,5},{5,4},{6,7},{7,6},{8,9},{9,8},{10,11... | collective-permute-start | bytes 589832 | tf_op jit(solution)/shard_map/ppermute | solution.py:42
  48.4 5.7 %collective-permute-start.4 = (f32[128,384]{0,1:T(8,128)S(1)}, f32[128,384]{0,1:T(8,128)S(1)}, u32[]{:S(2)}, u32[]{:S(2)}) collective-permute-start(f32[128,384]{0,1:T(8,128)S(1)} %fusion.38), channel_id=1, source_target_pairs={{0,2},{1,3},{2,0},{3,1},{4,6},{5,7},{6,4},{7,5},{8,10},{9,11},{10,... | collective-permute-start | bytes 589832 | tf_op jit(solution)/shard_map/ppermute | solution.py:42
  54.2 18.9 %collective-permute-start.5 = (f32[128,384]{0,1:T(8,128)S(1)}, f32[128,384]{0,1:T(8,128)S(1)}, u32[]{:S(2)}, u32[]{:S(2)}) collective-permute-start(f32[128,384]{0,1:T(8,128)S(1)} %add.47), channel_id=1, source_target_pairs={{0,4},{1,5},{2,6},{3,7},{4,0},{5,1},{6,2},{7,3},{8,12},{9,13},{10,... | collective-permute-start | bytes 589832 | tf_op jit(solution)/shard_map/ppermute | solution.py:42
  71.2 9.4 %collective-permute-start.2 = (f32[256,128]{0,1:T(8,128)}, f32[256,128]{0,1:T(8,128)S(1)}, u32[]{:S(2)}, u32[]{:S(2)}) collective-permute-start(f32[256,128]{0,1:T(8,128)} %bitcast.57), channel_id=1, source_target_pairs={{0,1},{1,0},{2,3},{3,2},{4,5},{5,4},{6,7},{7,6},{8,9},{9,8},{10,11... | collective-permute-start | bytes 393224 | tf_op jit(solution)/shard_map/ppermute | solution.py:32
  73.2 7.3 %copy-start.3 = (f32[128,256]{1,0:T(8,128)S(1)}, f32[128,256]{1,0:T(8,128)}, u32[]{:S(2)}) copy-start(f32[128,256]{1,0:T(8,128)} %shard_map.47) | copy-start | bytes 393220
  80.3 14.4 %collective-permute-start.7 = (f32[256,256]{1,0:T(8,128)S(1)}, f32[256,256]{1,0:T(8,128)S(1)}, u32[]{:S(2)}, u32[]{:S(2)}) collective-permute-start(f32[256,256]{1,0:T(8,128)S(1)} %bitcast_select_fusion), channel_id=1, source_target_pairs={{0,1},{1,0},{2,3},{3,2},{4,5},{5,4},{6,7},{7,6},{8,9},{9,8},{10,11... | collective-permute-start | bytes 786440 | tf_op jit(solution)/shard_map/ppermute | solution.py:221
  94.8 16.5 %collective-permute-start.8 = (f32[256,256]{1,0:T(8,128)S(1)}, f32[256,256]{1,0:T(8,128)S(1)}, u32[]{:S(2)}, u32[]{:S(2)}) collective-permute-start(f32[256,256]{1,0:T(8,128)S(1)} %add.51), channel_id=1, source_target_pairs={{0,2},{1,3},{2,0},{3,1},{4,6},{5,7},{6,4},{7,5},{8,10},{9,11},{10,... | collective-permute-start | bytes 786440 | tf_op jit(solution)/shard_map/ppermute | solution.py:221
  111.4 9.3 %copy-start.2 = (f32[128,256]{1,0:T(8,128)S(1)}, f32[128,256]{1,0:T(8,128)}, u32[]{:S(2)}) copy-start(f32[128,256]{1,0:T(8,128)} %shard_map.49) | copy-start | bytes 393220
  111.4 10.8 %collective-permute-start.9 = (f32[256,256]{1,0:T(8,128)S(1)}, f32[256,256]{1,0:T(8,128)S(1)}, u32[]{:S(2)}, u32[]{:S(2)}) collective-permute-start(f32[256,256]{1,0:T(8,128)S(1)} %add.52), channel_id=1, source_target_pairs={{0,4},{1,5},{2,6},{3,7},{4,0},{5,1},{6,2},{7,3},{8,12},{9,13},{10,... | collective-permute-start | bytes 786440 | tf_op jit(solution)/shard_map/ppermute | solution.py:228
  120.6 3.5 %collective-permute-start.12 = (f32[256,128]{0,1:T(8,128)S(1)}, f32[256,128]{0,1:T(8,128)S(1)}, u32[]{:S(2)}, u32[]{:S(2)}) collective-permute-start(f32[256,128]{0,1:T(8,128)S(1)} %bitcast.52), channel_id=1, source_target_pairs={{0,8},{8,0},{1,9},{9,1},{2,10},{10,2},{3,11},{11,3},{4,12},{12,4},... | collective-permute-start | bytes 393224 | tf_op jit(solution)/shard_map/ppermute | solution.py:32
  122.2 1.6 collective-permute-start.10
  122.7 1.5 collective-permute-start.11
  124.2 31.5 %collective-permute-start.13 = (f32[8192,128]{1,0:T(8,128)}, f32[8192,128]{1,0:T(8,128)}, u32[]{:S(2)}, u32[]{:S(2)}) collective-permute-start(f32[8192,128]{1,0:T(8,128)} %fusion.42), channel_id=1, source_target_pairs={{0,8},{8,0},{1,9},{9,1},{2,10},{10,2},{3,11},{11,3},{4,12},{12,4},... | collective-permute-start | bytes 12582920 | tf_op jit(solution)/shard_map/ppermute | solution.py:32

commit v13 on v8

--- a/solution.py
+++ b/solution.py
@@ -112,7 +112,7 @@
 def gram_schmidt_kernel(rows_ref, out_ref, work):
     count, width = rows_ref.shape
     blocks = count // 8
-    group = 4 if blocks % 4 == 0 else 1
+    group = 2 if blocks % 2 == 0 else 1
     work[...] = rows_ref[...]
     for first in range(0, blocks, group):
 

time: 167 us -> 167 us (level)
  no operation moved by 1% of the time
where the time goes in v13:
time: 167 us; the launch traced here: 166 us
  Pallas kernels  80.7 us (48%)
  matrix products  38.8 us (23%)
  starting transfers between devices  18.1 us (11%)
  waiting for transfers between devices  15.4 us (9%)
  local copies, waits for them, and re-layouts  10.8 us (6%)
  other arithmetic  2.41 us (1%)
    pallas_call x5, Pallas kernels, orthonormal(): pl.pallas_call(gram_schmidt_kernel, out_shape=jax.ShapeDtypeStruct(rows.s...  66.9 us
    dot_general x2, matrix products, cross_gram(): lax.dot_general(left_rows, right_rows, (((0,), (0,)), ((), ())), precisio...  13.8 us
    pallas_call x1, Pallas kernels, fluxes(): pl.pallas_call(functools.partial(flux_kernel, count), grid=(count,), in_s...  13.8 us
    dot_general x1, matrix products, on_device(): own_modes = jnp.dot(own_flux, own_basis, precision=high)  8.78 us
    ppermute x3, waiting for transfers between devices, tree_sum(): value = value + lax.ppermute(value, axis, route)  8.05 us
    ppermute x3, starting transfers between devices, tree_sum(): value = value + lax.ppermute(value, axis, route)  6.97 us
    ppermute x1, starting transfers between devices, halos(): lax.ppermute(lax.slice_in_dim(block, block.shape[0] - width, None, axis=0...  4.88 us
    dynamic_slice x1, local copies, waits for them, and re-layouts, on_device(): lax.dynamic_slice_in_dim(own_flux, (1 - member) * half_rows, half_rows, 0)  4.76 us
  transfers between devices with their start and end apart: 14, of which 7 were waited for; matrix products, arithmetic and copies ran while one was open for 20% of the time, Pallas kernels for 40%

profile of v13, /device:TPU:0, one launch (start us, length us, event | category | flops | bytes accessed | tf_op | source)
XLA Modules:
  0.0 166.5 jit_solution(9439766735224502043)
XLA Ops:
  0.0 1.0 fusion.38
  1.0 4.9 %collective-permute-start = (bf16[2,128,256]{2,1,0:T(8,128)(2,1)S(1)}, bf16[2,128,256]{2,1,0:T(8,128)(2,1)S(1)}, u32[]{:S(2)}, u32[]{:S(2)}) collective-permute-start(bf16[2,128,256]{2,1,0:T(8,128)(2,1)S(1)} %get-tuple-element.30), channel_id=1, source_target_pairs={{0,1},{1,2},{2,3},{3,4},{4,5},{5,6},{6,7},{8,9},{9,10},{10,11},{11... | collective-permute-start | bytes 393224 | tf_op jit(solution)/shard_map/ppermute | solution.py:20
  5.9 1.3 collective-permute-start.1
  7.2 1.4 collective-permute-done.low_ref
  8.7 4.1 %collective-permute-done.1.high_ref = bf16[2,128,256]{2,1,0:T(8,128)(2,1)S(1)} collective-permute-done((bf16[2,128,256]{2,1,0:T(8,128)(2,1)S(1)}, bf16[2,128,256]{2,1,0:T(8,128)(2,1)S(1)}, u32[]{:S(2)}, u32[]{:S(2)}) %collective-permute-start.1) | collective-permute-done | bytes 131104 | tf_op jit(solution)/shard_map/ppermute | solution.py:21
  12.8 0.7 copy-done.6
  13.4 13.8 %shard_map.46 = f32[64,128,256]{2,1,0:T(8,128)} custom-call(bf16[2,128,256]{2,1,0:T(8,128)(2,1)} %copy-done.5, bf16[2,128,256]{2,1,0:T(8,128)(2,1)} %copy-done.6, bf16[64,128,256]{2,1,0:T(8,128)(2,1)} %next_ref.1, bf16[64,128,256]{2,1,0:T(8,128)(2,1)} %next_ref.1, bf16[64,128,256]{2,1,0:T(8,128)(2,1)} %next_ref.1, f32[64,128]{1,0:T(8,128)} %coef_ref.1), custom_call_target="tpu_custom_call" | custom-call | tf_op jit(solution)/shard_map/pallas_call | solution.py:96
  27.2 4.8 %constant_dynamic-slice_fusion = f32[4096,256]{1,0:T(8,128)} fusion(f32[8192,256]{1,0:T(8,128)} %bitcast.45, s32[]{:T(128)S(6)} %select_n.90), kind=kLoop, calls=%fused_computation.45 | loop fusion | bytes 8388612 | tf_op jit(solution)/shard_map/dynamic_slice | solution.py:197
  32.0 1.4 copy-done.1
  33.4 1.5 fusion.2
  34.8 6.9 %fusion.6 = f32[256,256]{0,1:T(8,128)S(1)} fusion(f32[64,128,256]{2,1,0:T(8,128)S(1)} %copy-done.1, f32[256]{0:T(256)S(1)} %fusion.2), kind=kOutput, calls=%fused_computation.10 | convolution fusion | flops 3221422080 | bytes 8651776 | tf_op jit(solution)/shard_map/dot_general | solution.py:163
  41.8 2.5 %collective-permute-start.3 = (f32[128,384]{0,1:T(8,128)S(1)}, f32[128,384]{0,1:T(8,128)S(1)}, u32[]{:S(2)}, u32[]{:S(2)}) collective-permute-start(f32[128,384]{0,1:T(8,128)S(1)} %pad_maximum_fusion), channel_id=1, source_target_pairs={{0,1},{1,0},{2,3},{3,2},{4,5},{5,4},{6,7},{7,6},{8,9},{9,8},{10,11... | collective-permute-start | bytes 589832 | tf_op jit(solution)/shard_map/ppermute | solution.py:42
  44.3 4.2 %collective-permute-done.3 = f32[128,384]{0,1:T(8,128)S(1)} collective-permute-done((f32[128,384]{0,1:T(8,128)S(1)}, f32[128,384]{0,1:T(8,128)S(1)}, u32[]{:S(2)}, u32[]{:S(2)}) %collective-permute-start.3) | collective-permute-done | bytes 196640 | tf_op jit(solution)/shard_map/ppermute | solution.py:42
  48.5 1.6 collective-permute-start.4
  50.1 0.1 copy.13
  50.2 0.1 copy.6
  50.3 3.9 %collective-permute-done.4 = f32[128,384]{0,1:T(8,128)S(1)} collective-permute-done((f32[128,384]{0,1:T(8,128)S(1)}, f32[128,384]{0,1:T(8,128)S(1)}, u32[]{:S(2)}, u32[]{:S(2)}) %collective-permute-start.4) | collective-permute-done | bytes 196640 | tf_op jit(solution)/shard_map/ppermute | solution.py:42
  54.2 2.8 %collective-permute-start.5 = (f32[128,384]{0,1:T(8,128)S(1)}, f32[128,384]{0,1:T(8,128)S(1)}, u32[]{:S(2)}, u32[]{:S(2)}) collective-permute-start(f32[128,384]{0,1:T(8,128)S(1)} %add.47), channel_id=1, source_target_pairs={{0,4},{1,5},{2,6},{3,7},{4,0},{5,1},{6,2},{7,3},{8,12},{9,13},{10,... | collective-permute-start | bytes 589832 | tf_op jit(solution)/shard_map/ppermute | solution.py:42
  57.1 0.7 select_bitcast_fusion.rows_ref
  57.8 13.4 %shard_map.47 = f32[128,256]{1,0:T(8,128)} custom-call(f32[128,256]{1,0:T(8,128)} %select_bitcast_fusion.rows_ref), custom_call_target="tpu_custom_call" | custom-call | tf_op jit(solution)/shard_map/pallas_call | solution.py:148
  71.1 1.9 %collective-permute-start.2 = (f32[256,128]{0,1:T(8,128)}, f32[256,128]{0,1:T(8,128)S(1)}, u32[]{:S(2)}, u32[]{:S(2)}) collective-permute-start(f32[256,128]{0,1:T(8,128)} %bitcast.54), channel_id=1, source_target_pairs={{0,1},{1,0},{2,3},{3,2},{4,5},{5,4},{6,7},{7,6},{8,9},{9,8},{10,11... | collective-permute-start | bytes 393224 | tf_op jit(solution)/shard_map/ppermute | solution.py:32
  73.2 6.9 %fusion.3 = f32[256,256]{1,0:T(8,128)S(1)} fusion(f32[4096,256]{1,0:T(8,128)} %collective-permute-done.6, f32[8192,256]{1,0:T(8,128)} %bitcast.46, s32[]{:T(128)S(6)} %select_n.89), kind=kOutput, calls=%fused_computation.5 | convolution fusion | flops 1610612736 | bytes 8650756 | tf_op jit(solution)/shard_map/dot_general | solution.py:163
  80.2 0.1 copy.9
  80.3 0.2 collective-permute-start.7
  80.6 0.9 fusion.16.rows_ref
  81.5 13.3 %shard_map.48 = f32[128,256]{1,0:T(8,128)} custom-call(f32[128,256]{1,0:T(8,128)} %fusion.16.rows_ref), custom_call_target="tpu_custom_call" | custom-call | tf_op jit(solution)/shard_map/pallas_call | solution.py:148
  94.8 1.4 collective-permute-start.8
  96.2 1.8 %fusion.40.rows_ref = f32[128,256]{1,0:T(8,128)} fusion(f32[256,128]{0,1:T(8,128)} %bitcast.57, f32[256,256]{0,1:T(8,128)S(1)} %maximum_maximum_fusion), kind=kOutput, calls=%fused_computation.56 | convolution fusion | flops 100663296 | bytes 524288 | tf_op jit(solution)/shard_map/dot_general | solution.py:219
  98.1 13.4 %shard_map.49 = f32[128,256]{1,0:T(8,128)} custom-call(f32[128,256]{1,0:T(8,128)} %fusion.40.rows_ref), custom_call_target="tpu_custom_call" | custom-call | tf_op jit(solution)/shard_map/pallas_call | solution.py:148
  111.5 0.5 collective-permute-start.9
  112.0 8.8 %fusion.41 = f32[8192,128]{1,0:T(8,128)} fusion(f32[8192,256]{1,0:T(8,128)} %bitcast.47, f32[256,128]{0,1:T(8,128)} %bitcast.48), kind=kOutput, calls=%fused_computation.57 | convolution fusion | flops 1610612736 | bytes 12713984 | tf_op jit(solution)/shard_map/dot_general | solution.py:229
  120.8 0.6 fusion.42
  121.4 1.0 collective-permute-done.9
  122.5 0.4 fusion.43
  122.9 0.6 collective-permute-start.11
  123.4 0.6 collective-permute-done.10
  124.0 0.3 collective-permute-done.11
  124.3 0.4 collective-permute-start.13
  124.7 0.4 fusion.7
  125.1 0.3 fusion.13
  125.4 0.9 fusion.10.rows_ref
  126.4 13.3 %shard_map.50 = f32[128,256]{1,0:T(8,128)} custom-call(f32[128,256]{1,0:T(8,128)} %fusion.10.rows_ref), custom_call_target="tpu_custom_call" | custom-call | tf_op jit(solution)/shard_map/pallas_call | solution.py:148
  139.7 1.8 %fusion.9.rows_ref = f32[128,256]{1,0:T(8,128)} fusion(f32[128,256]{1,0:T(8,128)} %shard_map.50, f32[128,128]{0,1:T(8,128)S(1)} %get-tuple-element.34, f32[128,128]{0,1:T(8,128)S(1)} %bitcast.56, f32[128,128]{0,1:T(8,128)S(1)} %copy.10, f32[128,128]{0,1:T(8,128)S(1)} %get-tuple-element.33), kind=kOutput, calls=%fused_computation.19 | convolution fusion | flops 100859904 | bytes 524288 | tf_op jit(solution)/shard_map/dot_general | solution.py:158
  141.5 13.5 %shard_map.51 = f32[128,256]{1,0:T(8,128)} custom-call(f32[128,256]{1,0:T(8,128)} %fusion.9.rows_ref), custom_call_target="tpu_custom_call" | custom-call | tf_op jit(solution)/shard_map/pallas_call | solution.py:148
  155.0 0.8 dynamic-slice_bitcast_fusion
  155.8 4.5 %fusion.22 = f32[8192,64]{0,1:T(8,128)S(1)} fusion(f32[8192,128]{1,0:T(8,128)} %collective-permute-done.13, f32[256,64]{0,1:T(8,128)S(1)} %dynamic-slice_bitcast_fusion, pred[]{:T(512)S(6)} %eq.14), kind=kOutput, calls=%fused_computation.34 | convolution fusion | flops 402661376 | bytes 6356993 | tf_op jit(solution)/shard_map/dot_general | solution.py:265
  160.3 4.5 %fusion.5 = f32[8,64,8,128]{3,2,1,0:T(8,128)S(1)} fusion(f32[8192,64]{0,1:T(8,128)S(1)} %fusion.22, f32[8192,128]{1,0:T(8,128)} %fusion.41, f32[256,64]{0,1:T(8,128)S(1)} %dynamic-slice_bitcast_fusion, pred[]{:T(512)S(6)} %eq.14), kind=kOutput, calls=%fused_computation.8 | convolution fusion | flops 403185664 | bytes 8454145 | tf_op jit(solution)/shard_map/dot_general | solution.py:265
  164.9 1.6 copy.17
  (40 shorter events, 0.6 us)
Async XLA Ops:
  0.0 50.1 %copy-start = (s32[512,128]{1,0:T(8,128)S(1)}, s32[512,128]{1,0:T(8,128)}, u32[]{:S(2)}) copy-start(s32[512,128]{1,0:T(8,128)} %param.6) | copy-start | bytes 786436
  1.0 7.6 %collective-permute-start = (bf16[2,128,256]{2,1,0:T(8,128)(2,1)S(1)}, bf16[2,128,256]{2,1,0:T(8,128)(2,1)S(1)}, u32[]{:S(2)}, u32[]{:S(2)}) collective-permute-start(bf16[2,128,256]{2,1,0:T(8,128)(2,1)S(1)} %get-tuple-element.30), channel_id=1, source_target_pairs={{0,1},{1,2},{2,3},{3,4},{4,5},{5,6},{6,7},{8,9},{9,10},{10,11},{11... | collective-permute-start | bytes 393224 | tf_op jit(solution)/shard_map/ppermute | solution.py:20
  5.9 6.9 %collective-permute-start.1 = (bf16[2,128,256]{2,1,0:T(8,128)(2,1)S(1)}, bf16[2,128,256]{2,1,0:T(8,128)(2,1)S(1)}, u32[]{:S(2)}, u32[]{:S(2)}) collective-permute-start(bf16[2,128,256]{2,1,0:T(8,128)(2,1)S(1)} %get-tuple-element.29), channel_id=1, source_target_pairs={{1,0},{2,1},{3,2},{4,3},{5,4},{6,5},{7,6},{9,8},{10,9},{11,10},{12... | collective-permute-start | bytes 393224 | tf_op jit(solution)/shard_map/ppermute | solution.py:21
  8.7 4.1 %copy-start.5 = (bf16[2,128,256]{2,1,0:T(8,128)(2,1)}, bf16[2,128,256]{2,1,0:T(8,128)(2,1)S(1)}, u32[]{:S(2)}) copy-start(bf16[2,128,256]{2,1,0:T(8,128)(2,1)S(1)} %collective-permute-done.low_ref) | copy-start | bytes 393220
  12.8 0.7 copy-start.6
  27.2 6.2 %copy-start.1 = (f32[64,128,256]{2,1,0:T(8,128)S(1)}, f32[64,128,256]{2,1,0:T(8,128)}, u32[]{:S(2)}) copy-start(f32[64,128,256]{2,1,0:T(8,128)} %shard_map.46) | copy-start | bytes 25165828
  32.0 41.2 %collective-permute-start.6 = (f32[4096,256]{1,0:T(8,128)}, f32[4096,256]{1,0:T(8,128)}, u32[]{:S(2)}, u32[]{:S(2)}) collective-permute-start(f32[4096,256]{1,0:T(8,128)} %constant_dynamic-slice_fusion), channel_id=1, source_target_pairs={{0,8},{8,0},{1,9},{9,1},{2,10},{10,2},{3,11},{11,3},{4,12},{12,4},... | collective-permute-start | bytes 12582920 | tf_op jit(solution)/shard_map/ppermute | solution.py:32
  34.8 15.4 %copy-start.4 = (s32[256,128]{1,0:T(8,128)S(1)}, s32[256,128]{1,0:T(8,128)}, u32[]{:S(2)}) copy-start(s32[256,128]{1,0:T(8,128)} %param.7) | copy-start | bytes 393220
  41.8 6.7 %collective-permute-start.3 = (f32[128,384]{0,1:T(8,128)S(1)}, f32[128,384]{0,1:T(8,128)S(1)}, u32[]{:S(2)}, u32[]{:S(2)}) collective-permute-start(f32[128,384]{0,1:T(8,128)S(1)} %pad_maximum_fusion), channel_id=1, source_target_pairs={{0,1},{1,0},{2,3},{3,2},{4,5},{5,4},{6,7},{7,6},{8,9},{9,8},{10,11... | collective-permute-start | bytes 589832 | tf_op jit(solution)/shard_map/ppermute | solution.py:42
  48.5 5.7 %collective-permute-start.4 = (f32[128,384]{0,1:T(8,128)S(1)}, f32[128,384]{0,1:T(8,128)S(1)}, u32[]{:S(2)}, u32[]{:S(2)}) collective-permute-start(f32[128,384]{0,1:T(8,128)S(1)} %fusion.37), channel_id=1, source_target_pairs={{0,2},{1,3},{2,0},{3,1},{4,6},{5,7},{6,4},{7,5},{8,10},{9,11},{10,... | collective-permute-start | bytes 589832 | tf_op jit(solution)/shard_map/ppermute | solution.py:42
  54.2 18.8 %collective-permute-start.5 = (f32[128,384]{0,1:T(8,128)S(1)}, f32[128,384]{0,1:T(8,128)S(1)}, u32[]{:S(2)}, u32[]{:S(2)}) collective-permute-start(f32[128,384]{0,1:T(8,128)S(1)} %add.47), channel_id=1, source_target_pairs={{0,4},{1,5},{2,6},{3,7},{4,0},{5,1},{6,2},{7,3},{8,12},{9,13},{10,... | collective-permute-start | bytes 589832 | tf_op jit(solution)/shard_map/ppermute | solution.py:42
  71.1 9.4 %collective-permute-start.2 = (f32[256,128]{0,1:T(8,128)}, f32[256,128]{0,1:T(8,128)S(1)}, u32[]{:S(2)}, u32[]{:S(2)}) collective-permute-start(f32[256,128]{0,1:T(8,128)} %bitcast.54), channel_id=1, source_target_pairs={{0,1},{1,0},{2,3},{3,2},{4,5},{5,4},{6,7},{7,6},{8,9},{9,8},{10,11... | collective-permute-start | bytes 393224 | tf_op jit(solution)/shard_map/ppermute | solution.py:32
  73.2 7.3 %copy-start.3 = (f32[128,256]{1,0:T(8,128)S(1)}, f32[128,256]{1,0:T(8,128)}, u32[]{:S(2)}) copy-start(f32[128,256]{1,0:T(8,128)} %shard_map.47) | copy-start | bytes 393220
  80.3 14.5 %collective-permute-start.7 = (f32[256,256]{1,0:T(8,128)S(1)}, f32[256,256]{1,0:T(8,128)S(1)}, u32[]{:S(2)}, u32[]{:S(2)}) collective-permute-start(f32[256,256]{1,0:T(8,128)S(1)} %bitcast_select_fusion), channel_id=1, source_target_pairs={{0,1},{1,0},{2,3},{3,2},{4,5},{5,4},{6,7},{7,6},{8,9},{9,8},{10,11... | collective-permute-start | bytes 786440 | tf_op jit(solution)/shard_map/ppermute | solution.py:221
  94.8 16.7 %collective-permute-start.8 = (f32[256,256]{1,0:T(8,128)S(1)}, f32[256,256]{1,0:T(8,128)S(1)}, u32[]{:S(2)}, u32[]{:S(2)}) collective-permute-start(f32[256,256]{1,0:T(8,128)S(1)} %add.51), channel_id=1, source_target_pairs={{0,2},{1,3},{2,0},{3,1},{4,6},{5,7},{6,4},{7,5},{8,10},{9,11},{10,... | collective-permute-start | bytes 786440 | tf_op jit(solution)/shard_map/ppermute | solution.py:221
  111.5 9.3 %copy-start.2 = (f32[128,256]{1,0:T(8,128)S(1)}, f32[128,256]{1,0:T(8,128)}, u32[]{:S(2)}) copy-start(f32[128,256]{1,0:T(8,128)} %shard_map.49) | copy-start | bytes 393220
  111.5 10.8 %collective-permute-start.9 = (f32[256,256]{1,0:T(8,128)S(1)}, f32[256,256]{1,0:T(8,128)S(1)}, u32[]{:S(2)}, u32[]{:S(2)}) collective-permute-start(f32[256,256]{1,0:T(8,128)S(1)} %add.52), channel_id=1, source_target_pairs={{0,4},{1,5},{2,6},{3,7},{4,0},{5,1},{6,2},{7,3},{8,12},{9,13},{10,... | collective-permute-start | bytes 786440 | tf_op jit(solution)/shard_map/ppermute | solution.py:228
  120.8 3.5 %collective-permute-start.12 = (f32[256,128]{0,1:T(8,128)S(1)}, f32[256,128]{0,1:T(8,128)S(1)}, u32[]{:S(2)}, u32[]{:S(2)}) collective-permute-start(f32[256,128]{0,1:T(8,128)S(1)} %bitcast.49), channel_id=1, source_target_pairs={{0,8},{8,0},{1,9},{9,1},{2,10},{10,2},{3,11},{11,3},{4,12},{12,4},... | collective-permute-start | bytes 393224 | tf_op jit(solution)/shard_map/ppermute | solution.py:32
  122.4 1.6 collective-permute-start.10
  122.9 1.5 collective-permute-start.11
  124.3 31.5 %collective-permute-start.13 = (f32[8192,128]{1,0:T(8,128)}, f32[8192,128]{1,0:T(8,128)}, u32[]{:S(2)}, u32[]{:S(2)}) collective-permute-start(f32[8192,128]{1,0:T(8,128)} %fusion.41), channel_id=1, source_target_pairs={{0,8},{8,0},{1,9},{9,1},{2,10},{10,2},{3,11},{11,3},{4,12},{12,4},... | collective-permute-start | bytes 12582920 | tf_op jit(solution)/shard_map/ppermute | solution.py:32

commit v14 on v8

--- a/solution.py
+++ b/solution.py
@@ -87,7 +87,7 @@
 
 def fluxes(low, block, high, coefficient):
     nx, ny, ns = block.shape
-    bx = 8 if nx % 8 == 0 else nx
+    bx = 16 if nx % 16 == 0 else nx
     count = nx // bx
 
     def spec(index):

time: 167 us -> 166 us (level)
  no operation moved by 1% of the time
where the time goes in v14:
time: 166 us; the launch traced here: 165 us
  Pallas kernels  79.6 us (48%)
  matrix products  38.8 us (23%)
  starting transfers between devices  18.1 us (11%)
  waiting for transfers between devices  15.4 us (9%)
  local copies, waits for them, and re-layouts  10.8 us (7%)
  other arithmetic  2.41 us (1%)
    pallas_call x5, Pallas kernels, orthonormal(): pl.pallas_call(gram_schmidt_kernel, out_shape=jax.ShapeDtypeStruct(rows.s...  66.8 us
    dot_general x2, matrix products, cross_gram(): lax.dot_general(left_rows, right_rows, (((0,), (0,)), ((), ())), precisio...  13.8 us
    pallas_call x1, Pallas kernels, fluxes(): pl.pallas_call(functools.partial(flux_kernel, count), grid=(count,), in_s...  12.8 us
    dot_general x1, matrix products, on_device(): own_modes = jnp.dot(own_flux, own_basis, precision=high)  8.78 us
    ppermute x3, waiting for transfers between devices, tree_sum(): value = value + lax.ppermute(value, axis, route)  8.05 us
    ppermute x3, starting transfers between devices, tree_sum(): value = value + lax.ppermute(value, axis, route)  6.96 us
    ppermute x1, starting transfers between devices, halos(): lax.ppermute(lax.slice_in_dim(block, block.shape[0] - width, None, axis=0...  4.88 us
    dynamic_slice x1, local copies, waits for them, and re-layouts, on_device(): lax.dynamic_slice_in_dim(own_flux, (1 - member) * half_rows, half_rows, 0)  4.76 us
  transfers between devices with their start and end apart: 14, of which 7 were waited for; matrix products, arithmetic and copies ran while one was open for 20% of the time, Pallas kernels for 40%

profile of v14, /device:TPU:0, one launch (start us, length us, event | category | flops | bytes accessed | tf_op | source)
XLA Modules:
  0.0 165.4 jit_solution(2350609215265590642)
XLA Ops:
  0.0 1.0 fusion.38
  1.0 4.9 %collective-permute-start = (bf16[2,128,256]{2,1,0:T(8,128)(2,1)S(1)}, bf16[2,128,256]{2,1,0:T(8,128)(2,1)S(1)}, u32[]{:S(2)}, u32[]{:S(2)}) collective-permute-start(bf16[2,128,256]{2,1,0:T(8,128)(2,1)S(1)} %get-tuple-element.30), channel_id=1, source_target_pairs={{0,1},{1,2},{2,3},{3,4},{4,5},{5,6},{6,7},{8,9},{9,10},{10,11},{11... | collective-permute-start | bytes 393224 | tf_op jit(solution)/shard_map/ppermute | solution.py:20
  5.9 1.3 collective-permute-start.1
  7.2 1.4 collective-permute-done.low_ref
  8.7 4.1 %collective-permute-done.1.high_ref = bf16[2,128,256]{2,1,0:T(8,128)(2,1)S(1)} collective-permute-done((bf16[2,128,256]{2,1,0:T(8,128)(2,1)S(1)}, bf16[2,128,256]{2,1,0:T(8,128)(2,1)S(1)}, u32[]{:S(2)}, u32[]{:S(2)}) %collective-permute-start.1) | collective-permute-done | bytes 131104 | tf_op jit(solution)/shard_map/ppermute | solution.py:21
  12.8 0.7 copy-done.6
  13.4 12.8 %shard_map.46 = f32[64,128,256]{2,1,0:T(8,128)} custom-call(bf16[2,128,256]{2,1,0:T(8,128)(2,1)} %copy-done.5, bf16[2,128,256]{2,1,0:T(8,128)(2,1)} %copy-done.6, bf16[64,128,256]{2,1,0:T(8,128)(2,1)} %next_ref.1, bf16[64,128,256]{2,1,0:T(8,128)(2,1)} %next_ref.1, bf16[64,128,256]{2,1,0:T(8,128)(2,1)} %next_ref.1, f32[64,128]{1,0:T(8,128)} %coef_ref.1), custom_call_target="tpu_custom_call" | custom-call | tf_op jit(solution)/shard_map/pallas_call | solution.py:96
  26.2 4.8 %constant_dynamic-slice_fusion = f32[4096,256]{1,0:T(8,128)} fusion(f32[8192,256]{1,0:T(8,128)} %bitcast.45, s32[]{:T(128)S(6)} %select_n.90), kind=kLoop, calls=%fused_computation.45 | loop fusion | bytes 8388612 | tf_op jit(solution)/shard_map/dynamic_slice | solution.py:197
  31.0 1.4 copy-done.1
  32.4 1.5 fusion.2
  33.9 6.9 %fusion.6 = f32[256,256]{0,1:T(8,128)S(1)} fusion(f32[64,128,256]{2,1,0:T(8,128)S(1)} %copy-done.1, f32[256]{0:T(256)S(1)} %fusion.2), kind=kOutput, calls=%fused_computation.10 | convolution fusion | flops 3221422080 | bytes 8651776 | tf_op jit(solution)/shard_map/dot_general | solution.py:163
  40.8 2.5 %collective-permute-start.3 = (f32[128,384]{0,1:T(8,128)S(1)}, f32[128,384]{0,1:T(8,128)S(1)}, u32[]{:S(2)}, u32[]{:S(2)}) collective-permute-start(f32[128,384]{0,1:T(8,128)S(1)} %pad_maximum_fusion), channel_id=1, source_target_pairs={{0,1},{1,0},{2,3},{3,2},{4,5},{5,4},{6,7},{7,6},{8,9},{9,8},{10,11... | collective-permute-start | bytes 589832 | tf_op jit(solution)/shard_map/ppermute | solution.py:42
  43.3 4.2 %collective-permute-done.3 = f32[128,384]{0,1:T(8,128)S(1)} collective-permute-done((f32[128,384]{0,1:T(8,128)S(1)}, f32[128,384]{0,1:T(8,128)S(1)}, u32[]{:S(2)}, u32[]{:S(2)}) %collective-permute-start.3) | collective-permute-done | bytes 196640 | tf_op jit(solution)/shard_map/ppermute | solution.py:42
  47.5 1.6 collective-permute-start.4
  49.2 0.1 copy.13
  49.3 0.1 copy.6
  49.4 3.9 %collective-permute-done.4 = f32[128,384]{0,1:T(8,128)S(1)} collective-permute-done((f32[128,384]{0,1:T(8,128)S(1)}, f32[128,384]{0,1:T(8,128)S(1)}, u32[]{:S(2)}, u32[]{:S(2)}) %collective-permute-start.4) | collective-permute-done | bytes 196640 | tf_op jit(solution)/shard_map/ppermute | solution.py:42
  53.3 2.8 %collective-permute-start.5 = (f32[128,384]{0,1:T(8,128)S(1)}, f32[128,384]{0,1:T(8,128)S(1)}, u32[]{:S(2)}, u32[]{:S(2)}) collective-permute-start(f32[128,384]{0,1:T(8,128)S(1)} %add.47), channel_id=1, source_target_pairs={{0,4},{1,5},{2,6},{3,7},{4,0},{5,1},{6,2},{7,3},{8,12},{9,13},{10,... | collective-permute-start | bytes 589832 | tf_op jit(solution)/shard_map/ppermute | solution.py:42
  56.1 0.7 select_bitcast_fusion.rows_ref
  56.8 13.5 %shard_map.47 = f32[128,256]{1,0:T(8,128)} custom-call(f32[128,256]{1,0:T(8,128)} %select_bitcast_fusion.rows_ref), custom_call_target="tpu_custom_call" | custom-call | tf_op jit(solution)/shard_map/pallas_call | solution.py:148
  70.3 1.9 %collective-permute-start.2 = (f32[256,128]{0,1:T(8,128)}, f32[256,128]{0,1:T(8,128)S(1)}, u32[]{:S(2)}, u32[]{:S(2)}) collective-permute-start(f32[256,128]{0,1:T(8,128)} %bitcast.54), channel_id=1, source_target_pairs={{0,1},{1,0},{2,3},{3,2},{4,5},{5,4},{6,7},{7,6},{8,9},{9,8},{10,11... | collective-permute-start | bytes 393224 | tf_op jit(solution)/shard_map/ppermute | solution.py:32
  72.3 6.9 %fusion.3 = f32[256,256]{1,0:T(8,128)S(1)} fusion(f32[4096,256]{1,0:T(8,128)} %collective-permute-done.6, f32[8192,256]{1,0:T(8,128)} %bitcast.46, s32[]{:T(128)S(6)} %select_n.89), kind=kOutput, calls=%fused_computation.5 | convolution fusion | flops 1610612736 | bytes 8650756 | tf_op jit(solution)/shard_map/dot_general | solution.py:163
  79.3 0.1 copy.9
  79.4 0.2 collective-permute-start.7
  79.7 0.9 fusion.16.rows_ref
  80.6 13.3 %shard_map.48 = f32[128,256]{1,0:T(8,128)} custom-call(f32[128,256]{1,0:T(8,128)} %fusion.16.rows_ref), custom_call_target="tpu_custom_call" | custom-call | tf_op jit(solution)/shard_map/pallas_call | solution.py:148
  94.0 1.4 collective-permute-start.8
  95.4 1.8 %fusion.40.rows_ref = f32[128,256]{1,0:T(8,128)} fusion(f32[256,128]{0,1:T(8,128)} %bitcast.57, f32[256,256]{0,1:T(8,128)S(1)} %maximum_maximum_fusion), kind=kOutput, calls=%fused_computation.56 | convolution fusion | flops 100663296 | bytes 524288 | tf_op jit(solution)/shard_map/dot_general | solution.py:219
  97.2 13.3 %shard_map.49 = f32[128,256]{1,0:T(8,128)} custom-call(f32[128,256]{1,0:T(8,128)} %fusion.40.rows_ref), custom_call_target="tpu_custom_call" | custom-call | tf_op jit(solution)/shard_map/pallas_call | solution.py:148
  110.6 0.5 collective-permute-start.9
  111.1 8.8 %fusion.41 = f32[8192,128]{1,0:T(8,128)} fusion(f32[8192,256]{1,0:T(8,128)} %bitcast.47, f32[256,128]{0,1:T(8,128)} %bitcast.48), kind=kOutput, calls=%fused_computation.57 | convolution fusion | flops 1610612736 | bytes 12713984 | tf_op jit(solution)/shard_map/dot_general | solution.py:229
  119.9 0.6 fusion.42
  120.4 0.9 collective-permute-done.9
  121.5 0.4 fusion.43
  121.9 0.6 collective-permute-start.11
  122.5 0.6 collective-permute-done.10
  123.1 0.3 collective-permute-done.11
  123.4 0.4 collective-permute-start.13
  123.7 0.4 fusion.7
  124.1 0.3 fusion.13
  124.5 0.9 fusion.10.rows_ref
  125.4 13.3 %shard_map.50 = f32[128,256]{1,0:T(8,128)} custom-call(f32[128,256]{1,0:T(8,128)} %fusion.10.rows_ref), custom_call_target="tpu_custom_call" | custom-call | tf_op jit(solution)/shard_map/pallas_call | solution.py:148
  138.8 1.8 %fusion.9.rows_ref = f32[128,256]{1,0:T(8,128)} fusion(f32[128,256]{1,0:T(8,128)} %shard_map.50, f32[128,128]{0,1:T(8,128)S(1)} %get-tuple-element.34, f32[128,128]{0,1:T(8,128)S(1)} %bitcast.56, f32[128,128]{0,1:T(8,128)S(1)} %copy.10, f32[128,128]{0,1:T(8,128)S(1)} %get-tuple-element.33), kind=kOutput, calls=%fused_computation.19 | convolution fusion | flops 100859904 | bytes 524288 | tf_op jit(solution)/shard_map/dot_general | solution.py:158
  140.6 13.3 %shard_map.51 = f32[128,256]{1,0:T(8,128)} custom-call(f32[128,256]{1,0:T(8,128)} %fusion.9.rows_ref), custom_call_target="tpu_custom_call" | custom-call | tf_op jit(solution)/shard_map/pallas_call | solution.py:148
  153.9 0.8 dynamic-slice_bitcast_fusion
  154.8 4.5 %fusion.22 = f32[8192,64]{0,1:T(8,128)S(1)} fusion(f32[8192,128]{1,0:T(8,128)} %collective-permute-done.13, f32[256,64]{0,1:T(8,128)S(1)} %dynamic-slice_bitcast_fusion, pred[]{:T(512)S(6)} %eq.14), kind=kOutput, calls=%fused_computation.34 | convolution fusion | flops 402661376 | bytes 6356993 | tf_op jit(solution)/shard_map/dot_general | solution.py:265
  159.3 4.5 %fusion.5 = f32[8,64,8,128]{3,2,1,0:T(8,128)S(1)} fusion(f32[8192,64]{0,1:T(8,128)S(1)} %fusion.22, f32[8192,128]{1,0:T(8,128)} %fusion.41, f32[256,64]{0,1:T(8,128)S(1)} %dynamic-slice_bitcast_fusion, pred[]{:T(512)S(6)} %eq.14), kind=kOutput, calls=%fused_computation.8 | convolution fusion | flops 403185664 | bytes 8454145 | tf_op jit(solution)/shard_map/dot_general | solution.py:265
  163.8 1.6 copy.17
  (40 shorter events, 0.6 us)
Async XLA Ops:
  0.0 49.1 %copy-start = (s32[512,128]{1,0:T(8,128)S(1)}, s32[512,128]{1,0:T(8,128)}, u32[]{:S(2)}) copy-start(s32[512,128]{1,0:T(8,128)} %param.6) | copy-start | bytes 786436
  1.0 7.6 %collective-permute-start = (bf16[2,128,256]{2,1,0:T(8,128)(2,1)S(1)}, bf16[2,128,256]{2,1,0:T(8,128)(2,1)S(1)}, u32[]{:S(2)}, u32[]{:S(2)}) collective-permute-start(bf16[2,128,256]{2,1,0:T(8,128)(2,1)S(1)} %get-tuple-element.30), channel_id=1, source_target_pairs={{0,1},{1,2},{2,3},{3,4},{4,5},{5,6},{6,7},{8,9},{9,10},{10,11},{11... | collective-permute-start | bytes 393224 | tf_op jit(solution)/shard_map/ppermute | solution.py:20
  5.9 6.9 %collective-permute-start.1 = (bf16[2,128,256]{2,1,0:T(8,128)(2,1)S(1)}, bf16[2,128,256]{2,1,0:T(8,128)(2,1)S(1)}, u32[]{:S(2)}, u32[]{:S(2)}) collective-permute-start(bf16[2,128,256]{2,1,0:T(8,128)(2,1)S(1)} %get-tuple-element.29), channel_id=1, source_target_pairs={{1,0},{2,1},{3,2},{4,3},{5,4},{6,5},{7,6},{9,8},{10,9},{11,10},{12... | collective-permute-start | bytes 393224 | tf_op jit(solution)/shard_map/ppermute | solution.py:21
  8.7 4.1 %copy-start.5 = (bf16[2,128,256]{2,1,0:T(8,128)(2,1)}, bf16[2,128,256]{2,1,0:T(8,128)(2,1)S(1)}, u32[]{:S(2)}) copy-start(bf16[2,128,256]{2,1,0:T(8,128)(2,1)S(1)} %collective-permute-done.low_ref) | copy-start | bytes 393220
  12.8 0.7 copy-start.6
  26.2 6.2 %copy-start.1 = (f32[64,128,256]{2,1,0:T(8,128)S(1)}, f32[64,128,256]{2,1,0:T(8,128)}, u32[]{:S(2)}) copy-start(f32[64,128,256]{2,1,0:T(8,128)} %shard_map.46) | copy-start | bytes 25165828
  31.0 41.3 %collective-permute-start.6 = (f32[4096,256]{1,0:T(8,128)}, f32[4096,256]{1,0:T(8,128)}, u32[]{:S(2)}, u32[]{:S(2)}) collective-permute-start(f32[4096,256]{1,0:T(8,128)} %constant_dynamic-slice_fusion), channel_id=1, source_target_pairs={{0,8},{8,0},{1,9},{9,1},{2,10},{10,2},{3,11},{11,3},{4,12},{12,4},... | collective-permute-start | bytes 12582920 | tf_op jit(solution)/shard_map/ppermute | solution.py:32
  33.9 15.4 %copy-start.4 = (s32[256,128]{1,0:T(8,128)S(1)}, s32[256,128]{1,0:T(8,128)}, u32[]{:S(2)}) copy-start(s32[256,128]{1,0:T(8,128)} %param.7) | copy-start | bytes 393220
  40.8 6.7 %collective-permute-start.3 = (f32[128,384]{0,1:T(8,128)S(1)}, f32[128,384]{0,1:T(8,128)S(1)}, u32[]{:S(2)}, u32[]{:S(2)}) collective-permute-start(f32[128,384]{0,1:T(8,128)S(1)} %pad_maximum_fusion), channel_id=1, source_target_pairs={{0,1},{1,0},{2,3},{3,2},{4,5},{5,4},{6,7},{7,6},{8,9},{9,8},{10,11... | collective-permute-start | bytes 589832 | tf_op jit(solution)/shard_map/ppermute | solution.py:42
  47.5 5.7 %collective-permute-start.4 = (f32[128,384]{0,1:T(8,128)S(1)}, f32[128,384]{0,1:T(8,128)S(1)}, u32[]{:S(2)}, u32[]{:S(2)}) collective-permute-start(f32[128,384]{0,1:T(8,128)S(1)} %fusion.37), channel_id=1, source_target_pairs={{0,2},{1,3},{2,0},{3,1},{4,6},{5,7},{6,4},{7,5},{8,10},{9,11},{10,... | collective-permute-start | bytes 589832 | tf_op jit(solution)/shard_map/ppermute | solution.py:42
  53.3 18.9 %collective-permute-start.5 = (f32[128,384]{0,1:T(8,128)S(1)}, f32[128,384]{0,1:T(8,128)S(1)}, u32[]{:S(2)}, u32[]{:S(2)}) collective-permute-start(f32[128,384]{0,1:T(8,128)S(1)} %add.47), channel_id=1, source_target_pairs={{0,4},{1,5},{2,6},{3,7},{4,0},{5,1},{6,2},{7,3},{8,12},{9,13},{10,... | collective-permute-start | bytes 589832 | tf_op jit(solution)/shard_map/ppermute | solution.py:42
  70.3 9.4 %collective-permute-start.2 = (f32[256,128]{0,1:T(8,128)}, f32[256,128]{0,1:T(8,128)S(1)}, u32[]{:S(2)}, u32[]{:S(2)}) collective-permute-start(f32[256,128]{0,1:T(8,128)} %bitcast.54), channel_id=1, source_target_pairs={{0,1},{1,0},{2,3},{3,2},{4,5},{5,4},{6,7},{7,6},{8,9},{9,8},{10,11... | collective-permute-start | bytes 393224 | tf_op jit(solution)/shard_map/ppermute | solution.py:32
  72.3 7.3 %copy-start.3 = (f32[128,256]{1,0:T(8,128)S(1)}, f32[128,256]{1,0:T(8,128)}, u32[]{:S(2)}) copy-start(f32[128,256]{1,0:T(8,128)} %shard_map.47) | copy-start | bytes 393220
  79.4 14.5 %collective-permute-start.7 = (f32[256,256]{1,0:T(8,128)S(1)}, f32[256,256]{1,0:T(8,128)S(1)}, u32[]{:S(2)}, u32[]{:S(2)}) collective-permute-start(f32[256,256]{1,0:T(8,128)S(1)} %bitcast_select_fusion), channel_id=1, source_target_pairs={{0,1},{1,0},{2,3},{3,2},{4,5},{5,4},{6,7},{7,6},{8,9},{9,8},{10,11... | collective-permute-start | bytes 786440 | tf_op jit(solution)/shard_map/ppermute | solution.py:221
  94.0 16.6 %collective-permute-start.8 = (f32[256,256]{1,0:T(8,128)S(1)}, f32[256,256]{1,0:T(8,128)S(1)}, u32[]{:S(2)}, u32[]{:S(2)}) collective-permute-start(f32[256,256]{1,0:T(8,128)S(1)} %add.51), channel_id=1, source_target_pairs={{0,2},{1,3},{2,0},{3,1},{4,6},{5,7},{6,4},{7,5},{8,10},{9,11},{10,... | collective-permute-start | bytes 786440 | tf_op jit(solution)/shard_map/ppermute | solution.py:221
  110.6 9.3 %copy-start.2 = (f32[128,256]{1,0:T(8,128)S(1)}, f32[128,256]{1,0:T(8,128)}, u32[]{:S(2)}) copy-start(f32[128,256]{1,0:T(8,128)} %shard_map.49) | copy-start | bytes 393220
  110.6 10.8 %collective-permute-start.9 = (f32[256,256]{1,0:T(8,128)S(1)}, f32[256,256]{1,0:T(8,128)S(1)}, u32[]{:S(2)}, u32[]{:S(2)}) collective-permute-start(f32[256,256]{1,0:T(8,128)S(1)} %add.52), channel_id=1, source_target_pairs={{0,4},{1,5},{2,6},{3,7},{4,0},{5,1},{6,2},{7,3},{8,12},{9,13},{10,... | collective-permute-start | bytes 786440 | tf_op jit(solution)/shard_map/ppermute | solution.py:228
  119.8 3.5 %collective-permute-start.12 = (f32[256,128]{0,1:T(8,128)S(1)}, f32[256,128]{0,1:T(8,128)S(1)}, u32[]{:S(2)}, u32[]{:S(2)}) collective-permute-start(f32[256,128]{0,1:T(8,128)S(1)} %bitcast.49), channel_id=1, source_target_pairs={{0,8},{8,0},{1,9},{9,1},{2,10},{10,2},{3,11},{11,3},{4,12},{12,4},... | collective-permute-start | bytes 393224 | tf_op jit(solution)/shard_map/ppermute | solution.py:32
  121.4 1.6 collective-permute-start.10
  121.9 1.5 collective-permute-start.11
  123.4 31.4 %collective-permute-start.13 = (f32[8192,128]{1,0:T(8,128)}, f32[8192,128]{1,0:T(8,128)}, u32[]{:S(2)}, u32[]{:S(2)}) collective-permute-start(f32[8192,128]{1,0:T(8,128)} %fusion.41), channel_id=1, source_target_pairs={{0,8},{8,0},{1,9},{9,1},{2,10},{10,2},{3,11},{11,3},{4,12},{12,4},... | collective-permute-start | bytes 12582920 | tf_op jit(solution)/shard_map/ppermute | solution.py:32

commit v15 on v14

--- a/solution.py
+++ b/solution.py
@@ -87,7 +87,7 @@
 
 def fluxes(low, block, high, coefficient):
     nx, ny, ns = block.shape
-    bx = 16 if nx % 16 == 0 else nx
+    bx = 32 if nx % 32 == 0 else nx
     count = nx // bx
 
     def spec(index):

time: 166 us -> 167 us (level)
  no operation moved by 1% of the time
where the time goes in v15:
time: 167 us
  Pallas kernels  81 us (49%)
  matrix products  38.8 us (23%)
  starting transfers between devices  18.1 us (11%)
  waiting for transfers between devices  15.4 us (9%)
  local copies, waits for them, and re-layouts  10.8 us (6%)
  other arithmetic  2.41 us (1%)
    pallas_call x5, Pallas kernels, orthonormal(): pl.pallas_call(gram_schmidt_kernel, out_shape=jax.ShapeDtypeStruct(rows.s...  66.8 us
    pallas_call x1, Pallas kernels, fluxes(): pl.pallas_call(functools.partial(flux_kernel, count), grid=(count,), in_s...  14.2 us
    dot_general x2, matrix products, cross_gram(): lax.dot_general(left_rows, right_rows, (((0,), (0,)), ((), ())), precisio...  13.8 us
    dot_general x1, matrix products, on_device(): own_modes = jnp.dot(own_flux, own_basis, precision=high)  8.78 us
    ppermute x3, waiting for transfers between devices, tree_sum(): value = value + lax.ppermute(value, axis, route)  8.05 us
    ppermute x3, starting transfers between devices, tree_sum(): value = value + lax.ppermute(value, axis, route)  6.96 us
    ppermute x1, starting transfers between devices, halos(): lax.ppermute(lax.slice_in_dim(block, block.shape[0] - width, None, axis=0...  4.88 us
    dynamic_slice x1, local copies, waits for them, and re-layouts, on_device(): lax.dynamic_slice_in_dim(own_flux, (1 - member) * half_rows, half_rows, 0)  4.76 us
  transfers between devices with their start and end apart: 14, of which 7 were waited for; matrix products, arithmetic and copies ran while one was open for 20% of the time, Pallas kernels for 40%

profile of v15, /device:TPU:0, one launch (start us, length us, event | category | flops | bytes accessed | tf_op | source)
XLA Modules:
  0.0 166.8 jit_solution(5379157711215905798)
XLA Ops:
  0.0 1.0 fusion.38
  1.0 4.9 %collective-permute-start = (bf16[2,128,256]{2,1,0:T(8,128)(2,1)S(1)}, bf16[2,128,256]{2,1,0:T(8,128)(2,1)S(1)}, u32[]{:S(2)}, u32[]{:S(2)}) collective-permute-start(bf16[2,128,256]{2,1,0:T(8,128)(2,1)S(1)} %get-tuple-element.30), channel_id=1, source_target_pairs={{0,1},{1,2},{2,3},{3,4},{4,5},{5,6},{6,7},{8,9},{9,10},{10,11},{11... | collective-permute-start | bytes 393224 | tf_op jit(solution)/shard_map/ppermute | solution.py:20
  5.9 1.3 collective-permute-start.1
  7.2 1.4 collective-permute-done.low_ref
  8.7 4.1 %collective-permute-done.1.high_ref = bf16[2,128,256]{2,1,0:T(8,128)(2,1)S(1)} collective-permute-done((bf16[2,128,256]{2,1,0:T(8,128)(2,1)S(1)}, bf16[2,128,256]{2,1,0:T(8,128)(2,1)S(1)}, u32[]{:S(2)}, u32[]{:S(2)}) %collective-permute-start.1) | collective-permute-done | bytes 131104 | tf_op jit(solution)/shard_map/ppermute | solution.py:21
  12.8 0.7 copy-done.6
  13.4 14.2 %shard_map.46 = f32[64,128,256]{2,1,0:T(8,128)} custom-call(bf16[2,128,256]{2,1,0:T(8,128)(2,1)} %copy-done.5, bf16[2,128,256]{2,1,0:T(8,128)(2,1)} %copy-done.6, bf16[64,128,256]{2,1,0:T(8,128)(2,1)} %next_ref.1, bf16[64,128,256]{2,1,0:T(8,128)(2,1)} %next_ref.1, bf16[64,128,256]{2,1,0:T(8,128)(2,1)} %next_ref.1, f32[64,128]{1,0:T(8,128)} %coef_ref.1), custom_call_target="tpu_custom_call" | custom-call | tf_op jit(solution)/shard_map/pallas_call | solution.py:96
  27.6 4.8 %constant_dynamic-slice_fusion = f32[4096,256]{1,0:T(8,128)} fusion(f32[8192,256]{1,0:T(8,128)} %bitcast.45, s32[]{:T(128)S(6)} %select_n.90), kind=kLoop, calls=%fused_computation.45 | loop fusion | bytes 8388612 | tf_op jit(solution)/shard_map/dynamic_slice | solution.py:197
  32.4 1.4 copy-done.1
  33.8 1.5 fusion.2
  35.2 6.9 %fusion.6 = f32[256,256]{0,1:T(8,128)S(1)} fusion(f32[64,128,256]{2,1,0:T(8,128)S(1)} %copy-done.1, f32[256]{0:T(256)S(1)} %fusion.2), kind=kOutput, calls=%fused_computation.10 | convolution fusion | flops 3221422080 | bytes 8651776 | tf_op jit(solution)/shard_map/dot_general | solution.py:163
  42.2 2.5 %collective-permute-start.3 = (f32[128,384]{0,1:T(8,128)S(1)}, f32[128,384]{0,1:T(8,128)S(1)}, u32[]{:S(2)}, u32[]{:S(2)}) collective-permute-start(f32[128,384]{0,1:T(8,128)S(1)} %pad_maximum_fusion), channel_id=1, source_target_pairs={{0,1},{1,0},{2,3},{3,2},{4,5},{5,4},{6,7},{7,6},{8,9},{9,8},{10,11... | collective-permute-start | bytes 589832 | tf_op jit(solution)/shard_map/ppermute | solution.py:42
  44.7 4.2 %collective-permute-done.3 = f32[128,384]{0,1:T(8,128)S(1)} collective-permute-done((f32[128,384]{0,1:T(8,128)S(1)}, f32[128,384]{0,1:T(8,128)S(1)}, u32[]{:S(2)}, u32[]{:S(2)}) %collective-permute-start.3) | collective-permute-done | bytes 196640 | tf_op jit(solution)/shard_map/ppermute | solution.py:42
  48.9 1.6 collective-permute-start.4
  50.5 0.1 copy.13
  50.7 0.1 copy.6
  50.8 3.9 %collective-permute-done.4 = f32[128,384]{0,1:T(8,128)S(1)} collective-permute-done((f32[128,384]{0,1:T(8,128)S(1)}, f32[128,384]{0,1:T(8,128)S(1)}, u32[]{:S(2)}, u32[]{:S(2)}) %collective-permute-start.4) | collective-permute-done | bytes 196640 | tf_op jit(solution)/shard_map/ppermute | solution.py:42
  54.6 2.8 %collective-permute-start.5 = (f32[128,384]{0,1:T(8,128)S(1)}, f32[128,384]{0,1:T(8,128)S(1)}, u32[]{:S(2)}, u32[]{:S(2)}) collective-permute-start(f32[128,384]{0,1:T(8,128)S(1)} %add.47), channel_id=1, source_target_pairs={{0,4},{1,5},{2,6},{3,7},{4,0},{5,1},{6,2},{7,3},{8,12},{9,13},{10,... | collective-permute-start | bytes 589832 | tf_op jit(solution)/shard_map/ppermute | solution.py:42
  57.5 0.7 select_bitcast_fusion.rows_ref
  58.2 13.5 %shard_map.47 = f32[128,256]{1,0:T(8,128)} custom-call(f32[128,256]{1,0:T(8,128)} %select_bitcast_fusion.rows_ref), custom_call_target="tpu_custom_call" | custom-call | tf_op jit(solution)/shard_map/pallas_call | solution.py:148
  71.7 1.9 %collective-permute-start.2 = (f32[256,128]{0,1:T(8,128)}, f32[256,128]{0,1:T(8,128)S(1)}, u32[]{:S(2)}, u32[]{:S(2)}) collective-permute-start(f32[256,128]{0,1:T(8,128)} %bitcast.54), channel_id=1, source_target_pairs={{0,1},{1,0},{2,3},{3,2},{4,5},{5,4},{6,7},{7,6},{8,9},{9,8},{10,11... | collective-permute-start | bytes 393224 | tf_op jit(solution)/shard_map/ppermute | solution.py:32
  73.7 6.9 %fusion.3 = f32[256,256]{1,0:T(8,128)S(1)} fusion(f32[4096,256]{1,0:T(8,128)} %collective-permute-done.6, f32[8192,256]{1,0:T(8,128)} %bitcast.46, s32[]{:T(128)S(6)} %select_n.89), kind=kOutput, calls=%fused_computation.5 | convolution fusion | flops 1610612736 | bytes 8650756 | tf_op jit(solution)/shard_map/dot_general | solution.py:163
  80.7 0.1 copy.9
  80.8 0.2 collective-permute-start.7
  81.1 0.9 fusion.16.rows_ref
  82.0 13.3 %shard_map.48 = f32[128,256]{1,0:T(8,128)} custom-call(f32[128,256]{1,0:T(8,128)} %fusion.16.rows_ref), custom_call_target="tpu_custom_call" | custom-call | tf_op jit(solution)/shard_map/pallas_call | solution.py:148
  95.4 1.4 collective-permute-start.8
  96.8 1.8 %fusion.40.rows_ref = f32[128,256]{1,0:T(8,128)} fusion(f32[256,128]{0,1:T(8,128)} %bitcast.57, f32[256,256]{0,1:T(8,128)S(1)} %maximum_maximum_fusion), kind=kOutput, calls=%fused_computation.56 | convolution fusion | flops 100663296 | bytes 524288 | tf_op jit(solution)/shard_map/dot_general | solution.py:219
  98.6 13.3 %shard_map.49 = f32[128,256]{1,0:T(8,128)} custom-call(f32[128,256]{1,0:T(8,128)} %fusion.40.rows_ref), custom_call_target="tpu_custom_call" | custom-call | tf_op jit(solution)/shard_map/pallas_call | solution.py:148
  112.0 0.5 collective-permute-start.9
  112.5 8.8 %fusion.41 = f32[8192,128]{1,0:T(8,128)} fusion(f32[8192,256]{1,0:T(8,128)} %bitcast.47, f32[256,128]{0,1:T(8,128)} %bitcast.48), kind=kOutput, calls=%fused_computation.57 | convolution fusion | flops 1610612736 | bytes 12713984 | tf_op jit(solution)/shard_map/dot_general | solution.py:229
  121.3 0.6 fusion.42
  121.8 0.9 collective-permute-done.9
  122.9 0.4 fusion.43
  123.3 0.6 collective-permute-start.11
  123.9 0.6 collective-permute-done.10
  124.5 0.3 collective-permute-done.11
  124.8 0.4 collective-permute-start.13
  125.1 0.4 fusion.7
  125.5 0.3 fusion.13
  125.9 0.9 fusion.10.rows_ref
  126.8 13.3 %shard_map.50 = f32[128,256]{1,0:T(8,128)} custom-call(f32[128,256]{1,0:T(8,128)} %fusion.10.rows_ref), custom_call_target="tpu_custom_call" | custom-call | tf_op jit(solution)/shard_map/pallas_call | solution.py:148
  140.2 1.8 %fusion.9.rows_ref = f32[128,256]{1,0:T(8,128)} fusion(f32[128,256]{1,0:T(8,128)} %shard_map.50, f32[128,128]{0,1:T(8,128)S(1)} %get-tuple-element.34, f32[128,128]{0,1:T(8,128)S(1)} %bitcast.56, f32[128,128]{0,1:T(8,128)S(1)} %copy.10, f32[128,128]{0,1:T(8,128)S(1)} %get-tuple-element.33), kind=kOutput, calls=%fused_computation.19 | convolution fusion | flops 100859904 | bytes 524288 | tf_op jit(solution)/shard_map/dot_general | solution.py:158
  142.0 13.3 %shard_map.51 = f32[128,256]{1,0:T(8,128)} custom-call(f32[128,256]{1,0:T(8,128)} %fusion.9.rows_ref), custom_call_target="tpu_custom_call" | custom-call | tf_op jit(solution)/shard_map/pallas_call | solution.py:148
  155.3 0.8 dynamic-slice_bitcast_fusion
  156.2 4.5 %fusion.22 = f32[8192,64]{0,1:T(8,128)S(1)} fusion(f32[8192,128]{1,0:T(8,128)} %collective-permute-done.13, f32[256,64]{0,1:T(8,128)S(1)} %dynamic-slice_bitcast_fusion, pred[]{:T(512)S(6)} %eq.14), kind=kOutput, calls=%fused_computation.34 | convolution fusion | flops 402661376 | bytes 6356993 | tf_op jit(solution)/shard_map/dot_general | solution.py:265
  160.7 4.5 %fusion.5 = f32[8,64,8,128]{3,2,1,0:T(8,128)S(1)} fusion(f32[8192,64]{0,1:T(8,128)S(1)} %fusion.22, f32[8192,128]{1,0:T(8,128)} %fusion.41, f32[256,64]{0,1:T(8,128)S(1)} %dynamic-slice_bitcast_fusion, pred[]{:T(512)S(6)} %eq.14), kind=kOutput, calls=%fused_computation.8 | convolution fusion | flops 403185664 | bytes 8454145 | tf_op jit(solution)/shard_map/dot_general | solution.py:265
  165.2 1.6 copy.17
  (40 shorter events, 0.6 us)
Async XLA Ops:
  0.0 50.5 %copy-start = (s32[512,128]{1,0:T(8,128)S(1)}, s32[512,128]{1,0:T(8,128)}, u32[]{:S(2)}) copy-start(s32[512,128]{1,0:T(8,128)} %param.6) | copy-start | bytes 786436
  1.0 7.6 %collective-permute-start = (bf16[2,128,256]{2,1,0:T(8,128)(2,1)S(1)}, bf16[2,128,256]{2,1,0:T(8,128)(2,1)S(1)}, u32[]{:S(2)}, u32[]{:S(2)}) collective-permute-start(bf16[2,128,256]{2,1,0:T(8,128)(2,1)S(1)} %get-tuple-element.30), channel_id=1, source_target_pairs={{0,1},{1,2},{2,3},{3,4},{4,5},{5,6},{6,7},{8,9},{9,10},{10,11},{11... | collective-permute-start | bytes 393224 | tf_op jit(solution)/shard_map/ppermute | solution.py:20
  5.9 6.9 %collective-permute-start.1 = (bf16[2,128,256]{2,1,0:T(8,128)(2,1)S(1)}, bf16[2,128,256]{2,1,0:T(8,128)(2,1)S(1)}, u32[]{:S(2)}, u32[]{:S(2)}) collective-permute-start(bf16[2,128,256]{2,1,0:T(8,128)(2,1)S(1)} %get-tuple-element.29), channel_id=1, source_target_pairs={{1,0},{2,1},{3,2},{4,3},{5,4},{6,5},{7,6},{9,8},{10,9},{11,10},{12... | collective-permute-start | bytes 393224 | tf_op jit(solution)/shard_map/ppermute | solution.py:21
  8.7 4.1 %copy-start.5 = (bf16[2,128,256]{2,1,0:T(8,128)(2,1)}, bf16[2,128,256]{2,1,0:T(8,128)(2,1)S(1)}, u32[]{:S(2)}) copy-start(bf16[2,128,256]{2,1,0:T(8,128)(2,1)S(1)} %collective-permute-done.low_ref) | copy-start | bytes 393220
  12.8 0.7 copy-start.6
  27.6 6.2 %copy-start.1 = (f32[64,128,256]{2,1,0:T(8,128)S(1)}, f32[64,128,256]{2,1,0:T(8,128)}, u32[]{:S(2)}) copy-start(f32[64,128,256]{2,1,0:T(8,128)} %shard_map.46) | copy-start | bytes 25165828
  32.4 41.3 %collective-permute-start.6 = (f32[4096,256]{1,0:T(8,128)}, f32[4096,256]{1,0:T(8,128)}, u32[]{:S(2)}, u32[]{:S(2)}) collective-permute-start(f32[4096,256]{1,0:T(8,128)} %constant_dynamic-slice_fusion), channel_id=1, source_target_pairs={{0,8},{8,0},{1,9},{9,1},{2,10},{10,2},{3,11},{11,3},{4,12},{12,4},... | collective-permute-start | bytes 12582920 | tf_op jit(solution)/shard_map/ppermute | solution.py:32
  35.2 15.4 %copy-start.4 = (s32[256,128]{1,0:T(8,128)S(1)}, s32[256,128]{1,0:T(8,128)}, u32[]{:S(2)}) copy-start(s32[256,128]{1,0:T(8,128)} %param.7) | copy-start | bytes 393220
  42.2 6.7 %collective-permute-start.3 = (f32[128,384]{0,1:T(8,128)S(1)}, f32[128,384]{0,1:T(8,128)S(1)}, u32[]{:S(2)}, u32[]{:S(2)}) collective-permute-start(f32[128,384]{0,1:T(8,128)S(1)} %pad_maximum_fusion), channel_id=1, source_target_pairs={{0,1},{1,0},{2,3},{3,2},{4,5},{5,4},{6,7},{7,6},{8,9},{9,8},{10,11... | collective-permute-start | bytes 589832 | tf_op jit(solution)/shard_map/ppermute | solution.py:42
  48.9 5.7 %collective-permute-start.4 = (f32[128,384]{0,1:T(8,128)S(1)}, f32[128,384]{0,1:T(8,128)S(1)}, u32[]{:S(2)}, u32[]{:S(2)}) collective-permute-start(f32[128,384]{0,1:T(8,128)S(1)} %fusion.37), channel_id=1, source_target_pairs={{0,2},{1,3},{2,0},{3,1},{4,6},{5,7},{6,4},{7,5},{8,10},{9,11},{10,... | collective-permute-start | bytes 589832 | tf_op jit(solution)/shard_map/ppermute | solution.py:42
  54.6 18.9 %collective-permute-start.5 = (f32[128,384]{0,1:T(8,128)S(1)}, f32[128,384]{0,1:T(8,128)S(1)}, u32[]{:S(2)}, u32[]{:S(2)}) collective-permute-start(f32[128,384]{0,1:T(8,128)S(1)} %add.47), channel_id=1, source_target_pairs={{0,4},{1,5},{2,6},{3,7},{4,0},{5,1},{6,2},{7,3},{8,12},{9,13},{10,... | collective-permute-start | bytes 589832 | tf_op jit(solution)/shard_map/ppermute | solution.py:42
  71.7 9.4 %collective-permute-start.2 = (f32[256,128]{0,1:T(8,128)}, f32[256,128]{0,1:T(8,128)S(1)}, u32[]{:S(2)}, u32[]{:S(2)}) collective-permute-start(f32[256,128]{0,1:T(8,128)} %bitcast.54), channel_id=1, source_target_pairs={{0,1},{1,0},{2,3},{3,2},{4,5},{5,4},{6,7},{7,6},{8,9},{9,8},{10,11... | collective-permute-start | bytes 393224 | tf_op jit(solution)/shard_map/ppermute | solution.py:32
  73.7 7.3 %copy-start.3 = (f32[128,256]{1,0:T(8,128)S(1)}, f32[128,256]{1,0:T(8,128)}, u32[]{:S(2)}) copy-start(f32[128,256]{1,0:T(8,128)} %shard_map.47) | copy-start | bytes 393220
  80.8 14.5 %collective-permute-start.7 = (f32[256,256]{1,0:T(8,128)S(1)}, f32[256,256]{1,0:T(8,128)S(1)}, u32[]{:S(2)}, u32[]{:S(2)}) collective-permute-start(f32[256,256]{1,0:T(8,128)S(1)} %bitcast_select_fusion), channel_id=1, source_target_pairs={{0,1},{1,0},{2,3},{3,2},{4,5},{5,4},{6,7},{7,6},{8,9},{9,8},{10,11... | collective-permute-start | bytes 786440 | tf_op jit(solution)/shard_map/ppermute | solution.py:221
  95.4 16.6 %collective-permute-start.8 = (f32[256,256]{1,0:T(8,128)S(1)}, f32[256,256]{1,0:T(8,128)S(1)}, u32[]{:S(2)}, u32[]{:S(2)}) collective-permute-start(f32[256,256]{1,0:T(8,128)S(1)} %add.51), channel_id=1, source_target_pairs={{0,2},{1,3},{2,0},{3,1},{4,6},{5,7},{6,4},{7,5},{8,10},{9,11},{10,... | collective-permute-start | bytes 786440 | tf_op jit(solution)/shard_map/ppermute | solution.py:221
  112.0 9.3 %copy-start.2 = (f32[128,256]{1,0:T(8,128)S(1)}, f32[128,256]{1,0:T(8,128)}, u32[]{:S(2)}) copy-start(f32[128,256]{1,0:T(8,128)} %shard_map.49) | copy-start | bytes 393220
  112.0 10.8 %collective-permute-start.9 = (f32[256,256]{1,0:T(8,128)S(1)}, f32[256,256]{1,0:T(8,128)S(1)}, u32[]{:S(2)}, u32[]{:S(2)}) collective-permute-start(f32[256,256]{1,0:T(8,128)S(1)} %add.52), channel_id=1, source_target_pairs={{0,4},{1,5},{2,6},{3,7},{4,0},{5,1},{6,2},{7,3},{8,12},{9,13},{10,... | collective-permute-start | bytes 786440 | tf_op jit(solution)/shard_map/ppermute | solution.py:228
  121.2 3.5 %collective-permute-start.12 = (f32[256,128]{0,1:T(8,128)S(1)}, f32[256,128]{0,1:T(8,128)S(1)}, u32[]{:S(2)}, u32[]{:S(2)}) collective-permute-start(f32[256,128]{0,1:T(8,128)S(1)} %bitcast.49), channel_id=1, source_target_pairs={{0,8},{8,0},{1,9},{9,1},{2,10},{10,2},{3,11},{11,3},{4,12},{12,4},... | collective-permute-start | bytes 393224 | tf_op jit(solution)/shard_map/ppermute | solution.py:32
  122.8 1.6 collective-permute-start.10
  123.3 1.5 collective-permute-start.11
  124.8 31.4 %collective-permute-start.13 = (f32[8192,128]{1,0:T(8,128)}, f32[8192,128]{1,0:T(8,128)}, u32[]{:S(2)}, u32[]{:S(2)}) collective-permute-start(f32[8192,128]{1,0:T(8,128)} %fusion.41), channel_id=1, source_target_pairs={{0,8},{8,0},{1,9},{9,1},{2,10},{10,2},{3,11},{11,3},{4,12},{12,4},... | collective-permute-start | bytes 12582920 | tf_op jit(solution)/shard_map/ppermute | solution.py:32

commit v16 on v11

--- a/solution.py
+++ b/solution.py
@@ -87,7 +87,7 @@
 
 def fluxes(low, block, high, coefficient):
     nx, ny, ns = block.shape
-    bx = 8 if nx % 8 == 0 else nx
+    bx = 16 if nx % 16 == 0 else nx
     count = nx // bx
 
     def spec(index):

time: 167 us -> 166 us (level)
  no operation moved by 1% of the time
where the time goes in v16:
time: 166 us; the launch traced here: 165 us
  Pallas kernels  79.6 us (48%)
  matrix products  40.1 us (24%)
  starting transfers between devices  18.1 us (11%)
  waiting for transfers between devices  15.4 us (9%)
  local copies, waits for them, and re-layouts  9.24 us (6%)
  other arithmetic  2.41 us (1%)
    pallas_call x5, Pallas kernels, orthonormal(): pl.pallas_call(gram_schmidt_kernel, out_shape=jax.ShapeDtypeStruct(rows.s...  66.8 us
    dot_general x2, matrix products, cross_gram(): lax.dot_general(left_rows, right_rows, (((0,), (0,)), ((), ())), precisio...  13.8 us
    pallas_call x1, Pallas kernels, fluxes(): pl.pallas_call(functools.partial(flux_kernel, count), grid=(count,), in_s...  12.8 us
    dot_general x1, matrix products, on_device(): own_modes = jnp.dot(own_flux, own_basis, precision=high)  8.78 us
    ppermute x3, waiting for transfers between devices, tree_sum(): value = value + lax.ppermute(value, axis, route)  8.05 us
    ppermute x3, starting transfers between devices, tree_sum(): value = value + lax.ppermute(value, axis, route)  6.96 us
    dot_general x1, matrix products, on_device(): jnp.einsum('xyk,km->xym', own_modes.reshape(grid_shape), own_rotation, pr...  5.87 us
    ppermute x1, starting transfers between devices, halos(): lax.ppermute(lax.slice_in_dim(block, block.shape[0] - width, None, axis=0...  4.88 us
  transfers between devices with their start and end apart: 14, of which 7 were waited for; matrix products, arithmetic and copies ran while one was open for 20% of the time, Pallas kernels for 40%

profile of v16, /device:TPU:0, one launch (start us, length us, event | category | flops | bytes accessed | tf_op | source)
XLA Modules:
  0.0 165.1 jit_solution(11914731968625334342)
XLA Ops:
  0.0 1.0 fusion.39
  1.0 4.9 %collective-permute-start = (bf16[2,128,256]{2,1,0:T(8,128)(2,1)S(1)}, bf16[2,128,256]{2,1,0:T(8,128)(2,1)S(1)}, u32[]{:S(2)}, u32[]{:S(2)}) collective-permute-start(bf16[2,128,256]{2,1,0:T(8,128)(2,1)S(1)} %get-tuple-element.30), channel_id=1, source_target_pairs={{0,1},{1,2},{2,3},{3,4},{4,5},{5,6},{6,7},{8,9},{9,10},{10,11},{11... | collective-permute-start | bytes 393224 | tf_op jit(solution)/shard_map/ppermute | solution.py:20
  5.9 1.3 collective-permute-start.1
  7.2 1.4 collective-permute-done.low_ref
  8.7 4.1 %collective-permute-done.1.high_ref = bf16[2,128,256]{2,1,0:T(8,128)(2,1)S(1)} collective-permute-done((bf16[2,128,256]{2,1,0:T(8,128)(2,1)S(1)}, bf16[2,128,256]{2,1,0:T(8,128)(2,1)S(1)}, u32[]{:S(2)}, u32[]{:S(2)}) %collective-permute-start.1) | collective-permute-done | bytes 131104 | tf_op jit(solution)/shard_map/ppermute | solution.py:21
  12.8 0.7 copy-done.6
  13.4 12.8 %shard_map.46 = f32[64,128,256]{2,1,0:T(8,128)} custom-call(bf16[2,128,256]{2,1,0:T(8,128)(2,1)} %copy-done.5, bf16[2,128,256]{2,1,0:T(8,128)(2,1)} %copy-done.6, bf16[64,128,256]{2,1,0:T(8,128)(2,1)} %next_ref.1, bf16[64,128,256]{2,1,0:T(8,128)(2,1)} %next_ref.1, bf16[64,128,256]{2,1,0:T(8,128)(2,1)} %next_ref.1, f32[64,128]{1,0:T(8,128)} %coef_ref.1), custom_call_target="tpu_custom_call" | custom-call | tf_op jit(solution)/shard_map/pallas_call | solution.py:96
  26.2 4.8 %constant_dynamic-slice_fusion = f32[4096,256]{1,0:T(8,128)} fusion(f32[8192,256]{1,0:T(8,128)} %bitcast.48, s32[]{:T(128)S(6)} %select_n.90), kind=kLoop, calls=%fused_computation.45 | loop fusion | bytes 8388612 | tf_op jit(solution)/shard_map/dynamic_slice | solution.py:197
  31.0 1.4 copy-done.1
  32.4 1.5 fusion.2
  33.9 6.9 %fusion.5 = f32[256,256]{0,1:T(8,128)S(1)} fusion(f32[64,128,256]{2,1,0:T(8,128)S(1)} %copy-done.1, f32[256]{0:T(256)S(1)} %fusion.2), kind=kOutput, calls=%fused_computation.8 | convolution fusion | flops 3221422080 | bytes 8651776 | tf_op jit(solution)/shard_map/dot_general | solution.py:163
  40.8 2.5 %collective-permute-start.3 = (f32[128,384]{0,1:T(8,128)S(1)}, f32[128,384]{0,1:T(8,128)S(1)}, u32[]{:S(2)}, u32[]{:S(2)}) collective-permute-start(f32[128,384]{0,1:T(8,128)S(1)} %pad_maximum_fusion), channel_id=1, source_target_pairs={{0,1},{1,0},{2,3},{3,2},{4,5},{5,4},{6,7},{7,6},{8,9},{9,8},{10,11... | collective-permute-start | bytes 589832 | tf_op jit(solution)/shard_map/ppermute | solution.py:42
  43.3 4.2 %collective-permute-done.3 = f32[128,384]{0,1:T(8,128)S(1)} collective-permute-done((f32[128,384]{0,1:T(8,128)S(1)}, f32[128,384]{0,1:T(8,128)S(1)}, u32[]{:S(2)}, u32[]{:S(2)}) %collective-permute-start.3) | collective-permute-done | bytes 196640 | tf_op jit(solution)/shard_map/ppermute | solution.py:42
  47.5 1.6 collective-permute-start.4
  49.2 0.1 copy.12
  49.3 0.1 copy.6
  49.4 3.9 %collective-permute-done.4 = f32[128,384]{0,1:T(8,128)S(1)} collective-permute-done((f32[128,384]{0,1:T(8,128)S(1)}, f32[128,384]{0,1:T(8,128)S(1)}, u32[]{:S(2)}, u32[]{:S(2)}) %collective-permute-start.4) | collective-permute-done | bytes 196640 | tf_op jit(solution)/shard_map/ppermute | solution.py:42
  53.3 2.8 %collective-permute-start.5 = (f32[128,384]{0,1:T(8,128)S(1)}, f32[128,384]{0,1:T(8,128)S(1)}, u32[]{:S(2)}, u32[]{:S(2)}) collective-permute-start(f32[128,384]{0,1:T(8,128)S(1)} %add.47), channel_id=1, source_target_pairs={{0,4},{1,5},{2,6},{3,7},{4,0},{5,1},{6,2},{7,3},{8,12},{9,13},{10,... | collective-permute-start | bytes 589832 | tf_op jit(solution)/shard_map/ppermute | solution.py:42
  56.1 0.7 select_bitcast_fusion.rows_ref
  56.8 13.5 %shard_map.47 = f32[128,256]{1,0:T(8,128)} custom-call(f32[128,256]{1,0:T(8,128)} %select_bitcast_fusion.rows_ref), custom_call_target="tpu_custom_call" | custom-call | tf_op jit(solution)/shard_map/pallas_call | solution.py:148
  70.3 1.9 %collective-permute-start.2 = (f32[256,128]{0,1:T(8,128)}, f32[256,128]{0,1:T(8,128)S(1)}, u32[]{:S(2)}, u32[]{:S(2)}) collective-permute-start(f32[256,128]{0,1:T(8,128)} %bitcast.57), channel_id=1, source_target_pairs={{0,1},{1,0},{2,3},{3,2},{4,5},{5,4},{6,7},{7,6},{8,9},{9,8},{10,11... | collective-permute-start | bytes 393224 | tf_op jit(solution)/shard_map/ppermute | solution.py:32
  72.2 0.1 copy.13
  72.3 6.9 %fusion.3 = f32[256,256]{1,0:T(8,128)S(1)} fusion(f32[4096,256]{1,0:T(8,128)} %collective-permute-done.6, f32[8192,256]{1,0:T(8,128)} %bitcast.49, s32[]{:T(128)S(6)} %select_n.89), kind=kOutput, calls=%fused_computation.4 | convolution fusion | flops 1610612736 | bytes 8650756 | tf_op jit(solution)/shard_map/dot_general | solution.py:163
  79.3 0.1 copy.9
  79.4 0.2 collective-permute-start.7
  79.7 0.9 fusion.15.rows_ref
  80.6 13.3 %shard_map.48 = f32[128,256]{1,0:T(8,128)} custom-call(f32[128,256]{1,0:T(8,128)} %fusion.15.rows_ref), custom_call_target="tpu_custom_call" | custom-call | tf_op jit(solution)/shard_map/pallas_call | solution.py:148
  94.0 1.4 collective-permute-start.8
  95.4 1.8 %fusion.41.rows_ref = f32[128,256]{1,0:T(8,128)} fusion(f32[256,128]{0,1:T(8,128)} %bitcast.60, f32[256,256]{0,1:T(8,128)S(1)} %maximum_maximum_fusion), kind=kOutput, calls=%fused_computation.56 | convolution fusion | flops 100663296 | bytes 524288 | tf_op jit(solution)/shard_map/dot_general | solution.py:219
  97.2 13.3 %shard_map.49 = f32[128,256]{1,0:T(8,128)} custom-call(f32[128,256]{1,0:T(8,128)} %fusion.41.rows_ref), custom_call_target="tpu_custom_call" | custom-call | tf_op jit(solution)/shard_map/pallas_call | solution.py:148
  110.6 0.5 collective-permute-start.9
  111.1 8.8 %fusion.42 = f32[8192,128]{1,0:T(8,128)} fusion(f32[8192,256]{1,0:T(8,128)} %bitcast.50, f32[256,128]{0,1:T(8,128)} %bitcast.51), kind=kOutput, calls=%fused_computation.57 | convolution fusion | flops 1610612736 | bytes 12713984 | tf_op jit(solution)/shard_map/dot_general | solution.py:229
  119.9 0.6 fusion.43
  120.4 0.9 collective-permute-done.9
  121.5 0.4 fusion.44
  121.9 0.6 collective-permute-start.11
  122.5 0.6 collective-permute-done.10
  123.1 0.3 collective-permute-done.11
  123.4 0.4 collective-permute-start.13
  123.7 0.4 fusion.6
  124.1 0.3 fusion.12
  124.5 0.9 fusion.9.rows_ref
  125.4 13.3 %shard_map.50 = f32[128,256]{1,0:T(8,128)} custom-call(f32[128,256]{1,0:T(8,128)} %fusion.9.rows_ref), custom_call_target="tpu_custom_call" | custom-call | tf_op jit(solution)/shard_map/pallas_call | solution.py:148
  138.8 1.8 %fusion.8.rows_ref = f32[128,256]{1,0:T(8,128)} fusion(f32[128,256]{1,0:T(8,128)} %shard_map.50, f32[128,128]{0,1:T(8,128)S(1)} %get-tuple-element.34, f32[128,128]{0,1:T(8,128)S(1)} %bitcast.59, f32[128,128]{0,1:T(8,128)S(1)} %copy.10, f32[128,128]{0,1:T(8,128)S(1)} %get-tuple-element.33), kind=kOutput, calls=%fused_computation.17 | convolution fusion | flops 100859904 | bytes 524288 | tf_op jit(solution)/shard_map/dot_general | solution.py:158
  140.6 13.3 %shard_map.51 = f32[128,256]{1,0:T(8,128)} custom-call(f32[128,256]{1,0:T(8,128)} %fusion.8.rows_ref), custom_call_target="tpu_custom_call" | custom-call | tf_op jit(solution)/shard_map/pallas_call | solution.py:148
  153.9 0.8 dynamic-slice_bitcast_fusion
  154.8 4.5 %fusion.21 = f32[64,128,64]{1,2,0:T(8,128)S(1)} fusion(f32[64,128,128]{2,1,0:T(8,128)} %bitcast.12, f32[256,64]{0,1:T(8,128)S(1)} %dynamic-slice_bitcast_fusion, pred[]{:T(512)S(6)} %eq.14), kind=kOutput, calls=%fused_computation.32 | convolution fusion | flops 402661376 | bytes 6356993 | tf_op jit(solution)/shard_map/xyk,km->xym/dot_general | solution.py:268
  159.3 5.9 %convolution_add_fusion = f32[64,128,64]{1,2,0:T(8,128)} fusion(f32[64,128,64]{1,2,0:T(8,128)S(1)} %fusion.21, f32[64,128,128]{2,1,0:T(8,128)} %bitcast.8, f32[256,64]{0,1:T(8,128)S(1)} %dynamic-slice_bitcast_fusion, pred[]{:T(512)S(6)} %eq.14), kind=kOutput, calls=%fused_computation.6 | convolution fusion | flops 403185664 | bytes 8454145 | tf_op jit(solution)/shard_map/xyk,km->xym/dot_general | solution.py:266
  (39 shorter events, 0.5 us)
Async XLA Ops:
  0.0 49.1 %copy-start = (s32[512,128]{1,0:T(8,128)S(1)}, s32[512,128]{1,0:T(8,128)}, u32[]{:S(2)}) copy-start(s32[512,128]{1,0:T(8,128)} %param.6) | copy-start | bytes 786436
  1.0 7.6 %collective-permute-start = (bf16[2,128,256]{2,1,0:T(8,128)(2,1)S(1)}, bf16[2,128,256]{2,1,0:T(8,128)(2,1)S(1)}, u32[]{:S(2)}, u32[]{:S(2)}) collective-permute-start(bf16[2,128,256]{2,1,0:T(8,128)(2,1)S(1)} %get-tuple-element.30), channel_id=1, source_target_pairs={{0,1},{1,2},{2,3},{3,4},{4,5},{5,6},{6,7},{8,9},{9,10},{10,11},{11... | collective-permute-start | bytes 393224 | tf_op jit(solution)/shard_map/ppermute | solution.py:20
  5.9 6.9 %collective-permute-start.1 = (bf16[2,128,256]{2,1,0:T(8,128)(2,1)S(1)}, bf16[2,128,256]{2,1,0:T(8,128)(2,1)S(1)}, u32[]{:S(2)}, u32[]{:S(2)}) collective-permute-start(bf16[2,128,256]{2,1,0:T(8,128)(2,1)S(1)} %get-tuple-element.29), channel_id=1, source_target_pairs={{1,0},{2,1},{3,2},{4,3},{5,4},{6,5},{7,6},{9,8},{10,9},{11,10},{12... | collective-permute-start | bytes 393224 | tf_op jit(solution)/shard_map/ppermute | solution.py:21
  8.7 4.1 %copy-start.5 = (bf16[2,128,256]{2,1,0:T(8,128)(2,1)}, bf16[2,128,256]{2,1,0:T(8,128)(2,1)S(1)}, u32[]{:S(2)}) copy-start(bf16[2,128,256]{2,1,0:T(8,128)(2,1)S(1)} %collective-permute-done.low_ref) | copy-start | bytes 393220
  12.8 0.7 copy-start.6
  26.2 6.2 %copy-start.1 = (f32[64,128,256]{2,1,0:T(8,128)S(1)}, f32[64,128,256]{2,1,0:T(8,128)}, u32[]{:S(2)}) copy-start(f32[64,128,256]{2,1,0:T(8,128)} %shard_map.46) | copy-start | bytes 25165828
  31.0 41.3 %collective-permute-start.6 = (f32[4096,256]{1,0:T(8,128)}, f32[4096,256]{1,0:T(8,128)}, u32[]{:S(2)}, u32[]{:S(2)}) collective-permute-start(f32[4096,256]{1,0:T(8,128)} %constant_dynamic-slice_fusion), channel_id=1, source_target_pairs={{0,8},{8,0},{1,9},{9,1},{2,10},{10,2},{3,11},{11,3},{4,12},{12,4},... | collective-permute-start | bytes 12582920 | tf_op jit(solution)/shard_map/ppermute | solution.py:32
  33.9 15.4 %copy-start.4 = (s32[256,128]{1,0:T(8,128)S(1)}, s32[256,128]{1,0:T(8,128)}, u32[]{:S(2)}) copy-start(s32[256,128]{1,0:T(8,128)} %param.7) | copy-start | bytes 393220
  40.8 6.7 %collective-permute-start.3 = (f32[128,384]{0,1:T(8,128)S(1)}, f32[128,384]{0,1:T(8,128)S(1)}, u32[]{:S(2)}, u32[]{:S(2)}) collective-permute-start(f32[128,384]{0,1:T(8,128)S(1)} %pad_maximum_fusion), channel_id=1, source_target_pairs={{0,1},{1,0},{2,3},{3,2},{4,5},{5,4},{6,7},{7,6},{8,9},{9,8},{10,11... | collective-permute-start | bytes 589832 | tf_op jit(solution)/shard_map/ppermute | solution.py:42
  47.5 5.7 %collective-permute-start.4 = (f32[128,384]{0,1:T(8,128)S(1)}, f32[128,384]{0,1:T(8,128)S(1)}, u32[]{:S(2)}, u32[]{:S(2)}) collective-permute-start(f32[128,384]{0,1:T(8,128)S(1)} %fusion.38), channel_id=1, source_target_pairs={{0,2},{1,3},{2,0},{3,1},{4,6},{5,7},{6,4},{7,5},{8,10},{9,11},{10,... | collective-permute-start | bytes 589832 | tf_op jit(solution)/shard_map/ppermute | solution.py:42
  53.3 18.9 %collective-permute-start.5 = (f32[128,384]{0,1:T(8,128)S(1)}, f32[128,384]{0,1:T(8,128)S(1)}, u32[]{:S(2)}, u32[]{:S(2)}) collective-permute-start(f32[128,384]{0,1:T(8,128)S(1)} %add.47), channel_id=1, source_target_pairs={{0,4},{1,5},{2,6},{3,7},{4,0},{5,1},{6,2},{7,3},{8,12},{9,13},{10,... | collective-permute-start | bytes 589832 | tf_op jit(solution)/shard_map/ppermute | solution.py:42
  70.3 9.4 %collective-permute-start.2 = (f32[256,128]{0,1:T(8,128)}, f32[256,128]{0,1:T(8,128)S(1)}, u32[]{:S(2)}, u32[]{:S(2)}) collective-permute-start(f32[256,128]{0,1:T(8,128)} %bitcast.57), channel_id=1, source_target_pairs={{0,1},{1,0},{2,3},{3,2},{4,5},{5,4},{6,7},{7,6},{8,9},{9,8},{10,11... | collective-permute-start | bytes 393224 | tf_op jit(solution)/shard_map/ppermute | solution.py:32
  72.3 7.3 %copy-start.3 = (f32[128,256]{1,0:T(8,128)S(1)}, f32[128,256]{1,0:T(8,128)}, u32[]{:S(2)}) copy-start(f32[128,256]{1,0:T(8,128)} %shard_map.47) | copy-start | bytes 393220
  79.4 14.5 %collective-permute-start.7 = (f32[256,256]{1,0:T(8,128)S(1)}, f32[256,256]{1,0:T(8,128)S(1)}, u32[]{:S(2)}, u32[]{:S(2)}) collective-permute-start(f32[256,256]{1,0:T(8,128)S(1)} %bitcast_select_fusion), channel_id=1, source_target_pairs={{0,1},{1,0},{2,3},{3,2},{4,5},{5,4},{6,7},{7,6},{8,9},{9,8},{10,11... | collective-permute-start | bytes 786440 | tf_op jit(solution)/shard_map/ppermute | solution.py:221
  94.0 16.6 %collective-permute-start.8 = (f32[256,256]{1,0:T(8,128)S(1)}, f32[256,256]{1,0:T(8,128)S(1)}, u32[]{:S(2)}, u32[]{:S(2)}) collective-permute-start(f32[256,256]{1,0:T(8,128)S(1)} %add.51), channel_id=1, source_target_pairs={{0,2},{1,3},{2,0},{3,1},{4,6},{5,7},{6,4},{7,5},{8,10},{9,11},{10,... | collective-permute-start | bytes 786440 | tf_op jit(solution)/shard_map/ppermute | solution.py:221
  110.6 9.3 %copy-start.2 = (f32[128,256]{1,0:T(8,128)S(1)}, f32[128,256]{1,0:T(8,128)}, u32[]{:S(2)}) copy-start(f32[128,256]{1,0:T(8,128)} %shard_map.49) | copy-start | bytes 393220
  110.6 10.8 %collective-permute-start.9 = (f32[256,256]{1,0:T(8,128)S(1)}, f32[256,256]{1,0:T(8,128)S(1)}, u32[]{:S(2)}, u32[]{:S(2)}) collective-permute-start(f32[256,256]{1,0:T(8,128)S(1)} %add.52), channel_id=1, source_target_pairs={{0,4},{1,5},{2,6},{3,7},{4,0},{5,1},{6,2},{7,3},{8,12},{9,13},{10,... | collective-permute-start | bytes 786440 | tf_op jit(solution)/shard_map/ppermute | solution.py:228
  119.8 3.5 %collective-permute-start.12 = (f32[256,128]{0,1:T(8,128)S(1)}, f32[256,128]{0,1:T(8,128)S(1)}, u32[]{:S(2)}, u32[]{:S(2)}) collective-permute-start(f32[256,128]{0,1:T(8,128)S(1)} %bitcast.52), channel_id=1, source_target_pairs={{0,8},{8,0},{1,9},{9,1},{2,10},{10,2},{3,11},{11,3},{4,12},{12,4},... | collective-permute-start | bytes 393224 | tf_op jit(solution)/shard_map/ppermute | solution.py:32
  121.4 1.6 collective-permute-start.10
  121.9 1.5 collective-permute-start.11
  123.4 31.4 %collective-permute-start.13 = (f32[8192,128]{1,0:T(8,128)}, f32[8192,128]{1,0:T(8,128)}, u32[]{:S(2)}, u32[]{:S(2)}) collective-permute-start(f32[8192,128]{1,0:T(8,128)} %fusion.42), channel_id=1, source_target_pairs={{0,8},{8,0},{1,9},{9,1},{2,10},{10,2},{3,11},{11,3},{4,12},{12,4},... | collective-permute-start | bytes 12582920 | tf_op jit(solution)/shard_map/ppermute | solution.py:32
